TPU v7x, 32 devices: a whole 2x2x4 slice. The times are simulated.
32 devices in a mesh: dp: 8 (over y, x, core), fsdp: 4 (over z).
Axes of the slice: x: 2, y: 2, z: 4, core: 2. Of those that a mesh axis runs over, the one named last changes fastest.
Arguments:
- tokens: bfloat16 [64, 256, 768], P(('dp', 'fsdp')), may hold values from -6 to 6
- band_waves: int32 [64, 13], P(('dp', 'fsdp')), may hold values from 0 to 128, as said below
- visible_slot: int32 [64, 256], P(('dp', 'fsdp')), may hold values from 0 to 1023, as said below
- wave_table: bfloat16 [128, 768], P(('dp', 'fsdp')), may hold values from -1.75 to 1.75
- norm1_gain: bfloat16 [768], P(('dp', 'fsdp')), may hold values from 0.5 to 1.5
- norm1_bias: bfloat16 [768], P(('dp', 'fsdp')), may hold values from -1.75 to 1.75
- qkv_weight: bfloat16 [768, 2304], P(('dp', 'fsdp')), may hold values from -0.3125 to 0.3125
- out_weight: bfloat16 [768, 768], P(('dp', 'fsdp')), may hold values from -0.875 to 0.875
- norm2_gain: bfloat16 [768], P(('dp', 'fsdp')), may hold values from 0.5 to 1.5
- norm2_bias: bfloat16 [768], P(('dp', 'fsdp')), may hold values from -1.75 to 1.75
- mlp_in: bfloat16 [768, 3072], P(('dp', 'fsdp')), may hold values from -0.21875 to 0.21875
- mlp_in_bias: bfloat16 [3072], P(('dp', 'fsdp')), may hold values from -3 to 3
- mlp_out: bfloat16 [3072, 768], P(('dp', 'fsdp')), may hold values from -0.15625 to 0.15625
- mlp_out_bias: bfloat16 [768], P(('dp', 'fsdp')), may hold values from -1.75 to 1.75
- dec_weight: bfloat16 [768, 512], P(('dp', 'fsdp')), may hold values from -0.21875 to 0.21875
- dec_bias: bfloat16 [512], P(('dp', 'fsdp')), may hold values from -1.75 to 1.75
- mask_token: bfloat16 [512], P(('dp', 'fsdp')), may hold values from -6 to 6
- cot_decoded: bfloat16 [64, 1024, 512], P(None, ('dp', 'fsdp')), may hold values from -6 to 6
Outputs:
- decoded: bfloat16 [64, 1024, 512], P(None, ('dp', 'fsdp'))
- grad_tokens: float32 [64, 256, 768], P(('dp', 'fsdp'))
- grad_wave_table: float32 [128, 768], P(('dp', 'fsdp'))
- grad_norm1_gain: float32 [768], P(('dp', 'fsdp'))
- grad_norm1_bias: float32 [768], P(('dp', 'fsdp'))
- grad_qkv_weight: float32 [768, 2304], P(('dp', 'fsdp'))
- grad_out_weight: float32 [768, 768], P(('dp', 'fsdp'))
- grad_norm2_gain: float32 [768], P(('dp', 'fsdp'))
- grad_norm2_bias: float32 [768], P(('dp', 'fsdp'))
- grad_mlp_in: float32 [768, 3072], P(('dp', 'fsdp'))
- grad_mlp_in_bias: float32 [3072], P(('dp', 'fsdp'))
- grad_mlp_out: float32 [3072, 768], P(('dp', 'fsdp'))
- grad_mlp_out_bias: float32 [768], P(('dp', 'fsdp'))
- grad_dec_weight: float32 [768, 512], P(('dp', 'fsdp'))
- grad_dec_bias: float32 [512], P(('dp', 'fsdp'))
- grad_mask_token: float32 [512], P(('dp', 'fsdp'))
Inputs may be any that keep to these rules, and one draw needn't show every extreme that they name: `band_waves`: the first 4 entries of a row are ids below 128; an entry equal to 128 marks an unused band slot, so a chip has 4 to 13 bands; ids may repeat. `visible_slot`: the 256 entries of a row are distinct; the other slots of that chip hold the mask token.
All inputs are finite; a program needn't handle non-finite values.
Results may differ from a plain program's by a relative error of at most 0.012.
The roundings to bfloat16 on the way count: a program that leaves them out, or rounds other values in their place, can miss the bound.
Values may be sent and summed in bfloat16 or wider, within the bound.
No kernel may reach another device: no remote copies, remote signals or barrier semaphores. Data moves between devices by JAX's collectives and lax.ppermute only.
A program may use at most 128 MiB of HBM per device.

v0:
```python
import numpy as np
import jax
import jax.numpy as jnp
from jax import lax
from jax.sharding import PartitionSpec as P

D = 768
HD = 64
DEC = 512
WAVES = 128
L = 1024

NORM_EPSILON = 1e-05
ROOT_HALF = 0.7071067811865476
INVERSE_ROOT_TAU = 0.3989422804014327
HIGH_PRECISION = lax.Precision.HIGHEST
AX = ("dp", "fsdp")


def product(left_op, right_op):
    return jnp.dot(left_op, right_op, preferred_element_type=jnp.float32)


def inner_rows(left_op, right_op):
    return lax.dot_general(
        left_op, right_op, (((0,), (0,)), ((), ())), preferred_element_type=jnp.float32
    )


def outer_cols(left_op, right_op):
    return lax.dot_general(
        left_op, right_op, (((1,), (1,)), ((), ())), preferred_element_type=jnp.float32
    )


def norm_forward(residual, gain, shift):
    mean_val = jnp.mean(residual, axis=-1, keepdims=True)
    centered = residual - mean_val
    variance = jnp.mean(centered * centered, axis=-1, keepdims=True)
    inverse = lax.rsqrt(variance + NORM_EPSILON)
    normed = centered * inverse
    return (normed * gain + shift, normed, inverse)


def norm_backward(incoming, normed, inverse, gain):
    scaled = incoming * gain
    first_mean = jnp.mean(scaled, axis=-1, keepdims=True)
    second_mean = jnp.mean(scaled * normed, axis=-1, keepdims=True)
    grad_input = inverse * (scaled - first_mean - normed * second_mean)
    return (grad_input, jnp.sum(incoming * normed, axis=0), jnp.sum(incoming, axis=0))


def gelu_value(hidden):
    return 0.5 * hidden * (1.0 + lax.erf(hidden * ROOT_HALF))


def gelu_slope(hidden):
    return (
        0.5 * (1.0 + lax.erf(hidden * ROOT_HALF))
        + hidden * jnp.exp(-0.5 * hidden * hidden) * INVERSE_ROOT_TAU
    )


def core_bit_of(mesh):
    flat = list(mesh.devices.reshape(-1))
    cores = [d.core_on_chip for d in flat]
    stride = 1
    while stride < len(flat) and cores[stride] == cores[0]:
        stride *= 2
    return stride.bit_length() - 1


def halving_order(n_bits, core_bit):
    rest = [b for b in reversed(range(n_bits)) if b != core_bit]
    if len(rest) >= 2:
        rest[-2:] = rest[-2:][::-1]
    return [core_bit] + rest


def rs_chain(grad, n_bits, order):
    n_dev = 2 ** n_bits
    me = lax.axis_index(AX)
    rows = grad.shape[0] // n_dev
    current = grad.reshape((2,) * n_bits + (rows,) + grad.shape[1:])
    for bit in order:
        axis = n_bits - 1 - bit
        mine = (me >> bit) & 1
        keep = lax.dynamic_slice_in_dim(current, mine, 1, axis=axis)
        send = lax.dynamic_slice_in_dim(current, 1 - mine, 1, axis=axis)
        moved = lax.ppermute(
            send.astype(jnp.bfloat16), AX, [(i, i ^ (1 << bit)) for i in range(n_dev)]
        )
        current = keep + moved.astype(jnp.float32)
    return current.reshape((rows,) + grad.shape[1:])


def pack_rows(arrays, n_dev, dtype):
    flat = [a.reshape(n_dev, -1).astype(dtype) for a in arrays]
    widths = [f.shape[1] for f in flat]
    padded = -sum(widths) % 1024
    flat.append(jnp.zeros((n_dev, padded), dtype))
    packed = jnp.concatenate(flat, axis=1)
    return packed.reshape(n_dev, 8, -1), widths


def unpack_rows(packed, arrays, widths, n_dev, leading):
    flat = packed.reshape(packed.shape[0], -1)
    out = []
    offset = 0
    for a, width in zip(arrays, widths):
        piece = flat[:, offset : offset + width]
        out.append(piece.reshape((leading * a.shape[0] // n_dev,) + a.shape[1:]))
        offset += width
    return out


def attend(queries, key_rows, value_rows):
    score_scale = HD ** (-0.5)
    scores = (
        jnp.einsum("cqhd,ckhd->chqk", queries, key_rows, preferred_element_type=jnp.float32)
        * score_scale
    )
    row_peak = jnp.max(scores, axis=-1, keepdims=True)
    exponents = jnp.exp(scores - row_peak)
    row_total = jnp.sum(exponents, axis=-1, keepdims=True)
    soft_full = exponents / row_total
    soft_low = soft_full.astype(jnp.bfloat16)
    mixture = jnp.einsum(
        "chqk,ckhd->cqhd", soft_low, value_rows, preferred_element_type=jnp.float32
    )
    return mixture.astype(jnp.bfloat16), soft_full, soft_low


def attend_back(queries, key_rows, value_rows, soft_full, soft_low, grad_mixture):
    score_scale = HD ** (-0.5)
    grad_values = jnp.einsum(
        "chqk,cqhd->ckhd", soft_low, grad_mixture, preferred_element_type=jnp.float32
    )
    grad_soft = jnp.einsum(
        "cqhd,ckhd->chqk", grad_mixture, value_rows, preferred_element_type=jnp.float32
    )
    row_delta = jnp.sum(grad_soft * soft_full, axis=-1, keepdims=True)
    grad_scores = (soft_full * (grad_soft - row_delta)).astype(jnp.bfloat16)
    grad_queries = (
        jnp.einsum("chqk,ckhd->cqhd", grad_scores, key_rows, preferred_element_type=jnp.float32)
        * score_scale
    )
    grad_keys = (
        jnp.einsum("chqk,cqhd->ckhd", grad_scores, queries, preferred_element_type=jnp.float32)
        * score_scale
    )
    return grad_queries, grad_keys, grad_values


def make_local(n_bits, order):
    n_dev = 2 ** n_bits

    def local(
        tokens,
        band_waves,
        visible_slot,
        wave_table,
        norm1_gain,
        norm1_bias,
        qkv_weight,
        out_weight,
        norm2_gain,
        norm2_bias,
        mlp_in,
        mlp_in_bias,
        mlp_out,
        mlp_out_bias,
        dec_weight,
        dec_bias,
        mask_token,
        cot_decoded,
    ):
        shards = (
            wave_table,
            norm1_gain,
            norm1_bias,
            qkv_weight,
            out_weight,
            norm2_gain,
            norm2_bias,
            mlp_in,
            mlp_in_bias,
            mlp_out,
            mlp_out_bias,
            dec_weight,
            dec_bias,
            mask_token,
        )
        small = (wave_table, norm1_gain, norm1_bias, norm2_gain, norm2_bias, mlp_in_bias,
                 mlp_out_bias, dec_bias, mask_token)
        packed_small, small_widths = pack_rows(
            [a.reshape(1, -1) for a in small], 1, jnp.bfloat16
        )
        gathered_small = lax.all_gather(packed_small, AX, axis=0, tiled=True)
        (wave_full, gain_one, shift_one, gain_two, shift_two, inner_bias, outer_bias,
         dec_shift, mask_full) = unpack_rows(gathered_small, small, small_widths, 1, n_dev)
        wide = (qkv_weight, out_weight, mlp_in, dec_weight)
        wide_cols = [a.shape[1] for a in wide]
        gathered_wide = lax.all_gather(jnp.concatenate(wide, axis=1), AX, axis=0, tiled=True)
        wide_full = []
        offset = 0
        for cols in wide_cols:
            wide_full.append(gathered_wide[:, offset : offset + cols])
            offset += cols
        qkv_full, out_full, inner_full, dec_full = wide_full
        outer_full = lax.all_gather(mlp_out, AX, axis=0, tiled=True)

        chip_count, vis_len, feature_width = tokens.shape
        row_count = chip_count * vis_len
        heads = feature_width // HD
        counts = jnp.sum(
            (band_waves[:, :, None] == jnp.arange(WAVES, dtype=jnp.int32)[None, None, :]).astype(
                jnp.float32
            ),
            axis=1,
        )
        spectral = jnp.dot(
            counts.astype(jnp.bfloat16), wave_full, preferred_element_type=jnp.float32
        )
        residual = (tokens.astype(jnp.float32) + spectral[:, None, :]).reshape(row_count, D)
        norm_out_one, normed_one, inverse_one = norm_forward(
            residual, gain_one.astype(jnp.float32), shift_one.astype(jnp.float32)
        )
        act_one = norm_out_one.astype(jnp.bfloat16)
        qkv_vals = product(act_one, qkv_full).astype(jnp.bfloat16)
        head_shape = (chip_count, vis_len, heads, HD)
        queries = qkv_vals[:, :D].reshape(head_shape)
        key_rows = qkv_vals[:, D : 2 * D].reshape(head_shape)
        value_rows = qkv_vals[:, 2 * D :].reshape(head_shape)
        mixture4, soft_full, soft_low = attend(queries, key_rows, value_rows)
        mixture = mixture4.reshape(row_count, D)
        res_one = residual + product(mixture, out_full)
        norm_out_two, normed_two, inverse_two = norm_forward(
            res_one, gain_two.astype(jnp.float32), shift_two.astype(jnp.float32)
        )
        act_two = norm_out_two.astype(jnp.bfloat16)
        hidden = product(act_two, inner_full) + inner_bias.astype(jnp.float32)
        active = gelu_value(hidden).astype(jnp.bfloat16)
        res_two = res_one + (product(active, outer_full) + outer_bias.astype(jnp.float32))
        enc_low = res_two.astype(jnp.bfloat16)
        projected = (product(enc_low, dec_full) + dec_shift.astype(jnp.float32)).astype(
            jnp.bfloat16
        )
        slot_ids = jnp.arange(L, dtype=jnp.int32)
        one_hot = (visible_slot[:, None, :] == slot_ids[None, :, None]).astype(jnp.bfloat16)
        filled_vis = jnp.einsum(
            "csi,cie->cse",
            one_hot,
            projected.reshape(chip_count, vis_len, DEC),
            preferred_element_type=jnp.float32,
        )
        has_row = jnp.sum(one_hot.astype(jnp.float32), axis=2, keepdims=True) > 0.5
        filled = jnp.where(has_row, filled_vis, mask_full.astype(jnp.float32)[None, None, :])
        filled = filled.astype(jnp.bfloat16)
        decoded = lax.all_to_all(filled, AX, split_axis=1, concat_axis=0, tiled=True)
        grad_full = lax.all_to_all(cot_decoded, AX, split_axis=0, concat_axis=1, tiled=True)

        grad_vis_low = (
            jnp.einsum("csi,cse->cie", one_hot, grad_full, preferred_element_type=jnp.float32)
            .astype(jnp.bfloat16)
            .reshape(row_count, DEC)
        )
        grad_vis = grad_vis_low.astype(jnp.float32)
        grad_mask_token = jnp.sum(
            jnp.where(has_row, 0.0, grad_full.astype(jnp.float32)), axis=(0, 1)
        )
        grad_dec_bias = jnp.sum(grad_vis, axis=0)
        grad_dec_weight = inner_rows(enc_low, grad_vis_low)
        grad_res_two = outer_cols(grad_vis_low, dec_full)
        grad_ffo = grad_res_two.astype(jnp.bfloat16)
        grad_mlp_out_bias = jnp.sum(grad_ffo.astype(jnp.float32), axis=0)
        grad_mlp_out = inner_rows(active, grad_ffo)
        grad_hidden = (outer_cols(grad_ffo, outer_full) * gelu_slope(hidden)).astype(jnp.bfloat16)
        grad_mlp_in_bias = jnp.sum(grad_hidden.astype(jnp.float32), axis=0)
        grad_mlp_in = inner_rows(act_two, grad_hidden)
        grad_act_two = outer_cols(grad_hidden, inner_full)
        grad_norm_two, grad_norm2_gain, grad_norm2_bias = norm_backward(
            grad_act_two, normed_two, inverse_two, gain_two.astype(jnp.float32)
        )
        grad_res_one = grad_res_two + grad_norm_two
        grad_att = grad_res_one.astype(jnp.bfloat16)
        grad_out_weight = inner_rows(mixture, grad_att)
        grad_mixed = outer_cols(grad_att, out_full).astype(jnp.bfloat16).reshape(head_shape)
        grad_queries, grad_keys, grad_values = attend_back(
            queries, key_rows, value_rows, soft_full, soft_low, grad_mixed
        )
        grad_qkv = jnp.concatenate(
            [
                grad_queries.reshape(row_count, D),
                grad_keys.reshape(row_count, D),
                grad_values.reshape(row_count, D),
            ],
            axis=1,
        ).astype(jnp.bfloat16)
        grad_qkv_weight = inner_rows(act_one, grad_qkv)
        grad_act_one = outer_cols(grad_qkv, qkv_full)
        grad_norm_one, grad_norm1_gain, grad_norm1_bias = norm_backward(
            grad_act_one, normed_one, inverse_one, gain_one.astype(jnp.float32)
        )
        grad_tokens = (grad_res_one + grad_norm_one).reshape(chip_count, vis_len, D)
        chip_sums = jnp.sum(grad_tokens, axis=1)
        grad_wave_table = lax.dot_general(
            counts, chip_sums, (((0,), (0,)), ((), ())), precision=HIGH_PRECISION
        )
        small_grads = (grad_wave_table, grad_norm1_gain, grad_norm1_bias, grad_norm2_gain,
                       grad_norm2_bias, grad_mlp_in_bias, grad_mlp_out_bias, grad_dec_bias,
                       grad_mask_token)
        packed_sg, sg_widths = pack_rows(small_grads, n_dev, jnp.float32)
        reduced_sg = rs_chain(packed_sg, n_bits, order)
        (sum_wave, sum_g1, sum_b1, sum_g2, sum_b2, sum_ib, sum_ob, sum_db,
         sum_mask) = unpack_rows(reduced_sg, small_grads, sg_widths, n_dev, 1)
        sum_dec = rs_chain(grad_dec_weight, n_bits, order)
        sum_mlp_out = rs_chain(grad_mlp_out, n_bits, order)
        sum_mlp_in = rs_chain(grad_mlp_in, n_bits, order)
        sum_out = rs_chain(grad_out_weight, n_bits, order)
        sum_qkv = rs_chain(grad_qkv_weight, n_bits, order)
        summed = (sum_wave, sum_g1, sum_b1, sum_qkv, sum_out, sum_g2, sum_b2, sum_mlp_in,
                  sum_ib, sum_mlp_out, sum_ob, sum_dec, sum_db, sum_mask)
        return (decoded, grad_tokens, *summed)

    return local


def solution(mesh):
    n_dev = mesh.devices.size
    n_bits = n_dev.bit_length() - 1
    order = halving_order(n_bits, core_bit_of(mesh))
    placed = (
        P(AX, None, None),
        P(AX, None),
        P(AX, None),
        P(AX, None),
        P(AX),
        P(AX),
        P(AX, None),
        P(AX, None),
        P(AX),
        P(AX),
        P(AX, None),
        P(AX),
        P(AX, None),
        P(AX),
        P(AX, None),
        P(AX),
        P(AX),
        P(None, AX, None),
    )
    return jax.shard_map(
        make_local(n_bits, order),
        mesh=mesh,
        in_specs=placed,
        out_specs=(
            P(None, AX, None),
            P(AX, None, None),
            P(AX, None),
            P(AX),
            P(AX),
            P(AX, None),
            P(AX, None),
            P(AX),
            P(AX),
            P(AX, None),
            P(AX),
            P(AX, None),
            P(AX),
            P(AX, None),
            P(AX),
            P(AX),
        ),
        check_vma=False,
    )
```

profile of v0, /device:TPU:0, one launch (start us, length us, event | category | flops | bytes accessed | tf_op | source)
XLA Modules:
  0.0 442.5 jit_solution(17144914329273598163)
XLA Ops:
  9.1 7.5 %all-to-all-start.1 = ((bf16[64,32,512]{2,1,0:T(8,128)(2,1)}), bf16[64,32,512]{2,1,0:T(8,128)(2,1)}, u32[]{:S(2)}, u32[]{:S(2)}) async-start(bf16[64,32,512]{2,1,0:T(8,128)(2,1)} %param.35), calls=%async_computation.1 | async-start | bytes 4194304 | tf_op jit(solution)/shard_map/all_to_all | solution.py:261
  17.7 130.4 %all_gather.9 = bf16[32,8,512]{2,1,0:T(8,128)(2,1)S(1)} all-gather(bf16[1,8,512]{2,1,0:T(8,128)(2,1)S(1)} %reshape.336), channel_id=1, replica_groups=mesh['dp'=8,'fsdp'=4] {'dp','fsdp'}, dimensions={0}, use_global_device_ids=true | all-gather | bytes 270336 | tf_op jit(solution)/shard_map/all_gather | solution.py:199
  152.1 1.8 copy.126
  155.6 2.1 select_reduce_fusion
  157.9 4.0 convolution_convert_fusion
  162.9 2.3 copy.115
  165.2 3.0 reshape.340
  169.3 2.2 reshape.342
  172.7 2.2 reshape.341
  176.0 4.8 %fusion.78 = (f32[2,12,256]{2,1,0:T(8,128)S(1)}, f32[2,12,256,256]{2,3,1,0:T(8,128)S(1)}) fusion(f32[2,12,256,256]{2,3,1,0:T(8,128)S(1)} %fusion.58), kind=kOutput, calls=%fused_computation.194 | output fusion | flops 6291711 | bytes 12607488 | tf_op jit(solution)/shard_map/sub | solution.py:124
  181.4 2.6 copy-done
  187.7 5.7 %multiply_convert_fusion.1 = (bf16[512,3072]{1,0:T(8,128)(2,1)}, f32[512,3072]{1,0:T(8,128)}) fusion(f32[3072]{0:T(1024)S(1)} %reshape.380, bf16[768,6656]{1,0:T(8,128)(2,1)S(1)} %bitcast.200, f32[512,768]{1,0:T(8,128)S(1)} %get-tuple-element.50, f32[768]{0:T(1024)S(1)} %reshape.379, f32[768]{0:T(1024)S(1)} %reshape.378, f32[512]{0:T(512)S(1)} %add_rsqrt_fusion, ...), kind=kOutput, calls=%fused_computation.11 | convolution fusion | flops 2427322368 | bytes 15753216 | tf_op jit(solution)/shard_map/dot_general | solution.py:21
  193.4 7.6 %convert_reduce_fusion = (f32[3072]{0:T(1024)S(1)}, bf16[512,3072]{1,0:T(8,128)(2,1)S(1)}) fusion(f32[512,3072]{1,0:T(8,128)} %get-tuple-element.52, f32[3072]{0:T(1024)S(1)} %reshape.380, bf16[3072,768]{1,0:T(8,128)(2,1)} %all-gather.5.cloned.1.call-done, f32[512,768]{1,0:T(8,128)S(1)} %fusion.49), kind=kOutput, calls=%fused_computation.8 | convolution fusion | flops 2436756480 | bytes 15753216 | tf_op jit(solution)/shard_map/dot_general | solution.py:31
  201.1 6.5 %multiply_reduce_fusion.2 = (f32[768]{0:T(1024)S(1)}, f32[512]{0:T(512)S(1)}, f32[512]{0:T(512)S(1)}, f32[768]{0:T(1024)S(1)}, f32[512,768]{1,0:T(8,128)S(1)}) fusion(f32[512,768]{1,0:T(8,128)S(1)} %get-tuple-element.50, f32[512]{0:T(512)S(1)} %add_rsqrt_fusion, f32[512]{0:T(512)S(1)} %broadcast_multiply_fusion.4, f32[768]{0:T(1024)S(1)} %reshape.378, ...), kind=kOutput, calls=%fused_computation.51 | convolution fusion | flops 2419455488 | bytes 11027456 | tf_op jit(solution)/shard_map/dot_general | solution.py:31
  209.4 2.1 convolution_convert_fusion.1
  212.8 4.3 fusion.33
  217.6 3.8 multiply_reduce_fusion
  221.4 4.3 multiply_convert_fusion
  228.5 5.7 %fusion.75 = f32[768,3072]{1,0:T(8,128)} fusion(bf16[512,3072]{1,0:T(8,128)(2,1)S(1)} %copy-done.44, f32[512,768]{1,0:T(8,128)S(1)} %copy-done.6, f32[768]{0:T(1024)S(1)} %reshape.379, f32[768]{0:T(1024)S(1)} %reshape.378, f32[512]{0:T(512)S(1)} %add_rsqrt_fusion, f32[512]{0:T(512)S(1)} %broadcast_multiply_fusion.4), kind=kOutput, calls=%fused_computation.191 | convolution fusion | flops 2417885184 | bytes 14166016 | tf_op jit(solution)/shard_map/dot_general | solution.py:25
  234.1 5.0 %fusion.70 = f32[3072,768]{1,0:T(8,128)} fusion(bf16[512,3072]{1,0:T(8,128)(2,1)S(1)} %copy-done.22, f32[512,768]{1,0:T(8,128)S(1)} %copy-done.4), kind=kOutput, calls=%fused_computation.186 | convolution fusion | flops 2416312320 | bytes 14155776 | tf_op jit(solution)/shard_map/dot_general | solution.py:25
  239.2 2.6 add_convert_fusion
  241.8 2.0 fusion.41
  245.1 3.5 copy.124
  248.5 3.7 all-to-all-start
  258.8 5.2 %multiply_reduce_fusion.3 = (f32[768]{0:T(1024)S(1)}, f32[512]{0:T(512)S(1)}, f32[512]{0:T(512)S(1)}, f32[768]{0:T(1024)S(1)}, f32[512,768]{1,0:T(8,128)S(1)}) fusion(f32[2,256,768]{2,1,0:T(8,128)S(1)} %copy-done.2, f32[512]{0:T(512)S(1)} %bitcast.207, f32[512]{0:T(512)S(1)} %bitcast.210, f32[768]{0:T(1024)S(1)} %reshape.376, ...), kind=kOutput, calls=%fused_computation.52 | convolution fusion | flops 1822553600 | bytes 9061376 | tf_op jit(solution)/shard_map/dot_general | solution.py:31
  267.6 3.6 fusion.18
  278.2 4.1 dynamic-slice_convert_fusion.1
  283.9 4.1 dynamic-slice_convert_fusion
  292.6 2.9 collective-permute-start.4
  296.3 4.8 %collective-permute-done.4 = bf16[1,1,1,1,1,1,8,512]{7,6,5,4,3,2,1,0:T(8,128)(2,1)S(1)} collective-permute-done((bf16[1,1,1,1,1,1,8,512]{7,6,5,4,3,2,1,0:T(8,128)(2,1)S(1)}, bf16[1,1,1,1,1,1,8,512]{7,6,5,4,3,2,1,0:T(8,128)(2,1)S(1)}, u32[]{:S(2)}, u32[]{:S(2)}) %collective-permute-start.4) | collective-permute-done | bytes 8224 | tf_op jit(solution)/shard_map/ppermute | solution.py:90
  307.9 5.2 %collective-permute-done.26 = bf16[1,2,1,2,2,24,512]{6,5,4,3,2,1,0:T(8,128)(2,1)S(1)} collective-permute-done((bf16[1,2,1,2,2,24,512]{6,5,4,3,2,1,0:T(8,128)(2,1)S(1)}, bf16[1,2,1,2,2,24,512]{6,5,4,3,2,1,0:T(8,128)(2,1)S(1)}, u32[]{:S(2)}, u32[]{:S(2)}) %collective-permute-start.26) | collective-permute-done | bytes 196640 | tf_op jit(solution)/shard_map/ppermute | solution.py:90
  318.0 5.0 %collective-permute-done.11 = bf16[1,2,1,2,2,24,768]{6,5,4,3,2,1,0:T(8,128)(2,1)S(1)} collective-permute-done((bf16[1,2,1,2,2,24,768]{6,5,4,3,2,1,0:T(8,128)(2,1)S(1)}, bf16[1,2,1,2,2,24,768]{6,5,4,3,2,1,0:T(8,128)(2,1)S(1)}, u32[]{:S(2)}, u32[]{:S(2)}) %collective-permute-start.11) | collective-permute-done | bytes 294944 | tf_op jit(solution)/shard_map/ppermute | solution.py:90
  324.0 4.3 collective-permute-done.12
  328.5 3.1 convert_add_fusion.2
  333.3 1.8 collective-permute-start.29
  340.7 10.0 %collective-permute-done.6 = bf16[1,2,1,2,2,24,2304]{6,5,4,3,2,1,0:T(8,128)(2,1)S(1)} collective-permute-done((bf16[1,2,1,2,2,24,2304]{6,5,4,3,2,1,0:T(8,128)(2,1)S(1)}, bf16[1,2,1,2,2,24,2304]{6,5,4,3,2,1,0:T(8,128)(2,1)S(1)}, u32[]{:S(2)}, u32[]{:S(2)}) %collective-permute-start.6) | collective-permute-done | bytes 884768 | tf_op jit(solution)/shard_map/ppermute | solution.py:90
  351.9 3.1 convert_add_fusion.1
  356.7 2.9 collective-permute-done.7
  361.1 2.4 convert_add_fusion
  368.3 15.7 %collective-permute-done.16 = bf16[1,2,1,2,2,24,3072]{6,5,4,3,2,1,0:T(8,128)(2,1)S(1)} collective-permute-done((bf16[1,2,1,2,2,24,3072]{6,5,4,3,2,1,0:T(8,128)(2,1)S(1)}, bf16[1,2,1,2,2,24,3072]{6,5,4,3,2,1,0:T(8,128)(2,1)S(1)}, u32[]{:S(2)}, u32[]{:S(2)}) %collective-permute-start.16) | collective-permute-done | bytes 1179680 | tf_op jit(solution)/shard_map/ppermute | solution.py:90
  386.6 17.9 %collective-permute-done.21 = bf16[1,2,1,2,2,96,768]{6,5,4,3,2,1,0:T(8,128)(2,1)S(1)} collective-permute-done((bf16[1,2,1,2,2,96,768]{6,5,4,3,2,1,0:T(8,128)(2,1)S(1)}, bf16[1,2,1,2,2,96,768]{6,5,4,3,2,1,0:T(8,128)(2,1)S(1)}, u32[]{:S(2)}, u32[]{:S(2)}) %collective-permute-start.21) | collective-permute-done | bytes 1179680 | tf_op jit(solution)/shard_map/ppermute | solution.py:90
  407.7 3.4 copy.125
  413.8 3.0 collective-permute-done.22
  419.1 3.9 collective-permute-done.18
  423.7 2.8 collective-permute-done.23
  426.6 1.8 collective-permute-start.24
  428.4 3.2 collective-permute-done.19
  432.3 2.4 collective-permute-done.24
  (316 shorter events, 90.6 us)
Async XLA Ops:
  7.2 150.7 %all-gather.3.cloned.1.call-start = ((), (), s32[]{:S(2)}) async-start(), calls=%async_computation.2 | async-start | bytes 10543104 | tf_op jit(solution)/shard_map/all_gather | solution.py:204
  9.1 139.3 %copy-start.34 = (s32[2,13]{1,0:T(2,128)S(1)}, s32[2,13]{1,0:T(2,128)}, u32[]{:S(2)}) copy-start(s32[2,13]{1,0:T(2,128)} %param.19) | copy-start | bytes 316
  9.1 139.8 %copy-start.23 = (bf16[2,256,768]{2,1,0:T(8,128)(2,1)S(1)}, bf16[2,256,768]{2,1,0:T(8,128)(2,1)}, u32[]{:S(2)}) copy-start(bf16[2,256,768]{2,1,0:T(8,128)(2,1)} %param.18) | copy-start | bytes 2359300
  9.1 143.0 %all-to-all-start.1 = ((bf16[64,32,512]{2,1,0:T(8,128)(2,1)}), bf16[64,32,512]{2,1,0:T(8,128)(2,1)}, u32[]{:S(2)}, u32[]{:S(2)}) async-start(bf16[64,32,512]{2,1,0:T(8,128)(2,1)} %param.35), calls=%async_computation.1 | async-start | bytes 4194304 | tf_op jit(solution)/shard_map/all_to_all | solution.py:261
  16.6 176.9 %all-gather.5.cloned.1.call-start = ((), (), s32[]{:S(2)}) async-start(), calls=%async_computation.3 | async-start | bytes 4866048 | tf_op jit(solution)/shard_map/all_gather | solution.py:211
  149.5 35.5 %copy-start.1 = (f32[2,256,768]{2,1,0:T(8,128)}, f32[2,256,768]{2,1,0:T(8,128)S(1)}, u32[]{:S(2)}) copy-start(f32[2,256,768]{2,1,0:T(8,128)S(1)} %get-tuple-element.30) | copy-start | bytes 4718596
  186.8 20.8 %copy-start.5 = (f32[512,768]{1,0:T(8,128)}, f32[512,768]{1,0:T(8,128)S(1)}, u32[]{:S(2)}) copy-start(f32[512,768]{1,0:T(8,128)S(1)} %get-tuple-element.50) | copy-start | bytes 4718596
  187.7 19.9 %copy-start.3 = (f32[512,768]{1,0:T(8,128)}, f32[512,768]{1,0:T(8,128)S(1)}, u32[]{:S(2)}) copy-start(f32[512,768]{1,0:T(8,128)S(1)} %fusion.49) | copy-start | bytes 4718596
  226.8 12.4 %slice-start.11 = ((s8[4718592]{0:T(1024)(128)(4,1)}), s8[4194304]{0:T(1024)(128)(4,1)S(1)}, s32[]{:S(2)}) async-start(s8[4718592]{0:T(1024)(128)(4,1)} %bitcast.221), calls=%async_computation.15 | async-start | bytes 8388608
  228.5 10.7 %slice-start.12 = ((s8[4718592]{0:T(1024)(128)(4,1)}), s8[524288]{0:T(1024)(128)(4,1)S(1)}, s32[]{:S(2)}) async-start(s8[4718592]{0:T(1024)(128)(4,1)} %bitcast.221), calls=%async_computation.16 | async-start | bytes 1048576
  248.5 159.1 %all-to-all-start = ((bf16[2,1024,512]{2,0,1:T(2,128)(2,1)}), bf16[2,1024,512]{2,0,1:T(2,128)(2,1)}, u32[]{:S(2)}, u32[]{:S(2)}) async-start(bf16[2,1024,512]{2,0,1:T(2,128)(2,1)} %copy.124), calls=%async_computation | async-start | bytes 4194304 | tf_op jit(solution)/shard_map/all_to_all | solution.py:260
  267.5 9.1 %collective-permute-start = (bf16[2,2,1,2,2,1,8,512]{7,6,5,4,3,2,1,0:T(8,128)(2,1)S(1)}, bf16[2,2,1,2,2,1,8,512]{7,6,5,4,3,2,1,0:T(8,128)(2,1)S(1)}, u32[]{:S(2)}, u32[]{:S(2)}) collective-permute-start(bf16[2,2,1,2,2,1,8,512]{7,6,5,4,3,2,1,0:T(8,128)(2,1)S(1)} %dynamic-slice_convert_fusion.19), channel_id=1, source_target_pairs={{0,4},{1,5},{2,6},{3,7},{4,0},{5,1},{6,2},{7,3},{8,12},{9,13},{10,... | collective-permute-start | bytes 393224 | tf_op jit(solution)/shard_map/ppermute | solution.py:90
  272.6 55.9 %collective-permute-start.5 = (bf16[2,2,1,2,2,24,2304]{6,5,4,3,2,1,0:T(8,128)(2,1)}, bf16[2,2,1,2,2,24,2304]{6,5,4,3,2,1,0:T(8,128)(2,1)}, u32[]{:S(2)}, u32[]{:S(2)}) collective-permute-start(bf16[2,2,1,2,2,24,2304]{6,5,4,3,2,1,0:T(8,128)(2,1)} %dynamic-slice_convert_fusion.2), channel_id=1, source_target_pairs={{0,4},{1,5},{2,6},{3,7},{4,0},{5,1},{6,2},{7,3},{8,12},{9,13},{10,... | collective-permute-start | bytes 5308424 | tf_op jit(solution)/shard_map/ppermute | solution.py:90
  276.0 38.6 %collective-permute-start.10 = (bf16[2,2,1,2,2,24,768]{6,5,4,3,2,1,0:T(8,128)(2,1)S(1)}, bf16[2,2,1,2,2,24,768]{6,5,4,3,2,1,0:T(8,128)(2,1)S(1)}, u32[]{:S(2)}, u32[]{:S(2)}) collective-permute-start(bf16[2,2,1,2,2,24,768]{6,5,4,3,2,1,0:T(8,128)(2,1)S(1)} %dynamic-slice_convert_fusion.8), channel_id=1, source_target_pairs={{0,4},{1,5},{2,6},{3,7},{4,0},{5,1},{6,2},{7,3},{8,12},{9,13},{10,... | collective-permute-start | bytes 1769480 | tf_op jit(solution)/shard_map/ppermute | solution.py:90
  276.6 5.7 %collective-permute-start.1 = (bf16[1,2,1,2,2,1,8,512]{7,6,5,4,3,2,1,0:T(8,128)(2,1)S(1)}, bf16[1,2,1,2,2,1,8,512]{7,6,5,4,3,2,1,0:T(8,128)(2,1)S(1)}, u32[]{:S(2)}, u32[]{:S(2)}) collective-permute-start(bf16[1,2,1,2,2,1,8,512]{7,6,5,4,3,2,1,0:T(8,128)(2,1)S(1)} %dynamic-slice_convert_fusion.23), channel_id=1, source_target_pairs={{0,16},{1,17},{2,18},{3,19},{4,20},{5,21},{6,22},{7,23},{8,24},{9,... | collective-permute-start | bytes 196616 | tf_op jit(solution)/shard_map/ppermute | solution.py:90
  282.3 69.5 %collective-permute-start.15 = (bf16[2,2,1,2,2,24,3072]{6,5,4,3,2,1,0:T(8,128)(2,1)}, bf16[2,2,1,2,2,24,3072]{6,5,4,3,2,1,0:T(8,128)(2,1)}, u32[]{:S(2)}, u32[]{:S(2)}) collective-permute-start(bf16[2,2,1,2,2,24,3072]{6,5,4,3,2,1,0:T(8,128)(2,1)} %dynamic-slice_convert_fusion.1), channel_id=1, source_target_pairs={{0,4},{1,5},{2,6},{3,7},{4,0},{5,1},{6,2},{7,3},{8,12},{9,13},{10,... | collective-permute-start | bytes 7077896 | tf_op jit(solution)/shard_map/ppermute | solution.py:90
  282.4 6.2 %collective-permute-start.2 = (bf16[1,1,1,2,2,1,8,512]{7,6,5,4,3,2,1,0:T(8,128)(2,1)S(1)}, bf16[1,1,1,2,2,1,8,512]{7,6,5,4,3,2,1,0:T(8,128)(2,1)S(1)}, u32[]{:S(2)}, u32[]{:S(2)}) collective-permute-start(bf16[1,1,1,2,2,1,8,512]{7,6,5,4,3,2,1,0:T(8,128)(2,1)S(1)} %dynamic-slice_convert_fusion.26), channel_id=1, source_target_pairs={{0,8},{1,9},{2,10},{3,11},{4,12},{5,13},{6,14},{7,15},{8,0},{9,1},... | collective-permute-start | bytes 98312 | tf_op jit(solution)/shard_map/ppermute | solution.py:90
  288.0 73.1 %collective-permute-start.20 = (bf16[2,2,1,2,2,96,768]{6,5,4,3,2,1,0:T(8,128)(2,1)}, bf16[2,2,1,2,2,96,768]{6,5,4,3,2,1,0:T(8,128)(2,1)}, u32[]{:S(2)}, u32[]{:S(2)}) collective-permute-start(bf16[2,2,1,2,2,96,768]{6,5,4,3,2,1,0:T(8,128)(2,1)} %dynamic-slice_convert_fusion), channel_id=1, source_target_pairs={{0,4},{1,5},{2,6},{3,7},{4,0},{5,1},{6,2},{7,3},{8,12},{9,13},{10,... | collective-permute-start | bytes 7077896 | tf_op jit(solution)/shard_map/ppermute | solution.py:90
  288.6 4.0 collective-permute-start.3
  291.1 23.5 %copy-start.12 = (f32[2,2,2,2,2,24,768]{6,5,4,3,2,1,0:T(8,128)S(1)}, f32[2,2,2,2,2,24,768]{6,5,4,3,2,1,0:T(8,128)}, u32[]{:S(2)}) copy-start(f32[2,2,2,2,2,24,768]{6,5,4,3,2,1,0:T(8,128)} %copy-done.11) | copy-start | bytes 7077892
  292.6 8.6 %collective-permute-start.4 = (bf16[1,1,1,1,1,1,8,512]{7,6,5,4,3,2,1,0:T(8,128)(2,1)S(1)}, bf16[1,1,1,1,1,1,8,512]{7,6,5,4,3,2,1,0:T(8,128)(2,1)S(1)}, u32[]{:S(2)}, u32[]{:S(2)}) collective-permute-start(bf16[1,1,1,1,1,1,8,512]{7,6,5,4,3,2,1,0:T(8,128)(2,1)S(1)} %dynamic-slice_convert_fusion.29), channel_id=1, source_target_pairs={{0,2},{1,3},{2,0},{3,1},{4,6},{5,7},{6,4},{7,5},{8,10},{9,11},{10,... | collective-permute-start | bytes 24584 | tf_op jit(solution)/shard_map/ppermute | solution.py:90
  301.2 3.2 collective-permute-start.25
  305.8 7.4 %collective-permute-start.26 = (bf16[1,2,1,2,2,24,512]{6,5,4,3,2,1,0:T(8,128)(2,1)S(1)}, bf16[1,2,1,2,2,24,512]{6,5,4,3,2,1,0:T(8,128)(2,1)S(1)}, u32[]{:S(2)}, u32[]{:S(2)}) collective-permute-start(bf16[1,2,1,2,2,24,512]{6,5,4,3,2,1,0:T(8,128)(2,1)S(1)} %dynamic-slice_convert_fusion.15), channel_id=1, source_target_pairs={{0,16},{1,17},{2,18},{3,19},{4,20},{5,21},{6,22},{7,23},{8,24},{9,... | collective-permute-start | bytes 589832 | tf_op jit(solution)/shard_map/ppermute | solution.py:90
  313.2 4.7 %collective-permute-start.27 = (bf16[1,1,1,2,2,24,512]{6,5,4,3,2,1,0:T(8,128)(2,1)S(1)}, bf16[1,1,1,2,2,24,512]{6,5,4,3,2,1,0:T(8,128)(2,1)S(1)}, u32[]{:S(2)}, u32[]{:S(2)}) collective-permute-start(bf16[1,1,1,2,2,24,512]{6,5,4,3,2,1,0:T(8,128)(2,1)S(1)} %dynamic-slice_convert_fusion.21), channel_id=1, source_target_pairs={{0,8},{1,9},{2,10},{3,11},{4,12},{5,13},{6,14},{7,15},{8,0},{9,1},... | collective-permute-start | bytes 294920 | tf_op jit(solution)/shard_map/ppermute | solution.py:90
  314.7 8.3 %collective-permute-start.11 = (bf16[1,2,1,2,2,24,768]{6,5,4,3,2,1,0:T(8,128)(2,1)S(1)}, bf16[1,2,1,2,2,24,768]{6,5,4,3,2,1,0:T(8,128)(2,1)S(1)}, u32[]{:S(2)}, u32[]{:S(2)}) collective-permute-start(bf16[1,2,1,2,2,24,768]{6,5,4,3,2,1,0:T(8,128)(2,1)S(1)} %dynamic-slice_convert_fusion.13), channel_id=1, source_target_pairs={{0,16},{1,17},{2,18},{3,19},{4,20},{5,21},{6,22},{7,23},{8,24},{9,... | collective-permute-start | bytes 884744 | tf_op jit(solution)/shard_map/ppermute | solution.py:90
  318.0 6.1 %collective-permute-start.28 = (bf16[1,1,1,2,1,24,512]{6,5,4,3,2,1,0:T(8,128)(2,1)S(1)}, bf16[1,1,1,2,1,24,512]{6,5,4,3,2,1,0:T(8,128)(2,1)S(1)}, u32[]{:S(2)}, u32[]{:S(2)}) collective-permute-start(bf16[1,1,1,2,1,24,512]{6,5,4,3,2,1,0:T(8,128)(2,1)S(1)} %dynamic-slice_convert_fusion.24), channel_id=1, source_target_pairs={{0,1},{1,0},{2,3},{3,2},{4,5},{5,4},{6,7},{7,6},{8,9},{9,8},{10,11... | collective-permute-start | bytes 147464 | tf_op jit(solution)/shard_map/ppermute | solution.py:90
  323.1 28.8 %slice-start.5 = ((s8[9437184]{0:T(1024)(128)(4,1)}), s8[4194304]{0:T(1024)(128)(4,1)S(1)}, s32[]{:S(2)}) async-start(s8[9437184]{0:T(1024)(128)(4,1)} %bitcast.173), calls=%async_computation.9 | async-start | bytes 8388608
  323.2 5.2 %collective-permute-start.12 = (bf16[1,1,1,2,2,24,768]{6,5,4,3,2,1,0:T(8,128)(2,1)S(1)}, bf16[1,1,1,2,2,24,768]{6,5,4,3,2,1,0:T(8,128)(2,1)S(1)}, u32[]{:S(2)}, u32[]{:S(2)}) collective-permute-start(bf16[1,1,1,2,2,24,768]{6,5,4,3,2,1,0:T(8,128)(2,1)S(1)} %dynamic-slice_convert_fusion.18), channel_id=1, source_target_pairs={{0,8},{1,9},{2,10},{3,11},{4,12},{5,13},{6,14},{7,15},{8,0},{9,1},... | collective-permute-start | bytes 442376 | tf_op jit(solution)/shard_map/ppermute | solution.py:90
  328.4 23.4 %slice-start.6 = ((s8[9437184]{0:T(1024)(128)(4,1)}), s8[4194304]{0:T(1024)(128)(4,1)S(1)}, s32[]{:S(2)}) async-start(s8[9437184]{0:T(1024)(128)(4,1)} %bitcast.173), calls=%async_computation.10 | async-start | bytes 8388608
  328.4 6.6 %collective-permute-start.13 = (bf16[1,1,1,2,1,24,768]{6,5,4,3,2,1,0:T(8,128)(2,1)S(1)}, bf16[1,1,1,2,1,24,768]{6,5,4,3,2,1,0:T(8,128)(2,1)S(1)}, u32[]{:S(2)}, u32[]{:S(2)}) collective-permute-start(bf16[1,1,1,2,1,24,768]{6,5,4,3,2,1,0:T(8,128)(2,1)S(1)} %dynamic-slice_convert_fusion.22), channel_id=1, source_target_pairs={{0,1},{1,0},{2,3},{3,2},{4,5},{5,4},{6,7},{7,6},{8,9},{9,8},{10,11... | collective-permute-start | bytes 221192 | tf_op jit(solution)/shard_map/ppermute | solution.py:90
  331.6 20.2 %slice-start.7 = ((s8[9437184]{0:T(1024)(128)(4,1)}), s8[1048576]{0:T(1024)(128)(4,1)S(1)}, s32[]{:S(2)}) async-start(s8[9437184]{0:T(1024)(128)(4,1)} %bitcast.173), calls=%async_computation.11 | async-start | bytes 2097152
  331.7 19.0 %collective-permute-start.6 = (bf16[1,2,1,2,2,24,2304]{6,5,4,3,2,1,0:T(8,128)(2,1)S(1)}, bf16[1,2,1,2,2,24,2304]{6,5,4,3,2,1,0:T(8,128)(2,1)S(1)}, u32[]{:S(2)}, u32[]{:S(2)}) collective-permute-start(bf16[1,2,1,2,2,24,2304]{6,5,4,3,2,1,0:T(8,128)(2,1)S(1)} %dynamic-slice_convert_fusion.5), channel_id=1, source_target_pairs={{0,16},{1,17},{2,18},{3,19},{4,20},{5,21},{6,22},{7,23},{8,24},{9,... | collective-permute-start | bytes 2654216 | tf_op jit(solution)/shard_map/ppermute | solution.py:90
  333.3 4.7 %collective-permute-start.29 = (bf16[1,1,1,1,1,24,512]{6,5,4,3,2,1,0:T(8,128)(2,1)S(1)}, bf16[1,1,1,1,1,24,512]{6,5,4,3,2,1,0:T(8,128)(2,1)S(1)}, u32[]{:S(2)}, u32[]{:S(2)}) collective-permute-start(bf16[1,1,1,1,1,24,512]{6,5,4,3,2,1,0:T(8,128)(2,1)S(1)} %dynamic-slice_convert_fusion.27), channel_id=1, source_target_pairs={{0,2},{1,3},{2,0},{3,1},{4,6},{5,7},{6,4},{7,5},{8,10},{9,11},{10,... | collective-permute-start | bytes 73736 | tf_op jit(solution)/shard_map/ppermute | solution.py:90
  335.1 5.0 %collective-permute-start.14 = (bf16[1,1,1,1,1,24,768]{6,5,4,3,2,1,0:T(8,128)(2,1)S(1)}, bf16[1,1,1,1,1,24,768]{6,5,4,3,2,1,0:T(8,128)(2,1)S(1)}, u32[]{:S(2)}, u32[]{:S(2)}) collective-permute-start(bf16[1,1,1,1,1,24,768]{6,5,4,3,2,1,0:T(8,128)(2,1)S(1)} %dynamic-slice_convert_fusion.25), channel_id=1, source_target_pairs={{0,2},{1,3},{2,0},{3,1},{4,6},{5,7},{6,4},{7,5},{8,10},{9,11},{10,... | collective-permute-start | bytes 110600 | tf_op jit(solution)/shard_map/ppermute | solution.py:90
  350.9 10.2 %slice-start = ((s8[9437184]{0:T(1024)(128)(4,1)}), s8[4194304]{0:T(1024)(128)(4,1)S(1)}, s32[]{:S(2)}) async-start(s8[9437184]{0:T(1024)(128)(4,1)} %bitcast.164), calls=%async_computation.4 | async-start | bytes 8388608
  350.9 10.2 %slice-start.1 = ((s8[9437184]{0:T(1024)(128)(4,1)}), s8[4194304]{0:T(1024)(128)(4,1)S(1)}, s32[]{:S(2)}) async-start(s8[9437184]{0:T(1024)(128)(4,1)} %bitcast.164), calls=%async_computation.5 | async-start | bytes 8388608
  351.0 10.2 %slice-start.2 = ((s8[9437184]{0:T(1024)(128)(4,1)}), s8[1048576]{0:T(1024)(128)(4,1)S(1)}, s32[]{:S(2)}) async-start(s8[9437184]{0:T(1024)(128)(4,1)} %bitcast.164), calls=%async_computation.6 | async-start | bytes 2097152
  351.0 8.6 %collective-permute-start.7 = (bf16[1,1,1,2,2,24,2304]{6,5,4,3,2,1,0:T(8,128)(2,1)S(1)}, bf16[1,1,1,2,2,24,2304]{6,5,4,3,2,1,0:T(8,128)(2,1)S(1)}, u32[]{:S(2)}, u32[]{:S(2)}) collective-permute-start(bf16[1,1,1,2,2,24,2304]{6,5,4,3,2,1,0:T(8,128)(2,1)S(1)} %dynamic-slice_convert_fusion.9), channel_id=1, source_target_pairs={{0,8},{1,9},{2,10},{3,11},{4,12},{5,13},{6,14},{7,15},{8,0},{9,1},... | collective-permute-start | bytes 1327112 | tf_op jit(solution)/shard_map/ppermute | solution.py:90
  355.1 28.9 %collective-permute-start.16 = (bf16[1,2,1,2,2,24,3072]{6,5,4,3,2,1,0:T(8,128)(2,1)S(1)}, bf16[1,2,1,2,2,24,3072]{6,5,4,3,2,1,0:T(8,128)(2,1)S(1)}, u32[]{:S(2)}, u32[]{:S(2)}) collective-permute-start(bf16[1,2,1,2,2,24,3072]{6,5,4,3,2,1,0:T(8,128)(2,1)S(1)} %dynamic-slice_convert_fusion.4), channel_id=1, source_target_pairs={{0,16},{1,17},{2,18},{3,19},{4,20},{5,21},{6,22},{7,23},{8,24},{9,... | collective-permute-start | bytes 3538952 | tf_op jit(solution)/shard_map/ppermute | solution.py:90
  359.7 7.2 %collective-permute-start.8 = (bf16[1,1,1,2,1,24,2304]{6,5,4,3,2,1,0:T(8,128)(2,1)S(1)}, bf16[1,1,1,2,1,24,2304]{6,5,4,3,2,1,0:T(8,128)(2,1)S(1)}, u32[]{:S(2)}, u32[]{:S(2)}) collective-permute-start(bf16[1,1,1,2,1,24,2304]{6,5,4,3,2,1,0:T(8,128)(2,1)S(1)} %dynamic-slice_convert_fusion.14), channel_id=1, source_target_pairs={{0,1},{1,0},{2,3},{3,2},{4,5},{5,4},{6,7},{7,6},{8,9},{9,8},{10,11... | collective-permute-start | bytes 663560 | tf_op jit(solution)/shard_map/ppermute | solution.py:90
  363.7 40.7 %collective-permute-start.21 = (bf16[1,2,1,2,2,96,768]{6,5,4,3,2,1,0:T(8,128)(2,1)S(1)}, bf16[1,2,1,2,2,96,768]{6,5,4,3,2,1,0:T(8,128)(2,1)S(1)}, u32[]{:S(2)}, u32[]{:S(2)}) collective-permute-start(bf16[1,2,1,2,2,96,768]{6,5,4,3,2,1,0:T(8,128)(2,1)S(1)} %dynamic-slice_convert_fusion.3), channel_id=1, source_target_pairs={{0,16},{1,17},{2,18},{3,19},{4,20},{5,21},{6,22},{7,23},{8,24},{9,... | collective-permute-start | bytes 3538952 | tf_op jit(solution)/shard_map/ppermute | solution.py:90
  367.0 18.9 %collective-permute-start.9 = (bf16[1,1,1,1,1,24,2304]{6,5,4,3,2,1,0:T(8,128)(2,1)S(1)}, bf16[1,1,1,1,1,24,2304]{6,5,4,3,2,1,0:T(8,128)(2,1)S(1)}, u32[]{:S(2)}, u32[]{:S(2)}) collective-permute-start(bf16[1,1,1,1,1,24,2304]{6,5,4,3,2,1,0:T(8,128)(2,1)S(1)} %dynamic-slice_convert_fusion.20), channel_id=1, source_target_pairs={{0,2},{1,3},{2,0},{3,1},{4,6},{5,7},{6,4},{7,5},{8,10},{9,11},{10,... | collective-permute-start | bytes 331784 | tf_op jit(solution)/shard_map/ppermute | solution.py:90
  384.4 26.7 %collective-permute-start.17 = (bf16[1,1,1,2,2,24,3072]{6,5,4,3,2,1,0:T(8,128)(2,1)S(1)}, bf16[1,1,1,2,2,24,3072]{6,5,4,3,2,1,0:T(8,128)(2,1)}, u32[]{:S(2)}, u32[]{:S(2)}) collective-permute-start(bf16[1,1,1,2,2,24,3072]{6,5,4,3,2,1,0:T(8,128)(2,1)S(1)} %dynamic-slice_convert_fusion.7), channel_id=1, source_target_pairs={{0,8},{1,9},{2,10},{3,11},{4,12},{5,13},{6,14},{7,15},{8,0},{9,1},... | collective-permute-start | bytes 1769480 | tf_op jit(solution)/shard_map/ppermute | solution.py:90
  406.2 10.6 %collective-permute-start.22 = (bf16[1,1,1,2,2,96,768]{6,5,4,3,2,1,0:T(8,128)(2,1)S(1)}, bf16[1,1,1,2,2,96,768]{6,5,4,3,2,1,0:T(8,128)(2,1)}, u32[]{:S(2)}, u32[]{:S(2)}) collective-permute-start(bf16[1,1,1,2,2,96,768]{6,5,4,3,2,1,0:T(8,128)(2,1)S(1)} %dynamic-slice_convert_fusion.6), channel_id=1, source_target_pairs={{0,8},{1,9},{2,10},{3,11},{4,12},{5,13},{6,14},{7,15},{8,0},{9,1},... | collective-permute-start | bytes 1769480 | tf_op jit(solution)/shard_map/ppermute | solution.py:90
  412.4 10.5 %collective-permute-start.18 = (bf16[1,1,1,2,1,24,3072]{6,5,4,3,2,1,0:T(8,128)(2,1)S(1)}, bf16[1,1,1,2,1,24,3072]{6,5,4,3,2,1,0:T(8,128)(2,1)S(1)}, u32[]{:S(2)}, u32[]{:S(2)}) collective-permute-start(bf16[1,1,1,2,1,24,3072]{6,5,4,3,2,1,0:T(8,128)(2,1)S(1)} %dynamic-slice_convert_fusion.12), channel_id=1, source_target_pairs={{0,1},{1,0},{2,3},{3,2},{4,5},{5,4},{6,7},{7,6},{8,9},{9,8},{10,11... | collective-permute-start | bytes 884744 | tf_op jit(solution)/shard_map/ppermute | solution.py:90
  418.0 8.5 %collective-permute-start.23 = (bf16[1,1,1,2,1,96,768]{6,5,4,3,2,1,0:T(8,128)(2,1)S(1)}, bf16[1,1,1,2,1,96,768]{6,5,4,3,2,1,0:T(8,128)(2,1)S(1)}, u32[]{:S(2)}, u32[]{:S(2)}) collective-permute-start(bf16[1,1,1,2,1,96,768]{6,5,4,3,2,1,0:T(8,128)(2,1)S(1)} %dynamic-slice_convert_fusion.11), channel_id=1, source_target_pairs={{0,1},{1,0},{2,3},{3,2},{4,5},{5,4},{6,7},{7,6},{8,9},{9,8},{10,11... | collective-permute-start | bytes 884744 | tf_op jit(solution)/shard_map/ppermute | solution.py:90
  423.1 8.5 %collective-permute-start.19 = (bf16[1,1,1,1,1,24,3072]{6,5,4,3,2,1,0:T(8,128)(2,1)S(1)}, bf16[1,1,1,1,1,24,3072]{6,5,4,3,2,1,0:T(8,128)(2,1)S(1)}, u32[]{:S(2)}, u32[]{:S(2)}) collective-permute-start(bf16[1,1,1,1,1,24,3072]{6,5,4,3,2,1,0:T(8,128)(2,1)S(1)} %dynamic-slice_convert_fusion.17), channel_id=1, source_target_pairs={{0,2},{1,3},{2,0},{3,1},{4,6},{5,7},{6,4},{7,5},{8,10},{9,11},{10,... | collective-permute-start | bytes 442376 | tf_op jit(solution)/shard_map/ppermute | solution.py:90
  426.6 8.1 %collective-permute-start.24 = (bf16[1,1,1,1,1,96,768]{6,5,4,3,2,1,0:T(8,128)(2,1)S(1)}, bf16[1,1,1,1,1,96,768]{6,5,4,3,2,1,0:T(8,128)(2,1)S(1)}, u32[]{:S(2)}, u32[]{:S(2)}) collective-permute-start(bf16[1,1,1,1,1,96,768]{6,5,4,3,2,1,0:T(8,128)(2,1)S(1)} %dynamic-slice_convert_fusion.16), channel_id=1, source_target_pairs={{0,2},{1,3},{2,0},{3,1},{4,6},{5,7},{6,4},{7,5},{8,10},{9,11},{10,... | collective-permute-start | bytes 442376 | tf_op jit(solution)/shard_map/ppermute | solution.py:90
  (44 other events, 201.4 us)
Sparse Core Ops, SparseCore 0:
  11.4 108.0 all-gather.2
  122.2 62.8 all-gather.4
where the time goes:
time: 447 us; the launch traced here: 443 us
  blocking collectives  130 us (29%)
  waiting for transfers between devices  89.8 us (20%)
  matrix products  68 us (15%)
  local copies, waits for them, and re-layouts  60.6 us (14%)
  starting transfers between devices  44.8 us (10%)
  other arithmetic  33.3 us (7%)
  between operations  15.7 us (4%)
    all_gather x1, blocking collectives, local(): gathered_small = lax.all_gather(packed_small, AX, axis=0, tiled=True)  130 us
    ppermute x30, waiting for transfers between devices, rs_chain(): lax.ppermute(send.astype(jnp.bfloat16), AX, [(i, i ^ 1 << bit) for i in r...  89.1 us
    ppermute x30, starting transfers between devices, rs_chain(): lax.ppermute(send.astype(jnp.bfloat16), AX, [(i, i ^ 1 << bit) for i in r...  33.5 us
    dot_general x5, matrix products, outer_cols(): lax.dot_general(left_op, right_op, (((1,), (1,)), ((), ())), preferred_el...  22 us
    dot_general x5, matrix products, inner_rows(): lax.dot_general(left_op, right_op, (((0,), (0,)), ((), ())), preferred_el...  16 us
    dot_general x5, matrix products, product(): return jnp.dot(left_op, right_op, preferred_element_type=jnp.float32)  15.2 us
    add x24, other arithmetic, rs_chain(): current = keep + moved.astype(jnp.float32)  13.7 us
    unnamed x127, local copies, waits for them, and re-layouts  12.1 us
  transfers between devices with their start and end apart: 34, of which 18 were waited for; matrix products, arithmetic and copies ran while one was open for 22% of the time, Pallas kernels for 0%

commit v1 on v0

--- a/solution.py
+++ b/solution.py
@@ -61,20 +61,31 @@
     )
 
 
-def core_bit_of(mesh):
+def bit_groups(mesh):
     flat = list(mesh.devices.reshape(-1))
-    cores = [d.core_on_chip for d in flat]
-    stride = 1
-    while stride < len(flat) and cores[stride] == cores[0]:
-        stride *= 2
-    return stride.bit_length() - 1
-
-
-def halving_order(n_bits, core_bit):
-    rest = [b for b in reversed(range(n_bits)) if b != core_bit]
-    if len(rest) >= 2:
-        rest[-2:] = rest[-2:][::-1]
-    return [core_bit] + rest
+    n_bits = len(flat).bit_length() - 1
+    first = flat[0]
+    core_bit = None
+    groups = {}
+    for bit in range(n_bits):
+        other = flat[1 << bit]
+        if other.core_on_chip != first.core_on_chip:
+            core_bit = bit
+            continue
+        axis = [a for a in range(len(first.coords)) if first.coords[a] != other.coords[a]]
+        groups.setdefault(axis[0] if axis else -1, []).append(bit)
+    return core_bit, [sorted(bits) for _, bits in sorted(groups.items())]
+
+
+def halving_orders(core_bit, groups):
+    head = [] if core_bit is None else [core_bit]
+    orders = []
+    for turn in range(max(1, len(groups))):
+        rest = []
+        for i in range(len(groups)):
+            rest.extend(groups[(i + turn) % len(groups)])
+        orders.append(head + rest)
+    return orders
 
 
 def rs_chain(grad, n_bits, order):
@@ -152,7 +163,7 @@
     return grad_queries, grad_keys, grad_values
 
 
-def make_local(n_bits, order):
+def make_local(n_bits, orders):
     n_dev = 2 ** n_bits
 
     def local(
@@ -193,13 +204,15 @@
         )
         small = (wave_table, norm1_gain, norm1_bias, norm2_gain, norm2_bias, mlp_in_bias,
                  mlp_out_bias, dec_bias, mask_token)
-        packed_small, small_widths = pack_rows(
-            [a.reshape(1, -1) for a in small], 1, jnp.bfloat16
-        )
-        gathered_small = lax.all_gather(packed_small, AX, axis=0, tiled=True)
-        (wave_full, gain_one, shift_one, gain_two, shift_two, inner_bias, outer_bias,
-         dec_shift, mask_full) = unpack_rows(gathered_small, small, small_widths, 1, n_dev)
-        wide = (qkv_weight, out_weight, mlp_in, dec_weight)
+        small_flat = [a.reshape(-1) for a in small]
+        small_widths = [f.shape[0] for f in small_flat]
+        rows_here = qkv_weight.shape[0]
+        small_cols = -(-sum(small_widths) // (rows_here * 128)) * 128
+        small_pad = rows_here * small_cols - sum(small_widths)
+        small_block = jnp.concatenate(
+            small_flat + [jnp.zeros((small_pad,), jnp.bfloat16)]
+        ).reshape(rows_here, small_cols)
+        wide = (qkv_weight, out_weight, mlp_in, dec_weight, small_block)
         wide_cols = [a.shape[1] for a in wide]
         gathered_wide = lax.all_gather(jnp.concatenate(wide, axis=1), AX, axis=0, tiled=True)
         wide_full = []
@@ -207,7 +220,16 @@
         for cols in wide_cols:
             wide_full.append(gathered_wide[:, offset : offset + cols])
             offset += cols
-        qkv_full, out_full, inner_full, dec_full = wide_full
+        qkv_full, out_full, inner_full, dec_full, small_full = wide_full
+        small_rows = small_full.reshape(n_dev, rows_here * small_cols)
+        small_parts = []
+        offset = 0
+        for a, width in zip(small, small_widths):
+            piece = small_rows[:, offset : offset + width]
+            small_parts.append(piece.reshape((n_dev * a.shape[0],) + a.shape[1:]))
+            offset += width
+        (wave_full, gain_one, shift_one, gain_two, shift_two, inner_bias, outer_bias,
+         dec_shift, mask_full) = small_parts
         outer_full = lax.all_gather(mlp_out, AX, axis=0, tiled=True)
 
         chip_count, vis_len, feature_width = tokens.shape
@@ -311,14 +333,15 @@
                        grad_norm2_bias, grad_mlp_in_bias, grad_mlp_out_bias, grad_dec_bias,
                        grad_mask_token)
         packed_sg, sg_widths = pack_rows(small_grads, n_dev, jnp.float32)
-        reduced_sg = rs_chain(packed_sg, n_bits, order)
+        turn = lambda k: orders[k % len(orders)]
+        reduced_sg = rs_chain(packed_sg, n_bits, turn(2))
         (sum_wave, sum_g1, sum_b1, sum_g2, sum_b2, sum_ib, sum_ob, sum_db,
          sum_mask) = unpack_rows(reduced_sg, small_grads, sg_widths, n_dev, 1)
-        sum_dec = rs_chain(grad_dec_weight, n_bits, order)
-        sum_mlp_out = rs_chain(grad_mlp_out, n_bits, order)
-        sum_mlp_in = rs_chain(grad_mlp_in, n_bits, order)
-        sum_out = rs_chain(grad_out_weight, n_bits, order)
-        sum_qkv = rs_chain(grad_qkv_weight, n_bits, order)
+        sum_dec = rs_chain(grad_dec_weight, n_bits, turn(1))
+        sum_mlp_out = rs_chain(grad_mlp_out, n_bits, turn(1))
+        sum_mlp_in = rs_chain(grad_mlp_in, n_bits, turn(0))
+        sum_out = rs_chain(grad_out_weight, n_bits, turn(0))
+        sum_qkv = rs_chain(grad_qkv_weight, n_bits, turn(2))
         summed = (sum_wave, sum_g1, sum_b1, sum_qkv, sum_out, sum_g2, sum_b2, sum_mlp_in,
                   sum_ib, sum_mlp_out, sum_ob, sum_dec, sum_db, sum_mask)
         return (decoded, grad_tokens, *summed)
@@ -329,7 +352,7 @@
 def solution(mesh):
     n_dev = mesh.devices.size
     n_bits = n_dev.bit_length() - 1
-    order = halving_order(n_bits, core_bit_of(mesh))
+    orders = halving_orders(*bit_groups(mesh))
     placed = (
         P(AX, None, None),
         P(AX, None),
@@ -351,7 +374,7 @@
         P(None, AX, None),
     )
     return jax.shard_map(
-        make_local(n_bits, order),
+        make_local(n_bits, orders),
         mesh=mesh,
         in_specs=placed,
         out_specs=(

time: 447 us -> 478 us (1.069)
  waiting for transfers between devices: 89.8 us -> 227 us
  blocking collectives: 130 us -> 0 us
  matrix products: 68 us -> 81.2 us
  local copies, waits for them, and re-layouts: 60.6 us -> 70.2 us
    all_gather x1 -> x0, blocking collectives: 130 us -> none  [local(): gathered_small = lax.all_gather(packed_small, AX, axis=0, tiled=True)]
    all_to_all x1, waiting for transfers between devices: 0.01 us -> 66.6 us  [local(): lax.all_to_all(cot_decoded, AX, split_axis=0, concat_axis=1, tiled=True)]
    all_gather x1, waiting for transfers between devices: 0.01 us -> 32.6 us  [local(): lax.all_gather(jnp.concatenate(wide, axis=1), AX, axis=0, tiled=True)]
    ppermute x30, waiting for transfers between devices: 89.1 us -> 109 us  [rs_chain(): lax.ppermute(send.astype(jnp.bfloat16), AX, [(i, i ^ 1 << bit) for i in r...]
    all_gather x1, waiting for transfers between devices: 0.01 us -> 18 us  [local(): outer_full = lax.all_gather(mlp_out, AX, axis=0, tiled=True)]
    dot_general x5, matrix products: 15.2 us -> 21.4 us  [product(): return jnp.dot(left_op, right_op, preferred_element_type=jnp.float32)]
    concatenate x0 -> x2, local copies, waits for them, and re-layouts: none -> 5.42 us  [the longest x1 5.42 us: local(): jnp.concatenate(small_flat + [jnp.zeros((small_pad,), jnp.bfloat16)])]
    unnamed x127 -> x167, local copies, waits for them, and re-layouts: 12.1 us -> 14.7 us
  transfers between devices with their start and end apart: 34 -> 34, of which waited for: 18 -> 22; matrix products, arithmetic and copies ran while one was open for 22% -> 22% of each run, Pallas kernels for 0% -> 0%
where the time goes in v1:
time: 478 us; the launch traced here: 469 us
  waiting for transfers between devices  227 us (47%)
  matrix products  81.2 us (17%)
  local copies, waits for them, and re-layouts  70.2 us (15%)
  starting transfers between devices  42.5 us (9%)
  other arithmetic  31.6 us (7%)
  between operations  16.1 us (3%)
    ppermute x30, waiting for transfers between devices, rs_chain(): lax.ppermute(send.astype(jnp.bfloat16), AX, [(i, i ^ 1 << bit) for i in r...  109 us
    all_to_all x1, waiting for transfers between devices, local(): lax.all_to_all(cot_decoded, AX, split_axis=0, concat_axis=1, tiled=True)  66.6 us
    all_gather x1, waiting for transfers between devices, local(): lax.all_gather(jnp.concatenate(wide, axis=1), AX, axis=0, tiled=True)  32.6 us
    ppermute x30, starting transfers between devices, rs_chain(): lax.ppermute(send.astype(jnp.bfloat16), AX, [(i, i ^ 1 << bit) for i in r...  31.2 us
    dot_general x5, matrix products, outer_cols(): lax.dot_general(left_op, right_op, (((1,), (1,)), ((), ())), preferred_el...  23 us
    dot_general x5, matrix products, product(): return jnp.dot(left_op, right_op, preferred_element_type=jnp.float32)  21.4 us
    dot_general x5, matrix products, inner_rows(): lax.dot_general(left_op, right_op, (((0,), (0,)), ((), ())), preferred_el...  19.2 us
    all_gather x1, waiting for transfers between devices, local(): outer_full = lax.all_gather(mlp_out, AX, axis=0, tiled=True)  18 us
  transfers between devices with their start and end apart: 34, of which 22 were waited for; matrix products, arithmetic and copies ran while one was open for 22% of the time, Pallas kernels for 0%

profile of v1, /device:TPU:0, one launch (start us, length us, event | category | flops | bytes accessed | tf_op | source)
XLA Modules:
  0.0 468.8 jit_solution(2399642312233054196)
XLA Ops:
  8.8 5.4 %concatenate.13 = bf16[6144]{0:T(1024)(128)(2,1)S(1)} concatenate(bf16[3072]{0:T(1024)(128)(2,1)S(1)} %reshape.303, bf16[24]{0:T(256)(128)(2,1)} %param.22, bf16[24]{0:T(256)(128)(2,1)} %param.23, bf16[24]{0:T(256)(128)(2,1)} %param.26, bf16[24]{0:T(256)(128)(2,1)} %param.27, bf16[96]{0:T(256)(128)(2,1)} %param.29, bf16[24]{0:T(256)(128)(2,1)} %param.31, bf16[16]{0:T(256)(128)(2,1)} %param.33, ...), dimensions={0} | concatenate | bytes 24576 | tf_op jit(solution)/shard_map/concatenate | solution.py:212
  17.5 7.3 %all-to-all-start.1 = ((bf16[64,32,512]{2,1,0:T(8,128)(2,1)}), bf16[64,32,512]{2,1,0:T(8,128)(2,1)S(1)}, u32[]{:S(2)}, u32[]{:S(2)}) async-start(bf16[64,32,512]{2,1,0:T(8,128)(2,1)} %param.35), calls=%async_computation.1 | async-start | bytes 4194304 | tf_op jit(solution)/shard_map/all_to_all | solution.py:283
  26.2 66.6 %all-to-all-done.1 = bf16[64,32,512]{2,1,0:T(8,128)(2,1)S(1)} async-done(((bf16[64,32,512]{2,1,0:T(8,128)(2,1)}), bf16[64,32,512]{2,1,0:T(8,128)(2,1)S(1)}, u32[]{:S(2)}, u32[]{:S(2)}) %all-to-all-start.1) | async-done | bytes 2097184 | tf_op jit(solution)/shard_map/all_to_all | solution.py:283
  96.1 32.6 %all-gather.3.cloned.1.call-done = bf16[768,6912]{1,0:T(8,128)(2,1)} async-done(((bf16[24,6912]{1,0:T(8,128)(2,1)}), bf16[768,6912]{1,0:T(8,128)(2,1)}) %all-gather.3.cloned.1.call-update) | async-done | bytes 10616848 | tf_op jit(solution)/shard_map/all_gather | solution.py:217
  132.5 4.3 convolution_convert_fusion
  137.8 2.3 copy.115
  140.1 2.9 reshape.308
  144.2 2.2 reshape.310
  147.6 2.2 reshape.309
  150.9 5.0 %fusion.78 = (f32[2,12,256]{2,1,0:T(8,128)S(1)}, f32[2,12,256,256]{2,3,1,0:T(8,128)S(1)}) fusion(f32[2,12,256,256]{2,3,1,0:T(8,128)S(1)} %fusion.58), kind=kOutput, calls=%fused_computation.198 | output fusion | flops 6291711 | bytes 12607488 | tf_op jit(solution)/shard_map/sub | solution.py:135
  162.5 2.5 fusion.79
  168.0 7.7 %multiply_convert_fusion.1 = (bf16[512,3072]{1,0:T(8,128)(2,1)}, f32[512,3072]{1,0:T(8,128)}) fusion(f32[3072]{0:T(1024)S(1)} %copy-done.56, bf16[768,6912]{1,0:T(8,128)(2,1)} %all-gather.3.cloned.1.call-done, f32[512,768]{1,0:T(8,128)S(1)} %get-tuple-element.50, f32[768]{0:T(1024)S(1)} %copy-done.62, f32[768]{0:T(1024)S(1)} %copy-done.52, ...), kind=kOutput, calls=%fused_computation.11 | convolution fusion | flops 2427322368 | bytes 15751168 | tf_op jit(solution)/shard_map/dot_general | solution.py:21
  175.6 18.0 %all-gather.5.cloned.1.call-done = bf16[3072,768]{1,0:T(8,128)(2,1)} async-done(((bf16[96,768]{1,0:T(8,128)(2,1)}), bf16[3072,768]{1,0:T(8,128)(2,1)}) %all-gather.5.cloned.1.call-update) | async-done | bytes 4718608 | tf_op jit(solution)/shard_map/all_gather | solution.py:233
  193.7 7.5 %convert_reduce_fusion = (f32[3072]{0:T(1024)S(1)}, bf16[512,3072]{1,0:T(8,128)(2,1)S(1)}) fusion(f32[512,3072]{1,0:T(8,128)} %get-tuple-element.52, f32[3072]{0:T(1024)S(1)} %copy-done.57, bf16[3072,768]{1,0:T(8,128)(2,1)} %all-gather.5.cloned.1.call-done, f32[512,768]{1,0:T(8,128)S(1)} %fusion.49), kind=kOutput, calls=%fused_computation.8 | convolution fusion | flops 2436756480 | bytes 15753216 | tf_op jit(solution)/shard_map/dot_general | solution.py:31
  201.3 6.5 %multiply_reduce_fusion.2 = (f32[768]{0:T(1024)S(1)}, f32[512]{0:T(512)S(1)}, f32[512]{0:T(512)S(1)}, f32[768]{0:T(1024)S(1)}, f32[512,768]{1,0:T(8,128)S(1)}) fusion(f32[512,768]{1,0:T(8,128)S(1)} %get-tuple-element.50, f32[512]{0:T(512)S(1)} %copy-done.61, f32[512]{0:T(512)S(1)} %copy-done.51, f32[768]{0:T(1024)S(1)} %copy-done.53, ...), kind=kOutput, calls=%fused_computation.51 | convolution fusion | flops 2419455488 | bytes 11027456 | tf_op jit(solution)/shard_map/dot_general | solution.py:31
  213.1 5.2 %fusion.33 = bf16[2,256,12,64]{1,3,2,0:T(8,128)(2,1)} fusion(bf16[2,256,12,64]{1,0,3,2:T(2,128)(2,1)} %reshape.314, f32[2,12,256,256]{2,3,1,0:T(8,128)} %copy-done, f32[2,12,256]{2,1,0:T(8,128)S(1)} %copy-done.37), kind=kOutput, calls=%fused_computation.76 | convolution fusion | flops 204865536 | bytes 7888896 | tf_op jit(solution)/shard_map/chqk,cqhd->ckhd/dot_general | solution.py:147
  218.3 3.8 multiply_reduce_fusion
  222.1 4.3 multiply_convert_fusion
  229.9 5.7 %fusion.75 = f32[768,3072]{1,0:T(8,128)} fusion(bf16[512,3072]{1,0:T(8,128)(2,1)S(1)} %copy-done.68, f32[512,768]{1,0:T(8,128)S(1)} %copy-done.6, f32[768]{0:T(1024)S(1)} %copy-done.63, f32[768]{0:T(1024)S(1)} %copy-done.53, f32[512]{0:T(512)S(1)} %copy-done.61, f32[512]{0:T(512)S(1)} %copy-done.51), kind=kOutput, calls=%fused_computation.195 | convolution fusion | flops 2417885184 | bytes 14166016 | tf_op jit(solution)/shard_map/dot_general | solution.py:25
  235.9 8.3 %fusion.70 = f32[3072,768]{1,0:T(8,128)} fusion(bf16[512,3072]{1,0:T(8,128)(2,1)} %get-tuple-element.51, f32[512,768]{1,0:T(8,128)S(1)} %copy-done.4), kind=kOutput, calls=%fused_computation.190 | convolution fusion | flops 2416312320 | bytes 14155776 | tf_op jit(solution)/shard_map/dot_general | solution.py:25
  244.2 5.0 %add_convert_fusion = bf16[512,768]{1,0:T(8,128)(2,1)S(1)} fusion(f32[512,768]{1,0:T(8,128)S(1)} %copy-done.6, bf16[512,3072]{1,0:T(8,128)(2,1)S(1)} %copy-done.21, bf16[3072,768]{1,0:T(8,128)(2,1)} %all-gather.5.cloned.1.call-done, f32[768]{0:T(1024)S(1)} %reshape.349), kind=kOutput, calls=%fused_computation.59 | convolution fusion | flops 2417098752 | bytes 10226688 | tf_op jit(solution)/shard_map/dot_general | solution.py:21
  252.5 3.5 copy.124
  256.0 3.8 all-to-all-start
  266.3 5.2 %multiply_reduce_fusion.3 = (f32[768]{0:T(1024)S(1)}, f32[512]{0:T(512)S(1)}, f32[512]{0:T(512)S(1)}, f32[768]{0:T(1024)S(1)}, f32[512,768]{1,0:T(8,128)S(1)}) fusion(f32[2,256,768]{2,1,0:T(8,128)S(1)} %copy-done.2, f32[512]{0:T(512)S(1)} %bitcast.188, f32[512]{0:T(512)S(1)} %bitcast.191, f32[768]{0:T(1024)S(1)} %copy-done.44, ...), kind=kOutput, calls=%fused_computation.52 | convolution fusion | flops 1822553600 | bytes 9061376 | tf_op jit(solution)/shard_map/dot_general | solution.py:31
  276.4 3.8 fusion.18
  288.2 4.1 dynamic-slice_convert_fusion.1
  292.3 3.1 collective-permute-done.1
  295.5 4.6 collective-permute-start.2
  300.1 4.2 dynamic-slice_convert_fusion
  304.8 4.9 %collective-permute-done.2 = bf16[2,2,1,1,1,1,8,512]{7,6,5,4,3,2,1,0:T(8,128)(2,1)S(1)} collective-permute-done((bf16[2,2,1,1,1,1,8,512]{7,6,5,4,3,2,1,0:T(8,128)(2,1)S(1)}, bf16[2,2,1,1,1,1,8,512]{7,6,5,4,3,2,1,0:T(8,128)(2,1)S(1)}, u32[]{:S(2)}, u32[]{:S(2)}) %collective-permute-start.2) | collective-permute-done | bytes 32800 | tf_op jit(solution)/shard_map/ppermute | solution.py:101
  315.2 2.1 collective-permute-done.4
  322.6 5.2 %collective-permute-done.26 = bf16[1,2,1,2,2,24,512]{6,5,4,3,2,1,0:T(8,128)(2,1)S(1)} collective-permute-done((bf16[1,2,1,2,2,24,512]{6,5,4,3,2,1,0:T(8,128)(2,1)S(1)}, bf16[1,2,1,2,2,24,512]{6,5,4,3,2,1,0:T(8,128)(2,1)S(1)}, u32[]{:S(2)}, u32[]{:S(2)}) %collective-permute-start.26) | collective-permute-done | bytes 196640 | tf_op jit(solution)/shard_map/ppermute | solution.py:101
  332.8 5.2 %collective-permute-done.11 = bf16[2,1,1,2,2,24,768]{6,5,4,3,2,1,0:T(8,128)(2,1)S(1)} collective-permute-done((bf16[2,1,1,2,2,24,768]{6,5,4,3,2,1,0:T(8,128)(2,1)S(1)}, bf16[2,1,1,2,2,24,768]{6,5,4,3,2,1,0:T(8,128)(2,1)S(1)}, u32[]{:S(2)}, u32[]{:S(2)}) %collective-permute-start.11) | collective-permute-done | bytes 294944 | tf_op jit(solution)/shard_map/ppermute | solution.py:101
  339.6 3.6 collective-permute-done.12
  345.1 2.9 convert_add_fusion.2
  353.2 13.5 %collective-permute-done.14 = bf16[1,1,1,1,1,24,768]{6,5,4,3,2,1,0:T(8,128)(2,1)S(1)} collective-permute-done((bf16[1,1,1,1,1,24,768]{6,5,4,3,2,1,0:T(8,128)(2,1)S(1)}, bf16[1,1,1,1,1,24,768]{6,5,4,3,2,1,0:T(8,128)(2,1)S(1)}, u32[]{:S(2)}, u32[]{:S(2)}) %collective-permute-start.14) | collective-permute-done | bytes 36896 | tf_op jit(solution)/shard_map/ppermute | solution.py:101
  367.9 3.2 collective-permute-start.7
  371.2 2.6 convert_add_fusion.1
  375.3 12.6 %collective-permute-done.7 = bf16[2,2,1,1,1,24,2304]{6,5,4,3,2,1,0:T(8,128)(2,1)S(1)} collective-permute-done((bf16[2,2,1,1,1,24,2304]{6,5,4,3,2,1,0:T(8,128)(2,1)S(1)}, bf16[2,2,1,1,1,24,2304]{6,5,4,3,2,1,0:T(8,128)(2,1)S(1)}, u32[]{:S(2)}, u32[]{:S(2)}) %collective-permute-start.7) | collective-permute-done | bytes 442400 | tf_op jit(solution)/shard_map/ppermute | solution.py:101
  389.3 2.4 convert_add_fusion
  393.4 9.8 %collective-permute-done.8 = bf16[2,1,1,1,1,24,2304]{6,5,4,3,2,1,0:T(8,128)(2,1)S(1)} collective-permute-done((bf16[2,1,1,1,1,24,2304]{6,5,4,3,2,1,0:T(8,128)(2,1)S(1)}, bf16[2,1,1,1,1,24,2304]{6,5,4,3,2,1,0:T(8,128)(2,1)S(1)}, u32[]{:S(2)}, u32[]{:S(2)}) %collective-permute-start.8) | collective-permute-done | bytes 221216 | tf_op jit(solution)/shard_map/ppermute | solution.py:101
  405.9 17.3 %collective-permute-done.9 = bf16[1,1,1,1,1,24,2304]{6,5,4,3,2,1,0:T(8,128)(2,1)S(1)} collective-permute-done((bf16[1,1,1,1,1,24,2304]{6,5,4,3,2,1,0:T(8,128)(2,1)S(1)}, bf16[1,1,1,1,1,24,2304]{6,5,4,3,2,1,0:T(8,128)(2,1)S(1)}, u32[]{:S(2)}, u32[]{:S(2)}) %collective-permute-start.9) | collective-permute-done | bytes 110624 | tf_op jit(solution)/shard_map/ppermute | solution.py:101
  425.7 3.4 copy.125
  429.1 4.4 collective-permute-done.17
  434.8 2.6 collective-permute-done.22
  438.8 7.4 %collective-permute-done.18 = bf16[1,1,1,2,1,24,3072]{6,5,4,3,2,1,0:T(8,128)(2,1)S(1)} collective-permute-done((bf16[1,1,1,2,1,24,3072]{6,5,4,3,2,1,0:T(8,128)(2,1)S(1)}, bf16[1,1,1,2,1,24,3072]{6,5,4,3,2,1,0:T(8,128)(2,1)S(1)}, u32[]{:S(2)}, u32[]{:S(2)}) %collective-permute-start.18) | collective-permute-done | bytes 294944 | tf_op jit(solution)/shard_map/ppermute | solution.py:101
  446.3 9.2 %collective-permute-done.23 = bf16[1,2,1,1,1,96,768]{6,5,4,3,2,1,0:T(8,128)(2,1)S(1)} collective-permute-done((bf16[1,2,1,1,1,96,768]{6,5,4,3,2,1,0:T(8,128)(2,1)S(1)}, bf16[1,2,1,1,1,96,768]{6,5,4,3,2,1,0:T(8,128)(2,1)S(1)}, u32[]{:S(2)}, u32[]{:S(2)}) %collective-permute-start.23) | collective-permute-done | bytes 294944 | tf_op jit(solution)/shard_map/ppermute | solution.py:101
  457.8 3.0 collective-permute-done.24
  (355 shorter events, 99.6 us)
Async XLA Ops:
  7.2 121.5 %all-gather.3.cloned.1.call-start = ((), (), s32[]{:S(2)}) async-start(), calls=%async_computation.2 | async-start | bytes 10948608 | tf_op jit(solution)/shard_map/all_gather | solution.py:217
  17.5 75.4 %all-to-all-start.1 = ((bf16[64,32,512]{2,1,0:T(8,128)(2,1)}), bf16[64,32,512]{2,1,0:T(8,128)(2,1)S(1)}, u32[]{:S(2)}, u32[]{:S(2)}) async-start(bf16[64,32,512]{2,1,0:T(8,128)(2,1)} %param.35), calls=%async_computation.1 | async-start | bytes 4194304 | tf_op jit(solution)/shard_map/all_to_all | solution.py:283
  24.8 168.9 %all-gather.5.cloned.1.call-start = ((), (), s32[]{:S(2)}) async-start(), calls=%async_computation.3 | async-start | bytes 4866048 | tf_op jit(solution)/shard_map/all_gather | solution.py:233
  26.0 68.7 %copy-start.54 = (pred[2,1024]{1,0:T(4,128)(4,1)}, pred[2,1024]{1,0:T(4,128)(4,1)S(1)}, u32[]{:S(2)}) copy-start(pred[2,1024]{1,0:T(4,128)(4,1)S(1)} %broadcast_compare_fusion) | copy-start | bytes 6148
  26.2 104.7 %copy-start.58 = (f32[2,128]{1,0:T(2,128)}, f32[2,128]{1,0:T(2,128)S(1)}, u32[]{:S(2)}) copy-start(f32[2,128]{1,0:T(2,128)S(1)} %fusion.65) | copy-start | bytes 3076
  94.7 36.3 %copy-start.24 = (bf16[2,256,768]{2,1,0:T(8,128)(2,1)S(1)}, bf16[2,256,768]{2,1,0:T(8,128)(2,1)}, u32[]{:S(2)}) copy-start(bf16[2,256,768]{2,1,0:T(8,128)(2,1)} %param.18) | copy-start | bytes 2359300
  131.7 30.9 %copy-start.1 = (f32[2,256,768]{2,1,0:T(8,128)}, f32[2,256,768]{2,1,0:T(8,128)S(1)}, u32[]{:S(2)}) copy-start(f32[2,256,768]{2,1,0:T(8,128)S(1)} %get-tuple-element.30) | copy-start | bytes 4718596
  165.0 42.7 %copy-start.5 = (f32[512,768]{1,0:T(8,128)}, f32[512,768]{1,0:T(8,128)S(1)}, u32[]{:S(2)}) copy-start(f32[512,768]{1,0:T(8,128)S(1)} %get-tuple-element.50) | copy-start | bytes 4718596
  167.9 39.8 %copy-start.3 = (f32[512,768]{1,0:T(8,128)}, f32[512,768]{1,0:T(8,128)S(1)}, u32[]{:S(2)}) copy-start(f32[512,768]{1,0:T(8,128)S(1)} %fusion.49) | copy-start | bytes 4718596
  168.0 25.7 %copy-start.57 = (f32[3072]{0:T(1024)S(1)}, f32[3072]{0:T(1024)}, u32[]{:S(2)}) copy-start(f32[3072]{0:T(1024)} %reshape.348) | copy-start | bytes 36868
  256.0 169.7 %all-to-all-start = ((bf16[2,1024,512]{2,0,1:T(2,128)(2,1)}), bf16[2,1024,512]{2,0,1:T(2,128)(2,1)}, u32[]{:S(2)}, u32[]{:S(2)}) async-start(bf16[2,1024,512]{2,0,1:T(2,128)(2,1)} %copy.124), calls=%async_computation | async-start | bytes 4194304 | tf_op jit(solution)/shard_map/all_to_all | solution.py:282
  275.0 11.4 %collective-permute-start = (bf16[2,2,1,2,2,1,8,512]{7,6,5,4,3,2,1,0:T(8,128)(2,1)S(1)}, bf16[2,2,1,2,2,1,8,512]{7,6,5,4,3,2,1,0:T(8,128)(2,1)S(1)}, u32[]{:S(2)}, u32[]{:S(2)}) collective-permute-start(bf16[2,2,1,2,2,1,8,512]{7,6,5,4,3,2,1,0:T(8,128)(2,1)S(1)} %dynamic-slice_convert_fusion.19), channel_id=1, source_target_pairs={{0,4},{1,5},{2,6},{3,7},{4,0},{5,1},{6,2},{7,3},{8,12},{9,13},{10,... | collective-permute-start | bytes 393224 | tf_op jit(solution)/shard_map/ppermute | solution.py:101
  281.6 63.5 %collective-permute-start.5 = (bf16[2,2,1,2,2,24,2304]{6,5,4,3,2,1,0:T(8,128)(2,1)}, bf16[2,2,1,2,2,24,2304]{6,5,4,3,2,1,0:T(8,128)(2,1)}, u32[]{:S(2)}, u32[]{:S(2)}) collective-permute-start(bf16[2,2,1,2,2,24,2304]{6,5,4,3,2,1,0:T(8,128)(2,1)} %dynamic-slice_convert_fusion.2), channel_id=1, source_target_pairs={{0,4},{1,5},{2,6},{3,7},{4,0},{5,1},{6,2},{7,3},{8,12},{9,13},{10,... | collective-permute-start | bytes 5308424 | tf_op jit(solution)/shard_map/ppermute | solution.py:101
  286.0 42.0 %collective-permute-start.10 = (bf16[2,2,1,2,2,24,768]{6,5,4,3,2,1,0:T(8,128)(2,1)}, bf16[2,2,1,2,2,24,768]{6,5,4,3,2,1,0:T(8,128)(2,1)}, u32[]{:S(2)}, u32[]{:S(2)}) collective-permute-start(bf16[2,2,1,2,2,24,768]{6,5,4,3,2,1,0:T(8,128)(2,1)} %dynamic-slice_convert_fusion.8), channel_id=1, source_target_pairs={{0,4},{1,5},{2,6},{3,7},{4,0},{5,1},{6,2},{7,3},{8,12},{9,13},{10,... | collective-permute-start | bytes 1769480 | tf_op jit(solution)/shard_map/ppermute | solution.py:101
  286.5 8.9 %collective-permute-start.1 = (bf16[2,2,1,2,1,1,8,512]{7,6,5,4,3,2,1,0:T(8,128)(2,1)S(1)}, bf16[2,2,1,2,1,1,8,512]{7,6,5,4,3,2,1,0:T(8,128)(2,1)S(1)}, u32[]{:S(2)}, u32[]{:S(2)}) collective-permute-start(bf16[2,2,1,2,1,1,8,512]{7,6,5,4,3,2,1,0:T(8,128)(2,1)S(1)} %dynamic-slice_convert_fusion.23), channel_id=1, source_target_pairs={{0,1},{1,0},{2,3},{3,2},{4,5},{5,4},{6,7},{7,6},{8,9},{9,8},{10,11... | collective-permute-start | bytes 196616 | tf_op jit(solution)/shard_map/ppermute | solution.py:101
  292.3 78.9 %collective-permute-start.15 = (bf16[2,2,1,2,2,24,3072]{6,5,4,3,2,1,0:T(8,128)(2,1)}, bf16[2,2,1,2,2,24,3072]{6,5,4,3,2,1,0:T(8,128)(2,1)}, u32[]{:S(2)}, u32[]{:S(2)}) collective-permute-start(bf16[2,2,1,2,2,24,3072]{6,5,4,3,2,1,0:T(8,128)(2,1)} %dynamic-slice_convert_fusion.1), channel_id=1, source_target_pairs={{0,4},{1,5},{2,6},{3,7},{4,0},{5,1},{6,2},{7,3},{8,12},{9,13},{10,... | collective-permute-start | bytes 7077896 | tf_op jit(solution)/shard_map/ppermute | solution.py:101
  295.5 14.3 %collective-permute-start.2 = (bf16[2,2,1,1,1,1,8,512]{7,6,5,4,3,2,1,0:T(8,128)(2,1)S(1)}, bf16[2,2,1,1,1,1,8,512]{7,6,5,4,3,2,1,0:T(8,128)(2,1)S(1)}, u32[]{:S(2)}, u32[]{:S(2)}) collective-permute-start(bf16[2,2,1,1,1,1,8,512]{7,6,5,4,3,2,1,0:T(8,128)(2,1)S(1)} %dynamic-slice_convert_fusion.26), channel_id=1, source_target_pairs={{0,2},{1,3},{2,0},{3,1},{4,6},{5,7},{6,4},{7,5},{8,10},{9,11},{10,... | collective-permute-start | bytes 98312 | tf_op jit(solution)/shard_map/ppermute | solution.py:101
  304.3 85.0 %collective-permute-start.20 = (bf16[2,2,1,2,2,96,768]{6,5,4,3,2,1,0:T(8,128)(2,1)}, bf16[2,2,1,2,2,96,768]{6,5,4,3,2,1,0:T(8,128)(2,1)}, u32[]{:S(2)}, u32[]{:S(2)}) collective-permute-start(bf16[2,2,1,2,2,96,768]{6,5,4,3,2,1,0:T(8,128)(2,1)} %dynamic-slice_convert_fusion), channel_id=1, source_target_pairs={{0,4},{1,5},{2,6},{3,7},{4,0},{5,1},{6,2},{7,3},{8,12},{9,13},{10,... | collective-permute-start | bytes 7077896 | tf_op jit(solution)/shard_map/ppermute | solution.py:101
  309.8 3.8 collective-permute-start.3
  311.7 16.3 %copy-start.12 = (f32[2,2,2,2,2,24,768]{6,5,4,3,2,1,0:T(8,128)S(1)}, f32[2,2,2,2,2,24,768]{6,5,4,3,2,1,0:T(8,128)}, u32[]{:S(2)}) copy-start(f32[2,2,2,2,2,24,768]{6,5,4,3,2,1,0:T(8,128)} %copy-done.11) | copy-start | bytes 7077892
  313.6 3.7 collective-permute-start.4
  317.3 1.9 collective-permute-start.25
  320.5 7.4 %collective-permute-start.26 = (bf16[1,2,1,2,2,24,512]{6,5,4,3,2,1,0:T(8,128)(2,1)S(1)}, bf16[1,2,1,2,2,24,512]{6,5,4,3,2,1,0:T(8,128)(2,1)S(1)}, u32[]{:S(2)}, u32[]{:S(2)}) collective-permute-start(bf16[1,2,1,2,2,24,512]{6,5,4,3,2,1,0:T(8,128)(2,1)S(1)} %dynamic-slice_convert_fusion.15), channel_id=1, source_target_pairs={{0,16},{1,17},{2,18},{3,19},{4,20},{5,21},{6,22},{7,23},{8,24},{9,... | collective-permute-start | bytes 589832 | tf_op jit(solution)/shard_map/ppermute | solution.py:101
  328.0 4.7 collective-permute-start.27
  329.3 8.6 %collective-permute-start.11 = (bf16[2,1,1,2,2,24,768]{6,5,4,3,2,1,0:T(8,128)(2,1)S(1)}, bf16[2,1,1,2,2,24,768]{6,5,4,3,2,1,0:T(8,128)(2,1)S(1)}, u32[]{:S(2)}, u32[]{:S(2)}) collective-permute-start(bf16[2,1,1,2,2,24,768]{6,5,4,3,2,1,0:T(8,128)(2,1)S(1)} %dynamic-slice_convert_fusion.13), channel_id=1, source_target_pairs={{0,8},{1,9},{2,10},{3,11},{4,12},{5,13},{6,14},{7,15},{8,0},{9,1},... | collective-permute-start | bytes 884744 | tf_op jit(solution)/shard_map/ppermute | solution.py:101
  332.7 6.9 %collective-permute-start.28 = (bf16[1,2,1,1,1,24,512]{6,5,4,3,2,1,0:T(8,128)(2,1)S(1)}, bf16[1,2,1,1,1,24,512]{6,5,4,3,2,1,0:T(8,128)(2,1)S(1)}, u32[]{:S(2)}, u32[]{:S(2)}) collective-permute-start(bf16[1,2,1,1,1,24,512]{6,5,4,3,2,1,0:T(8,128)(2,1)S(1)} %dynamic-slice_convert_fusion.24), channel_id=1, source_target_pairs={{0,2},{1,3},{2,0},{3,1},{4,6},{5,7},{6,4},{7,5},{8,10},{9,11},{10,... | collective-permute-start | bytes 147464 | tf_op jit(solution)/shard_map/ppermute | solution.py:101
  337.9 33.2 %slice-start.5 = ((s8[9437184]{0:T(1024)(128)(4,1)}), s8[4194304]{0:T(1024)(128)(4,1)S(1)}, s32[]{:S(2)}) async-start(s8[9437184]{0:T(1024)(128)(4,1)} %bitcast.162), calls=%async_computation.9 | async-start | bytes 8388608
  338.0 5.2 %collective-permute-start.12 = (bf16[1,1,1,2,2,24,768]{6,5,4,3,2,1,0:T(8,128)(2,1)S(1)}, bf16[1,1,1,2,2,24,768]{6,5,4,3,2,1,0:T(8,128)(2,1)S(1)}, u32[]{:S(2)}, u32[]{:S(2)}) collective-permute-start(bf16[1,1,1,2,2,24,768]{6,5,4,3,2,1,0:T(8,128)(2,1)S(1)} %dynamic-slice_convert_fusion.18), channel_id=1, source_target_pairs={{0,16},{1,17},{2,18},{3,19},{4,20},{5,21},{6,22},{7,23},{8,24},{9,... | collective-permute-start | bytes 442376 | tf_op jit(solution)/shard_map/ppermute | solution.py:101
  343.3 27.9 %slice-start.6 = ((s8[9437184]{0:T(1024)(128)(4,1)}), s8[4194304]{0:T(1024)(128)(4,1)S(1)}, s32[]{:S(2)}) async-start(s8[9437184]{0:T(1024)(128)(4,1)} %bitcast.162), calls=%async_computation.10 | async-start | bytes 8388608
  343.3 6.6 %collective-permute-start.13 = (bf16[1,1,1,2,1,24,768]{6,5,4,3,2,1,0:T(8,128)(2,1)S(1)}, bf16[1,1,1,2,1,24,768]{6,5,4,3,2,1,0:T(8,128)(2,1)S(1)}, u32[]{:S(2)}, u32[]{:S(2)}) collective-permute-start(bf16[1,1,1,2,1,24,768]{6,5,4,3,2,1,0:T(8,128)(2,1)S(1)} %dynamic-slice_convert_fusion.22), channel_id=1, source_target_pairs={{0,1},{1,0},{2,3},{3,2},{4,5},{5,4},{6,7},{7,6},{8,9},{9,8},{10,11... | collective-permute-start | bytes 221192 | tf_op jit(solution)/shard_map/ppermute | solution.py:101
  348.0 23.2 %slice-start.7 = ((s8[9437184]{0:T(1024)(128)(4,1)}), s8[1048576]{0:T(1024)(128)(4,1)S(1)}, s32[]{:S(2)}) async-start(s8[9437184]{0:T(1024)(128)(4,1)} %bitcast.162), calls=%async_computation.11 | async-start | bytes 2097152
  348.1 19.5 %collective-permute-start.6 = (bf16[2,2,1,2,1,24,2304]{6,5,4,3,2,1,0:T(8,128)(2,1)S(1)}, bf16[2,2,1,2,1,24,2304]{6,5,4,3,2,1,0:T(8,128)(2,1)S(1)}, u32[]{:S(2)}, u32[]{:S(2)}) collective-permute-start(bf16[2,2,1,2,1,24,2304]{6,5,4,3,2,1,0:T(8,128)(2,1)S(1)} %dynamic-slice_convert_fusion.5), channel_id=1, source_target_pairs={{0,1},{1,0},{2,3},{3,2},{4,5},{5,4},{6,7},{7,6},{8,9},{9,8},{10,11... | collective-permute-start | bytes 2654216 | tf_op jit(solution)/shard_map/ppermute | solution.py:101
  348.7 3.8 collective-permute-start.29
  350.0 16.7 %collective-permute-start.14 = (bf16[1,1,1,1,1,24,768]{6,5,4,3,2,1,0:T(8,128)(2,1)S(1)}, bf16[1,1,1,1,1,24,768]{6,5,4,3,2,1,0:T(8,128)(2,1)S(1)}, u32[]{:S(2)}, u32[]{:S(2)}) collective-permute-start(bf16[1,1,1,1,1,24,768]{6,5,4,3,2,1,0:T(8,128)(2,1)S(1)} %dynamic-slice_convert_fusion.25), channel_id=1, source_target_pairs={{0,2},{1,3},{2,0},{3,1},{4,6},{5,7},{6,4},{7,5},{8,10},{9,11},{10,... | collective-permute-start | bytes 110600 | tf_op jit(solution)/shard_map/ppermute | solution.py:101
  367.8 21.5 %slice-start = ((s8[9437184]{0:T(1024)(128)(4,1)}), s8[4194304]{0:T(1024)(128)(4,1)S(1)}, s32[]{:S(2)}) async-start(s8[9437184]{0:T(1024)(128)(4,1)} %bitcast.151), calls=%async_computation.4 | async-start | bytes 8388608
  367.9 21.4 %slice-start.1 = ((s8[9437184]{0:T(1024)(128)(4,1)}), s8[4194304]{0:T(1024)(128)(4,1)S(1)}, s32[]{:S(2)}) async-start(s8[9437184]{0:T(1024)(128)(4,1)} %bitcast.151), calls=%async_computation.5 | async-start | bytes 8388608
  367.9 21.4 %slice-start.2 = ((s8[9437184]{0:T(1024)(128)(4,1)}), s8[1048576]{0:T(1024)(128)(4,1)S(1)}, s32[]{:S(2)}) async-start(s8[9437184]{0:T(1024)(128)(4,1)} %bitcast.151), calls=%async_computation.6 | async-start | bytes 2097152
  367.9 19.9 %collective-permute-start.7 = (bf16[2,2,1,1,1,24,2304]{6,5,4,3,2,1,0:T(8,128)(2,1)S(1)}, bf16[2,2,1,1,1,24,2304]{6,5,4,3,2,1,0:T(8,128)(2,1)S(1)}, u32[]{:S(2)}, u32[]{:S(2)}) collective-permute-start(bf16[2,2,1,1,1,24,2304]{6,5,4,3,2,1,0:T(8,128)(2,1)S(1)} %dynamic-slice_convert_fusion.9), channel_id=1, source_target_pairs={{0,2},{1,3},{2,0},{3,1},{4,6},{5,7},{6,4},{7,5},{8,10},{9,11},{10,... | collective-permute-start | bytes 1327112 | tf_op jit(solution)/shard_map/ppermute | solution.py:101
  374.0 30.9 %collective-permute-start.16 = (bf16[2,1,1,2,2,24,3072]{6,5,4,3,2,1,0:T(8,128)(2,1)S(1)}, bf16[2,1,1,2,2,24,3072]{6,5,4,3,2,1,0:T(8,128)(2,1)S(1)}, u32[]{:S(2)}, u32[]{:S(2)}) collective-permute-start(bf16[2,1,1,2,2,24,3072]{6,5,4,3,2,1,0:T(8,128)(2,1)S(1)} %dynamic-slice_convert_fusion.4), channel_id=1, source_target_pairs={{0,8},{1,9},{2,10},{3,11},{4,12},{5,13},{6,14},{7,15},{8,0},{9,1},... | collective-permute-start | bytes 3538952 | tf_op jit(solution)/shard_map/ppermute | solution.py:101
  388.0 15.3 %collective-permute-start.8 = (bf16[2,1,1,1,1,24,2304]{6,5,4,3,2,1,0:T(8,128)(2,1)S(1)}, bf16[2,1,1,1,1,24,2304]{6,5,4,3,2,1,0:T(8,128)(2,1)S(1)}, u32[]{:S(2)}, u32[]{:S(2)}) collective-permute-start(bf16[2,1,1,1,1,24,2304]{6,5,4,3,2,1,0:T(8,128)(2,1)S(1)} %dynamic-slice_convert_fusion.14), channel_id=1, source_target_pairs={{0,8},{1,9},{2,10},{3,11},{4,12},{5,13},{6,14},{7,15},{8,0},{9,1},... | collective-permute-start | bytes 663560 | tf_op jit(solution)/shard_map/ppermute | solution.py:101
  391.9 32.0 %collective-permute-start.21 = (bf16[1,2,1,2,2,96,768]{6,5,4,3,2,1,0:T(8,128)(2,1)S(1)}, bf16[1,2,1,2,2,96,768]{6,5,4,3,2,1,0:T(8,128)(2,1)S(1)}, u32[]{:S(2)}, u32[]{:S(2)}) collective-permute-start(bf16[1,2,1,2,2,96,768]{6,5,4,3,2,1,0:T(8,128)(2,1)S(1)} %dynamic-slice_convert_fusion.3), channel_id=1, source_target_pairs={{0,16},{1,17},{2,18},{3,19},{4,20},{5,21},{6,22},{7,23},{8,24},{9,... | collective-permute-start | bytes 3538952 | tf_op jit(solution)/shard_map/ppermute | solution.py:101
  403.3 19.8 %collective-permute-start.9 = (bf16[1,1,1,1,1,24,2304]{6,5,4,3,2,1,0:T(8,128)(2,1)S(1)}, bf16[1,1,1,1,1,24,2304]{6,5,4,3,2,1,0:T(8,128)(2,1)S(1)}, u32[]{:S(2)}, u32[]{:S(2)}) collective-permute-start(bf16[1,1,1,1,1,24,2304]{6,5,4,3,2,1,0:T(8,128)(2,1)S(1)} %dynamic-slice_convert_fusion.20), channel_id=1, source_target_pairs={{0,16},{1,17},{2,18},{3,19},{4,20},{5,21},{6,22},{7,23},{8,24},{9,... | collective-permute-start | bytes 331784 | tf_op jit(solution)/shard_map/ppermute | solution.py:101
  405.3 28.3 %collective-permute-start.17 = (bf16[1,1,1,2,2,24,3072]{6,5,4,3,2,1,0:T(8,128)(2,1)S(1)}, bf16[1,1,1,2,2,24,3072]{6,5,4,3,2,1,0:T(8,128)(2,1)}, u32[]{:S(2)}, u32[]{:S(2)}) collective-permute-start(bf16[1,1,1,2,2,24,3072]{6,5,4,3,2,1,0:T(8,128)(2,1)S(1)} %dynamic-slice_convert_fusion.7), channel_id=1, source_target_pairs={{0,16},{1,17},{2,18},{3,19},{4,20},{5,21},{6,22},{7,23},{8,24},{9,... | collective-permute-start | bytes 1769480 | tf_op jit(solution)/shard_map/ppermute | solution.py:101
  425.6 11.9 %collective-permute-start.22 = (bf16[1,2,1,2,1,96,768]{6,5,4,3,2,1,0:T(8,128)(2,1)S(1)}, bf16[1,2,1,2,1,96,768]{6,5,4,3,2,1,0:T(8,128)(2,1)}, u32[]{:S(2)}, u32[]{:S(2)}) collective-permute-start(bf16[1,2,1,2,1,96,768]{6,5,4,3,2,1,0:T(8,128)(2,1)S(1)} %dynamic-slice_convert_fusion.6), channel_id=1, source_target_pairs={{0,1},{1,0},{2,3},{3,2},{4,5},{5,4},{6,7},{7,6},{8,9},{9,8},{10,11... | collective-permute-start | bytes 1769480 | tf_op jit(solution)/shard_map/ppermute | solution.py:101
  434.7 11.4 %collective-permute-start.18 = (bf16[1,1,1,2,1,24,3072]{6,5,4,3,2,1,0:T(8,128)(2,1)S(1)}, bf16[1,1,1,2,1,24,3072]{6,5,4,3,2,1,0:T(8,128)(2,1)S(1)}, u32[]{:S(2)}, u32[]{:S(2)}) collective-permute-start(bf16[1,1,1,2,1,24,3072]{6,5,4,3,2,1,0:T(8,128)(2,1)S(1)} %dynamic-slice_convert_fusion.12), channel_id=1, source_target_pairs={{0,1},{1,0},{2,3},{3,2},{4,5},{5,4},{6,7},{7,6},{8,9},{9,8},{10,11... | collective-permute-start | bytes 884744 | tf_op jit(solution)/shard_map/ppermute | solution.py:101
  438.7 16.8 %collective-permute-start.23 = (bf16[1,2,1,1,1,96,768]{6,5,4,3,2,1,0:T(8,128)(2,1)S(1)}, bf16[1,2,1,1,1,96,768]{6,5,4,3,2,1,0:T(8,128)(2,1)S(1)}, u32[]{:S(2)}, u32[]{:S(2)}) collective-permute-start(bf16[1,2,1,1,1,96,768]{6,5,4,3,2,1,0:T(8,128)(2,1)S(1)} %dynamic-slice_convert_fusion.11), channel_id=1, source_target_pairs={{0,2},{1,3},{2,0},{3,1},{4,6},{5,7},{6,4},{7,5},{8,10},{9,11},{10,... | collective-permute-start | bytes 884744 | tf_op jit(solution)/shard_map/ppermute | solution.py:101
  446.3 10.8 %collective-permute-start.19 = (bf16[1,1,1,1,1,24,3072]{6,5,4,3,2,1,0:T(8,128)(2,1)S(1)}, bf16[1,1,1,1,1,24,3072]{6,5,4,3,2,1,0:T(8,128)(2,1)S(1)}, u32[]{:S(2)}, u32[]{:S(2)}) collective-permute-start(bf16[1,1,1,1,1,24,3072]{6,5,4,3,2,1,0:T(8,128)(2,1)S(1)} %dynamic-slice_convert_fusion.17), channel_id=1, source_target_pairs={{0,2},{1,3},{2,0},{3,1},{4,6},{5,7},{6,4},{7,5},{8,10},{9,11},{10,... | collective-permute-start | bytes 442376 | tf_op jit(solution)/shard_map/ppermute | solution.py:101
  455.6 5.2 %collective-permute-start.24 = (bf16[1,1,1,1,1,96,768]{6,5,4,3,2,1,0:T(8,128)(2,1)S(1)}, bf16[1,1,1,1,1,96,768]{6,5,4,3,2,1,0:T(8,128)(2,1)S(1)}, u32[]{:S(2)}, u32[]{:S(2)}) collective-permute-start(bf16[1,1,1,1,1,96,768]{6,5,4,3,2,1,0:T(8,128)(2,1)S(1)} %dynamic-slice_convert_fusion.16), channel_id=1, source_target_pairs={{0,8},{1,9},{2,10},{3,11},{4,12},{5,13},{6,14},{7,15},{8,0},{9,1},... | collective-permute-start | bytes 442376 | tf_op jit(solution)/shard_map/ppermute | solution.py:101
  (63 other events, 232.3 us)
Sparse Core Ops, SparseCore 0:
  17.6 111.0 all-gather.2
  131.4 62.1 all-gather.4

commit v2 on v1

--- a/solution.py
+++ b/solution.py
@@ -103,6 +103,17 @@
         )
         current = keep + moved.astype(jnp.float32)
     return current.reshape((rows,) + grad.shape[1:])
+
+
+def rs_split(grad, n_bits, orders, first):
+    cols = grad.shape[-1]
+    parts = 3 if cols % 384 == 0 else (2 if cols % 256 == 0 else 1)
+    width = cols // parts
+    pieces = [
+        rs_chain(grad[..., k * width : (k + 1) * width], n_bits, orders[(first + k) % len(orders)])
+        for k in range(parts)
+    ]
+    return pieces[0] if parts == 1 else jnp.concatenate(pieces, axis=-1)
 
 
 def pack_rows(arrays, n_dev, dtype):
@@ -294,19 +305,23 @@
         grad_dec_bias = jnp.sum(grad_vis, axis=0)
         grad_dec_weight = inner_rows(enc_low, grad_vis_low)
         grad_res_two = outer_cols(grad_vis_low, dec_full)
+        grad_dec_weight, grad_res_two = lax.optimization_barrier((grad_dec_weight, grad_res_two))
         grad_ffo = grad_res_two.astype(jnp.bfloat16)
         grad_mlp_out_bias = jnp.sum(grad_ffo.astype(jnp.float32), axis=0)
         grad_mlp_out = inner_rows(active, grad_ffo)
         grad_hidden = (outer_cols(grad_ffo, outer_full) * gelu_slope(hidden)).astype(jnp.bfloat16)
+        grad_mlp_out, grad_hidden = lax.optimization_barrier((grad_mlp_out, grad_hidden))
         grad_mlp_in_bias = jnp.sum(grad_hidden.astype(jnp.float32), axis=0)
         grad_mlp_in = inner_rows(act_two, grad_hidden)
         grad_act_two = outer_cols(grad_hidden, inner_full)
+        grad_mlp_in, grad_act_two = lax.optimization_barrier((grad_mlp_in, grad_act_two))
         grad_norm_two, grad_norm2_gain, grad_norm2_bias = norm_backward(
             grad_act_two, normed_two, inverse_two, gain_two.astype(jnp.float32)
         )
         grad_res_one = grad_res_two + grad_norm_two
         grad_att = grad_res_one.astype(jnp.bfloat16)
         grad_out_weight = inner_rows(mixture, grad_att)
+        grad_out_weight, grad_att = lax.optimization_barrier((grad_out_weight, grad_att))
         grad_mixed = outer_cols(grad_att, out_full).astype(jnp.bfloat16).reshape(head_shape)
         grad_queries, grad_keys, grad_values = attend_back(
             queries, key_rows, value_rows, soft_full, soft_low, grad_mixed
@@ -337,11 +352,11 @@
         reduced_sg = rs_chain(packed_sg, n_bits, turn(2))
         (sum_wave, sum_g1, sum_b1, sum_g2, sum_b2, sum_ib, sum_ob, sum_db,
          sum_mask) = unpack_rows(reduced_sg, small_grads, sg_widths, n_dev, 1)
-        sum_dec = rs_chain(grad_dec_weight, n_bits, turn(1))
-        sum_mlp_out = rs_chain(grad_mlp_out, n_bits, turn(1))
-        sum_mlp_in = rs_chain(grad_mlp_in, n_bits, turn(0))
-        sum_out = rs_chain(grad_out_weight, n_bits, turn(0))
-        sum_qkv = rs_chain(grad_qkv_weight, n_bits, turn(2))
+        sum_dec = rs_split(grad_dec_weight, n_bits, orders, 1)
+        sum_mlp_out = rs_split(grad_mlp_out, n_bits, orders, 1)
+        sum_mlp_in = rs_split(grad_mlp_in, n_bits, orders, 0)
+        sum_out = rs_split(grad_out_weight, n_bits, orders, 0)
+        sum_qkv = rs_split(grad_qkv_weight, n_bits, orders, 2)
         summed = (sum_wave, sum_g1, sum_b1, sum_qkv, sum_out, sum_g2, sum_b2, sum_mlp_in,
                   sum_ib, sum_mlp_out, sum_ob, sum_dec, sum_db, sum_mask)
         return (decoded, grad_tokens, *summed)

time: 478 us -> 584 us (1.22)
  starting transfers between devices: 42.5 us -> 100 us
  local copies, waits for them, and re-layouts: 70.2 us -> 106 us
  waiting for transfers between devices: 227 us -> 247 us
  matrix products: 81.2 us -> 71.4 us
    ppermute x30 -> x75, starting transfers between devices: 31.2 us -> 89 us  [rs_chain(): lax.ppermute(send.astype(jnp.bfloat16), AX, [(i, i ^ 1 << bit) for i in r...]
    slice x0 -> x5, local copies, waits for them, and re-layouts: none -> 19.4 us  [rs_split(): grad[..., k * width:(k + 1) * width]]
    ppermute x30 -> x75, waiting for transfers between devices: 109 us -> 122 us  [rs_chain(): lax.ppermute(send.astype(jnp.bfloat16), AX, [(i, i ^ 1 << bit) for i in r...]
    convert_element_type x30 -> x75, local copies, waits for them, and re-layouts: 11.7 us -> 23.7 us  [rs_chain(): send.astype(jnp.bfloat16)]
    dot_general x5, matrix products: 23 us -> 14.2 us  [outer_cols(): lax.dot_general(left_op, right_op, (((1,), (1,)), ((), ())), preferred_el...]
    all_gather x1, waiting for transfers between devices: 18 us -> 25.2 us  [local(): outer_full = lax.all_gather(mlp_out, AX, axis=0, tiled=True)]
    unnamed x167 -> x193, local copies, waits for them, and re-layouts: 14.7 us -> 17.1 us
    add x24 -> x60, other arithmetic: 13.9 us -> 12.9 us  [rs_chain(): current = keep + moved.astype(jnp.float32)]
  transfers between devices with their start and end apart: 34 -> 79, of which waited for: 22 -> 47; matrix products, arithmetic and copies ran while one was open for 22% -> 23% of each run, Pallas kernels for 0% -> 0%
where the time goes in v2:
time: 584 us; the launch traced here: 573 us
  waiting for transfers between devices  247 us (42%)
  local copies, waits for them, and re-layouts  106 us (18%)
  starting transfers between devices  100 us (17%)
  matrix products  71.4 us (12%)
  other arithmetic  32.3 us (6%)
  between operations  16.6 us (3%)
    ppermute x75, waiting for transfers between devices, rs_chain(): lax.ppermute(send.astype(jnp.bfloat16), AX, [(i, i ^ 1 << bit) for i in r...  122 us
    ppermute x75, starting transfers between devices, rs_chain(): lax.ppermute(send.astype(jnp.bfloat16), AX, [(i, i ^ 1 << bit) for i in r...  89 us
    all_to_all x1, waiting for transfers between devices, local(): lax.all_to_all(cot_decoded, AX, split_axis=0, concat_axis=1, tiled=True)  66.7 us
    all_gather x1, waiting for transfers between devices, local(): lax.all_gather(jnp.concatenate(wide, axis=1), AX, axis=0, tiled=True)  32 us
    all_gather x1, waiting for transfers between devices, local(): outer_full = lax.all_gather(mlp_out, AX, axis=0, tiled=True)  25.2 us
    convert_element_type x75, local copies, waits for them, and re-layouts, rs_chain(): send.astype(jnp.bfloat16)  23.7 us
    dot_general x5, matrix products, inner_rows(): lax.dot_general(left_op, right_op, (((0,), (0,)), ((), ())), preferred_el...  20.3 us
    slice x5, local copies, waits for them, and re-layouts, rs_split(): grad[..., k * width:(k + 1) * width]  19.4 us
  transfers between devices with their start and end apart: 79, of which 47 were waited for; matrix products, arithmetic and copies ran while one was open for 23% of the time, Pallas kernels for 0%

profile of v2, /device:TPU:0, one launch (start us, length us, event | category | flops | bytes accessed | tf_op | source)
XLA Modules:
  0.0 573.0 jit_solution(604321813798275115)
XLA Ops:
  7.9 5.4 concatenate.28
  17.5 7.3 %all-to-all-start.1 = ((bf16[64,32,512]{2,1,0:T(8,128)(2,1)}), bf16[64,32,512]{2,1,0:T(8,128)(2,1)S(1)}, u32[]{:S(2)}, u32[]{:S(2)}) async-start(bf16[64,32,512]{2,1,0:T(8,128)(2,1)} %param.35), calls=%async_computation.1 | async-start | bytes 4194304 | tf_op jit(solution)/shard_map/all_to_all | solution.py:294
  26.2 66.7 %all-to-all-done.1 = bf16[64,32,512]{2,1,0:T(8,128)(2,1)S(1)} async-done(((bf16[64,32,512]{2,1,0:T(8,128)(2,1)}), bf16[64,32,512]{2,1,0:T(8,128)(2,1)S(1)}, u32[]{:S(2)}, u32[]{:S(2)}) %all-to-all-start.1) | async-done | bytes 2097184 | tf_op jit(solution)/shard_map/all_to_all | solution.py:294
  96.6 32.0 %all-gather.3.cloned.1.call-done = bf16[768,6912]{1,0:T(8,128)(2,1)} async-done(((bf16[24,6912]{1,0:T(8,128)(2,1)}), bf16[768,6912]{1,0:T(8,128)(2,1)}) %all-gather.3.cloned.1.call-update) | async-done | bytes 10616848 | tf_op jit(solution)/shard_map/all_gather | solution.py:228
  132.9 4.3 convolution_convert_fusion
  145.0 2.6 copy.103
  147.6 2.9 reshape.365
  151.6 4.8 fusion.96
  162.9 5.7 multiply_convert_fusion.1
  168.5 25.2 %all-gather.5.cloned.1.call-done = bf16[3072,768]{1,0:T(8,128)(2,1)} async-done(((bf16[96,768]{1,0:T(8,128)(2,1)}), bf16[3072,768]{1,0:T(8,128)(2,1)}) %all-gather.5.cloned.1.call-update) | async-done | bytes 4718608 | tf_op jit(solution)/shard_map/all_gather | solution.py:244
  193.7 6.0 %add_convert_fusion = bf16[512,768]{1,0:T(8,128)(2,1)S(1)} fusion(f32[512,768]{1,0:T(8,128)S(1)} %get-tuple-element.81, bf16[512,3072]{1,0:T(8,128)(2,1)} %get-tuple-element.82, bf16[3072,768]{1,0:T(8,128)(2,1)} %all-gather.5.cloned.1.call-done, f32[768]{0:T(1024)S(1)} %reshape.427), kind=kOutput, calls=%fused_computation.56 | convolution fusion | flops 2417098752 | bytes 10226688 | tf_op jit(solution)/shard_map/dot_general | solution.py:21
  203.1 5.6 fusion.83
  209.0 4.6 fusion.6
  214.3 5.9 %fusion.87 = f32[768,3072]{1,0:T(8,128)} fusion(bf16[512,3072]{1,0:T(8,128)(2,1)S(1)} %fusion.6, f32[512,768]{1,0:T(8,128)S(1)} %get-tuple-element.81, f32[768]{0:T(1024)S(1)} %reshape.425, f32[768]{0:T(1024)S(1)} %reshape.424, f32[512]{0:T(512)S(1)} %add_rsqrt_fusion, f32[512]{0:T(512)S(1)} %broadcast_multiply_fusion.4), kind=kOutput, calls=%fused_computation.304 | convolution fusion | flops 2417885184 | bytes 14166016 | tf_op jit(solution)/shard_map/dot_general | solution.py:25
  220.1 2.6 fusion.10
  231.8 5.2 fusion.31
  237.0 3.9 multiply_reduce_fusion
  240.9 4.3 multiply_convert_fusion
  254.7 3.5 copy.112
  258.2 3.7 all-to-all-start
  261.9 7.3 %fusion.89 = (f32[3072,256]{1,0:T(8,128)}, f32[3072,256]{1,0:T(8,128)S(1)}, f32[3072,256]{1,0:T(8,128)}) fusion(f32[3072,768]{1,0:T(8,128)} %fusion.83), kind=kLoop, calls=%fused_computation.306 | loop fusion | bytes 18874368 | tf_op jit(solution)/shard_map/slice | solution.py:113
  275.8 8.1 %fusion.90 = (f32[768,1024]{1,0:T(8,128)}, f32[768,1024]{1,0:T(8,128)S(1)}, f32[768,1024]{1,0:T(8,128)}) fusion(f32[768,3072]{1,0:T(8,128)} %fusion.87), kind=kLoop, calls=%fused_computation.307 | loop fusion | bytes 18874368 | tf_op jit(solution)/shard_map/slice | solution.py:113
  296.1 4.9 fusion.101
  301.0 4.7 multiply_reduce_fusion.3
  315.2 3.6 fusion.91
  321.7 3.2 dynamic-slice_convert_fusion.4
  333.4 2.6 collective-permute-start.2
  357.3 3.2 collective-permute-done.26
  377.1 2.9 collective-permute-done.72
  388.4 2.8 collective-permute-start.32
  393.4 3.1 collective-permute-start.68
  402.1 2.9 collective-permute-start.28
  425.6 3.1 collective-permute-start.24
  459.7 17.0 %collective-permute-done.12 = bf16[1,1,1,2,2,24,768]{6,5,4,3,2,1,0:T(8,128)(2,1)S(1)} collective-permute-done((bf16[1,1,1,2,2,24,768]{6,5,4,3,2,1,0:T(8,128)(2,1)S(1)}, bf16[1,1,1,2,2,24,768]{6,5,4,3,2,1,0:T(8,128)(2,1)S(1)}, u32[]{:S(2)}, u32[]{:S(2)}) %collective-permute-start.12) | collective-permute-done | bytes 147488 | tf_op jit(solution)/shard_map/ppermute | solution.py:101
  476.7 2.9 collective-permute-start.7
  479.6 5.9 %collective-permute-done.7 = bf16[2,2,1,1,1,24,768]{6,5,4,3,2,1,0:T(8,128)(2,1)S(1)} collective-permute-done((bf16[2,2,1,1,1,24,768]{6,5,4,3,2,1,0:T(8,128)(2,1)S(1)}, bf16[2,2,1,1,1,24,768]{6,5,4,3,2,1,0:T(8,128)(2,1)S(1)}, u32[]{:S(2)}, u32[]{:S(2)}) %collective-permute-start.7) | collective-permute-done | bytes 147488 | tf_op jit(solution)/shard_map/ppermute | solution.py:101
  485.6 5.5 collective-permute-done.17
  491.4 4.0 collective-permute-done.13
  495.8 4.0 collective-permute-done.8
  500.9 5.4 collective-permute-done.18
  506.4 4.8 collective-permute-done.14
  515.9 3.2 collective-permute-done.19
  520.8 3.0 collective-permute-start.57
  528.2 7.3 %collective-permute-done.46 = bf16[2,2,1,2,1,24,1024]{6,5,4,3,2,1,0:T(8,128)(2,1)S(1)} collective-permute-done((bf16[2,2,1,2,1,24,1024]{6,5,4,3,2,1,0:T(8,128)(2,1)S(1)}, bf16[2,2,1,2,1,24,1024]{6,5,4,3,2,1,0:T(8,128)(2,1)S(1)}, u32[]{:S(2)}, u32[]{:S(2)}) %collective-permute-start.46) | collective-permute-done | bytes 393248 | tf_op jit(solution)/shard_map/ppermute | solution.py:101
  537.4 3.0 collective-permute-done.52
  542.0 2.8 collective-permute-done.42
  544.9 2.6 collective-permute-start.43
  562.4 3.4 copy.113
  (571 shorter events, 227.4 us)
Async XLA Ops:
  7.2 121.5 %all-gather.3.cloned.1.call-start = ((), (), s32[]{:S(2)}) async-start(), calls=%async_computation.2 | async-start | bytes 10948608 | tf_op jit(solution)/shard_map/all_gather | solution.py:228
  17.5 75.4 %all-to-all-start.1 = ((bf16[64,32,512]{2,1,0:T(8,128)(2,1)}), bf16[64,32,512]{2,1,0:T(8,128)(2,1)S(1)}, u32[]{:S(2)}, u32[]{:S(2)}) async-start(bf16[64,32,512]{2,1,0:T(8,128)(2,1)} %param.35), calls=%async_computation.1 | async-start | bytes 4194304 | tf_op jit(solution)/shard_map/all_to_all | solution.py:294
  24.8 168.9 %all-gather.5.cloned.1.call-start = ((), (), s32[]{:S(2)}) async-start(), calls=%async_computation.3 | async-start | bytes 4866048 | tf_op jit(solution)/shard_map/all_gather | solution.py:244
  251.2 74.2 %collective-permute-start.65 = (bf16[2,2,1,2,2,24,256]{6,5,4,3,2,1,0:T(8,128)(2,1)}, bf16[2,2,1,2,2,24,256]{6,5,4,3,2,1,0:T(8,128)(2,1)}, u32[]{:S(2)}, u32[]{:S(2)}) collective-permute-start(bf16[2,2,1,2,2,24,256]{6,5,4,3,2,1,0:T(8,128)(2,1)} %dynamic-slice_convert_fusion.19), channel_id=1, source_target_pairs={{0,4},{1,5},{2,6},{3,7},{4,0},{5,1},{6,2},{7,3},{8,12},{9,13},{10,... | collective-permute-start | bytes 589832 | tf_op jit(solution)/shard_map/ppermute | solution.py:101
  251.5 75.2 %collective-permute-start.70 = (bf16[2,2,1,2,2,24,256]{6,5,4,3,2,1,0:T(8,128)(2,1)}, bf16[2,2,1,2,2,24,256]{6,5,4,3,2,1,0:T(8,128)(2,1)}, u32[]{:S(2)}, u32[]{:S(2)}) collective-permute-start(bf16[2,2,1,2,2,24,256]{6,5,4,3,2,1,0:T(8,128)(2,1)} %dynamic-slice_convert_fusion.18), channel_id=1, source_target_pairs={{0,4},{1,5},{2,6},{3,7},{4,0},{5,1},{6,2},{7,3},{8,12},{9,13},{10,... | collective-permute-start | bytes 589832 | tf_op jit(solution)/shard_map/ppermute | solution.py:101
  258.2 304.2 %all-to-all-start = ((bf16[2,1024,512]{2,0,1:T(2,128)(2,1)}), bf16[2,1024,512]{2,0,1:T(2,128)(2,1)}, u32[]{:S(2)}, u32[]{:S(2)}) async-start(bf16[2,1024,512]{2,0,1:T(2,128)(2,1)} %copy.112), calls=%async_computation | async-start | bytes 4194304 | tf_op jit(solution)/shard_map/all_to_all | solution.py:293
  275.3 163.8 %collective-permute-start.55 = (bf16[2,2,1,2,2,96,256]{6,5,4,3,2,1,0:T(8,128)(2,1)}, bf16[2,2,1,2,2,96,256]{6,5,4,3,2,1,0:T(8,128)(2,1)}, u32[]{:S(2)}, u32[]{:S(2)}) collective-permute-start(bf16[2,2,1,2,2,96,256]{6,5,4,3,2,1,0:T(8,128)(2,1)} %dynamic-slice_convert_fusion.1), channel_id=1, source_target_pairs={{0,4},{1,5},{2,6},{3,7},{4,0},{5,1},{6,2},{7,3},{8,12},{9,13},{10,... | collective-permute-start | bytes 2359304 | tf_op jit(solution)/shard_map/ppermute | solution.py:101
  275.4 166.2 %collective-permute-start.50 = (bf16[2,2,1,2,2,96,256]{6,5,4,3,2,1,0:T(8,128)(2,1)}, bf16[2,2,1,2,2,96,256]{6,5,4,3,2,1,0:T(8,128)(2,1)}, u32[]{:S(2)}, u32[]{:S(2)}) collective-permute-start(bf16[2,2,1,2,2,96,256]{6,5,4,3,2,1,0:T(8,128)(2,1)} %dynamic-slice_convert_fusion.2), channel_id=1, source_target_pairs={{0,4},{1,5},{2,6},{3,7},{4,0},{5,1},{6,2},{7,3},{8,12},{9,13},{10,... | collective-permute-start | bytes 2359304 | tf_op jit(solution)/shard_map/ppermute | solution.py:101
  315.1 9.7 %collective-permute-start = (bf16[2,2,1,2,2,1,8,512]{7,6,5,4,3,2,1,0:T(8,128)(2,1)S(1)}, bf16[2,2,1,2,2,1,8,512]{7,6,5,4,3,2,1,0:T(8,128)(2,1)S(1)}, u32[]{:S(2)}, u32[]{:S(2)}) collective-permute-start(bf16[2,2,1,2,2,1,8,512]{7,6,5,4,3,2,1,0:T(8,128)(2,1)S(1)} %dynamic-slice_convert_fusion.32), channel_id=1, source_target_pairs={{0,4},{1,5},{2,6},{3,7},{4,0},{5,1},{6,2},{7,3},{8,12},{9,13},{10,... | collective-permute-start | bytes 393224 | tf_op jit(solution)/shard_map/ppermute | solution.py:101
  324.8 119.7 %collective-permute-start.60 = (bf16[2,2,1,2,2,96,256]{6,5,4,3,2,1,0:T(8,128)(2,1)}, bf16[2,2,1,2,2,96,256]{6,5,4,3,2,1,0:T(8,128)(2,1)}, u32[]{:S(2)}, u32[]{:S(2)}) collective-permute-start(bf16[2,2,1,2,2,96,256]{6,5,4,3,2,1,0:T(8,128)(2,1)} %dynamic-slice_convert_fusion), channel_id=1, source_target_pairs={{0,4},{1,5},{2,6},{3,7},{4,0},{5,1},{6,2},{7,3},{8,12},{9,13},{10,... | collective-permute-start | bytes 2359304 | tf_op jit(solution)/shard_map/ppermute | solution.py:101
  325.5 6.4 %collective-permute-start.25 = (bf16[2,2,1,2,2,24,256]{6,5,4,3,2,1,0:T(8,128)(2,1)S(1)}, bf16[2,2,1,2,2,24,256]{6,5,4,3,2,1,0:T(8,128)(2,1)S(1)}, u32[]{:S(2)}, u32[]{:S(2)}) collective-permute-start(bf16[2,2,1,2,2,24,256]{6,5,4,3,2,1,0:T(8,128)(2,1)S(1)} %copy-done.62), channel_id=1, source_target_pairs={{0,4},{1,5},{2,6},{3,7},{4,0},{5,1},{6,2},{7,3},{8,12},{9,13},{10,... | collective-permute-start | bytes 589832 | tf_op jit(solution)/shard_map/ppermute | solution.py:101
  332.6 102.8 %collective-permute-start.10 = (bf16[2,2,1,2,2,24,768]{6,5,4,3,2,1,0:T(8,128)(2,1)}, bf16[2,2,1,2,2,24,768]{6,5,4,3,2,1,0:T(8,128)(2,1)}, u32[]{:S(2)}, u32[]{:S(2)}) collective-permute-start(bf16[2,2,1,2,2,24,768]{6,5,4,3,2,1,0:T(8,128)(2,1)} %dynamic-slice_convert_fusion.7), channel_id=1, source_target_pairs={{0,4},{1,5},{2,6},{3,7},{4,0},{5,1},{6,2},{7,3},{8,12},{9,13},{10,... | collective-permute-start | bytes 1769480 | tf_op jit(solution)/shard_map/ppermute | solution.py:101
  365.3 5.1 collective-permute-start.31
  374.5 5.4 collective-permute-start.72
  388.4 5.0 collective-permute-start.32
  437.1 11.0 %collective-permute-start.40 = (bf16[2,2,1,2,2,24,1024]{6,5,4,3,2,1,0:T(8,128)(2,1)S(1)}, bf16[2,2,1,2,2,24,1024]{6,5,4,3,2,1,0:T(8,128)(2,1)S(1)}, u32[]{:S(2)}, u32[]{:S(2)}) collective-permute-start(bf16[2,2,1,2,2,24,1024]{6,5,4,3,2,1,0:T(8,128)(2,1)S(1)} %copy-done.50), channel_id=1, source_target_pairs={{0,4},{1,5},{2,6},{3,7},{4,0},{5,1},{6,2},{7,3},{8,12},{9,13},{10,... | collective-permute-start | bytes 2359304 | tf_op jit(solution)/shard_map/ppermute | solution.py:101
  438.1 11.9 %collective-permute-start.35 = (bf16[2,2,1,2,2,24,1024]{6,5,4,3,2,1,0:T(8,128)(2,1)S(1)}, bf16[2,2,1,2,2,24,1024]{6,5,4,3,2,1,0:T(8,128)(2,1)S(1)}, u32[]{:S(2)}, u32[]{:S(2)}) collective-permute-start(bf16[2,2,1,2,2,24,1024]{6,5,4,3,2,1,0:T(8,128)(2,1)S(1)} %copy-done.49), channel_id=1, source_target_pairs={{0,4},{1,5},{2,6},{3,7},{4,0},{5,1},{6,2},{7,3},{8,12},{9,13},{10,... | collective-permute-start | bytes 2359304 | tf_op jit(solution)/shard_map/ppermute | solution.py:101
  439.1 11.4 %collective-permute-start.45 = (bf16[2,2,1,2,2,24,1024]{6,5,4,3,2,1,0:T(8,128)(2,1)S(1)}, bf16[2,2,1,2,2,24,1024]{6,5,4,3,2,1,0:T(8,128)(2,1)S(1)}, u32[]{:S(2)}, u32[]{:S(2)}) collective-permute-start(bf16[2,2,1,2,2,24,1024]{6,5,4,3,2,1,0:T(8,128)(2,1)S(1)} %copy-done.48), channel_id=1, source_target_pairs={{0,4},{1,5},{2,6},{3,7},{4,0},{5,1},{6,2},{7,3},{8,12},{9,13},{10,... | collective-permute-start | bytes 2359304 | tf_op jit(solution)/shard_map/ppermute | solution.py:101
  441.6 10.7 %collective-permute-start.11 = (bf16[2,1,1,2,2,24,768]{6,5,4,3,2,1,0:T(8,128)(2,1)S(1)}, bf16[2,1,1,2,2,24,768]{6,5,4,3,2,1,0:T(8,128)(2,1)S(1)}, u32[]{:S(2)}, u32[]{:S(2)}) collective-permute-start(bf16[2,1,1,2,2,24,768]{6,5,4,3,2,1,0:T(8,128)(2,1)S(1)} %dynamic-slice_convert_fusion.16), channel_id=1, source_target_pairs={{0,8},{1,9},{2,10},{3,11},{4,12},{5,13},{6,14},{7,15},{8,0},{9,1},... | collective-permute-start | bytes 884744 | tf_op jit(solution)/shard_map/ppermute | solution.py:101
  444.5 10.0 %collective-permute-start.6 = (bf16[2,2,1,2,1,24,768]{6,5,4,3,2,1,0:T(8,128)(2,1)S(1)}, bf16[2,2,1,2,1,24,768]{6,5,4,3,2,1,0:T(8,128)(2,1)S(1)}, u32[]{:S(2)}, u32[]{:S(2)}) collective-permute-start(bf16[2,2,1,2,1,24,768]{6,5,4,3,2,1,0:T(8,128)(2,1)S(1)} %dynamic-slice_convert_fusion.17), channel_id=1, source_target_pairs={{0,1},{1,0},{2,3},{3,2},{4,5},{5,4},{6,7},{7,6},{8,9},{9,8},{10,11... | collective-permute-start | bytes 884744 | tf_op jit(solution)/shard_map/ppermute | solution.py:101
  448.1 9.9 %collective-permute-start.16 = (bf16[1,2,1,2,2,24,768]{6,5,4,3,2,1,0:T(8,128)(2,1)S(1)}, bf16[1,2,1,2,2,24,768]{6,5,4,3,2,1,0:T(8,128)(2,1)S(1)}, u32[]{:S(2)}, u32[]{:S(2)}) collective-permute-start(bf16[1,2,1,2,2,24,768]{6,5,4,3,2,1,0:T(8,128)(2,1)S(1)} %dynamic-slice_convert_fusion.15), channel_id=1, source_target_pairs={{0,16},{1,17},{2,18},{3,19},{4,20},{5,21},{6,22},{7,23},{8,24},{9,... | collective-permute-start | bytes 884744 | tf_op jit(solution)/shard_map/ppermute | solution.py:101
  450.0 70.5 %collective-permute-start.56 = (bf16[2,2,1,2,1,96,256]{6,5,4,3,2,1,0:T(8,128)(2,1)S(1)}, bf16[2,2,1,2,1,96,256]{6,5,4,3,2,1,0:T(8,128)(2,1)S(1)}, u32[]{:S(2)}, u32[]{:S(2)}) collective-permute-start(bf16[2,2,1,2,1,96,256]{6,5,4,3,2,1,0:T(8,128)(2,1)S(1)} %dynamic-slice_convert_fusion.10), channel_id=1, source_target_pairs={{0,1},{1,0},{2,3},{3,2},{4,5},{5,4},{6,7},{7,6},{8,9},{9,8},{10,11... | collective-permute-start | bytes 1179656 | tf_op jit(solution)/shard_map/ppermute | solution.py:101
  450.6 70.2 %collective-permute-start.51 = (bf16[1,2,1,2,2,96,256]{6,5,4,3,2,1,0:T(8,128)(2,1)S(1)}, bf16[1,2,1,2,2,96,256]{6,5,4,3,2,1,0:T(8,128)(2,1)S(1)}, u32[]{:S(2)}, u32[]{:S(2)}) collective-permute-start(bf16[1,2,1,2,2,96,256]{6,5,4,3,2,1,0:T(8,128)(2,1)S(1)} %dynamic-slice_convert_fusion.11), channel_id=1, source_target_pairs={{0,16},{1,17},{2,18},{3,19},{4,20},{5,21},{6,22},{7,23},{8,24},{9,... | collective-permute-start | bytes 1179656 | tf_op jit(solution)/shard_map/ppermute | solution.py:101
  452.3 71.7 %collective-permute-start.61 = (bf16[2,1,1,2,2,96,256]{6,5,4,3,2,1,0:T(8,128)(2,1)S(1)}, bf16[2,1,1,2,2,96,256]{6,5,4,3,2,1,0:T(8,128)(2,1)S(1)}, u32[]{:S(2)}, u32[]{:S(2)}) collective-permute-start(bf16[2,1,1,2,2,96,256]{6,5,4,3,2,1,0:T(8,128)(2,1)S(1)} %dynamic-slice_convert_fusion.9), channel_id=1, source_target_pairs={{0,8},{1,9},{2,10},{3,11},{4,12},{5,13},{6,14},{7,15},{8,0},{9,1},... | collective-permute-start | bytes 1179656 | tf_op jit(solution)/shard_map/ppermute | solution.py:101
  454.5 69.7 %collective-permute-start.41 = (bf16[1,2,1,2,2,24,1024]{6,5,4,3,2,1,0:T(8,128)(2,1)S(1)}, bf16[1,2,1,2,2,24,1024]{6,5,4,3,2,1,0:T(8,128)(2,1)S(1)}, u32[]{:S(2)}, u32[]{:S(2)}) collective-permute-start(bf16[1,2,1,2,2,24,1024]{6,5,4,3,2,1,0:T(8,128)(2,1)S(1)} %dynamic-slice_convert_fusion.13), channel_id=1, source_target_pairs={{0,16},{1,17},{2,18},{3,19},{4,20},{5,21},{6,22},{7,23},{8,24},{9,... | collective-permute-start | bytes 1179656 | tf_op jit(solution)/shard_map/ppermute | solution.py:101
  458.0 18.6 %collective-permute-start.12 = (bf16[1,1,1,2,2,24,768]{6,5,4,3,2,1,0:T(8,128)(2,1)S(1)}, bf16[1,1,1,2,2,24,768]{6,5,4,3,2,1,0:T(8,128)(2,1)S(1)}, u32[]{:S(2)}, u32[]{:S(2)}) collective-permute-start(bf16[1,1,1,2,2,24,768]{6,5,4,3,2,1,0:T(8,128)(2,1)S(1)} %dynamic-slice_convert_fusion.30), channel_id=1, source_target_pairs={{0,16},{1,17},{2,18},{3,19},{4,20},{5,21},{6,22},{7,23},{8,24},{9,... | collective-permute-start | bytes 442376 | tf_op jit(solution)/shard_map/ppermute | solution.py:101
  476.7 8.8 %collective-permute-start.7 = (bf16[2,2,1,1,1,24,768]{6,5,4,3,2,1,0:T(8,128)(2,1)S(1)}, bf16[2,2,1,1,1,24,768]{6,5,4,3,2,1,0:T(8,128)(2,1)S(1)}, u32[]{:S(2)}, u32[]{:S(2)}) collective-permute-start(bf16[2,2,1,1,1,24,768]{6,5,4,3,2,1,0:T(8,128)(2,1)S(1)} %dynamic-slice_convert_fusion.31), channel_id=1, source_target_pairs={{0,2},{1,3},{2,0},{3,1},{4,6},{5,7},{6,4},{7,5},{8,10},{9,11},{10,... | collective-permute-start | bytes 442376 | tf_op jit(solution)/shard_map/ppermute | solution.py:101
  485.5 5.6 collective-permute-start.17
  499.8 6.6 %collective-permute-start.18 = (bf16[1,2,1,1,1,24,768]{6,5,4,3,2,1,0:T(8,128)(2,1)S(1)}, bf16[1,2,1,1,1,24,768]{6,5,4,3,2,1,0:T(8,128)(2,1)S(1)}, u32[]{:S(2)}, u32[]{:S(2)}) collective-permute-start(bf16[1,2,1,1,1,24,768]{6,5,4,3,2,1,0:T(8,128)(2,1)S(1)} %dynamic-slice_convert_fusion.44), channel_id=1, source_target_pairs={{0,2},{1,3},{2,0},{3,1},{4,6},{5,7},{6,4},{7,5},{8,10},{9,11},{10,... | collective-permute-start | bytes 221192 | tf_op jit(solution)/shard_map/ppermute | solution.py:101
  519.1 8.0 %collective-permute-start.36 = (bf16[2,1,1,2,2,24,1024]{6,5,4,3,2,1,0:T(8,128)(2,1)S(1)}, bf16[2,1,1,2,2,24,1024]{6,5,4,3,2,1,0:T(8,128)(2,1)S(1)}, u32[]{:S(2)}, u32[]{:S(2)}) collective-permute-start(bf16[2,1,1,2,2,24,1024]{6,5,4,3,2,1,0:T(8,128)(2,1)S(1)} %dynamic-slice_convert_fusion.14), channel_id=1, source_target_pairs={{0,8},{1,9},{2,10},{3,11},{4,12},{5,13},{6,14},{7,15},{8,0},{9,1},... | collective-permute-start | bytes 1179656 | tf_op jit(solution)/shard_map/ppermute | solution.py:101
  520.5 15.0 %collective-permute-start.46 = (bf16[2,2,1,2,1,24,1024]{6,5,4,3,2,1,0:T(8,128)(2,1)S(1)}, bf16[2,2,1,2,1,24,1024]{6,5,4,3,2,1,0:T(8,128)(2,1)S(1)}, u32[]{:S(2)}, u32[]{:S(2)}) collective-permute-start(bf16[2,2,1,2,1,24,1024]{6,5,4,3,2,1,0:T(8,128)(2,1)S(1)} %dynamic-slice_convert_fusion.12), channel_id=1, source_target_pairs={{0,1},{1,0},{2,3},{3,2},{4,5},{5,4},{6,7},{7,6},{8,9},{9,8},{10,11... | collective-permute-start | bytes 1179656 | tf_op jit(solution)/shard_map/ppermute | solution.py:101
  520.8 16.3 %collective-permute-start.57 = (bf16[2,2,1,1,1,96,256]{6,5,4,3,2,1,0:T(8,128)(2,1)S(1)}, bf16[2,2,1,1,1,96,256]{6,5,4,3,2,1,0:T(8,128)(2,1)S(1)}, u32[]{:S(2)}, u32[]{:S(2)}) collective-permute-start(bf16[2,2,1,1,1,96,256]{6,5,4,3,2,1,0:T(8,128)(2,1)S(1)} %dynamic-slice_convert_fusion.21), channel_id=1, source_target_pairs={{0,2},{1,3},{2,0},{3,1},{4,6},{5,7},{6,4},{7,5},{8,10},{9,11},{10,... | collective-permute-start | bytes 589832 | tf_op jit(solution)/shard_map/ppermute | solution.py:101
  524.0 16.4 %collective-permute-start.52 = (bf16[1,2,1,2,1,96,256]{6,5,4,3,2,1,0:T(8,128)(2,1)S(1)}, bf16[1,2,1,2,1,96,256]{6,5,4,3,2,1,0:T(8,128)(2,1)S(1)}, u32[]{:S(2)}, u32[]{:S(2)}) collective-permute-start(bf16[1,2,1,2,1,96,256]{6,5,4,3,2,1,0:T(8,128)(2,1)S(1)} %dynamic-slice_convert_fusion.22), channel_id=1, source_target_pairs={{0,1},{1,0},{2,3},{3,2},{4,5},{5,4},{6,7},{7,6},{8,9},{9,8},{10,11... | collective-permute-start | bytes 589832 | tf_op jit(solution)/shard_map/ppermute | solution.py:101
  524.2 17.5 %collective-permute-start.62 = (bf16[1,1,1,2,2,96,256]{6,5,4,3,2,1,0:T(8,128)(2,1)S(1)}, bf16[1,1,1,2,2,96,256]{6,5,4,3,2,1,0:T(8,128)(2,1)S(1)}, u32[]{:S(2)}, u32[]{:S(2)}) collective-permute-start(bf16[1,1,1,2,2,96,256]{6,5,4,3,2,1,0:T(8,128)(2,1)S(1)} %dynamic-slice_convert_fusion.20), channel_id=1, source_target_pairs={{0,16},{1,17},{2,18},{3,19},{4,20},{5,21},{6,22},{7,23},{8,24},{9,... | collective-permute-start | bytes 589832 | tf_op jit(solution)/shard_map/ppermute | solution.py:101
  527.1 17.7 %collective-permute-start.42 = (bf16[1,2,1,2,1,24,1024]{6,5,4,3,2,1,0:T(8,128)(2,1)S(1)}, bf16[1,2,1,2,1,24,1024]{6,5,4,3,2,1,0:T(8,128)(2,1)S(1)}, u32[]{:S(2)}, u32[]{:S(2)}) collective-permute-start(bf16[1,2,1,2,1,24,1024]{6,5,4,3,2,1,0:T(8,128)(2,1)S(1)} %dynamic-slice_convert_fusion.24), channel_id=1, source_target_pairs={{0,1},{1,0},{2,3},{3,2},{4,5},{5,4},{6,7},{7,6},{8,9},{9,8},{10,11... | collective-permute-start | bytes 589832 | tf_op jit(solution)/shard_map/ppermute | solution.py:101
  535.5 9.4 %collective-permute-start.37 = (bf16[1,1,1,2,2,24,1024]{6,5,4,3,2,1,0:T(8,128)(2,1)S(1)}, bf16[1,1,1,2,2,24,1024]{6,5,4,3,2,1,0:T(8,128)(2,1)S(1)}, u32[]{:S(2)}, u32[]{:S(2)}) collective-permute-start(bf16[1,1,1,2,2,24,1024]{6,5,4,3,2,1,0:T(8,128)(2,1)S(1)} %dynamic-slice_convert_fusion.25), channel_id=1, source_target_pairs={{0,16},{1,17},{2,18},{3,19},{4,20},{5,21},{6,22},{7,23},{8,24},{9,... | collective-permute-start | bytes 589832 | tf_op jit(solution)/shard_map/ppermute | solution.py:101
  537.2 11.1 %collective-permute-start.47 = (bf16[2,2,1,1,1,24,1024]{6,5,4,3,2,1,0:T(8,128)(2,1)S(1)}, bf16[2,2,1,1,1,24,1024]{6,5,4,3,2,1,0:T(8,128)(2,1)S(1)}, u32[]{:S(2)}, u32[]{:S(2)}) collective-permute-start(bf16[2,2,1,1,1,24,1024]{6,5,4,3,2,1,0:T(8,128)(2,1)S(1)} %dynamic-slice_convert_fusion.23), channel_id=1, source_target_pairs={{0,2},{1,3},{2,0},{3,1},{4,6},{5,7},{6,4},{7,5},{8,10},{9,11},{10,... | collective-permute-start | bytes 589832 | tf_op jit(solution)/shard_map/ppermute | solution.py:101
  540.3 8.0 %collective-permute-start.58 = (bf16[2,1,1,1,1,96,256]{6,5,4,3,2,1,0:T(8,128)(2,1)S(1)}, bf16[2,1,1,1,1,96,256]{6,5,4,3,2,1,0:T(8,128)(2,1)S(1)}, u32[]{:S(2)}, u32[]{:S(2)}) collective-permute-start(bf16[2,1,1,1,1,96,256]{6,5,4,3,2,1,0:T(8,128)(2,1)S(1)} %dynamic-slice_convert_fusion.36), channel_id=1, source_target_pairs={{0,8},{1,9},{2,10},{3,11},{4,12},{5,13},{6,14},{7,15},{8,0},{9,1},... | collective-permute-start | bytes 294920 | tf_op jit(solution)/shard_map/ppermute | solution.py:101
  541.7 8.6 %collective-permute-start.53 = (bf16[1,2,1,1,1,96,256]{6,5,4,3,2,1,0:T(8,128)(2,1)S(1)}, bf16[1,2,1,1,1,96,256]{6,5,4,3,2,1,0:T(8,128)(2,1)S(1)}, u32[]{:S(2)}, u32[]{:S(2)}) collective-permute-start(bf16[1,2,1,1,1,96,256]{6,5,4,3,2,1,0:T(8,128)(2,1)S(1)} %dynamic-slice_convert_fusion.37), channel_id=1, source_target_pairs={{0,2},{1,3},{2,0},{3,1},{4,6},{5,7},{6,4},{7,5},{8,10},{9,11},{10,... | collective-permute-start | bytes 294920 | tf_op jit(solution)/shard_map/ppermute | solution.py:101
  544.8 7.2 %collective-permute-start.63 = (bf16[1,1,1,2,1,96,256]{6,5,4,3,2,1,0:T(8,128)(2,1)S(1)}, bf16[1,1,1,2,1,96,256]{6,5,4,3,2,1,0:T(8,128)(2,1)S(1)}, u32[]{:S(2)}, u32[]{:S(2)}) collective-permute-start(bf16[1,1,1,2,1,96,256]{6,5,4,3,2,1,0:T(8,128)(2,1)S(1)} %dynamic-slice_convert_fusion.35), channel_id=1, source_target_pairs={{0,1},{1,0},{2,3},{3,2},{4,5},{5,4},{6,7},{7,6},{8,9},{9,8},{10,11... | collective-permute-start | bytes 294920 | tf_op jit(solution)/shard_map/ppermute | solution.py:101
  544.9 8.0 %collective-permute-start.43 = (bf16[1,2,1,1,1,24,1024]{6,5,4,3,2,1,0:T(8,128)(2,1)S(1)}, bf16[1,2,1,1,1,24,1024]{6,5,4,3,2,1,0:T(8,128)(2,1)S(1)}, u32[]{:S(2)}, u32[]{:S(2)}) collective-permute-start(bf16[1,2,1,1,1,24,1024]{6,5,4,3,2,1,0:T(8,128)(2,1)S(1)} %dynamic-slice_convert_fusion.39), channel_id=1, source_target_pairs={{0,2},{1,3},{2,0},{3,1},{4,6},{5,7},{6,4},{7,5},{8,10},{9,11},{10,... | collective-permute-start | bytes 294920 | tf_op jit(solution)/shard_map/ppermute | solution.py:101
  548.3 6.2 %collective-permute-start.38 = (bf16[1,1,1,2,1,24,1024]{6,5,4,3,2,1,0:T(8,128)(2,1)S(1)}, bf16[1,1,1,2,1,24,1024]{6,5,4,3,2,1,0:T(8,128)(2,1)S(1)}, u32[]{:S(2)}, u32[]{:S(2)}) collective-permute-start(bf16[1,1,1,2,1,24,1024]{6,5,4,3,2,1,0:T(8,128)(2,1)S(1)} %dynamic-slice_convert_fusion.40), channel_id=1, source_target_pairs={{0,1},{1,0},{2,3},{3,2},{4,5},{5,4},{6,7},{7,6},{8,9},{9,8},{10,11... | collective-permute-start | bytes 294920 | tf_op jit(solution)/shard_map/ppermute | solution.py:101
  548.4 7.5 %collective-permute-start.48 = (bf16[2,1,1,1,1,24,1024]{6,5,4,3,2,1,0:T(8,128)(2,1)S(1)}, bf16[2,1,1,1,1,24,1024]{6,5,4,3,2,1,0:T(8,128)(2,1)S(1)}, u32[]{:S(2)}, u32[]{:S(2)}) collective-permute-start(bf16[2,1,1,1,1,24,1024]{6,5,4,3,2,1,0:T(8,128)(2,1)S(1)} %dynamic-slice_convert_fusion.38), channel_id=1, source_target_pairs={{0,8},{1,9},{2,10},{3,11},{4,12},{5,13},{6,14},{7,15},{8,0},{9,1},... | collective-permute-start | bytes 294920 | tf_op jit(solution)/shard_map/ppermute | solution.py:101
  550.3 7.1 %collective-permute-start.59 = (bf16[1,1,1,1,1,96,256]{6,5,4,3,2,1,0:T(8,128)(2,1)S(1)}, bf16[1,1,1,1,1,96,256]{6,5,4,3,2,1,0:T(8,128)(2,1)S(1)}, u32[]{:S(2)}, u32[]{:S(2)}) collective-permute-start(bf16[1,1,1,1,1,96,256]{6,5,4,3,2,1,0:T(8,128)(2,1)S(1)} %dynamic-slice_convert_fusion.51), channel_id=1, source_target_pairs={{0,16},{1,17},{2,18},{3,19},{4,20},{5,21},{6,22},{7,23},{8,24},{9,... | collective-permute-start | bytes 147464 | tf_op jit(solution)/shard_map/ppermute | solution.py:101
  552.0 7.4 %collective-permute-start.54 = (bf16[1,1,1,1,1,96,256]{6,5,4,3,2,1,0:T(8,128)(2,1)S(1)}, bf16[1,1,1,1,1,96,256]{6,5,4,3,2,1,0:T(8,128)(2,1)S(1)}, u32[]{:S(2)}, u32[]{:S(2)}) collective-permute-start(bf16[1,1,1,1,1,96,256]{6,5,4,3,2,1,0:T(8,128)(2,1)S(1)} %dynamic-slice_convert_fusion.52), channel_id=1, source_target_pairs={{0,8},{1,9},{2,10},{3,11},{4,12},{5,13},{6,14},{7,15},{8,0},{9,1},... | collective-permute-start | bytes 147464 | tf_op jit(solution)/shard_map/ppermute | solution.py:101
  552.9 6.6 %collective-permute-start.64 = (bf16[1,1,1,1,1,96,256]{6,5,4,3,2,1,0:T(8,128)(2,1)S(1)}, bf16[1,1,1,1,1,96,256]{6,5,4,3,2,1,0:T(8,128)(2,1)S(1)}, u32[]{:S(2)}, u32[]{:S(2)}) collective-permute-start(bf16[1,1,1,1,1,96,256]{6,5,4,3,2,1,0:T(8,128)(2,1)S(1)} %dynamic-slice_convert_fusion.50), channel_id=1, source_target_pairs={{0,2},{1,3},{2,0},{3,1},{4,6},{5,7},{6,4},{7,5},{8,10},{9,11},{10,... | collective-permute-start | bytes 147464 | tf_op jit(solution)/shard_map/ppermute | solution.py:101
  554.5 5.1 collective-permute-start.44
  555.8 5.1 collective-permute-start.39
  (120 other events, 1038.3 us)
Sparse Core Ops, SparseCore 0:
  17.6 111.0 all-gather.2
  131.5 62.1 all-gather.4

commit v3 on v1

--- a/solution.py
+++ b/solution.py
@@ -1,4 +1,3 @@
-import numpy as np
 import jax
 import jax.numpy as jnp
 from jax import lax
@@ -85,6 +84,9 @@
         for i in range(len(groups)):
             rest.extend(groups[(i + turn) % len(groups)])
         orders.append(head + rest)
+    if len(groups) >= 2:
+        swapped = [groups[1], groups[0]] + groups[2:]
+        orders.insert(0, head + [b for g in swapped for b in g])
     return orders
 
 
@@ -186,22 +188,6 @@
         mask_token,
         cot_decoded,
     ):
-        shards = (
-            wave_table,
-            norm1_gain,
-            norm1_bias,
-            qkv_weight,
-            out_weight,
-            norm2_gain,
-            norm2_bias,
-            mlp_in,
-            mlp_in_bias,
-            mlp_out,
-            mlp_out_bias,
-            dec_weight,
-            dec_bias,
-            mask_token,
-        )
         small = (wave_table, norm1_gain, norm1_bias, norm2_gain, norm2_bias, mlp_in_bias,
                  mlp_out_bias, dec_bias, mask_token)
         small_flat = [a.reshape(-1) for a in small]
@@ -293,13 +279,16 @@
         )
         grad_dec_bias = jnp.sum(grad_vis, axis=0)
         grad_dec_weight = inner_rows(enc_low, grad_vis_low)
+        sum_dec = rs_chain(grad_dec_weight, n_bits, orders[0])
         grad_res_two = outer_cols(grad_vis_low, dec_full)
         grad_ffo = grad_res_two.astype(jnp.bfloat16)
         grad_mlp_out_bias = jnp.sum(grad_ffo.astype(jnp.float32), axis=0)
         grad_mlp_out = inner_rows(active, grad_ffo)
+        sum_mlp_out = rs_chain(grad_mlp_out, n_bits, orders[0])
         grad_hidden = (outer_cols(grad_ffo, outer_full) * gelu_slope(hidden)).astype(jnp.bfloat16)
         grad_mlp_in_bias = jnp.sum(grad_hidden.astype(jnp.float32), axis=0)
         grad_mlp_in = inner_rows(act_two, grad_hidden)
+        sum_mlp_in = rs_chain(grad_mlp_in, n_bits, orders[0])
         grad_act_two = outer_cols(grad_hidden, inner_full)
         grad_norm_two, grad_norm2_gain, grad_norm2_bias = norm_backward(
             grad_act_two, normed_two, inverse_two, gain_two.astype(jnp.float32)
@@ -307,6 +296,7 @@
         grad_res_one = grad_res_two + grad_norm_two
         grad_att = grad_res_one.astype(jnp.bfloat16)
         grad_out_weight = inner_rows(mixture, grad_att)
+        sum_out = rs_chain(grad_out_weight, n_bits, orders[0])
         grad_mixed = outer_cols(grad_att, out_full).astype(jnp.bfloat16).reshape(head_shape)
         grad_queries, grad_keys, grad_values = attend_back(
             queries, key_rows, value_rows, soft_full, soft_low, grad_mixed
@@ -320,6 +310,7 @@
             axis=1,
         ).astype(jnp.bfloat16)
         grad_qkv_weight = inner_rows(act_one, grad_qkv)
+        sum_qkv = rs_chain(grad_qkv_weight, n_bits, orders[0])
         grad_act_one = outer_cols(grad_qkv, qkv_full)
         grad_norm_one, grad_norm1_gain, grad_norm1_bias = norm_backward(
             grad_act_one, normed_one, inverse_one, gain_one.astype(jnp.float32)
@@ -333,15 +324,9 @@
                        grad_norm2_bias, grad_mlp_in_bias, grad_mlp_out_bias, grad_dec_bias,
                        grad_mask_token)
         packed_sg, sg_widths = pack_rows(small_grads, n_dev, jnp.float32)
-        turn = lambda k: orders[k % len(orders)]
-        reduced_sg = rs_chain(packed_sg, n_bits, turn(2))
+        reduced_sg = rs_chain(packed_sg, n_bits, orders[0])
         (sum_wave, sum_g1, sum_b1, sum_g2, sum_b2, sum_ib, sum_ob, sum_db,
          sum_mask) = unpack_rows(reduced_sg, small_grads, sg_widths, n_dev, 1)
-        sum_dec = rs_chain(grad_dec_weight, n_bits, turn(1))
-        sum_mlp_out = rs_chain(grad_mlp_out, n_bits, turn(1))
-        sum_mlp_in = rs_chain(grad_mlp_in, n_bits, turn(0))
-        sum_out = rs_chain(grad_out_weight, n_bits, turn(0))
-        sum_qkv = rs_chain(grad_qkv_weight, n_bits, turn(2))
         summed = (sum_wave, sum_g1, sum_b1, sum_qkv, sum_out, sum_g2, sum_b2, sum_mlp_in,
                   sum_ib, sum_mlp_out, sum_ob, sum_dec, sum_db, sum_mask)
         return (decoded, grad_tokens, *summed)
@@ -373,8 +358,10 @@
         P(AX),
         P(None, AX, None),
     )
+    body = make_local(n_bits, orders)
+
     return jax.shard_map(
-        make_local(n_bits, orders),
+        body,
         mesh=mesh,
         in_specs=placed,
         out_specs=(

time: 478 us -> 460 us (0.962)
  waiting for transfers between devices: 227 us -> 206 us
    ppermute x30, waiting for transfers between devices: 109 us -> 87.9 us  [rs_chain(): lax.ppermute(send.astype(jnp.bfloat16), AX, [(i, i ^ 1 << bit) for i in r...]
  transfers between devices with their start and end apart: 34 -> 34, of which waited for: 22 -> 21; matrix products, arithmetic and copies ran while one was open for 22% -> 23% of each run, Pallas kernels for 0% -> 0%
where the time goes in v3:
time: 460 us; the launch traced here: 451 us
  waiting for transfers between devices  206 us (45%)
  matrix products  81.2 us (18%)
  local copies, waits for them, and re-layouts  70.2 us (15%)
  starting transfers between devices  45.7 us (10%)
  other arithmetic  32.3 us (7%)
  between operations  16 us (3%)
    ppermute x30, waiting for transfers between devices, rs_chain(): lax.ppermute(send.astype(jnp.bfloat16), AX, [(i, i ^ 1 << bit) for i in r...  87.9 us
    all_to_all x1, waiting for transfers between devices, local(): lax.all_to_all(cot_decoded, AX, split_axis=0, concat_axis=1, tiled=True)  66.6 us
    ppermute x30, starting transfers between devices, rs_chain(): lax.ppermute(send.astype(jnp.bfloat16), AX, [(i, i ^ 1 << bit) for i in r...  34.5 us
    all_gather x1, waiting for transfers between devices, local(): lax.all_gather(jnp.concatenate(wide, axis=1), AX, axis=0, tiled=True)  32.6 us
    dot_general x5, matrix products, outer_cols(): lax.dot_general(left_op, right_op, (((1,), (1,)), ((), ())), preferred_el...  23 us
    dot_general x5, matrix products, product(): return jnp.dot(left_op, right_op, preferred_element_type=jnp.float32)  21.4 us
    dot_general x5, matrix products, inner_rows(): lax.dot_general(left_op, right_op, (((0,), (0,)), ((), ())), preferred_el...  19.2 us
    all_gather x1, waiting for transfers between devices, local(): outer_full = lax.all_gather(mlp_out, AX, axis=0, tiled=True)  18 us
  transfers between devices with their start and end apart: 34, of which 21 were waited for; matrix products, arithmetic and copies ran while one was open for 23% of the time, Pallas kernels for 0%

profile of v3, /device:TPU:0, one launch (start us, length us, event | category | flops | bytes accessed | tf_op | source)
XLA Modules:
  0.0 451.4 jit_solution(8533517393682402486)
XLA Ops:
  8.8 5.4 %concatenate.13 = bf16[6144]{0:T(1024)(128)(2,1)S(1)} concatenate(bf16[3072]{0:T(1024)(128)(2,1)S(1)} %reshape.303, bf16[24]{0:T(256)(128)(2,1)} %param.22, bf16[24]{0:T(256)(128)(2,1)} %param.23, bf16[24]{0:T(256)(128)(2,1)} %param.26, bf16[24]{0:T(256)(128)(2,1)} %param.27, bf16[96]{0:T(256)(128)(2,1)} %param.29, bf16[24]{0:T(256)(128)(2,1)} %param.31, bf16[16]{0:T(256)(128)(2,1)} %param.33, ...), dimensions={0} | concatenate | bytes 24576 | tf_op jit(solution)/shard_map/concatenate | solution.py:198
  17.5 7.3 %all-to-all-start.1 = ((bf16[64,32,512]{2,1,0:T(8,128)(2,1)}), bf16[64,32,512]{2,1,0:T(8,128)(2,1)S(1)}, u32[]{:S(2)}, u32[]{:S(2)}) async-start(bf16[64,32,512]{2,1,0:T(8,128)(2,1)} %param.35), calls=%async_computation.1 | async-start | bytes 4194304 | tf_op jit(solution)/shard_map/all_to_all | solution.py:269
  26.2 66.6 %all-to-all-done.1 = bf16[64,32,512]{2,1,0:T(8,128)(2,1)S(1)} async-done(((bf16[64,32,512]{2,1,0:T(8,128)(2,1)}), bf16[64,32,512]{2,1,0:T(8,128)(2,1)S(1)}, u32[]{:S(2)}, u32[]{:S(2)}) %all-to-all-start.1) | async-done | bytes 2097184 | tf_op jit(solution)/shard_map/all_to_all | solution.py:269
  96.1 32.6 %all-gather.3.cloned.1.call-done = bf16[768,6912]{1,0:T(8,128)(2,1)} async-done(((bf16[24,6912]{1,0:T(8,128)(2,1)}), bf16[768,6912]{1,0:T(8,128)(2,1)}) %all-gather.3.cloned.1.call-update) | async-done | bytes 10616848 | tf_op jit(solution)/shard_map/all_gather | solution.py:203
  132.5 4.3 convolution_convert_fusion
  137.8 2.3 copy.115
  140.1 2.9 reshape.308
  144.2 2.2 reshape.310
  147.6 2.2 reshape.309
  150.9 5.0 %fusion.78 = (f32[2,12,256]{2,1,0:T(8,128)S(1)}, f32[2,12,256,256]{2,3,1,0:T(8,128)S(1)}) fusion(f32[2,12,256,256]{2,3,1,0:T(8,128)S(1)} %fusion.58), kind=kOutput, calls=%fused_computation.198 | output fusion | flops 6291711 | bytes 12607488 | tf_op jit(solution)/shard_map/sub | solution.py:137
  162.5 2.5 fusion.79
  168.0 7.7 %multiply_convert_fusion.1 = (bf16[512,3072]{1,0:T(8,128)(2,1)}, f32[512,3072]{1,0:T(8,128)}) fusion(f32[3072]{0:T(1024)S(1)} %copy-done.56, bf16[768,6912]{1,0:T(8,128)(2,1)} %all-gather.3.cloned.1.call-done, f32[512,768]{1,0:T(8,128)S(1)} %get-tuple-element.50, f32[768]{0:T(1024)S(1)} %copy-done.62, f32[768]{0:T(1024)S(1)} %copy-done.52, ...), kind=kOutput, calls=%fused_computation.11 | convolution fusion | flops 2427322368 | bytes 15751168 | tf_op jit(solution)/shard_map/dot_general | solution.py:20
  175.6 18.0 %all-gather.5.cloned.1.call-done = bf16[3072,768]{1,0:T(8,128)(2,1)} async-done(((bf16[96,768]{1,0:T(8,128)(2,1)}), bf16[3072,768]{1,0:T(8,128)(2,1)}) %all-gather.5.cloned.1.call-update) | async-done | bytes 4718608 | tf_op jit(solution)/shard_map/all_gather | solution.py:219
  193.7 7.5 %convert_reduce_fusion = (f32[3072]{0:T(1024)S(1)}, bf16[512,3072]{1,0:T(8,128)(2,1)S(1)}) fusion(f32[512,3072]{1,0:T(8,128)} %get-tuple-element.52, f32[3072]{0:T(1024)S(1)} %copy-done.57, bf16[3072,768]{1,0:T(8,128)(2,1)} %all-gather.5.cloned.1.call-done, f32[512,768]{1,0:T(8,128)S(1)} %fusion.49), kind=kOutput, calls=%fused_computation.8 | convolution fusion | flops 2436756480 | bytes 15753216 | tf_op jit(solution)/shard_map/dot_general | solution.py:30
  201.3 6.5 %multiply_reduce_fusion.2 = (f32[768]{0:T(1024)S(1)}, f32[512]{0:T(512)S(1)}, f32[512]{0:T(512)S(1)}, f32[768]{0:T(1024)S(1)}, f32[512,768]{1,0:T(8,128)S(1)}) fusion(f32[512,768]{1,0:T(8,128)S(1)} %get-tuple-element.50, f32[512]{0:T(512)S(1)} %copy-done.61, f32[512]{0:T(512)S(1)} %copy-done.51, f32[768]{0:T(1024)S(1)} %copy-done.53, ...), kind=kOutput, calls=%fused_computation.51 | convolution fusion | flops 2419455488 | bytes 11027456 | tf_op jit(solution)/shard_map/dot_general | solution.py:30
  209.6 2.1 convolution_convert_fusion.1
  213.1 5.2 %fusion.33 = bf16[2,256,12,64]{1,3,2,0:T(8,128)(2,1)} fusion(bf16[2,256,12,64]{1,0,3,2:T(2,128)(2,1)} %reshape.314, f32[2,12,256,256]{2,3,1,0:T(8,128)} %copy-done, f32[2,12,256]{2,1,0:T(8,128)S(1)} %copy-done.37), kind=kOutput, calls=%fused_computation.76 | convolution fusion | flops 204865536 | bytes 7888896 | tf_op jit(solution)/shard_map/chqk,cqhd->ckhd/dot_general | solution.py:149
  218.3 3.8 multiply_reduce_fusion
  222.1 4.3 multiply_convert_fusion
  229.9 5.7 %fusion.75 = f32[768,3072]{1,0:T(8,128)} fusion(bf16[512,3072]{1,0:T(8,128)(2,1)S(1)} %copy-done.68, f32[512,768]{1,0:T(8,128)S(1)} %copy-done.6, f32[768]{0:T(1024)S(1)} %copy-done.63, f32[768]{0:T(1024)S(1)} %copy-done.53, f32[512]{0:T(512)S(1)} %copy-done.61, f32[512]{0:T(512)S(1)} %copy-done.51), kind=kOutput, calls=%fused_computation.195 | convolution fusion | flops 2417885184 | bytes 14166016 | tf_op jit(solution)/shard_map/dot_general | solution.py:24
  235.9 8.3 %fusion.70 = f32[3072,768]{1,0:T(8,128)} fusion(bf16[512,3072]{1,0:T(8,128)(2,1)} %get-tuple-element.51, f32[512,768]{1,0:T(8,128)S(1)} %copy-done.4), kind=kOutput, calls=%fused_computation.190 | convolution fusion | flops 2416312320 | bytes 14155776 | tf_op jit(solution)/shard_map/dot_general | solution.py:24
  244.2 5.0 %add_convert_fusion = bf16[512,768]{1,0:T(8,128)(2,1)S(1)} fusion(f32[512,768]{1,0:T(8,128)S(1)} %copy-done.6, bf16[512,3072]{1,0:T(8,128)(2,1)S(1)} %copy-done.21, bf16[3072,768]{1,0:T(8,128)(2,1)} %all-gather.5.cloned.1.call-done, f32[768]{0:T(1024)S(1)} %reshape.349), kind=kOutput, calls=%fused_computation.59 | convolution fusion | flops 2417098752 | bytes 10226688 | tf_op jit(solution)/shard_map/dot_general | solution.py:20
  252.5 3.5 copy.124
  256.0 3.8 all-to-all-start
  266.3 5.2 %multiply_reduce_fusion.3 = (f32[768]{0:T(1024)S(1)}, f32[512]{0:T(512)S(1)}, f32[512]{0:T(512)S(1)}, f32[768]{0:T(1024)S(1)}, f32[512,768]{1,0:T(8,128)S(1)}) fusion(f32[2,256,768]{2,1,0:T(8,128)S(1)} %copy-done.2, f32[512]{0:T(512)S(1)} %bitcast.188, f32[512]{0:T(512)S(1)} %bitcast.191, f32[768]{0:T(1024)S(1)} %copy-done.44, ...), kind=kOutput, calls=%fused_computation.52 | convolution fusion | flops 1822553600 | bytes 9061376 | tf_op jit(solution)/shard_map/dot_general | solution.py:30
  276.4 3.8 fusion.18
  288.2 4.1 dynamic-slice_convert_fusion.1
  293.9 4.2 dynamic-slice_convert_fusion
  303.0 2.5 collective-permute-start.4
  305.5 3.1 collective-permute-done.4
  314.0 5.2 %collective-permute-done.26 = bf16[1,2,1,2,2,24,512]{6,5,4,3,2,1,0:T(8,128)(2,1)S(1)} collective-permute-done((bf16[1,2,1,2,2,24,512]{6,5,4,3,2,1,0:T(8,128)(2,1)S(1)}, bf16[1,2,1,2,2,24,512]{6,5,4,3,2,1,0:T(8,128)(2,1)S(1)}, u32[]{:S(2)}, u32[]{:S(2)}) %collective-permute-start.26) | collective-permute-done | bytes 196640 | tf_op jit(solution)/shard_map/ppermute | solution.py:103
  324.7 5.4 %collective-permute-done.11 = bf16[1,2,1,2,2,24,768]{6,5,4,3,2,1,0:T(8,128)(2,1)S(1)} collective-permute-done((bf16[1,2,1,2,2,24,768]{6,5,4,3,2,1,0:T(8,128)(2,1)S(1)}, bf16[1,2,1,2,2,24,768]{6,5,4,3,2,1,0:T(8,128)(2,1)S(1)}, u32[]{:S(2)}, u32[]{:S(2)}) %collective-permute-start.11) | collective-permute-done | bytes 294944 | tf_op jit(solution)/shard_map/ppermute | solution.py:103
  331.1 4.3 collective-permute-done.12
  336.5 3.2 convert_add_fusion.2
  348.1 10.6 %collective-permute-done.6 = bf16[1,2,1,2,2,24,2304]{6,5,4,3,2,1,0:T(8,128)(2,1)S(1)} collective-permute-done((bf16[1,2,1,2,2,24,2304]{6,5,4,3,2,1,0:T(8,128)(2,1)S(1)}, bf16[1,2,1,2,2,24,2304]{6,5,4,3,2,1,0:T(8,128)(2,1)S(1)}, u32[]{:S(2)}, u32[]{:S(2)}) %collective-permute-start.6) | collective-permute-done | bytes 884768 | tf_op jit(solution)/shard_map/ppermute | solution.py:103
  359.3 2.9 convert_add_fusion.1
  363.9 3.5 collective-permute-done.7
  368.8 2.4 convert_add_fusion
  375.9 15.4 %collective-permute-done.16 = bf16[1,2,1,2,2,24,3072]{6,5,4,3,2,1,0:T(8,128)(2,1)S(1)} collective-permute-done((bf16[1,2,1,2,2,24,3072]{6,5,4,3,2,1,0:T(8,128)(2,1)S(1)}, bf16[1,2,1,2,2,24,3072]{6,5,4,3,2,1,0:T(8,128)(2,1)S(1)}, u32[]{:S(2)}, u32[]{:S(2)}) %collective-permute-start.16) | collective-permute-done | bytes 1179680 | tf_op jit(solution)/shard_map/ppermute | solution.py:103
  391.7 2.2 collective-permute-start.17
  394.6 17.0 %collective-permute-done.21 = bf16[1,2,1,2,2,96,768]{6,5,4,3,2,1,0:T(8,128)(2,1)S(1)} collective-permute-done((bf16[1,2,1,2,2,96,768]{6,5,4,3,2,1,0:T(8,128)(2,1)S(1)}, bf16[1,2,1,2,2,96,768]{6,5,4,3,2,1,0:T(8,128)(2,1)S(1)}, u32[]{:S(2)}, u32[]{:S(2)}) %collective-permute-start.21) | collective-permute-done | bytes 1179680 | tf_op jit(solution)/shard_map/ppermute | solution.py:103
  413.3 2.3 collective-permute-start.22
  415.6 3.4 copy.125
  421.7 2.7 collective-permute-done.22
  427.1 3.7 collective-permute-done.18
  431.5 4.1 collective-permute-done.23
  436.0 3.8 collective-permute-done.19
  440.6 2.8 collective-permute-done.24
  (355 shorter events, 102.8 us)
Async XLA Ops:
  7.2 121.5 %all-gather.3.cloned.1.call-start = ((), (), s32[]{:S(2)}) async-start(), calls=%async_computation.2 | async-start | bytes 10948608 | tf_op jit(solution)/shard_map/all_gather | solution.py:203
  17.5 75.4 %all-to-all-start.1 = ((bf16[64,32,512]{2,1,0:T(8,128)(2,1)}), bf16[64,32,512]{2,1,0:T(8,128)(2,1)S(1)}, u32[]{:S(2)}, u32[]{:S(2)}) async-start(bf16[64,32,512]{2,1,0:T(8,128)(2,1)} %param.35), calls=%async_computation.1 | async-start | bytes 4194304 | tf_op jit(solution)/shard_map/all_to_all | solution.py:269
  24.8 168.9 %all-gather.5.cloned.1.call-start = ((), (), s32[]{:S(2)}) async-start(), calls=%async_computation.3 | async-start | bytes 4866048 | tf_op jit(solution)/shard_map/all_gather | solution.py:219
  26.0 68.7 %copy-start.54 = (pred[2,1024]{1,0:T(4,128)(4,1)}, pred[2,1024]{1,0:T(4,128)(4,1)S(1)}, u32[]{:S(2)}) copy-start(pred[2,1024]{1,0:T(4,128)(4,1)S(1)} %broadcast_compare_fusion) | copy-start | bytes 6148
  26.2 104.7 %copy-start.58 = (f32[2,128]{1,0:T(2,128)}, f32[2,128]{1,0:T(2,128)S(1)}, u32[]{:S(2)}) copy-start(f32[2,128]{1,0:T(2,128)S(1)} %fusion.65) | copy-start | bytes 3076
  94.7 36.3 %copy-start.24 = (bf16[2,256,768]{2,1,0:T(8,128)(2,1)S(1)}, bf16[2,256,768]{2,1,0:T(8,128)(2,1)}, u32[]{:S(2)}) copy-start(bf16[2,256,768]{2,1,0:T(8,128)(2,1)} %param.18) | copy-start | bytes 2359300
  131.7 30.9 %copy-start.1 = (f32[2,256,768]{2,1,0:T(8,128)}, f32[2,256,768]{2,1,0:T(8,128)S(1)}, u32[]{:S(2)}) copy-start(f32[2,256,768]{2,1,0:T(8,128)S(1)} %get-tuple-element.30) | copy-start | bytes 4718596
  165.0 42.7 %copy-start.5 = (f32[512,768]{1,0:T(8,128)}, f32[512,768]{1,0:T(8,128)S(1)}, u32[]{:S(2)}) copy-start(f32[512,768]{1,0:T(8,128)S(1)} %get-tuple-element.50) | copy-start | bytes 4718596
  167.9 39.8 %copy-start.3 = (f32[512,768]{1,0:T(8,128)}, f32[512,768]{1,0:T(8,128)S(1)}, u32[]{:S(2)}) copy-start(f32[512,768]{1,0:T(8,128)S(1)} %fusion.49) | copy-start | bytes 4718596
  168.0 25.7 %copy-start.57 = (f32[3072]{0:T(1024)S(1)}, f32[3072]{0:T(1024)}, u32[]{:S(2)}) copy-start(f32[3072]{0:T(1024)} %reshape.348) | copy-start | bytes 36868
  256.0 159.7 %all-to-all-start = ((bf16[2,1024,512]{2,0,1:T(2,128)(2,1)}), bf16[2,1024,512]{2,0,1:T(2,128)(2,1)}, u32[]{:S(2)}, u32[]{:S(2)}) async-start(bf16[2,1024,512]{2,0,1:T(2,128)(2,1)} %copy.124), calls=%async_computation | async-start | bytes 4194304 | tf_op jit(solution)/shard_map/all_to_all | solution.py:268
  275.0 11.4 %collective-permute-start = (bf16[2,2,1,2,2,1,8,512]{7,6,5,4,3,2,1,0:T(8,128)(2,1)S(1)}, bf16[2,2,1,2,2,1,8,512]{7,6,5,4,3,2,1,0:T(8,128)(2,1)S(1)}, u32[]{:S(2)}, u32[]{:S(2)}) collective-permute-start(bf16[2,2,1,2,2,1,8,512]{7,6,5,4,3,2,1,0:T(8,128)(2,1)S(1)} %dynamic-slice_convert_fusion.19), channel_id=1, source_target_pairs={{0,4},{1,5},{2,6},{3,7},{4,0},{5,1},{6,2},{7,3},{8,12},{9,13},{10,... | collective-permute-start | bytes 393224 | tf_op jit(solution)/shard_map/ppermute | solution.py:103
  281.6 54.9 %collective-permute-start.5 = (bf16[2,2,1,2,2,24,2304]{6,5,4,3,2,1,0:T(8,128)(2,1)}, bf16[2,2,1,2,2,24,2304]{6,5,4,3,2,1,0:T(8,128)(2,1)}, u32[]{:S(2)}, u32[]{:S(2)}) collective-permute-start(bf16[2,2,1,2,2,24,2304]{6,5,4,3,2,1,0:T(8,128)(2,1)} %dynamic-slice_convert_fusion.2), channel_id=1, source_target_pairs={{0,4},{1,5},{2,6},{3,7},{4,0},{5,1},{6,2},{7,3},{8,12},{9,13},{10,... | collective-permute-start | bytes 5308424 | tf_op jit(solution)/shard_map/ppermute | solution.py:103
  286.0 34.6 %collective-permute-start.10 = (bf16[2,2,1,2,2,24,768]{6,5,4,3,2,1,0:T(8,128)(2,1)}, bf16[2,2,1,2,2,24,768]{6,5,4,3,2,1,0:T(8,128)(2,1)}, u32[]{:S(2)}, u32[]{:S(2)}) collective-permute-start(bf16[2,2,1,2,2,24,768]{6,5,4,3,2,1,0:T(8,128)(2,1)} %dynamic-slice_convert_fusion.8), channel_id=1, source_target_pairs={{0,4},{1,5},{2,6},{3,7},{4,0},{5,1},{6,2},{7,3},{8,12},{9,13},{10,... | collective-permute-start | bytes 1769480 | tf_op jit(solution)/shard_map/ppermute | solution.py:103
  286.5 5.7 %collective-permute-start.1 = (bf16[1,2,1,2,2,1,8,512]{7,6,5,4,3,2,1,0:T(8,128)(2,1)S(1)}, bf16[1,2,1,2,2,1,8,512]{7,6,5,4,3,2,1,0:T(8,128)(2,1)S(1)}, u32[]{:S(2)}, u32[]{:S(2)}) collective-permute-start(bf16[1,2,1,2,2,1,8,512]{7,6,5,4,3,2,1,0:T(8,128)(2,1)S(1)} %dynamic-slice_convert_fusion.23), channel_id=1, source_target_pairs={{0,16},{1,17},{2,18},{3,19},{4,20},{5,21},{6,22},{7,23},{8,24},{9,... | collective-permute-start | bytes 196616 | tf_op jit(solution)/shard_map/ppermute | solution.py:103
  292.3 67.1 %collective-permute-start.15 = (bf16[2,2,1,2,2,24,3072]{6,5,4,3,2,1,0:T(8,128)(2,1)}, bf16[2,2,1,2,2,24,3072]{6,5,4,3,2,1,0:T(8,128)(2,1)}, u32[]{:S(2)}, u32[]{:S(2)}) collective-permute-start(bf16[2,2,1,2,2,24,3072]{6,5,4,3,2,1,0:T(8,128)(2,1)} %dynamic-slice_convert_fusion.1), channel_id=1, source_target_pairs={{0,4},{1,5},{2,6},{3,7},{4,0},{5,1},{6,2},{7,3},{8,12},{9,13},{10,... | collective-permute-start | bytes 7077896 | tf_op jit(solution)/shard_map/ppermute | solution.py:103
  292.3 6.5 %collective-permute-start.2 = (bf16[1,1,1,2,2,1,8,512]{7,6,5,4,3,2,1,0:T(8,128)(2,1)S(1)}, bf16[1,1,1,2,2,1,8,512]{7,6,5,4,3,2,1,0:T(8,128)(2,1)S(1)}, u32[]{:S(2)}, u32[]{:S(2)}) collective-permute-start(bf16[1,1,1,2,2,1,8,512]{7,6,5,4,3,2,1,0:T(8,128)(2,1)S(1)} %dynamic-slice_convert_fusion.26), channel_id=1, source_target_pairs={{0,8},{1,9},{2,10},{3,11},{4,12},{5,13},{6,14},{7,15},{8,0},{9,1},... | collective-permute-start | bytes 98312 | tf_op jit(solution)/shard_map/ppermute | solution.py:103
  298.0 70.8 %collective-permute-start.20 = (bf16[2,2,1,2,2,96,768]{6,5,4,3,2,1,0:T(8,128)(2,1)}, bf16[2,2,1,2,2,96,768]{6,5,4,3,2,1,0:T(8,128)(2,1)}, u32[]{:S(2)}, u32[]{:S(2)}) collective-permute-start(bf16[2,2,1,2,2,96,768]{6,5,4,3,2,1,0:T(8,128)(2,1)} %dynamic-slice_convert_fusion), channel_id=1, source_target_pairs={{0,4},{1,5},{2,6},{3,7},{4,0},{5,1},{6,2},{7,3},{8,12},{9,13},{10,... | collective-permute-start | bytes 7077896 | tf_op jit(solution)/shard_map/ppermute | solution.py:103
  298.9 4.1 collective-permute-start.3
  301.5 19.0 %copy-start.12 = (f32[2,2,2,2,2,24,768]{6,5,4,3,2,1,0:T(8,128)S(1)}, f32[2,2,2,2,2,24,768]{6,5,4,3,2,1,0:T(8,128)}, u32[]{:S(2)}) copy-start(f32[2,2,2,2,2,24,768]{6,5,4,3,2,1,0:T(8,128)} %copy-done.11) | copy-start | bytes 7077892
  303.0 5.7 %collective-permute-start.4 = (bf16[1,1,1,1,1,1,8,512]{7,6,5,4,3,2,1,0:T(8,128)(2,1)S(1)}, bf16[1,1,1,1,1,1,8,512]{7,6,5,4,3,2,1,0:T(8,128)(2,1)S(1)}, u32[]{:S(2)}, u32[]{:S(2)}) collective-permute-start(bf16[1,1,1,1,1,1,8,512]{7,6,5,4,3,2,1,0:T(8,128)(2,1)S(1)} %dynamic-slice_convert_fusion.29), channel_id=1, source_target_pairs={{0,2},{1,3},{2,0},{3,1},{4,6},{5,7},{6,4},{7,5},{8,10},{9,11},{10,... | collective-permute-start | bytes 24584 | tf_op jit(solution)/shard_map/ppermute | solution.py:103
  308.6 1.9 collective-permute-start.25
  311.8 7.4 %collective-permute-start.26 = (bf16[1,2,1,2,2,24,512]{6,5,4,3,2,1,0:T(8,128)(2,1)S(1)}, bf16[1,2,1,2,2,24,512]{6,5,4,3,2,1,0:T(8,128)(2,1)S(1)}, u32[]{:S(2)}, u32[]{:S(2)}) collective-permute-start(bf16[1,2,1,2,2,24,512]{6,5,4,3,2,1,0:T(8,128)(2,1)S(1)} %dynamic-slice_convert_fusion.15), channel_id=1, source_target_pairs={{0,16},{1,17},{2,18},{3,19},{4,20},{5,21},{6,22},{7,23},{8,24},{9,... | collective-permute-start | bytes 589832 | tf_op jit(solution)/shard_map/ppermute | solution.py:103
  319.3 4.7 %collective-permute-start.27 = (bf16[1,1,1,2,2,24,512]{6,5,4,3,2,1,0:T(8,128)(2,1)S(1)}, bf16[1,1,1,2,2,24,512]{6,5,4,3,2,1,0:T(8,128)(2,1)S(1)}, u32[]{:S(2)}, u32[]{:S(2)}) collective-permute-start(bf16[1,1,1,2,2,24,512]{6,5,4,3,2,1,0:T(8,128)(2,1)S(1)} %dynamic-slice_convert_fusion.21), channel_id=1, source_target_pairs={{0,8},{1,9},{2,10},{3,11},{4,12},{5,13},{6,14},{7,15},{8,0},{9,1},... | collective-permute-start | bytes 294920 | tf_op jit(solution)/shard_map/ppermute | solution.py:103
  321.8 8.3 %collective-permute-start.11 = (bf16[1,2,1,2,2,24,768]{6,5,4,3,2,1,0:T(8,128)(2,1)S(1)}, bf16[1,2,1,2,2,24,768]{6,5,4,3,2,1,0:T(8,128)(2,1)S(1)}, u32[]{:S(2)}, u32[]{:S(2)}) collective-permute-start(bf16[1,2,1,2,2,24,768]{6,5,4,3,2,1,0:T(8,128)(2,1)S(1)} %dynamic-slice_convert_fusion.13), channel_id=1, source_target_pairs={{0,16},{1,17},{2,18},{3,19},{4,20},{5,21},{6,22},{7,23},{8,24},{9,... | collective-permute-start | bytes 884744 | tf_op jit(solution)/shard_map/ppermute | solution.py:103
  324.0 7.1 %collective-permute-start.28 = (bf16[1,1,1,2,1,24,512]{6,5,4,3,2,1,0:T(8,128)(2,1)S(1)}, bf16[1,1,1,2,1,24,512]{6,5,4,3,2,1,0:T(8,128)(2,1)S(1)}, u32[]{:S(2)}, u32[]{:S(2)}) collective-permute-start(bf16[1,1,1,2,1,24,512]{6,5,4,3,2,1,0:T(8,128)(2,1)S(1)} %dynamic-slice_convert_fusion.24), channel_id=1, source_target_pairs={{0,1},{1,0},{2,3},{3,2},{4,5},{5,4},{6,7},{7,6},{8,9},{9,8},{10,11... | collective-permute-start | bytes 147464 | tf_op jit(solution)/shard_map/ppermute | solution.py:103
  330.1 29.2 %slice-start.5 = ((s8[9437184]{0:T(1024)(128)(4,1)}), s8[4194304]{0:T(1024)(128)(4,1)S(1)}, s32[]{:S(2)}) async-start(s8[9437184]{0:T(1024)(128)(4,1)} %bitcast.162), calls=%async_computation.9 | async-start | bytes 8388608
  330.2 5.2 %collective-permute-start.12 = (bf16[1,1,1,2,2,24,768]{6,5,4,3,2,1,0:T(8,128)(2,1)S(1)}, bf16[1,1,1,2,2,24,768]{6,5,4,3,2,1,0:T(8,128)(2,1)S(1)}, u32[]{:S(2)}, u32[]{:S(2)}) collective-permute-start(bf16[1,1,1,2,2,24,768]{6,5,4,3,2,1,0:T(8,128)(2,1)S(1)} %dynamic-slice_convert_fusion.18), channel_id=1, source_target_pairs={{0,8},{1,9},{2,10},{3,11},{4,12},{5,13},{6,14},{7,15},{8,0},{9,1},... | collective-permute-start | bytes 442376 | tf_op jit(solution)/shard_map/ppermute | solution.py:103
  335.5 23.8 %slice-start.6 = ((s8[9437184]{0:T(1024)(128)(4,1)}), s8[4194304]{0:T(1024)(128)(4,1)S(1)}, s32[]{:S(2)}) async-start(s8[9437184]{0:T(1024)(128)(4,1)} %bitcast.162), calls=%async_computation.10 | async-start | bytes 8388608
  335.5 6.9 %collective-permute-start.13 = (bf16[1,1,1,2,1,24,768]{6,5,4,3,2,1,0:T(8,128)(2,1)S(1)}, bf16[1,1,1,2,1,24,768]{6,5,4,3,2,1,0:T(8,128)(2,1)S(1)}, u32[]{:S(2)}, u32[]{:S(2)}) collective-permute-start(bf16[1,1,1,2,1,24,768]{6,5,4,3,2,1,0:T(8,128)(2,1)S(1)} %dynamic-slice_convert_fusion.22), channel_id=1, source_target_pairs={{0,1},{1,0},{2,3},{3,2},{4,5},{5,4},{6,7},{7,6},{8,9},{9,8},{10,11... | collective-permute-start | bytes 221192 | tf_op jit(solution)/shard_map/ppermute | solution.py:103
  339.7 19.6 %slice-start.7 = ((s8[9437184]{0:T(1024)(128)(4,1)}), s8[1048576]{0:T(1024)(128)(4,1)S(1)}, s32[]{:S(2)}) async-start(s8[9437184]{0:T(1024)(128)(4,1)} %bitcast.162), calls=%async_computation.11 | async-start | bytes 2097152
  339.8 18.8 %collective-permute-start.6 = (bf16[1,2,1,2,2,24,2304]{6,5,4,3,2,1,0:T(8,128)(2,1)S(1)}, bf16[1,2,1,2,2,24,2304]{6,5,4,3,2,1,0:T(8,128)(2,1)S(1)}, u32[]{:S(2)}, u32[]{:S(2)}) collective-permute-start(bf16[1,2,1,2,2,24,2304]{6,5,4,3,2,1,0:T(8,128)(2,1)S(1)} %dynamic-slice_convert_fusion.5), channel_id=1, source_target_pairs={{0,16},{1,17},{2,18},{3,19},{4,20},{5,21},{6,22},{7,23},{8,24},{9,... | collective-permute-start | bytes 2654216 | tf_op jit(solution)/shard_map/ppermute | solution.py:103
  341.4 4.7 %collective-permute-start.29 = (bf16[1,1,1,1,1,24,512]{6,5,4,3,2,1,0:T(8,128)(2,1)S(1)}, bf16[1,1,1,1,1,24,512]{6,5,4,3,2,1,0:T(8,128)(2,1)S(1)}, u32[]{:S(2)}, u32[]{:S(2)}) collective-permute-start(bf16[1,1,1,1,1,24,512]{6,5,4,3,2,1,0:T(8,128)(2,1)S(1)} %dynamic-slice_convert_fusion.27), channel_id=1, source_target_pairs={{0,2},{1,3},{2,0},{3,1},{4,6},{5,7},{6,4},{7,5},{8,10},{9,11},{10,... | collective-permute-start | bytes 73736 | tf_op jit(solution)/shard_map/ppermute | solution.py:103
  342.5 4.9 %collective-permute-start.14 = (bf16[1,1,1,1,1,24,768]{6,5,4,3,2,1,0:T(8,128)(2,1)S(1)}, bf16[1,1,1,1,1,24,768]{6,5,4,3,2,1,0:T(8,128)(2,1)S(1)}, u32[]{:S(2)}, u32[]{:S(2)}) collective-permute-start(bf16[1,1,1,1,1,24,768]{6,5,4,3,2,1,0:T(8,128)(2,1)S(1)} %dynamic-slice_convert_fusion.25), channel_id=1, source_target_pairs={{0,2},{1,3},{2,0},{3,1},{4,6},{5,7},{6,4},{7,5},{8,10},{9,11},{10,... | collective-permute-start | bytes 110600 | tf_op jit(solution)/shard_map/ppermute | solution.py:103
  358.8 10.0 %slice-start = ((s8[9437184]{0:T(1024)(128)(4,1)}), s8[4194304]{0:T(1024)(128)(4,1)S(1)}, s32[]{:S(2)}) async-start(s8[9437184]{0:T(1024)(128)(4,1)} %bitcast.151), calls=%async_computation.4 | async-start | bytes 8388608
  358.9 10.0 %slice-start.1 = ((s8[9437184]{0:T(1024)(128)(4,1)}), s8[4194304]{0:T(1024)(128)(4,1)S(1)}, s32[]{:S(2)}) async-start(s8[9437184]{0:T(1024)(128)(4,1)} %bitcast.151), calls=%async_computation.5 | async-start | bytes 8388608
  358.9 10.0 %slice-start.2 = ((s8[9437184]{0:T(1024)(128)(4,1)}), s8[1048576]{0:T(1024)(128)(4,1)S(1)}, s32[]{:S(2)}) async-start(s8[9437184]{0:T(1024)(128)(4,1)} %bitcast.151), calls=%async_computation.6 | async-start | bytes 2097152
  358.9 8.5 %collective-permute-start.7 = (bf16[1,1,1,2,2,24,2304]{6,5,4,3,2,1,0:T(8,128)(2,1)S(1)}, bf16[1,1,1,2,2,24,2304]{6,5,4,3,2,1,0:T(8,128)(2,1)S(1)}, u32[]{:S(2)}, u32[]{:S(2)}) collective-permute-start(bf16[1,1,1,2,2,24,2304]{6,5,4,3,2,1,0:T(8,128)(2,1)S(1)} %dynamic-slice_convert_fusion.9), channel_id=1, source_target_pairs={{0,8},{1,9},{2,10},{3,11},{4,12},{5,13},{6,14},{7,15},{8,0},{9,1},... | collective-permute-start | bytes 1327112 | tf_op jit(solution)/shard_map/ppermute | solution.py:103
  362.4 28.9 %collective-permute-start.16 = (bf16[1,2,1,2,2,24,3072]{6,5,4,3,2,1,0:T(8,128)(2,1)S(1)}, bf16[1,2,1,2,2,24,3072]{6,5,4,3,2,1,0:T(8,128)(2,1)S(1)}, u32[]{:S(2)}, u32[]{:S(2)}) collective-permute-start(bf16[1,2,1,2,2,24,3072]{6,5,4,3,2,1,0:T(8,128)(2,1)S(1)} %dynamic-slice_convert_fusion.4), channel_id=1, source_target_pairs={{0,16},{1,17},{2,18},{3,19},{4,20},{5,21},{6,22},{7,23},{8,24},{9,... | collective-permute-start | bytes 3538952 | tf_op jit(solution)/shard_map/ppermute | solution.py:103
  367.5 7.2 %collective-permute-start.8 = (bf16[1,1,1,2,1,24,2304]{6,5,4,3,2,1,0:T(8,128)(2,1)S(1)}, bf16[1,1,1,2,1,24,2304]{6,5,4,3,2,1,0:T(8,128)(2,1)S(1)}, u32[]{:S(2)}, u32[]{:S(2)}) collective-permute-start(bf16[1,1,1,2,1,24,2304]{6,5,4,3,2,1,0:T(8,128)(2,1)S(1)} %dynamic-slice_convert_fusion.14), channel_id=1, source_target_pairs={{0,1},{1,0},{2,3},{3,2},{4,5},{5,4},{6,7},{7,6},{8,9},{9,8},{10,11... | collective-permute-start | bytes 663560 | tf_op jit(solution)/shard_map/ppermute | solution.py:103
  371.4 40.2 %collective-permute-start.21 = (bf16[1,2,1,2,2,96,768]{6,5,4,3,2,1,0:T(8,128)(2,1)S(1)}, bf16[1,2,1,2,2,96,768]{6,5,4,3,2,1,0:T(8,128)(2,1)S(1)}, u32[]{:S(2)}, u32[]{:S(2)}) collective-permute-start(bf16[1,2,1,2,2,96,768]{6,5,4,3,2,1,0:T(8,128)(2,1)S(1)} %dynamic-slice_convert_fusion.3), channel_id=1, source_target_pairs={{0,16},{1,17},{2,18},{3,19},{4,20},{5,21},{6,22},{7,23},{8,24},{9,... | collective-permute-start | bytes 3538952 | tf_op jit(solution)/shard_map/ppermute | solution.py:103
  374.7 19.2 %collective-permute-start.9 = (bf16[1,1,1,1,1,24,2304]{6,5,4,3,2,1,0:T(8,128)(2,1)S(1)}, bf16[1,1,1,1,1,24,2304]{6,5,4,3,2,1,0:T(8,128)(2,1)S(1)}, u32[]{:S(2)}, u32[]{:S(2)}) collective-permute-start(bf16[1,1,1,1,1,24,2304]{6,5,4,3,2,1,0:T(8,128)(2,1)S(1)} %dynamic-slice_convert_fusion.20), channel_id=1, source_target_pairs={{0,2},{1,3},{2,0},{3,1},{4,6},{5,7},{6,4},{7,5},{8,10},{9,11},{10,... | collective-permute-start | bytes 331784 | tf_op jit(solution)/shard_map/ppermute | solution.py:103
  391.7 27.4 %collective-permute-start.17 = (bf16[1,1,1,2,2,24,3072]{6,5,4,3,2,1,0:T(8,128)(2,1)S(1)}, bf16[1,1,1,2,2,24,3072]{6,5,4,3,2,1,0:T(8,128)(2,1)}, u32[]{:S(2)}, u32[]{:S(2)}) collective-permute-start(bf16[1,1,1,2,2,24,3072]{6,5,4,3,2,1,0:T(8,128)(2,1)S(1)} %dynamic-slice_convert_fusion.7), channel_id=1, source_target_pairs={{0,8},{1,9},{2,10},{3,11},{4,12},{5,13},{6,14},{7,15},{8,0},{9,1},... | collective-permute-start | bytes 1769480 | tf_op jit(solution)/shard_map/ppermute | solution.py:103
  413.3 11.1 %collective-permute-start.22 = (bf16[1,1,1,2,2,96,768]{6,5,4,3,2,1,0:T(8,128)(2,1)S(1)}, bf16[1,1,1,2,2,96,768]{6,5,4,3,2,1,0:T(8,128)(2,1)}, u32[]{:S(2)}, u32[]{:S(2)}) collective-permute-start(bf16[1,1,1,2,2,96,768]{6,5,4,3,2,1,0:T(8,128)(2,1)S(1)} %dynamic-slice_convert_fusion.6), channel_id=1, source_target_pairs={{0,8},{1,9},{2,10},{3,11},{4,12},{5,13},{6,14},{7,15},{8,0},{9,1},... | collective-permute-start | bytes 1769480 | tf_op jit(solution)/shard_map/ppermute | solution.py:103
  420.4 10.4 %collective-permute-start.18 = (bf16[1,1,1,2,1,24,3072]{6,5,4,3,2,1,0:T(8,128)(2,1)S(1)}, bf16[1,1,1,2,1,24,3072]{6,5,4,3,2,1,0:T(8,128)(2,1)S(1)}, u32[]{:S(2)}, u32[]{:S(2)}) collective-permute-start(bf16[1,1,1,2,1,24,3072]{6,5,4,3,2,1,0:T(8,128)(2,1)S(1)} %dynamic-slice_convert_fusion.12), channel_id=1, source_target_pairs={{0,1},{1,0},{2,3},{3,2},{4,5},{5,4},{6,7},{7,6},{8,9},{9,8},{10,11... | collective-permute-start | bytes 884744 | tf_op jit(solution)/shard_map/ppermute | solution.py:103
  425.6 9.9 %collective-permute-start.23 = (bf16[1,1,1,2,1,96,768]{6,5,4,3,2,1,0:T(8,128)(2,1)S(1)}, bf16[1,1,1,2,1,96,768]{6,5,4,3,2,1,0:T(8,128)(2,1)S(1)}, u32[]{:S(2)}, u32[]{:S(2)}) collective-permute-start(bf16[1,1,1,2,1,96,768]{6,5,4,3,2,1,0:T(8,128)(2,1)S(1)} %dynamic-slice_convert_fusion.11), channel_id=1, source_target_pairs={{0,1},{1,0},{2,3},{3,2},{4,5},{5,4},{6,7},{7,6},{8,9},{9,8},{10,11... | collective-permute-start | bytes 884744 | tf_op jit(solution)/shard_map/ppermute | solution.py:103
  430.9 8.9 %collective-permute-start.19 = (bf16[1,1,1,1,1,24,3072]{6,5,4,3,2,1,0:T(8,128)(2,1)S(1)}, bf16[1,1,1,1,1,24,3072]{6,5,4,3,2,1,0:T(8,128)(2,1)S(1)}, u32[]{:S(2)}, u32[]{:S(2)}) collective-permute-start(bf16[1,1,1,1,1,24,3072]{6,5,4,3,2,1,0:T(8,128)(2,1)S(1)} %dynamic-slice_convert_fusion.17), channel_id=1, source_target_pairs={{0,2},{1,3},{2,0},{3,1},{4,6},{5,7},{6,4},{7,5},{8,10},{9,11},{10,... | collective-permute-start | bytes 442376 | tf_op jit(solution)/shard_map/ppermute | solution.py:103
  435.7 7.7 %collective-permute-start.24 = (bf16[1,1,1,1,1,96,768]{6,5,4,3,2,1,0:T(8,128)(2,1)S(1)}, bf16[1,1,1,1,1,96,768]{6,5,4,3,2,1,0:T(8,128)(2,1)S(1)}, u32[]{:S(2)}, u32[]{:S(2)}) collective-permute-start(bf16[1,1,1,1,1,96,768]{6,5,4,3,2,1,0:T(8,128)(2,1)S(1)} %dynamic-slice_convert_fusion.16), channel_id=1, source_target_pairs={{0,2},{1,3},{2,0},{3,1},{4,6},{5,7},{6,4},{7,5},{8,10},{9,11},{10,... | collective-permute-start | bytes 442376 | tf_op jit(solution)/shard_map/ppermute | solution.py:103
  (63 other events, 226.1 us)
Sparse Core Ops, SparseCore 0:
  17.6 111.0 all-gather.2
  131.4 62.1 all-gather.4

commit v4 on v0

--- a/solution.py
+++ b/solution.py
@@ -315,7 +315,7 @@
         (sum_wave, sum_g1, sum_b1, sum_g2, sum_b2, sum_ib, sum_ob, sum_db,
          sum_mask) = unpack_rows(reduced_sg, small_grads, sg_widths, n_dev, 1)
         sum_dec = rs_chain(grad_dec_weight, n_bits, order)
-        sum_mlp_out = rs_chain(grad_mlp_out, n_bits, order)
+        sum_mlp_out = lax.psum_scatter(grad_mlp_out, AX, scatter_dimension=0, tiled=True)
         sum_mlp_in = rs_chain(grad_mlp_in, n_bits, order)
         sum_out = rs_chain(grad_out_weight, n_bits, order)
         sum_qkv = rs_chain(grad_qkv_weight, n_bits, order)

time: 447 us -> 456 us (1.020)
  waiting for transfers between devices: 89.8 us -> 114 us
  starting transfers between devices: 44.8 us -> 37.3 us
  local copies, waits for them, and re-layouts: 60.6 us -> 54.9 us
  other arithmetic: 33.3 us -> 28 us
    ppermute x30 -> x25, waiting for transfers between devices: 89.1 us -> 103 us  [rs_chain(): lax.ppermute(send.astype(jnp.bfloat16), AX, [(i, i ^ 1 << bit) for i in r...]
    reduce_scatter x0 -> x1, waiting for transfers between devices: none -> 10.4 us  [local(): lax.psum_scatter(grad_mlp_out, AX, scatter_dimension=0, tiled=True)]
    ppermute x30 -> x25, starting transfers between devices: 33.5 us -> 26 us  [rs_chain(): lax.ppermute(send.astype(jnp.bfloat16), AX, [(i, i ^ 1 << bit) for i in r...]
    add x24 -> x20, other arithmetic: 13.7 us -> 9.25 us  [rs_chain(): current = keep + moved.astype(jnp.float32)]
    convert_element_type x30 -> x25, local copies, waits for them, and re-layouts: 11.5 us -> 7.35 us  [rs_chain(): send.astype(jnp.bfloat16)]
    unnamed x127 -> x109, local copies, waits for them, and re-layouts: 12.1 us -> 10.6 us
  transfers between devices with their start and end apart: 34 -> 30, of which waited for: 18 -> 16; matrix products, arithmetic and copies ran while one was open for 22% -> 19% of each run, Pallas kernels for 0% -> 0%
where the time goes in v4:
time: 456 us; the launch traced here: 452 us
  blocking collectives  130 us (29%)
  waiting for transfers between devices  114 us (25%)
  matrix products  71.8 us (16%)
  local copies, waits for them, and re-layouts  54.9 us (12%)
  starting transfers between devices  37.3 us (8%)
  other arithmetic  28 us (6%)
  between operations  15.3 us (3%)
    all_gather x1, blocking collectives, local(): gathered_small = lax.all_gather(packed_small, AX, axis=0, tiled=True)  130 us
    ppermute x25, waiting for transfers between devices, rs_chain(): lax.ppermute(send.astype(jnp.bfloat16), AX, [(i, i ^ 1 << bit) for i in r...  103 us
    ppermute x25, starting transfers between devices, rs_chain(): lax.ppermute(send.astype(jnp.bfloat16), AX, [(i, i ^ 1 << bit) for i in r...  26 us
    dot_general x5, matrix products, outer_cols(): lax.dot_general(left_op, right_op, (((1,), (1,)), ((), ())), preferred_el...  22 us
    dot_general x5, matrix products, product(): return jnp.dot(left_op, right_op, preferred_element_type=jnp.float32)  18.4 us
    dot_general x5, matrix products, inner_rows(): lax.dot_general(left_op, right_op, (((0,), (0,)), ((), ())), preferred_el...  15.7 us
    unnamed x109, local copies, waits for them, and re-layouts  10.6 us
    reduce_scatter x1, waiting for transfers between devices, local(): lax.psum_scatter(grad_mlp_out, AX, scatter_dimension=0, tiled=True)  10.4 us
  transfers between devices with their start and end apart: 30, of which 16 were waited for; matrix products, arithmetic and copies ran while one was open for 19% of the time, Pallas kernels for 0%

profile of v4, /device:TPU:0, one launch (start us, length us, event | category | flops | bytes accessed | tf_op | source)
XLA Modules:
  0.0 451.7 jit_solution(1361779155633070353)
XLA Ops:
  7.2 1.8 pad_maximum_fusion.3
  9.1 7.5 %all-to-all-start.1 = ((bf16[64,32,512]{2,1,0:T(8,128)(2,1)}), bf16[64,32,512]{2,1,0:T(8,128)(2,1)}, u32[]{:S(2)}, u32[]{:S(2)}) async-start(bf16[64,32,512]{2,1,0:T(8,128)(2,1)} %param.35), calls=%async_computation.1 | async-start | bytes 4194304 | tf_op jit(solution)/shard_map/all_to_all | solution.py:261
  17.7 130.4 %all_gather.9 = bf16[32,8,512]{2,1,0:T(8,128)(2,1)S(1)} all-gather(bf16[1,8,512]{2,1,0:T(8,128)(2,1)S(1)} %reshape.330), channel_id=1, replica_groups=mesh['dp'=8,'fsdp'=4] {'dp','fsdp'}, dimensions={0}, use_global_device_ids=true | all-gather | bytes 270336 | tf_op jit(solution)/shard_map/all_gather | solution.py:199
  152.1 1.8 copy.126
  155.6 2.1 select_reduce_fusion
  157.8 4.0 convolution_convert_fusion
  162.9 2.3 copy.115
  165.2 3.0 reshape.334
  169.3 2.2 reshape.336
  172.7 2.2 reshape.335
  176.0 4.8 %fusion.78 = (f32[2,12,256]{2,1,0:T(8,128)S(1)}, f32[2,12,256,256]{2,3,1,0:T(8,128)S(1)}) fusion(f32[2,12,256,256]{2,3,1,0:T(8,128)S(1)} %fusion.58), kind=kOutput, calls=%fused_computation.184 | output fusion | flops 6291711 | bytes 12607488 | tf_op jit(solution)/shard_map/sub | solution.py:124
  181.4 2.6 copy-done
  187.7 5.6 %multiply_convert_fusion.1 = (bf16[512,3072]{1,0:T(8,128)(2,1)}, f32[512,3072]{1,0:T(8,128)}) fusion(f32[3072]{0:T(1024)S(1)} %reshape.372, bf16[768,6656]{1,0:T(8,128)(2,1)S(1)} %bitcast.191, f32[512,768]{1,0:T(8,128)S(1)} %get-tuple-element.50, f32[768]{0:T(1024)S(1)} %reshape.371, f32[768]{0:T(1024)S(1)} %reshape.370, f32[512]{0:T(512)S(1)} %add_rsqrt_fusion, ...), kind=kOutput, calls=%fused_computation.11 | convolution fusion | flops 2427322368 | bytes 15753216 | tf_op jit(solution)/shard_map/dot_general | solution.py:21
  193.3 7.6 %convert_reduce_fusion = (f32[3072]{0:T(1024)S(1)}, bf16[512,3072]{1,0:T(8,128)(2,1)S(1)}) fusion(f32[512,3072]{1,0:T(8,128)} %get-tuple-element.52, f32[3072]{0:T(1024)S(1)} %reshape.372, bf16[3072,768]{1,0:T(8,128)(2,1)} %all-gather.5.cloned.1.call-done, f32[512,768]{1,0:T(8,128)S(1)} %fusion.49), kind=kOutput, calls=%fused_computation.8 | convolution fusion | flops 2436756480 | bytes 15753216 | tf_op jit(solution)/shard_map/dot_general | solution.py:31
  201.0 6.5 %multiply_reduce_fusion.2 = (f32[768]{0:T(1024)S(1)}, f32[512]{0:T(512)S(1)}, f32[512]{0:T(512)S(1)}, f32[768]{0:T(1024)S(1)}, f32[512,768]{1,0:T(8,128)S(1)}) fusion(f32[512,768]{1,0:T(8,128)S(1)} %get-tuple-element.50, f32[512]{0:T(512)S(1)} %add_rsqrt_fusion, f32[512]{0:T(512)S(1)} %broadcast_multiply_fusion.4, f32[768]{0:T(1024)S(1)} %reshape.370, ...), kind=kOutput, calls=%fused_computation.47 | convolution fusion | flops 2419455488 | bytes 11027456 | tf_op jit(solution)/shard_map/dot_general | solution.py:31
  209.3 2.1 convolution_convert_fusion.1
  212.7 4.3 fusion.33
  217.5 3.8 multiply_reduce_fusion
  221.3 4.3 multiply_convert_fusion
  229.3 5.7 %fusion.75 = f32[768,3072]{1,0:T(8,128)} fusion(bf16[512,3072]{1,0:T(8,128)(2,1)S(1)} %copy-done.43, f32[512,768]{1,0:T(8,128)S(1)} %copy-done.6, f32[768]{0:T(1024)S(1)} %reshape.371, f32[768]{0:T(1024)S(1)} %reshape.370, f32[512]{0:T(512)S(1)} %add_rsqrt_fusion, f32[512]{0:T(512)S(1)} %broadcast_multiply_fusion.4), kind=kOutput, calls=%fused_computation.181 | convolution fusion | flops 2417885184 | bytes 14166016 | tf_op jit(solution)/shard_map/dot_general | solution.py:25
  235.0 5.0 %fusion.70 = f32[3072,768]{1,0:T(8,128)} fusion(bf16[512,3072]{1,0:T(8,128)(2,1)S(1)} %copy-done.20, f32[512,768]{1,0:T(8,128)S(1)} %copy-done.4), kind=kOutput, calls=%fused_computation.176 | convolution fusion | flops 2416312320 | bytes 14155776 | tf_op jit(solution)/shard_map/dot_general | solution.py:25
  240.1 5.9 %add_convert_fusion = bf16[512,768]{1,0:T(8,128)(2,1)S(1)} fusion(f32[512,768]{1,0:T(8,128)S(1)} %copy-done.6, bf16[512,3072]{1,0:T(8,128)(2,1)} %get-tuple-element.51, bf16[3072,768]{1,0:T(8,128)(2,1)} %all-gather.5.cloned.1.call-done, f32[768]{0:T(1024)S(1)} %reshape.373), kind=kOutput, calls=%fused_computation.55 | convolution fusion | flops 2417098752 | bytes 10226688 | tf_op jit(solution)/shard_map/dot_general | solution.py:21
  246.0 2.0 fusion.41
  249.2 3.5 copy.124
  252.7 3.5 all-to-all-start
  263.0 5.2 %multiply_reduce_fusion.3 = (f32[768]{0:T(1024)S(1)}, f32[512]{0:T(512)S(1)}, f32[512]{0:T(512)S(1)}, f32[768]{0:T(1024)S(1)}, f32[512,768]{1,0:T(8,128)S(1)}) fusion(f32[2,256,768]{2,1,0:T(8,128)S(1)} %copy-done.2, f32[512]{0:T(512)S(1)} %bitcast.198, f32[512]{0:T(512)S(1)} %bitcast.201, f32[768]{0:T(1024)S(1)} %reshape.368, ...), kind=kOutput, calls=%fused_computation.48 | convolution fusion | flops 1822553600 | bytes 9061376 | tf_op jit(solution)/shard_map/dot_general | solution.py:31
  271.8 3.6 fusion.18
  280.9 2.6 collective-permute-done.1
  283.5 2.3 collective-permute-start.2
  285.8 4.1 dynamic-slice_convert_fusion
  293.2 2.1 collective-permute-done.3
  295.3 4.8 %collective-permute-start.4 = (bf16[1,1,1,1,1,1,8,512]{7,6,5,4,3,2,1,0:T(8,128)(2,1)S(1)}, bf16[1,1,1,1,1,1,8,512]{7,6,5,4,3,2,1,0:T(8,128)(2,1)S(1)}, u32[]{:S(2)}, u32[]{:S(2)}) collective-permute-start(bf16[1,1,1,1,1,1,8,512]{7,6,5,4,3,2,1,0:T(8,128)(2,1)S(1)} %dynamic-slice_convert_fusion.24), channel_id=1, source_target_pairs={{0,2},{1,3},{2,0},{3,1},{4,6},{5,7},{6,4},{7,5},{8,10},{9,11},{10,... | collective-permute-start | bytes 24584 | tf_op jit(solution)/shard_map/ppermute | solution.py:90
  301.1 4.2 collective-permute-done.4
  312.1 4.0 collective-permute-done.21
  321.0 3.8 collective-permute-done.11
  326.0 4.1 collective-permute-done.12
  331.2 3.3 collective-permute-done.13
  334.6 2.9 convert_add_fusion.1
  339.4 3.7 convert_add_fusion
  343.2 24.1 %collective-permute-done.6 = bf16[1,2,1,2,2,24,2304]{6,5,4,3,2,1,0:T(8,128)(2,1)S(1)} collective-permute-done((bf16[1,2,1,2,2,24,2304]{6,5,4,3,2,1,0:T(8,128)(2,1)S(1)}, bf16[1,2,1,2,2,24,2304]{6,5,4,3,2,1,0:T(8,128)(2,1)S(1)}, u32[]{:S(2)}, u32[]{:S(2)}) %collective-permute-start.6) | collective-permute-done | bytes 884768 | tf_op jit(solution)/shard_map/ppermute | solution.py:90
  370.3 12.4 %collective-permute-done.7 = bf16[1,1,1,2,2,24,2304]{6,5,4,3,2,1,0:T(8,128)(2,1)S(1)} collective-permute-done((bf16[1,1,1,2,2,24,2304]{6,5,4,3,2,1,0:T(8,128)(2,1)S(1)}, bf16[1,1,1,2,2,24,2304]{6,5,4,3,2,1,0:T(8,128)(2,1)S(1)}, u32[]{:S(2)}, u32[]{:S(2)}) %collective-permute-start.7) | collective-permute-done | bytes 442400 | tf_op jit(solution)/shard_map/ppermute | solution.py:90
  382.9 14.0 %collective-permute-done.16 = bf16[1,2,1,2,2,24,3072]{6,5,4,3,2,1,0:T(8,128)(2,1)S(1)} collective-permute-done((bf16[1,2,1,2,2,24,3072]{6,5,4,3,2,1,0:T(8,128)(2,1)S(1)}, bf16[1,2,1,2,2,24,3072]{6,5,4,3,2,1,0:T(8,128)(2,1)S(1)}, u32[]{:S(2)}, u32[]{:S(2)}) %collective-permute-start.16) | collective-permute-done | bytes 1179680 | tf_op jit(solution)/shard_map/ppermute | solution.py:90
  398.3 13.2 %collective-permute-done.17 = bf16[1,1,1,2,2,24,3072]{6,5,4,3,2,1,0:T(8,128)(2,1)S(1)} collective-permute-done((bf16[1,1,1,2,2,24,3072]{6,5,4,3,2,1,0:T(8,128)(2,1)S(1)}, bf16[1,1,1,2,2,24,3072]{6,5,4,3,2,1,0:T(8,128)(2,1)S(1)}, u32[]{:S(2)}, u32[]{:S(2)}) %collective-permute-start.17) | collective-permute-done | bytes 589856 | tf_op jit(solution)/shard_map/ppermute | solution.py:90
  411.8 3.1 collective-permute-start.9
  414.9 10.8 %collective-permute-done.18 = bf16[1,1,1,2,1,24,3072]{6,5,4,3,2,1,0:T(8,128)(2,1)S(1)} collective-permute-done((bf16[1,1,1,2,1,24,3072]{6,5,4,3,2,1,0:T(8,128)(2,1)S(1)}, bf16[1,1,1,2,1,24,3072]{6,5,4,3,2,1,0:T(8,128)(2,1)S(1)}, u32[]{:S(2)}, u32[]{:S(2)}) %collective-permute-start.18) | collective-permute-done | bytes 294944 | tf_op jit(solution)/shard_map/ppermute | solution.py:90
  428.0 3.4 copy.125
  431.4 2.3 collective-permute-done.19
  434.4 10.4 %reduce-scatter.2.cloned.1.call-done = f32[96,768]{1,0:T(8,128)} async-done(((f32[3072,768]{1,0:T(8,128)}), f32[96,768]{1,0:T(8,128)}) %reduce-scatter.2.cloned.1.call-update) | async-done | bytes 294928 | tf_op jit(solution)/shard_map/reduce_scatter | solution.py:318
  (278 shorter events, 67.9 us)
Async XLA Ops:
  7.2 150.7 %all-gather.3.cloned.1.call-start = ((), (), s32[]{:S(2)}) async-start(), calls=%async_computation.3 | async-start | bytes 10543104 | tf_op jit(solution)/shard_map/all_gather | solution.py:204
  9.0 8.4 %copy-start.31 = (bf16[4,768]{1,0:T(4,128)(2,1)S(1)}, bf16[4,768]{1,0:T(4,128)(2,1)}, u32[]{:S(2)}) copy-start(bf16[4,768]{1,0:T(4,128)(2,1)} %param.21) | copy-start | bytes 18436
  9.0 8.4 %copy-start.34 = (bf16[24]{0:T(256)(128)(2,1)S(1)}, bf16[24]{0:T(256)(128)(2,1)}, u32[]{:S(2)}) copy-start(bf16[24]{0:T(256)(128)(2,1)} %param.22) | copy-start | bytes 148
  9.0 8.4 %copy-start.35 = (bf16[24]{0:T(256)(128)(2,1)S(1)}, bf16[24]{0:T(256)(128)(2,1)}, u32[]{:S(2)}) copy-start(bf16[24]{0:T(256)(128)(2,1)} %param.23) | copy-start | bytes 148
  9.0 8.4 %copy-start.36 = (bf16[24]{0:T(256)(128)(2,1)S(1)}, bf16[24]{0:T(256)(128)(2,1)}, u32[]{:S(2)}) copy-start(bf16[24]{0:T(256)(128)(2,1)} %param.26) | copy-start | bytes 148
  9.0 8.4 %copy-start.37 = (bf16[24]{0:T(256)(128)(2,1)S(1)}, bf16[24]{0:T(256)(128)(2,1)}, u32[]{:S(2)}) copy-start(bf16[24]{0:T(256)(128)(2,1)} %param.27) | copy-start | bytes 148
  9.0 8.4 %copy-start.38 = (bf16[96]{0:T(256)(128)(2,1)S(1)}, bf16[96]{0:T(256)(128)(2,1)}, u32[]{:S(2)}) copy-start(bf16[96]{0:T(256)(128)(2,1)} %param.29) | copy-start | bytes 580
  9.0 8.4 %copy-start.39 = (bf16[24]{0:T(256)(128)(2,1)S(1)}, bf16[24]{0:T(256)(128)(2,1)}, u32[]{:S(2)}) copy-start(bf16[24]{0:T(256)(128)(2,1)} %param.31) | copy-start | bytes 148
  9.0 8.4 %copy-start.40 = (bf16[16]{0:T(256)(128)(2,1)S(1)}, bf16[16]{0:T(256)(128)(2,1)}, u32[]{:S(2)}) copy-start(bf16[16]{0:T(256)(128)(2,1)} %param.33) | copy-start | bytes 100
  9.0 8.4 %copy-start.41 = (bf16[16]{0:T(256)(128)(2,1)S(1)}, bf16[16]{0:T(256)(128)(2,1)}, u32[]{:S(2)}) copy-start(bf16[16]{0:T(256)(128)(2,1)} %param.34) | copy-start | bytes 100
  9.1 139.3 %copy-start.33 = (s32[2,13]{1,0:T(2,128)S(1)}, s32[2,13]{1,0:T(2,128)}, u32[]{:S(2)}) copy-start(s32[2,13]{1,0:T(2,128)} %param.19) | copy-start | bytes 316
  9.1 139.8 %copy-start.22 = (bf16[2,256,768]{2,1,0:T(8,128)(2,1)S(1)}, bf16[2,256,768]{2,1,0:T(8,128)(2,1)}, u32[]{:S(2)}) copy-start(bf16[2,256,768]{2,1,0:T(8,128)(2,1)} %param.18) | copy-start | bytes 2359300
  9.1 143.0 %all-to-all-start.1 = ((bf16[64,32,512]{2,1,0:T(8,128)(2,1)}), bf16[64,32,512]{2,1,0:T(8,128)(2,1)}, u32[]{:S(2)}, u32[]{:S(2)}) async-start(bf16[64,32,512]{2,1,0:T(8,128)(2,1)} %param.35), calls=%async_computation.1 | async-start | bytes 4194304 | tf_op jit(solution)/shard_map/all_to_all | solution.py:261
  16.6 176.7 %all-gather.5.cloned.1.call-start = ((), (), s32[]{:S(2)}) async-start(), calls=%async_computation.4 | async-start | bytes 4866048 | tf_op jit(solution)/shard_map/all_gather | solution.py:211
  149.5 35.5 %copy-start.1 = (f32[2,256,768]{2,1,0:T(8,128)}, f32[2,256,768]{2,1,0:T(8,128)S(1)}, u32[]{:S(2)}) copy-start(f32[2,256,768]{2,1,0:T(8,128)S(1)} %get-tuple-element.30) | copy-start | bytes 4718596
  176.0 9.0 %slice-start.2 = ((s8[10223616]{0:T(1024)(128)(4,1)}), s8[4194304]{0:T(1024)(128)(4,1)S(1)}, s32[]{:S(2)}) async-start(s8[10223616]{0:T(1024)(128)(4,1)} %bitcast.190), calls=%async_computation.8 | async-start | bytes 8388608
  186.8 20.7 %copy-start.5 = (f32[512,768]{1,0:T(8,128)}, f32[512,768]{1,0:T(8,128)S(1)}, u32[]{:S(2)}) copy-start(f32[512,768]{1,0:T(8,128)S(1)} %get-tuple-element.50) | copy-start | bytes 4718596
  187.7 19.8 %copy-start.3 = (f32[512,768]{1,0:T(8,128)}, f32[512,768]{1,0:T(8,128)S(1)}, u32[]{:S(2)}) copy-start(f32[512,768]{1,0:T(8,128)S(1)} %fusion.49) | copy-start | bytes 4718596
  201.0 6.5 %copy-start.42 = (bf16[512,3072]{1,0:T(8,128)(2,1)}, bf16[512,3072]{1,0:T(8,128)(2,1)S(1)}, u32[]{:S(2)}) copy-start(bf16[512,3072]{1,0:T(8,128)(2,1)S(1)} %get-tuple-element.58) | copy-start | bytes 9437188
  252.7 175.3 %all-to-all-start = ((bf16[2,1024,512]{2,0,1:T(2,128)(2,1)}), bf16[2,1024,512]{2,0,1:T(2,128)(2,1)}, u32[]{:S(2)}, u32[]{:S(2)}) async-start(bf16[2,1024,512]{2,0,1:T(2,128)(2,1)} %copy.124), calls=%async_computation | async-start | bytes 4194304 | tf_op jit(solution)/shard_map/all_to_all | solution.py:260
  256.2 188.7 %reduce-scatter.2.cloned.1.call-start = ((), (), s32[]{:S(2)}) async-start(), calls=%async_computation.5 | async-start | bytes 9732096 | tf_op jit(solution)/shard_map/reduce_scatter | solution.py:318
  271.7 7.1 %collective-permute-start = (bf16[2,2,1,2,2,1,8,512]{7,6,5,4,3,2,1,0:T(8,128)(2,1)S(1)}, bf16[2,2,1,2,2,1,8,512]{7,6,5,4,3,2,1,0:T(8,128)(2,1)S(1)}, u32[]{:S(2)}, u32[]{:S(2)}) collective-permute-start(bf16[2,2,1,2,2,1,8,512]{7,6,5,4,3,2,1,0:T(8,128)(2,1)S(1)} %dynamic-slice_convert_fusion.14), channel_id=1, source_target_pairs={{0,4},{1,5},{2,6},{3,7},{4,0},{5,1},{6,2},{7,3},{8,12},{9,13},{10,... | collective-permute-start | bytes 393224 | tf_op jit(solution)/shard_map/ppermute | solution.py:90
  276.9 57.7 %collective-permute-start.5 = (bf16[2,2,1,2,2,24,2304]{6,5,4,3,2,1,0:T(8,128)(2,1)}, bf16[2,2,1,2,2,24,2304]{6,5,4,3,2,1,0:T(8,128)(2,1)}, u32[]{:S(2)}, u32[]{:S(2)}) collective-permute-start(bf16[2,2,1,2,2,24,2304]{6,5,4,3,2,1,0:T(8,128)(2,1)} %dynamic-slice_convert_fusion.1), channel_id=1, source_target_pairs={{0,4},{1,5},{2,6},{3,7},{4,0},{5,1},{6,2},{7,3},{8,12},{9,13},{10,... | collective-permute-start | bytes 5308424 | tf_op jit(solution)/shard_map/ppermute | solution.py:90
  278.9 4.5 %collective-permute-start.1 = (bf16[1,2,1,2,2,1,8,512]{7,6,5,4,3,2,1,0:T(8,128)(2,1)S(1)}, bf16[1,2,1,2,2,1,8,512]{7,6,5,4,3,2,1,0:T(8,128)(2,1)S(1)}, u32[]{:S(2)}, u32[]{:S(2)}) collective-permute-start(bf16[1,2,1,2,2,1,8,512]{7,6,5,4,3,2,1,0:T(8,128)(2,1)S(1)} %dynamic-slice_convert_fusion.18), channel_id=1, source_target_pairs={{0,16},{1,17},{2,18},{3,19},{4,20},{5,21},{6,22},{7,23},{8,24},{9,... | collective-permute-start | bytes 196616 | tf_op jit(solution)/shard_map/ppermute | solution.py:90
  280.7 36.8 %collective-permute-start.10 = (bf16[2,2,1,2,2,24,768]{6,5,4,3,2,1,0:T(8,128)(2,1)S(1)}, bf16[2,2,1,2,2,24,768]{6,5,4,3,2,1,0:T(8,128)(2,1)S(1)}, u32[]{:S(2)}, u32[]{:S(2)}) collective-permute-start(bf16[2,2,1,2,2,24,768]{6,5,4,3,2,1,0:T(8,128)(2,1)S(1)} %dynamic-slice_convert_fusion.5), channel_id=1, source_target_pairs={{0,4},{1,5},{2,6},{3,7},{4,0},{5,1},{6,2},{7,3},{8,12},{9,13},{10,... | collective-permute-start | bytes 1769480 | tf_op jit(solution)/shard_map/ppermute | solution.py:90
  283.5 7.7 %collective-permute-start.2 = (bf16[1,1,1,2,2,1,8,512]{7,6,5,4,3,2,1,0:T(8,128)(2,1)S(1)}, bf16[1,1,1,2,2,1,8,512]{7,6,5,4,3,2,1,0:T(8,128)(2,1)S(1)}, u32[]{:S(2)}, u32[]{:S(2)}) collective-permute-start(bf16[1,1,1,2,2,1,8,512]{7,6,5,4,3,2,1,0:T(8,128)(2,1)S(1)} %dynamic-slice_convert_fusion.21), channel_id=1, source_target_pairs={{0,8},{1,9},{2,10},{3,11},{4,12},{5,13},{6,14},{7,15},{8,0},{9,1},... | collective-permute-start | bytes 98312 | tf_op jit(solution)/shard_map/ppermute | solution.py:90
  289.8 49.6 %collective-permute-start.15 = (bf16[2,2,1,2,2,24,3072]{6,5,4,3,2,1,0:T(8,128)(2,1)}, bf16[2,2,1,2,2,24,3072]{6,5,4,3,2,1,0:T(8,128)(2,1)}, u32[]{:S(2)}, u32[]{:S(2)}) collective-permute-start(bf16[2,2,1,2,2,24,3072]{6,5,4,3,2,1,0:T(8,128)(2,1)} %dynamic-slice_convert_fusion), channel_id=1, source_target_pairs={{0,4},{1,5},{2,6},{3,7},{4,0},{5,1},{6,2},{7,3},{8,12},{9,13},{10,... | collective-permute-start | bytes 7077896 | tf_op jit(solution)/shard_map/ppermute | solution.py:90
  291.3 4.0 collective-permute-start.3
  293.2 6.9 %copy-start.18 = (f32[2,2,2,2,2,24,512]{6,5,4,3,2,1,0:T(8,128)}, f32[2,2,2,2,2,24,512]{6,5,4,3,2,1,0:T(8,128)S(1)}, u32[]{:S(2)}) copy-start(f32[2,2,2,2,2,24,512]{6,5,4,3,2,1,0:T(8,128)S(1)} %fusion.81) | copy-start | bytes 4718596
  293.2 24.3 %copy-start.10 = (f32[2,2,2,2,2,24,768]{6,5,4,3,2,1,0:T(8,128)S(1)}, f32[2,2,2,2,2,24,768]{6,5,4,3,2,1,0:T(8,128)}, u32[]{:S(2)}) copy-start(f32[2,2,2,2,2,24,768]{6,5,4,3,2,1,0:T(8,128)} %copy-done.9) | copy-start | bytes 7077892
  295.3 10.1 %collective-permute-start.4 = (bf16[1,1,1,1,1,1,8,512]{7,6,5,4,3,2,1,0:T(8,128)(2,1)S(1)}, bf16[1,1,1,1,1,1,8,512]{7,6,5,4,3,2,1,0:T(8,128)(2,1)S(1)}, u32[]{:S(2)}, u32[]{:S(2)}) collective-permute-start(bf16[1,1,1,1,1,1,8,512]{7,6,5,4,3,2,1,0:T(8,128)(2,1)S(1)} %dynamic-slice_convert_fusion.24), channel_id=1, source_target_pairs={{0,2},{1,3},{2,0},{3,1},{4,6},{5,7},{6,4},{7,5},{8,10},{9,11},{10,... | collective-permute-start | bytes 24584 | tf_op jit(solution)/shard_map/ppermute | solution.py:90
  301.1 7.4 %collective-permute-start.20 = (bf16[2,2,1,2,2,24,512]{6,5,4,3,2,1,0:T(8,128)(2,1)}, bf16[2,2,1,2,2,24,512]{6,5,4,3,2,1,0:T(8,128)(2,1)}, u32[]{:S(2)}, u32[]{:S(2)}) collective-permute-start(bf16[2,2,1,2,2,24,512]{6,5,4,3,2,1,0:T(8,128)(2,1)} %dynamic-slice_convert_fusion.7), channel_id=1, source_target_pairs={{0,4},{1,5},{2,6},{3,7},{4,0},{5,1},{6,2},{7,3},{8,12},{9,13},{10,... | collective-permute-start | bytes 1179656 | tf_op jit(solution)/shard_map/ppermute | solution.py:90
  310.0 6.1 %collective-permute-start.21 = (bf16[1,2,1,2,2,24,512]{6,5,4,3,2,1,0:T(8,128)(2,1)S(1)}, bf16[1,2,1,2,2,24,512]{6,5,4,3,2,1,0:T(8,128)(2,1)S(1)}, u32[]{:S(2)}, u32[]{:S(2)}) collective-permute-start(bf16[1,2,1,2,2,24,512]{6,5,4,3,2,1,0:T(8,128)(2,1)S(1)} %dynamic-slice_convert_fusion.11), channel_id=1, source_target_pairs={{0,16},{1,17},{2,18},{3,19},{4,20},{5,21},{6,22},{7,23},{8,24},{9,... | collective-permute-start | bytes 589832 | tf_op jit(solution)/shard_map/ppermute | solution.py:90
  316.2 4.7 %collective-permute-start.22 = (bf16[1,1,1,2,2,24,512]{6,5,4,3,2,1,0:T(8,128)(2,1)S(1)}, bf16[1,1,1,2,2,24,512]{6,5,4,3,2,1,0:T(8,128)(2,1)S(1)}, u32[]{:S(2)}, u32[]{:S(2)}) collective-permute-start(bf16[1,1,1,2,2,24,512]{6,5,4,3,2,1,0:T(8,128)(2,1)S(1)} %dynamic-slice_convert_fusion.16), channel_id=1, source_target_pairs={{0,8},{1,9},{2,10},{3,11},{4,12},{5,13},{6,14},{7,15},{8,0},{9,1},... | collective-permute-start | bytes 294920 | tf_op jit(solution)/shard_map/ppermute | solution.py:90
  317.7 7.1 %collective-permute-start.11 = (bf16[1,2,1,2,2,24,768]{6,5,4,3,2,1,0:T(8,128)(2,1)S(1)}, bf16[1,2,1,2,2,24,768]{6,5,4,3,2,1,0:T(8,128)(2,1)S(1)}, u32[]{:S(2)}, u32[]{:S(2)}) collective-permute-start(bf16[1,2,1,2,2,24,768]{6,5,4,3,2,1,0:T(8,128)(2,1)S(1)} %dynamic-slice_convert_fusion.9), channel_id=1, source_target_pairs={{0,16},{1,17},{2,18},{3,19},{4,20},{5,21},{6,22},{7,23},{8,24},{9,... | collective-permute-start | bytes 884744 | tf_op jit(solution)/shard_map/ppermute | solution.py:90
  320.9 4.8 %collective-permute-start.23 = (bf16[1,1,1,2,1,24,512]{6,5,4,3,2,1,0:T(8,128)(2,1)S(1)}, bf16[1,1,1,2,1,24,512]{6,5,4,3,2,1,0:T(8,128)(2,1)S(1)}, u32[]{:S(2)}, u32[]{:S(2)}) collective-permute-start(bf16[1,1,1,2,1,24,512]{6,5,4,3,2,1,0:T(8,128)(2,1)S(1)} %dynamic-slice_convert_fusion.19), channel_id=1, source_target_pairs={{0,1},{1,0},{2,3},{3,2},{4,5},{5,4},{6,7},{7,6},{8,9},{9,8},{10,11... | collective-permute-start | bytes 147464 | tf_op jit(solution)/shard_map/ppermute | solution.py:90
  324.9 5.2 %collective-permute-start.12 = (bf16[1,1,1,2,2,24,768]{6,5,4,3,2,1,0:T(8,128)(2,1)S(1)}, bf16[1,1,1,2,2,24,768]{6,5,4,3,2,1,0:T(8,128)(2,1)S(1)}, u32[]{:S(2)}, u32[]{:S(2)}) collective-permute-start(bf16[1,1,1,2,2,24,768]{6,5,4,3,2,1,0:T(8,128)(2,1)S(1)} %dynamic-slice_convert_fusion.13), channel_id=1, source_target_pairs={{0,8},{1,9},{2,10},{3,11},{4,12},{5,13},{6,14},{7,15},{8,0},{9,1},... | collective-permute-start | bytes 442376 | tf_op jit(solution)/shard_map/ppermute | solution.py:90
  325.8 4.8 %collective-permute-start.24 = (bf16[1,1,1,1,1,24,512]{6,5,4,3,2,1,0:T(8,128)(2,1)S(1)}, bf16[1,1,1,1,1,24,512]{6,5,4,3,2,1,0:T(8,128)(2,1)S(1)}, u32[]{:S(2)}, u32[]{:S(2)}) collective-permute-start(bf16[1,1,1,1,1,24,512]{6,5,4,3,2,1,0:T(8,128)(2,1)S(1)} %dynamic-slice_convert_fusion.22), channel_id=1, source_target_pairs={{0,2},{1,3},{2,0},{3,1},{4,6},{5,7},{6,4},{7,5},{8,10},{9,11},{10,... | collective-permute-start | bytes 73736 | tf_op jit(solution)/shard_map/ppermute | solution.py:90
  330.2 4.4 collective-permute-start.13
  337.6 29.6 %collective-permute-start.6 = (bf16[1,2,1,2,2,24,2304]{6,5,4,3,2,1,0:T(8,128)(2,1)S(1)}, bf16[1,2,1,2,2,24,2304]{6,5,4,3,2,1,0:T(8,128)(2,1)S(1)}, u32[]{:S(2)}, u32[]{:S(2)}) collective-permute-start(bf16[1,2,1,2,2,24,2304]{6,5,4,3,2,1,0:T(8,128)(2,1)S(1)} %dynamic-slice_convert_fusion.3), channel_id=1, source_target_pairs={{0,16},{1,17},{2,18},{3,19},{4,20},{5,21},{6,22},{7,23},{8,24},{9,... | collective-permute-start | bytes 2654216 | tf_op jit(solution)/shard_map/ppermute | solution.py:90
  339.2 30.5 %collective-permute-start.14 = (bf16[1,1,1,1,1,24,768]{6,5,4,3,2,1,0:T(8,128)(2,1)S(1)}, bf16[1,1,1,1,1,24,768]{6,5,4,3,2,1,0:T(8,128)(2,1)S(1)}, u32[]{:S(2)}, u32[]{:S(2)}) collective-permute-start(bf16[1,1,1,1,1,24,768]{6,5,4,3,2,1,0:T(8,128)(2,1)S(1)} %dynamic-slice_convert_fusion.20), channel_id=1, source_target_pairs={{0,2},{1,3},{2,0},{3,1},{4,6},{5,7},{6,4},{7,5},{8,10},{9,11},{10,... | collective-permute-start | bytes 110600 | tf_op jit(solution)/shard_map/ppermute | solution.py:90
  367.4 15.2 %collective-permute-start.7 = (bf16[1,1,1,2,2,24,2304]{6,5,4,3,2,1,0:T(8,128)(2,1)S(1)}, bf16[1,1,1,2,2,24,2304]{6,5,4,3,2,1,0:T(8,128)(2,1)S(1)}, u32[]{:S(2)}, u32[]{:S(2)}) collective-permute-start(bf16[1,1,1,2,2,24,2304]{6,5,4,3,2,1,0:T(8,128)(2,1)S(1)} %dynamic-slice_convert_fusion.6), channel_id=1, source_target_pairs={{0,8},{1,9},{2,10},{3,11},{4,12},{5,13},{6,14},{7,15},{8,0},{9,1},... | collective-permute-start | bytes 1327112 | tf_op jit(solution)/shard_map/ppermute | solution.py:90
  368.0 28.9 %collective-permute-start.16 = (bf16[1,2,1,2,2,24,3072]{6,5,4,3,2,1,0:T(8,128)(2,1)S(1)}, bf16[1,2,1,2,2,24,3072]{6,5,4,3,2,1,0:T(8,128)(2,1)S(1)}, u32[]{:S(2)}, u32[]{:S(2)}) collective-permute-start(bf16[1,2,1,2,2,24,3072]{6,5,4,3,2,1,0:T(8,128)(2,1)S(1)} %dynamic-slice_convert_fusion.2), channel_id=1, source_target_pairs={{0,16},{1,17},{2,18},{3,19},{4,20},{5,21},{6,22},{7,23},{8,24},{9,... | collective-permute-start | bytes 3538952 | tf_op jit(solution)/shard_map/ppermute | solution.py:90
  382.8 15.4 %collective-permute-start.8 = (bf16[1,1,1,2,1,24,2304]{6,5,4,3,2,1,0:T(8,128)(2,1)S(1)}, bf16[1,1,1,2,1,24,2304]{6,5,4,3,2,1,0:T(8,128)(2,1)S(1)}, u32[]{:S(2)}, u32[]{:S(2)}) collective-permute-start(bf16[1,1,1,2,1,24,2304]{6,5,4,3,2,1,0:T(8,128)(2,1)S(1)} %dynamic-slice_convert_fusion.10), channel_id=1, source_target_pairs={{0,1},{1,0},{2,3},{3,2},{4,5},{5,4},{6,7},{7,6},{8,9},{9,8},{10,11... | collective-permute-start | bytes 663560 | tf_op jit(solution)/shard_map/ppermute | solution.py:90
  397.3 14.2 %collective-permute-start.17 = (bf16[1,1,1,2,2,24,3072]{6,5,4,3,2,1,0:T(8,128)(2,1)S(1)}, bf16[1,1,1,2,2,24,3072]{6,5,4,3,2,1,0:T(8,128)(2,1)S(1)}, u32[]{:S(2)}, u32[]{:S(2)}) collective-permute-start(bf16[1,1,1,2,2,24,3072]{6,5,4,3,2,1,0:T(8,128)(2,1)S(1)} %dynamic-slice_convert_fusion.4), channel_id=1, source_target_pairs={{0,8},{1,9},{2,10},{3,11},{4,12},{5,13},{6,14},{7,15},{8,0},{9,1},... | collective-permute-start | bytes 1769480 | tf_op jit(solution)/shard_map/ppermute | solution.py:90
  411.7 14.0 %collective-permute-start.18 = (bf16[1,1,1,2,1,24,3072]{6,5,4,3,2,1,0:T(8,128)(2,1)S(1)}, bf16[1,1,1,2,1,24,3072]{6,5,4,3,2,1,0:T(8,128)(2,1)S(1)}, u32[]{:S(2)}, u32[]{:S(2)}) collective-permute-start(bf16[1,1,1,2,1,24,3072]{6,5,4,3,2,1,0:T(8,128)(2,1)S(1)} %dynamic-slice_convert_fusion.8), channel_id=1, source_target_pairs={{0,1},{1,0},{2,3},{3,2},{4,5},{5,4},{6,7},{7,6},{8,9},{9,8},{10,11... | collective-permute-start | bytes 884744 | tf_op jit(solution)/shard_map/ppermute | solution.py:90
  411.8 15.5 %collective-permute-start.9 = (bf16[1,1,1,1,1,24,2304]{6,5,4,3,2,1,0:T(8,128)(2,1)S(1)}, bf16[1,1,1,1,1,24,2304]{6,5,4,3,2,1,0:T(8,128)(2,1)S(1)}, u32[]{:S(2)}, u32[]{:S(2)}) collective-permute-start(bf16[1,1,1,1,1,24,2304]{6,5,4,3,2,1,0:T(8,128)(2,1)S(1)} %dynamic-slice_convert_fusion.15), channel_id=1, source_target_pairs={{0,2},{1,3},{2,0},{3,1},{4,6},{5,7},{6,4},{7,5},{8,10},{9,11},{10,... | collective-permute-start | bytes 331784 | tf_op jit(solution)/shard_map/ppermute | solution.py:90
  425.7 8.0 %collective-permute-start.19 = (bf16[1,1,1,1,1,24,3072]{6,5,4,3,2,1,0:T(8,128)(2,1)S(1)}, bf16[1,1,1,1,1,24,3072]{6,5,4,3,2,1,0:T(8,128)(2,1)S(1)}, u32[]{:S(2)}, u32[]{:S(2)}) collective-permute-start(bf16[1,1,1,1,1,24,3072]{6,5,4,3,2,1,0:T(8,128)(2,1)S(1)} %dynamic-slice_convert_fusion.12), channel_id=1, source_target_pairs={{0,2},{1,3},{2,0},{3,1},{4,6},{5,7},{6,4},{7,5},{8,10},{9,11},{10,... | collective-permute-start | bytes 442376 | tf_op jit(solution)/shard_map/ppermute | solution.py:90
  (31 other events, 94.9 us)
Sparse Core Ops, SparseCore 0:
  11.4 108.0 all-gather.2
  122.2 62.7 all-gather.4
  290.0 154.8 reduce-scatter.1

commit v5 on v4

--- a/solution.py
+++ b/solution.py
@@ -275,6 +275,8 @@
         grad_ffo = grad_res_two.astype(jnp.bfloat16)
         grad_mlp_out_bias = jnp.sum(grad_ffo.astype(jnp.float32), axis=0)
         grad_mlp_out = inner_rows(active, grad_ffo)
+        grad_ffo, grad_mlp_out = lax.optimization_barrier((grad_ffo, grad_mlp_out))
+        sum_mlp_out = lax.psum_scatter(grad_mlp_out, AX, scatter_dimension=0, tiled=True)
         grad_hidden = (outer_cols(grad_ffo, outer_full) * gelu_slope(hidden)).astype(jnp.bfloat16)
         grad_mlp_in_bias = jnp.sum(grad_hidden.astype(jnp.float32), axis=0)
         grad_mlp_in = inner_rows(act_two, grad_hidden)
@@ -315,7 +317,6 @@
         (sum_wave, sum_g1, sum_b1, sum_g2, sum_b2, sum_ib, sum_ob, sum_db,
          sum_mask) = unpack_rows(reduced_sg, small_grads, sg_widths, n_dev, 1)
         sum_dec = rs_chain(grad_dec_weight, n_bits, order)
-        sum_mlp_out = lax.psum_scatter(grad_mlp_out, AX, scatter_dimension=0, tiled=True)
         sum_mlp_in = rs_chain(grad_mlp_in, n_bits, order)
         sum_out = rs_chain(grad_out_weight, n_bits, order)
         sum_qkv = rs_chain(grad_qkv_weight, n_bits, order)

time: 456 us -> 455 us (level)
  waiting for transfers between devices: 114 us -> 121 us
  starting transfers between devices: 37.3 us -> 32.1 us
  matrix products: 71.8 us -> 66.7 us
    ppermute x25, waiting for transfers between devices: 103 us -> 120 us  [rs_chain(): lax.ppermute(send.astype(jnp.bfloat16), AX, [(i, i ^ 1 << bit) for i in r...]
    reduce_scatter x1, waiting for transfers between devices: 10.4 us -> 0.01 us  [local(): lax.psum_scatter(grad_mlp_out, AX, scatter_dimension=0, tiled=True)]
    ppermute x25, starting transfers between devices: 26 us -> 20.9 us  [rs_chain(): lax.ppermute(send.astype(jnp.bfloat16), AX, [(i, i ^ 1 << bit) for i in r...]
    dot_general x5, matrix products: 22 us -> 17.1 us  [outer_cols(): lax.dot_general(left_op, right_op, (((1,), (1,)), ((), ())), preferred_el...]
    unnamed x109 -> x117, local copies, waits for them, and re-layouts: 10.6 us -> 11.8 us
  transfers between devices with their start and end apart: 30 -> 30, of which waited for: 16 -> 16; matrix products, arithmetic and copies ran while one was open for 19% -> 21% of each run, Pallas kernels for 0% -> 0%
where the time goes in v5:
time: 455 us; the launch traced here: 450 us
  blocking collectives  130 us (29%)
  waiting for transfers between devices  121 us (27%)
  matrix products  66.7 us (15%)
  local copies, waits for them, and re-layouts  57.9 us (13%)
  starting transfers between devices  32.1 us (7%)
  other arithmetic  26.9 us (6%)
  between operations  15.3 us (3%)
    all_gather x1, blocking collectives, local(): gathered_small = lax.all_gather(packed_small, AX, axis=0, tiled=True)  130 us
    ppermute x25, waiting for transfers between devices, rs_chain(): lax.ppermute(send.astype(jnp.bfloat16), AX, [(i, i ^ 1 << bit) for i in r...  120 us
    ppermute x25, starting transfers between devices, rs_chain(): lax.ppermute(send.astype(jnp.bfloat16), AX, [(i, i ^ 1 << bit) for i in r...  20.9 us
    dot_general x5, matrix products, product(): return jnp.dot(left_op, right_op, preferred_element_type=jnp.float32)  18.5 us
    dot_general x5, matrix products, outer_cols(): lax.dot_general(left_op, right_op, (((1,), (1,)), ((), ())), preferred_el...  17.1 us
    dot_general x5, matrix products, inner_rows(): lax.dot_general(left_op, right_op, (((0,), (0,)), ((), ())), preferred_el...  14.4 us
    unnamed x117, local copies, waits for them, and re-layouts  11.8 us
  transfers between devices with their start and end apart: 30, of which 16 were waited for; matrix products, arithmetic and copies ran while one was open for 21% of the time, Pallas kernels for 0%

profile of v5, /device:TPU:0, one launch (start us, length us, event | category | flops | bytes accessed | tf_op | source)
XLA Modules:
  0.0 450.1 jit_solution(4655829997742819838)
XLA Ops:
  7.2 1.8 pad_maximum_fusion.3
  9.1 7.5 %all-to-all-start.1 = ((bf16[64,32,512]{2,1,0:T(8,128)(2,1)}), bf16[64,32,512]{2,1,0:T(8,128)(2,1)}, u32[]{:S(2)}, u32[]{:S(2)}) async-start(bf16[64,32,512]{2,1,0:T(8,128)(2,1)} %param.35), calls=%async_computation.1 | async-start | bytes 4194304 | tf_op jit(solution)/shard_map/all_to_all | solution.py:261
  18.2 129.9 %all_gather.9 = bf16[32,8,512]{2,1,0:T(8,128)(2,1)S(1)} all-gather(bf16[1,8,512]{2,1,0:T(8,128)(2,1)S(1)} %reshape.330), channel_id=1, replica_groups=mesh['dp'=8,'fsdp'=4] {'dp','fsdp'}, dimensions={0}, use_global_device_ids=true | all-gather | bytes 270336 | tf_op jit(solution)/shard_map/all_gather | solution.py:199
  151.6 1.8 copy.126
  155.1 2.1 select_reduce_fusion
  157.3 4.0 convolution_convert_fusion
  163.5 2.2 reshape.335
  166.9 2.2 reshape.336
  169.1 2.6 copy.115
  171.7 2.9 reshape.334
  175.6 4.8 %fusion.75 = (f32[2,12,256]{2,1,0:T(8,128)S(1)}, f32[2,12,256,256]{2,3,1,0:T(8,128)S(1)}) fusion(f32[2,12,256,256]{2,3,1,0:T(8,128)S(1)} %fusion.58), kind=kOutput, calls=%fused_computation.181 | output fusion | flops 6291711 | bytes 12607488 | tf_op jit(solution)/shard_map/sub | solution.py:124
  181.1 2.5 copy-done
  188.4 5.1 %multiply_convert_fusion.1 = (bf16[512,3072]{1,0:T(8,128)(2,1)S(1)}, f32[512,3072]{1,0:T(8,128)}) fusion(f32[3072]{0:T(1024)S(1)} %reshape.372, bf16[768,6656]{1,0:T(8,128)(2,1)S(1)} %bitcast.193, f32[512,768]{1,0:T(8,128)S(1)} %get-tuple-element.54, f32[768]{0:T(1024)S(1)} %reshape.371, f32[768]{0:T(1024)S(1)} %reshape.370, f32[512]{0:T(512)S(1)} %add_rsqrt_fusion, ...), kind=kOutput, calls=%fused_computation.11 | convolution fusion | flops 2427322368 | bytes 15753216 | tf_op jit(solution)/shard_map/dot_general | solution.py:21
  195.2 5.5 %fusion.77 = f32[3072,768]{1,0:T(8,128)} fusion(bf16[512,3072]{1,0:T(8,128)(2,1)S(1)} %get-tuple-element.55, bf16[512,768]{1,0:T(8,128)(2,1)S(1)} %get-tuple-element.18), kind=kOutput, calls=%fused_computation.183 | convolution fusion | flops 2415919104 | bytes 13369344 | tf_op jit(solution)/shard_map/dot_general | solution.py:25
  200.7 7.4 %convert_reduce_fusion = (f32[3072]{0:T(1024)S(1)}, bf16[512,3072]{1,0:T(8,128)(2,1)S(1)}) fusion(f32[512,3072]{1,0:T(8,128)} %get-tuple-element.56, f32[3072]{0:T(1024)S(1)} %reshape.372, bf16[512,768]{1,0:T(8,128)(2,1)} %copy-done.32, bf16[3072,768]{1,0:T(8,128)(2,1)} %all-gather.5.cloned.1.call-done), kind=kOutput, calls=%fused_computation.8 | convolution fusion | flops 2436363264 | bytes 14966784 | tf_op jit(solution)/shard_map/dot_general | solution.py:31
  208.2 5.5 %fusion.72 = f32[768,3072]{1,0:T(8,128)} fusion(bf16[512,3072]{1,0:T(8,128)(2,1)S(1)} %get-tuple-element.63, f32[512,768]{1,0:T(8,128)S(1)} %get-tuple-element.54, f32[768]{0:T(1024)S(1)} %reshape.371, f32[768]{0:T(1024)S(1)} %reshape.370, f32[512]{0:T(512)S(1)} %add_rsqrt_fusion, f32[512]{0:T(512)S(1)} %broadcast_multiply_fusion.4), kind=kOutput, calls=%fused_computation.178 | convolution fusion | flops 2417885184 | bytes 14166016 | tf_op jit(solution)/shard_map/dot_general | solution.py:25
  213.7 3.0 multiply_reduce_fusion.2
  220.6 5.2 %fusion.33 = bf16[2,256,12,64]{1,3,2,0:T(8,128)(2,1)} fusion(bf16[2,256,12,64]{1,0,3,2:T(2,128)(2,1)} %reshape.340, f32[2,12,256,256]{2,3,1,0:T(8,128)} %copy-done, f32[2,12,256]{2,1,0:T(8,128)S(1)} %get-tuple-element.51), kind=kOutput, calls=%fused_computation.72 | convolution fusion | flops 204865536 | bytes 7888896 | tf_op jit(solution)/shard_map/chqk,cqhd->ckhd/dot_general | solution.py:136
  225.8 3.8 multiply_reduce_fusion
  229.6 4.3 multiply_convert_fusion
  233.9 2.0 fusion.40
  237.3 6.8 %add_convert_fusion = bf16[512,768]{1,0:T(8,128)(2,1)} fusion(f32[512,768]{1,0:T(8,128)S(1)} %copy-done.4, bf16[512,3072]{1,0:T(8,128)(2,1)} %copy-done.44, bf16[3072,768]{1,0:T(8,128)(2,1)} %all-gather.5.cloned.1.call-done, f32[768]{0:T(1024)S(1)} %reshape.373), kind=kOutput, calls=%fused_computation.55 | convolution fusion | flops 2417098752 | bytes 10226688 | tf_op jit(solution)/shard_map/dot_general | solution.py:21
  248.2 1.7 fusion.41
  251.2 3.5 copy.124
  254.7 3.5 all-to-all-start
  265.8 5.2 %multiply_reduce_fusion.3 = (f32[768]{0:T(1024)S(1)}, f32[512]{0:T(512)S(1)}, f32[512]{0:T(512)S(1)}, f32[768]{0:T(1024)S(1)}, f32[512,768]{1,0:T(8,128)S(1)}) fusion(f32[2,256,768]{2,1,0:T(8,128)S(1)} %copy-done.2, f32[512]{0:T(512)S(1)} %bitcast.205, f32[512]{0:T(512)S(1)} %bitcast.202, f32[768]{0:T(1024)S(1)} %reshape.368, ...), kind=kOutput, calls=%fused_computation.48 | convolution fusion | flops 1822553600 | bytes 9061376 | tf_op jit(solution)/shard_map/dot_general | solution.py:31
  277.5 2.5 collective-permute-done.1
  280.0 3.2 collective-permute-start.2
  283.3 4.5 dynamic-slice_convert_fusion
  287.9 2.0 fusion.18
  289.9 3.0 collective-permute-done.3
  293.0 4.6 %collective-permute-start.4 = (bf16[1,1,1,1,1,1,8,512]{7,6,5,4,3,2,1,0:T(8,128)(2,1)S(1)}, bf16[1,1,1,1,1,1,8,512]{7,6,5,4,3,2,1,0:T(8,128)(2,1)S(1)}, u32[]{:S(2)}, u32[]{:S(2)}) collective-permute-start(bf16[1,1,1,1,1,1,8,512]{7,6,5,4,3,2,1,0:T(8,128)(2,1)S(1)} %dynamic-slice_convert_fusion.24), channel_id=1, source_target_pairs={{0,2},{1,3},{2,0},{3,1},{4,6},{5,7},{6,4},{7,5},{8,10},{9,11},{10,... | collective-permute-start | bytes 24584 | tf_op jit(solution)/shard_map/ppermute | solution.py:90
  299.0 8.3 %collective-permute-done.4 = bf16[1,1,1,1,1,1,8,512]{7,6,5,4,3,2,1,0:T(8,128)(2,1)S(1)} collective-permute-done((bf16[1,1,1,1,1,1,8,512]{7,6,5,4,3,2,1,0:T(8,128)(2,1)S(1)}, bf16[1,1,1,1,1,1,8,512]{7,6,5,4,3,2,1,0:T(8,128)(2,1)S(1)}, u32[]{:S(2)}, u32[]{:S(2)}) %collective-permute-start.4) | collective-permute-done | bytes 8224 | tf_op jit(solution)/shard_map/ppermute | solution.py:90
  314.0 4.0 collective-permute-done.21
  321.1 3.6 collective-permute-done.22
  325.1 9.6 %collective-permute-done.11 = bf16[1,2,1,2,2,24,768]{6,5,4,3,2,1,0:T(8,128)(2,1)S(1)} collective-permute-done((bf16[1,2,1,2,2,24,768]{6,5,4,3,2,1,0:T(8,128)(2,1)S(1)}, bf16[1,2,1,2,2,24,768]{6,5,4,3,2,1,0:T(8,128)(2,1)S(1)}, u32[]{:S(2)}, u32[]{:S(2)}) %collective-permute-start.11) | collective-permute-done | bytes 294944 | tf_op jit(solution)/shard_map/ppermute | solution.py:90
  335.3 4.7 %collective-permute-done.12 = bf16[1,1,1,2,2,24,768]{6,5,4,3,2,1,0:T(8,128)(2,1)S(1)} collective-permute-done((bf16[1,1,1,2,2,24,768]{6,5,4,3,2,1,0:T(8,128)(2,1)S(1)}, bf16[1,1,1,2,2,24,768]{6,5,4,3,2,1,0:T(8,128)(2,1)S(1)}, u32[]{:S(2)}, u32[]{:S(2)}) %collective-permute-start.12) | collective-permute-done | bytes 147488 | tf_op jit(solution)/shard_map/ppermute | solution.py:90
  342.2 5.9 %collective-permute-done.13 = bf16[1,1,1,2,1,24,768]{6,5,4,3,2,1,0:T(8,128)(2,1)S(1)} collective-permute-done((bf16[1,1,1,2,1,24,768]{6,5,4,3,2,1,0:T(8,128)(2,1)S(1)}, bf16[1,1,1,2,1,24,768]{6,5,4,3,2,1,0:T(8,128)(2,1)S(1)}, u32[]{:S(2)}, u32[]{:S(2)}) %collective-permute-start.13) | collective-permute-done | bytes 73760 | tf_op jit(solution)/shard_map/ppermute | solution.py:90
  348.2 1.9 convert_add_fusion.1
  351.7 3.8 convert_add_fusion
  355.5 19.1 %collective-permute-done.6 = bf16[1,2,1,2,2,24,2304]{6,5,4,3,2,1,0:T(8,128)(2,1)S(1)} collective-permute-done((bf16[1,2,1,2,2,24,2304]{6,5,4,3,2,1,0:T(8,128)(2,1)S(1)}, bf16[1,2,1,2,2,24,2304]{6,5,4,3,2,1,0:T(8,128)(2,1)S(1)}, u32[]{:S(2)}, u32[]{:S(2)}) %collective-permute-start.6) | collective-permute-done | bytes 884768 | tf_op jit(solution)/shard_map/ppermute | solution.py:90
  377.9 12.1 %collective-permute-done.7 = bf16[1,1,1,2,2,24,2304]{6,5,4,3,2,1,0:T(8,128)(2,1)S(1)} collective-permute-done((bf16[1,1,1,2,2,24,2304]{6,5,4,3,2,1,0:T(8,128)(2,1)S(1)}, bf16[1,1,1,2,2,24,2304]{6,5,4,3,2,1,0:T(8,128)(2,1)S(1)}, u32[]{:S(2)}, u32[]{:S(2)}) %collective-permute-start.7) | collective-permute-done | bytes 442400 | tf_op jit(solution)/shard_map/ppermute | solution.py:90
  390.2 20.1 %collective-permute-done.16 = bf16[1,2,1,2,2,24,3072]{6,5,4,3,2,1,0:T(8,128)(2,1)S(1)} collective-permute-done((bf16[1,2,1,2,2,24,3072]{6,5,4,3,2,1,0:T(8,128)(2,1)S(1)}, bf16[1,2,1,2,2,24,3072]{6,5,4,3,2,1,0:T(8,128)(2,1)S(1)}, u32[]{:S(2)}, u32[]{:S(2)}) %collective-permute-start.16) | collective-permute-done | bytes 1179680 | tf_op jit(solution)/shard_map/ppermute | solution.py:90
  410.8 1.7 collective-permute-start.17
  412.5 13.3 %collective-permute-done.17 = bf16[1,1,1,2,2,24,3072]{6,5,4,3,2,1,0:T(8,128)(2,1)S(1)} collective-permute-done((bf16[1,1,1,2,2,24,3072]{6,5,4,3,2,1,0:T(8,128)(2,1)S(1)}, bf16[1,1,1,2,2,24,3072]{6,5,4,3,2,1,0:T(8,128)(2,1)S(1)}, u32[]{:S(2)}, u32[]{:S(2)}) %collective-permute-start.17) | collective-permute-done | bytes 589856 | tf_op jit(solution)/shard_map/ppermute | solution.py:90
  426.3 9.0 %collective-permute-done.18 = bf16[1,1,1,2,1,24,3072]{6,5,4,3,2,1,0:T(8,128)(2,1)S(1)} collective-permute-done((bf16[1,1,1,2,1,24,3072]{6,5,4,3,2,1,0:T(8,128)(2,1)S(1)}, bf16[1,1,1,2,1,24,3072]{6,5,4,3,2,1,0:T(8,128)(2,1)S(1)}, u32[]{:S(2)}, u32[]{:S(2)}) %collective-permute-start.18) | collective-permute-done | bytes 294944 | tf_op jit(solution)/shard_map/ppermute | solution.py:90
  436.2 3.4 copy.125
  439.6 2.9 collective-permute-done.19
  (287 shorter events, 64.7 us)
Async XLA Ops:
  7.2 150.1 %all-gather.3.cloned.1.call-start = ((), (), s32[]{:S(2)}) async-start(), calls=%async_computation.3 | async-start | bytes 10543104 | tf_op jit(solution)/shard_map/all_gather | solution.py:204
  9.0 8.9 %copy-start.33 = (bf16[4,768]{1,0:T(4,128)(2,1)S(1)}, bf16[4,768]{1,0:T(4,128)(2,1)}, u32[]{:S(2)}) copy-start(bf16[4,768]{1,0:T(4,128)(2,1)} %param.21) | copy-start | bytes 18436
  9.0 8.9 %copy-start.36 = (bf16[24]{0:T(256)(128)(2,1)S(1)}, bf16[24]{0:T(256)(128)(2,1)}, u32[]{:S(2)}) copy-start(bf16[24]{0:T(256)(128)(2,1)} %param.22) | copy-start | bytes 148
  9.0 8.9 %copy-start.37 = (bf16[24]{0:T(256)(128)(2,1)S(1)}, bf16[24]{0:T(256)(128)(2,1)}, u32[]{:S(2)}) copy-start(bf16[24]{0:T(256)(128)(2,1)} %param.23) | copy-start | bytes 148
  9.0 8.9 %copy-start.38 = (bf16[24]{0:T(256)(128)(2,1)S(1)}, bf16[24]{0:T(256)(128)(2,1)}, u32[]{:S(2)}) copy-start(bf16[24]{0:T(256)(128)(2,1)} %param.26) | copy-start | bytes 148
  9.0 8.9 %copy-start.39 = (bf16[24]{0:T(256)(128)(2,1)S(1)}, bf16[24]{0:T(256)(128)(2,1)}, u32[]{:S(2)}) copy-start(bf16[24]{0:T(256)(128)(2,1)} %param.27) | copy-start | bytes 148
  9.0 8.9 %copy-start.40 = (bf16[96]{0:T(256)(128)(2,1)S(1)}, bf16[96]{0:T(256)(128)(2,1)}, u32[]{:S(2)}) copy-start(bf16[96]{0:T(256)(128)(2,1)} %param.29) | copy-start | bytes 580
  9.0 8.9 %copy-start.41 = (bf16[24]{0:T(256)(128)(2,1)S(1)}, bf16[24]{0:T(256)(128)(2,1)}, u32[]{:S(2)}) copy-start(bf16[24]{0:T(256)(128)(2,1)} %param.31) | copy-start | bytes 148
  9.1 8.9 %copy-start.42 = (bf16[16]{0:T(256)(128)(2,1)S(1)}, bf16[16]{0:T(256)(128)(2,1)}, u32[]{:S(2)}) copy-start(bf16[16]{0:T(256)(128)(2,1)} %param.33) | copy-start | bytes 100
  9.1 8.9 %copy-start.43 = (bf16[16]{0:T(256)(128)(2,1)S(1)}, bf16[16]{0:T(256)(128)(2,1)}, u32[]{:S(2)}) copy-start(bf16[16]{0:T(256)(128)(2,1)} %param.34) | copy-start | bytes 100
  9.1 140.0 %copy-start.20 = (bf16[2,256,768]{2,1,0:T(8,128)(2,1)S(1)}, bf16[2,256,768]{2,1,0:T(8,128)(2,1)}, u32[]{:S(2)}) copy-start(bf16[2,256,768]{2,1,0:T(8,128)(2,1)} %param.18) | copy-start | bytes 2359300
  9.1 142.5 %all-to-all-start.1 = ((bf16[64,32,512]{2,1,0:T(8,128)(2,1)}), bf16[64,32,512]{2,1,0:T(8,128)(2,1)}, u32[]{:S(2)}, u32[]{:S(2)}) async-start(bf16[64,32,512]{2,1,0:T(8,128)(2,1)} %param.35), calls=%async_computation.1 | async-start | bytes 4194304 | tf_op jit(solution)/shard_map/all_to_all | solution.py:261
  16.6 184.1 %all-gather.5.cloned.1.call-start = ((), (), s32[]{:S(2)}) async-start(), calls=%async_computation.4 | async-start | bytes 4866048 | tf_op jit(solution)/shard_map/all_gather | solution.py:211
  150.1 34.6 %copy-start.1 = (f32[2,256,768]{2,1,0:T(8,128)}, f32[2,256,768]{2,1,0:T(8,128)S(1)}, u32[]{:S(2)}) copy-start(f32[2,256,768]{2,1,0:T(8,128)S(1)} %get-tuple-element.34) | copy-start | bytes 4718596
  165.7 8.9 %copy-start.11 = (bf16[2,256,12,64]{1,0,3,2:T(2,128)(2,1)}, bf16[2,256,12,64]{1,0,3,2:T(2,128)(2,1)S(1)}, u32[]{:S(2)}) copy-start(bf16[2,256,12,64]{1,0,3,2:T(2,128)(2,1)S(1)} %reshape.335) | copy-start | bytes 2359300
  175.6 9.0 %slice-start.2 = ((s8[10223616]{0:T(1024)(128)(4,1)}), s8[1835008]{0:T(1024)(128)(4,1)S(1)}, s32[]{:S(2)}) async-start(s8[10223616]{0:T(1024)(128)(4,1)} %bitcast.192), calls=%async_computation.8 | async-start | bytes 3670016
  187.5 29.2 %copy-start.3 = (f32[512,768]{1,0:T(8,128)}, f32[512,768]{1,0:T(8,128)S(1)}, u32[]{:S(2)}) copy-start(f32[512,768]{1,0:T(8,128)S(1)} %get-tuple-element.54) | copy-start | bytes 4718596
  200.7 13.0 %slice-start.5 = ((s8[10223616]{0:T(1024)(128)(4,1)}), s8[4194304]{0:T(1024)(128)(4,1)S(1)}, s32[]{:S(2)}) async-start(s8[10223616]{0:T(1024)(128)(4,1)} %bitcast.194), calls=%async_computation.11 | async-start | bytes 8388608
  200.7 13.0 %slice-start.6 = ((s8[10223616]{0:T(1024)(128)(4,1)}), s8[4194304]{0:T(1024)(128)(4,1)S(1)}, s32[]{:S(2)}) async-start(s8[10223616]{0:T(1024)(128)(4,1)} %bitcast.194), calls=%async_computation.12 | async-start | bytes 8388608
  248.2 62.3 %collective-permute-start.20 = (bf16[2,2,1,2,2,24,512]{6,5,4,3,2,1,0:T(8,128)(2,1)}, bf16[2,2,1,2,2,24,512]{6,5,4,3,2,1,0:T(8,128)(2,1)}, u32[]{:S(2)}, u32[]{:S(2)}) collective-permute-start(bf16[2,2,1,2,2,24,512]{6,5,4,3,2,1,0:T(8,128)(2,1)} %dynamic-slice_convert_fusion.7), channel_id=1, source_target_pairs={{0,4},{1,5},{2,6},{3,7},{4,0},{5,1},{6,2},{7,3},{8,12},{9,13},{10,... | collective-permute-start | bytes 1179656 | tf_op jit(solution)/shard_map/ppermute | solution.py:90
  254.7 181.6 %all-to-all-start = ((bf16[2,1024,512]{2,0,1:T(2,128)(2,1)}), bf16[2,1024,512]{2,0,1:T(2,128)(2,1)}, u32[]{:S(2)}, u32[]{:S(2)}) async-start(bf16[2,1024,512]{2,0,1:T(2,128)(2,1)} %copy.124), calls=%async_computation | async-start | bytes 4194304 | tf_op jit(solution)/shard_map/all_to_all | solution.py:260
  258.2 185.2 %reduce-scatter.2.cloned.1.call-start = ((), (), s32[]{:S(2)}) async-start(), calls=%async_computation.5 | async-start | bytes 9732096 | tf_op jit(solution)/shard_map/reduce_scatter | solution.py:279
  274.2 1.4 collective-permute-start
  275.6 4.3 collective-permute-start.1
  277.4 42.0 %collective-permute-start.10 = (bf16[2,2,1,2,2,24,768]{6,5,4,3,2,1,0:T(8,128)(2,1)S(1)}, bf16[2,2,1,2,2,24,768]{6,5,4,3,2,1,0:T(8,128)(2,1)S(1)}, u32[]{:S(2)}, u32[]{:S(2)}) collective-permute-start(bf16[2,2,1,2,2,24,768]{6,5,4,3,2,1,0:T(8,128)(2,1)S(1)} %dynamic-slice_convert_fusion.5), channel_id=1, source_target_pairs={{0,4},{1,5},{2,6},{3,7},{4,0},{5,1},{6,2},{7,3},{8,12},{9,13},{10,... | collective-permute-start | bytes 1769480 | tf_op jit(solution)/shard_map/ppermute | solution.py:90
  280.0 7.7 %collective-permute-start.2 = (bf16[1,1,1,2,2,1,8,512]{7,6,5,4,3,2,1,0:T(8,128)(2,1)S(1)}, bf16[1,1,1,2,2,1,8,512]{7,6,5,4,3,2,1,0:T(8,128)(2,1)S(1)}, u32[]{:S(2)}, u32[]{:S(2)}) collective-permute-start(bf16[1,1,1,2,2,1,8,512]{7,6,5,4,3,2,1,0:T(8,128)(2,1)S(1)} %dynamic-slice_convert_fusion.21), channel_id=1, source_target_pairs={{0,8},{1,9},{2,10},{3,11},{4,12},{5,13},{6,14},{7,15},{8,0},{9,1},... | collective-permute-start | bytes 98312 | tf_op jit(solution)/shard_map/ppermute | solution.py:90
  287.7 63.9 %collective-permute-start.15 = (bf16[2,2,1,2,2,24,3072]{6,5,4,3,2,1,0:T(8,128)(2,1)}, bf16[2,2,1,2,2,24,3072]{6,5,4,3,2,1,0:T(8,128)(2,1)}, u32[]{:S(2)}, u32[]{:S(2)}) collective-permute-start(bf16[2,2,1,2,2,24,3072]{6,5,4,3,2,1,0:T(8,128)(2,1)} %dynamic-slice_convert_fusion), channel_id=1, source_target_pairs={{0,4},{1,5},{2,6},{3,7},{4,0},{5,1},{6,2},{7,3},{8,12},{9,13},{10,... | collective-permute-start | bytes 7077896 | tf_op jit(solution)/shard_map/ppermute | solution.py:90
  287.8 5.2 %collective-permute-start.3 = (bf16[1,1,1,2,1,1,8,512]{7,6,5,4,3,2,1,0:T(8,128)(2,1)S(1)}, bf16[1,1,1,2,1,1,8,512]{7,6,5,4,3,2,1,0:T(8,128)(2,1)S(1)}, u32[]{:S(2)}, u32[]{:S(2)}) collective-permute-start(bf16[1,1,1,2,1,1,8,512]{7,6,5,4,3,2,1,0:T(8,128)(2,1)S(1)} %dynamic-slice_convert_fusion.23), channel_id=1, source_target_pairs={{0,1},{1,0},{2,3},{3,2},{4,5},{5,4},{6,7},{7,6},{8,9},{9,8},{10,11... | collective-permute-start | bytes 49160 | tf_op jit(solution)/shard_map/ppermute | solution.py:90
  293.0 14.3 %collective-permute-start.4 = (bf16[1,1,1,1,1,1,8,512]{7,6,5,4,3,2,1,0:T(8,128)(2,1)S(1)}, bf16[1,1,1,1,1,1,8,512]{7,6,5,4,3,2,1,0:T(8,128)(2,1)S(1)}, u32[]{:S(2)}, u32[]{:S(2)}) collective-permute-start(bf16[1,1,1,1,1,1,8,512]{7,6,5,4,3,2,1,0:T(8,128)(2,1)S(1)} %dynamic-slice_convert_fusion.24), channel_id=1, source_target_pairs={{0,2},{1,3},{2,0},{3,1},{4,6},{5,7},{6,4},{7,5},{8,10},{9,11},{10,... | collective-permute-start | bytes 24584 | tf_op jit(solution)/shard_map/ppermute | solution.py:90
  299.0 20.4 %copy-start.8 = (f32[2,2,2,2,2,24,768]{6,5,4,3,2,1,0:T(8,128)S(1)}, f32[2,2,2,2,2,24,768]{6,5,4,3,2,1,0:T(8,128)}, u32[]{:S(2)}) copy-start(f32[2,2,2,2,2,24,768]{6,5,4,3,2,1,0:T(8,128)} %copy-done.7) | copy-start | bytes 7077892
  299.0 49.2 %collective-permute-start.5 = (bf16[2,2,1,2,2,24,2304]{6,5,4,3,2,1,0:T(8,128)(2,1)}, bf16[2,2,1,2,2,24,2304]{6,5,4,3,2,1,0:T(8,128)(2,1)}, u32[]{:S(2)}, u32[]{:S(2)}) collective-permute-start(bf16[2,2,1,2,2,24,2304]{6,5,4,3,2,1,0:T(8,128)(2,1)} %dynamic-slice_convert_fusion.1), channel_id=1, source_target_pairs={{0,4},{1,5},{2,6},{3,7},{4,0},{5,1},{6,2},{7,3},{8,12},{9,13},{10,... | collective-permute-start | bytes 5308424 | tf_op jit(solution)/shard_map/ppermute | solution.py:90
  311.9 6.1 %collective-permute-start.21 = (bf16[1,2,1,2,2,24,512]{6,5,4,3,2,1,0:T(8,128)(2,1)S(1)}, bf16[1,2,1,2,2,24,512]{6,5,4,3,2,1,0:T(8,128)(2,1)S(1)}, u32[]{:S(2)}, u32[]{:S(2)}) collective-permute-start(bf16[1,2,1,2,2,24,512]{6,5,4,3,2,1,0:T(8,128)(2,1)S(1)} %dynamic-slice_convert_fusion.11), channel_id=1, source_target_pairs={{0,16},{1,17},{2,18},{3,19},{4,20},{5,21},{6,22},{7,23},{8,24},{9,... | collective-permute-start | bytes 589832 | tf_op jit(solution)/shard_map/ppermute | solution.py:90
  318.1 6.7 %collective-permute-start.22 = (bf16[1,1,1,2,2,24,512]{6,5,4,3,2,1,0:T(8,128)(2,1)S(1)}, bf16[1,1,1,2,2,24,512]{6,5,4,3,2,1,0:T(8,128)(2,1)S(1)}, u32[]{:S(2)}, u32[]{:S(2)}) collective-permute-start(bf16[1,1,1,2,2,24,512]{6,5,4,3,2,1,0:T(8,128)(2,1)S(1)} %dynamic-slice_convert_fusion.16), channel_id=1, source_target_pairs={{0,8},{1,9},{2,10},{3,11},{4,12},{5,13},{6,14},{7,15},{8,0},{9,1},... | collective-permute-start | bytes 294920 | tf_op jit(solution)/shard_map/ppermute | solution.py:90
  319.4 28.8 %copy-start.18 = (f32[2,2,2,2,2,24,2304]{6,5,4,3,2,1,0:T(8,128)S(1)}, f32[2,2,2,2,2,24,2304]{6,5,4,3,2,1,0:T(8,128)}, u32[]{:S(2)}) copy-start(f32[2,2,2,2,2,24,2304]{6,5,4,3,2,1,0:T(8,128)} %copy-done.17) | copy-start | bytes 21233668
  319.6 15.2 %collective-permute-start.11 = (bf16[1,2,1,2,2,24,768]{6,5,4,3,2,1,0:T(8,128)(2,1)S(1)}, bf16[1,2,1,2,2,24,768]{6,5,4,3,2,1,0:T(8,128)(2,1)S(1)}, u32[]{:S(2)}, u32[]{:S(2)}) collective-permute-start(bf16[1,2,1,2,2,24,768]{6,5,4,3,2,1,0:T(8,128)(2,1)S(1)} %dynamic-slice_convert_fusion.9), channel_id=1, source_target_pairs={{0,16},{1,17},{2,18},{3,19},{4,20},{5,21},{6,22},{7,23},{8,24},{9,... | collective-permute-start | bytes 884744 | tf_op jit(solution)/shard_map/ppermute | solution.py:90
  325.0 10.2 %collective-permute-start.23 = (bf16[1,1,1,2,1,24,512]{6,5,4,3,2,1,0:T(8,128)(2,1)S(1)}, bf16[1,1,1,2,1,24,512]{6,5,4,3,2,1,0:T(8,128)(2,1)S(1)}, u32[]{:S(2)}, u32[]{:S(2)}) collective-permute-start(bf16[1,1,1,2,1,24,512]{6,5,4,3,2,1,0:T(8,128)(2,1)S(1)} %dynamic-slice_convert_fusion.19), channel_id=1, source_target_pairs={{0,1},{1,0},{2,3},{3,2},{4,5},{5,4},{6,7},{7,6},{8,9},{9,8},{10,11... | collective-permute-start | bytes 147464 | tf_op jit(solution)/shard_map/ppermute | solution.py:90
  334.8 5.2 %collective-permute-start.12 = (bf16[1,1,1,2,2,24,768]{6,5,4,3,2,1,0:T(8,128)(2,1)S(1)}, bf16[1,1,1,2,2,24,768]{6,5,4,3,2,1,0:T(8,128)(2,1)S(1)}, u32[]{:S(2)}, u32[]{:S(2)}) collective-permute-start(bf16[1,1,1,2,2,24,768]{6,5,4,3,2,1,0:T(8,128)(2,1)S(1)} %dynamic-slice_convert_fusion.13), channel_id=1, source_target_pairs={{0,8},{1,9},{2,10},{3,11},{4,12},{5,13},{6,14},{7,15},{8,0},{9,1},... | collective-permute-start | bytes 442376 | tf_op jit(solution)/shard_map/ppermute | solution.py:90
  335.2 6.3 %collective-permute-start.24 = (bf16[1,1,1,1,1,24,512]{6,5,4,3,2,1,0:T(8,128)(2,1)S(1)}, bf16[1,1,1,1,1,24,512]{6,5,4,3,2,1,0:T(8,128)(2,1)S(1)}, u32[]{:S(2)}, u32[]{:S(2)}) collective-permute-start(bf16[1,1,1,1,1,24,512]{6,5,4,3,2,1,0:T(8,128)(2,1)S(1)} %dynamic-slice_convert_fusion.22), channel_id=1, source_target_pairs={{0,2},{1,3},{2,0},{3,1},{4,6},{5,7},{6,4},{7,5},{8,10},{9,11},{10,... | collective-permute-start | bytes 73736 | tf_op jit(solution)/shard_map/ppermute | solution.py:90
  340.1 8.0 %collective-permute-start.13 = (bf16[1,1,1,2,1,24,768]{6,5,4,3,2,1,0:T(8,128)(2,1)S(1)}, bf16[1,1,1,2,1,24,768]{6,5,4,3,2,1,0:T(8,128)(2,1)S(1)}, u32[]{:S(2)}, u32[]{:S(2)}) collective-permute-start(bf16[1,1,1,2,1,24,768]{6,5,4,3,2,1,0:T(8,128)(2,1)S(1)} %dynamic-slice_convert_fusion.17), channel_id=1, source_target_pairs={{0,1},{1,0},{2,3},{3,2},{4,5},{5,4},{6,7},{7,6},{8,9},{9,8},{10,11... | collective-permute-start | bytes 221192 | tf_op jit(solution)/shard_map/ppermute | solution.py:90
  350.2 24.4 %collective-permute-start.6 = (bf16[1,2,1,2,2,24,2304]{6,5,4,3,2,1,0:T(8,128)(2,1)S(1)}, bf16[1,2,1,2,2,24,2304]{6,5,4,3,2,1,0:T(8,128)(2,1)S(1)}, u32[]{:S(2)}, u32[]{:S(2)}) collective-permute-start(bf16[1,2,1,2,2,24,2304]{6,5,4,3,2,1,0:T(8,128)(2,1)S(1)} %dynamic-slice_convert_fusion.3), channel_id=1, source_target_pairs={{0,16},{1,17},{2,18},{3,19},{4,20},{5,21},{6,22},{7,23},{8,24},{9,... | collective-permute-start | bytes 2654216 | tf_op jit(solution)/shard_map/ppermute | solution.py:90
  351.7 25.6 %collective-permute-start.14 = (bf16[1,1,1,1,1,24,768]{6,5,4,3,2,1,0:T(8,128)(2,1)S(1)}, bf16[1,1,1,1,1,24,768]{6,5,4,3,2,1,0:T(8,128)(2,1)S(1)}, u32[]{:S(2)}, u32[]{:S(2)}) collective-permute-start(bf16[1,1,1,1,1,24,768]{6,5,4,3,2,1,0:T(8,128)(2,1)S(1)} %dynamic-slice_convert_fusion.20), channel_id=1, source_target_pairs={{0,2},{1,3},{2,0},{3,1},{4,6},{5,7},{6,4},{7,5},{8,10},{9,11},{10,... | collective-permute-start | bytes 110600 | tf_op jit(solution)/shard_map/ppermute | solution.py:90
  374.8 15.2 %collective-permute-start.7 = (bf16[1,1,1,2,2,24,2304]{6,5,4,3,2,1,0:T(8,128)(2,1)S(1)}, bf16[1,1,1,2,2,24,2304]{6,5,4,3,2,1,0:T(8,128)(2,1)S(1)}, u32[]{:S(2)}, u32[]{:S(2)}) collective-permute-start(bf16[1,1,1,2,2,24,2304]{6,5,4,3,2,1,0:T(8,128)(2,1)S(1)} %dynamic-slice_convert_fusion.6), channel_id=1, source_target_pairs={{0,8},{1,9},{2,10},{3,11},{4,12},{5,13},{6,14},{7,15},{8,0},{9,1},... | collective-permute-start | bytes 1327112 | tf_op jit(solution)/shard_map/ppermute | solution.py:90
  375.8 34.5 %collective-permute-start.16 = (bf16[1,2,1,2,2,24,3072]{6,5,4,3,2,1,0:T(8,128)(2,1)S(1)}, bf16[1,2,1,2,2,24,3072]{6,5,4,3,2,1,0:T(8,128)(2,1)S(1)}, u32[]{:S(2)}, u32[]{:S(2)}) collective-permute-start(bf16[1,2,1,2,2,24,3072]{6,5,4,3,2,1,0:T(8,128)(2,1)S(1)} %dynamic-slice_convert_fusion.2), channel_id=1, source_target_pairs={{0,16},{1,17},{2,18},{3,19},{4,20},{5,21},{6,22},{7,23},{8,24},{9,... | collective-permute-start | bytes 3538952 | tf_op jit(solution)/shard_map/ppermute | solution.py:90
  390.1 22.3 %collective-permute-start.8 = (bf16[1,1,1,2,1,24,2304]{6,5,4,3,2,1,0:T(8,128)(2,1)S(1)}, bf16[1,1,1,2,1,24,2304]{6,5,4,3,2,1,0:T(8,128)(2,1)S(1)}, u32[]{:S(2)}, u32[]{:S(2)}) collective-permute-start(bf16[1,1,1,2,1,24,2304]{6,5,4,3,2,1,0:T(8,128)(2,1)S(1)} %dynamic-slice_convert_fusion.10), channel_id=1, source_target_pairs={{0,1},{1,0},{2,3},{3,2},{4,5},{5,4},{6,7},{7,6},{8,9},{9,8},{10,11... | collective-permute-start | bytes 663560 | tf_op jit(solution)/shard_map/ppermute | solution.py:90
  410.8 15.0 %collective-permute-start.17 = (bf16[1,1,1,2,2,24,3072]{6,5,4,3,2,1,0:T(8,128)(2,1)S(1)}, bf16[1,1,1,2,2,24,3072]{6,5,4,3,2,1,0:T(8,128)(2,1)S(1)}, u32[]{:S(2)}, u32[]{:S(2)}) collective-permute-start(bf16[1,1,1,2,2,24,3072]{6,5,4,3,2,1,0:T(8,128)(2,1)S(1)} %dynamic-slice_convert_fusion.4), channel_id=1, source_target_pairs={{0,8},{1,9},{2,10},{3,11},{4,12},{5,13},{6,14},{7,15},{8,0},{9,1},... | collective-permute-start | bytes 1769480 | tf_op jit(solution)/shard_map/ppermute | solution.py:90
  426.0 9.3 %collective-permute-start.18 = (bf16[1,1,1,2,1,24,3072]{6,5,4,3,2,1,0:T(8,128)(2,1)S(1)}, bf16[1,1,1,2,1,24,3072]{6,5,4,3,2,1,0:T(8,128)(2,1)S(1)}, u32[]{:S(2)}, u32[]{:S(2)}) collective-permute-start(bf16[1,1,1,2,1,24,3072]{6,5,4,3,2,1,0:T(8,128)(2,1)S(1)} %dynamic-slice_convert_fusion.8), channel_id=1, source_target_pairs={{0,1},{1,0},{2,3},{3,2},{4,5},{5,4},{6,7},{7,6},{8,9},{9,8},{10,11... | collective-permute-start | bytes 884744 | tf_op jit(solution)/shard_map/ppermute | solution.py:90
  426.1 9.4 %collective-permute-start.9 = (bf16[1,1,1,1,1,24,2304]{6,5,4,3,2,1,0:T(8,128)(2,1)S(1)}, bf16[1,1,1,1,1,24,2304]{6,5,4,3,2,1,0:T(8,128)(2,1)S(1)}, u32[]{:S(2)}, u32[]{:S(2)}) collective-permute-start(bf16[1,1,1,1,1,24,2304]{6,5,4,3,2,1,0:T(8,128)(2,1)S(1)} %dynamic-slice_convert_fusion.15), channel_id=1, source_target_pairs={{0,2},{1,3},{2,0},{3,1},{4,6},{5,7},{6,4},{7,5},{8,10},{9,11},{10,... | collective-permute-start | bytes 331784 | tf_op jit(solution)/shard_map/ppermute | solution.py:90
  435.4 7.2 %collective-permute-start.19 = (bf16[1,1,1,1,1,24,3072]{6,5,4,3,2,1,0:T(8,128)(2,1)S(1)}, bf16[1,1,1,1,1,24,3072]{6,5,4,3,2,1,0:T(8,128)(2,1)S(1)}, u32[]{:S(2)}, u32[]{:S(2)}) collective-permute-start(bf16[1,1,1,1,1,24,3072]{6,5,4,3,2,1,0:T(8,128)(2,1)S(1)} %dynamic-slice_convert_fusion.12), channel_id=1, source_target_pairs={{0,2},{1,3},{2,0},{3,1},{4,6},{5,7},{6,4},{7,5},{8,10},{9,11},{10,... | collective-permute-start | bytes 442376 | tf_op jit(solution)/shard_map/ppermute | solution.py:90
  (35 other events, 144.3 us)
Sparse Core Ops, SparseCore 0:
  11.4 108.0 all-gather.2
  122.2 62.8 all-gather.4
  265.4 161.4 reduce-scatter.1

commit v6 on v4

--- a/solution.py
+++ b/solution.py
@@ -68,6 +68,35 @@
     while stride < len(flat) and cores[stride] == cores[0]:
         stride *= 2
     return stride.bit_length() - 1
+
+
+def bit_groups(mesh):
+    flat = list(mesh.devices.reshape(-1))
+    n_bits = len(flat).bit_length() - 1
+    first = flat[0]
+    core_bit = None
+    groups = {}
+    for bit in range(n_bits):
+        other = flat[1 << bit]
+        if other.core_on_chip != first.core_on_chip:
+            core_bit = bit
+            continue
+        axis = [a for a in range(len(first.coords)) if first.coords[a] != other.coords[a]]
+        groups.setdefault(axis[0] if axis else -1, []).append(bit)
+    return core_bit, [sorted(bits) for _, bits in sorted(groups.items())]
+
+
+def chain_orders(core_bit, groups):
+    head = [] if core_bit is None else [core_bit]
+    if len(groups) < 3:
+        flat = head + [b for g in reversed(groups) for b in g]
+        return {"y": flat, "x": flat, "yz": flat}
+    x_bits, y_bits, z_bits = groups[0], groups[1], [b for g in groups[2:] for b in g]
+    return {
+        "y": head + y_bits + x_bits + z_bits,
+        "x": head + x_bits + y_bits + z_bits,
+        "yz": head + y_bits + z_bits + x_bits,
+    }
 
 
 def halving_order(n_bits, core_bit):
@@ -152,7 +181,7 @@
     return grad_queries, grad_keys, grad_values
 
 
-def make_local(n_bits, order):
+def make_local(n_bits, order, orders):
     n_dev = 2 ** n_bits
 
     def local(
@@ -311,14 +340,14 @@
                        grad_norm2_bias, grad_mlp_in_bias, grad_mlp_out_bias, grad_dec_bias,
                        grad_mask_token)
         packed_sg, sg_widths = pack_rows(small_grads, n_dev, jnp.float32)
-        reduced_sg = rs_chain(packed_sg, n_bits, order)
+        reduced_sg = rs_chain(packed_sg, n_bits, orders["yz"])
         (sum_wave, sum_g1, sum_b1, sum_g2, sum_b2, sum_ib, sum_ob, sum_db,
          sum_mask) = unpack_rows(reduced_sg, small_grads, sg_widths, n_dev, 1)
-        sum_dec = rs_chain(grad_dec_weight, n_bits, order)
-        sum_mlp_out = lax.psum_scatter(grad_mlp_out, AX, scatter_dimension=0, tiled=True)
-        sum_mlp_in = rs_chain(grad_mlp_in, n_bits, order)
-        sum_out = rs_chain(grad_out_weight, n_bits, order)
-        sum_qkv = rs_chain(grad_qkv_weight, n_bits, order)
+        sum_dec = rs_chain(grad_dec_weight, n_bits, orders["y"])
+        sum_mlp_out = rs_chain(grad_mlp_out, n_bits, orders["x"])
+        sum_mlp_in = rs_chain(grad_mlp_in, n_bits, orders["y"])
+        sum_out = rs_chain(grad_out_weight, n_bits, orders["x"])
+        sum_qkv = rs_chain(grad_qkv_weight, n_bits, orders["yz"])
         summed = (sum_wave, sum_g1, sum_b1, sum_qkv, sum_out, sum_g2, sum_b2, sum_mlp_in,
                   sum_ib, sum_mlp_out, sum_ob, sum_dec, sum_db, sum_mask)
         return (decoded, grad_tokens, *summed)
@@ -330,6 +359,7 @@
     n_dev = mesh.devices.size
     n_bits = n_dev.bit_length() - 1
     order = halving_order(n_bits, core_bit_of(mesh))
+    orders = chain_orders(*bit_groups(mesh))
     placed = (
         P(AX, None, None),
         P(AX, None),
@@ -351,7 +381,7 @@
         P(None, AX, None),
     )
     return jax.shard_map(
-        make_local(n_bits, order),
+        make_local(n_bits, order, orders),
         mesh=mesh,
         in_specs=placed,
         out_specs=(

time: 456 us -> 443 us (0.971)
  waiting for transfers between devices: 114 us -> 88.8 us
  local copies, waits for them, and re-layouts: 54.9 us -> 60.6 us
  other arithmetic: 28 us -> 33.5 us
  starting transfers between devices: 37.3 us -> 42.2 us
    ppermute x25 -> x30, waiting for transfers between devices: 103 us -> 88.1 us  [rs_chain(): lax.ppermute(send.astype(jnp.bfloat16), AX, [(i, i ^ 1 << bit) for i in r...]
    reduce_scatter x1 -> x0, waiting for transfers between devices: 10.4 us -> none  [local(): lax.psum_scatter(grad_mlp_out, AX, scatter_dimension=0, tiled=True)]
    ppermute x25 -> x30, starting transfers between devices: 26 us -> 30.9 us  [rs_chain(): lax.ppermute(send.astype(jnp.bfloat16), AX, [(i, i ^ 1 << bit) for i in r...]
    add x20 -> x24, other arithmetic: 9.25 us -> 14 us  [rs_chain(): current = keep + moved.astype(jnp.float32)]
    convert_element_type x25 -> x30, local copies, waits for them, and re-layouts: 7.35 us -> 11.5 us  [rs_chain(): send.astype(jnp.bfloat16)]
    unnamed x109 -> x127, local copies, waits for them, and re-layouts: 10.6 us -> 12.1 us
  transfers between devices with their start and end apart: 30 -> 34, of which waited for: 16 -> 18; matrix products, arithmetic and copies ran while one was open for 19% -> 22% of each run, Pallas kernels for 0% -> 0%
where the time goes in v6:
time: 443 us; the launch traced here: 439 us
  blocking collectives  130 us (29%)
  waiting for transfers between devices  88.8 us (20%)
  matrix products  68 us (15%)
  local copies, waits for them, and re-layouts  60.6 us (14%)
  starting transfers between devices  42.2 us (10%)
  other arithmetic  33.5 us (8%)
  between operations  15.8 us (4%)
    all_gather x1, blocking collectives, local(): gathered_small = lax.all_gather(packed_small, AX, axis=0, tiled=True)  130 us
    ppermute x30, waiting for transfers between devices, rs_chain(): lax.ppermute(send.astype(jnp.bfloat16), AX, [(i, i ^ 1 << bit) for i in r...  88.1 us
    ppermute x30, starting transfers between devices, rs_chain(): lax.ppermute(send.astype(jnp.bfloat16), AX, [(i, i ^ 1 << bit) for i in r...  30.9 us
    dot_general x5, matrix products, outer_cols(): lax.dot_general(left_op, right_op, (((1,), (1,)), ((), ())), preferred_el...  22 us
    dot_general x5, matrix products, inner_rows(): lax.dot_general(left_op, right_op, (((0,), (0,)), ((), ())), preferred_el...  16 us
    dot_general x5, matrix products, product(): return jnp.dot(left_op, right_op, preferred_element_type=jnp.float32)  15.2 us
    add x24, other arithmetic, rs_chain(): current = keep + moved.astype(jnp.float32)  14 us
    unnamed x127, local copies, waits for them, and re-layouts  12.1 us
  transfers between devices with their start and end apart: 34, of which 18 were waited for; matrix products, arithmetic and copies ran while one was open for 22% of the time, Pallas kernels for 0%

profile of v6, /device:TPU:0, one launch (start us, length us, event | category | flops | bytes accessed | tf_op | source)
XLA Modules:
  0.0 439.3 jit_solution(2297952506866170964)
XLA Ops:
  9.1 7.5 %all-to-all-start.1 = ((bf16[64,32,512]{2,1,0:T(8,128)(2,1)}), bf16[64,32,512]{2,1,0:T(8,128)(2,1)}, u32[]{:S(2)}, u32[]{:S(2)}) async-start(bf16[64,32,512]{2,1,0:T(8,128)(2,1)} %param.35), calls=%async_computation.1 | async-start | bytes 4194304 | tf_op jit(solution)/shard_map/all_to_all | solution.py:290
  17.7 130.4 %all_gather.9 = bf16[32,8,512]{2,1,0:T(8,128)(2,1)S(1)} all-gather(bf16[1,8,512]{2,1,0:T(8,128)(2,1)S(1)} %reshape.336), channel_id=1, replica_groups=mesh['dp'=8,'fsdp'=4] {'dp','fsdp'}, dimensions={0}, use_global_device_ids=true | all-gather | bytes 270336 | tf_op jit(solution)/shard_map/all_gather | solution.py:228
  152.1 1.8 copy.126
  155.6 2.1 select_reduce_fusion
  157.9 4.0 convolution_convert_fusion
  162.9 2.3 copy.115
  165.2 3.0 reshape.340
  169.3 2.2 reshape.342
  172.7 2.2 reshape.341
  176.0 4.8 %fusion.78 = (f32[2,12,256]{2,1,0:T(8,128)S(1)}, f32[2,12,256,256]{2,3,1,0:T(8,128)S(1)}) fusion(f32[2,12,256,256]{2,3,1,0:T(8,128)S(1)} %fusion.58), kind=kOutput, calls=%fused_computation.194 | output fusion | flops 6291711 | bytes 12607488 | tf_op jit(solution)/shard_map/sub | solution.py:153
  181.4 2.6 copy-done
  187.7 5.7 %multiply_convert_fusion.1 = (bf16[512,3072]{1,0:T(8,128)(2,1)}, f32[512,3072]{1,0:T(8,128)}) fusion(f32[3072]{0:T(1024)S(1)} %reshape.380, bf16[768,6656]{1,0:T(8,128)(2,1)S(1)} %bitcast.200, f32[512,768]{1,0:T(8,128)S(1)} %get-tuple-element.50, f32[768]{0:T(1024)S(1)} %reshape.379, f32[768]{0:T(1024)S(1)} %reshape.378, f32[512]{0:T(512)S(1)} %add_rsqrt_fusion, ...), kind=kOutput, calls=%fused_computation.11 | convolution fusion | flops 2427322368 | bytes 15753216 | tf_op jit(solution)/shard_map/dot_general | solution.py:21
  193.4 7.6 %convert_reduce_fusion = (f32[3072]{0:T(1024)S(1)}, bf16[512,3072]{1,0:T(8,128)(2,1)S(1)}) fusion(f32[512,3072]{1,0:T(8,128)} %get-tuple-element.52, f32[3072]{0:T(1024)S(1)} %reshape.380, bf16[3072,768]{1,0:T(8,128)(2,1)} %all-gather.5.cloned.1.call-done, f32[512,768]{1,0:T(8,128)S(1)} %fusion.49), kind=kOutput, calls=%fused_computation.8 | convolution fusion | flops 2436756480 | bytes 15753216 | tf_op jit(solution)/shard_map/dot_general | solution.py:31
  201.1 6.5 %multiply_reduce_fusion.2 = (f32[768]{0:T(1024)S(1)}, f32[512]{0:T(512)S(1)}, f32[512]{0:T(512)S(1)}, f32[768]{0:T(1024)S(1)}, f32[512,768]{1,0:T(8,128)S(1)}) fusion(f32[512,768]{1,0:T(8,128)S(1)} %get-tuple-element.50, f32[512]{0:T(512)S(1)} %add_rsqrt_fusion, f32[512]{0:T(512)S(1)} %broadcast_multiply_fusion.4, f32[768]{0:T(1024)S(1)} %reshape.378, ...), kind=kOutput, calls=%fused_computation.51 | convolution fusion | flops 2419455488 | bytes 11027456 | tf_op jit(solution)/shard_map/dot_general | solution.py:31
  209.4 2.1 convolution_convert_fusion.1
  212.8 4.3 fusion.33
  217.6 3.8 multiply_reduce_fusion
  221.4 4.3 multiply_convert_fusion
  228.5 5.7 %fusion.75 = f32[768,3072]{1,0:T(8,128)} fusion(bf16[512,3072]{1,0:T(8,128)(2,1)S(1)} %copy-done.44, f32[512,768]{1,0:T(8,128)S(1)} %copy-done.6, f32[768]{0:T(1024)S(1)} %reshape.379, f32[768]{0:T(1024)S(1)} %reshape.378, f32[512]{0:T(512)S(1)} %add_rsqrt_fusion, f32[512]{0:T(512)S(1)} %broadcast_multiply_fusion.4), kind=kOutput, calls=%fused_computation.191 | convolution fusion | flops 2417885184 | bytes 14166016 | tf_op jit(solution)/shard_map/dot_general | solution.py:25
  234.1 5.0 %fusion.70 = f32[3072,768]{1,0:T(8,128)} fusion(bf16[512,3072]{1,0:T(8,128)(2,1)S(1)} %copy-done.22, f32[512,768]{1,0:T(8,128)S(1)} %copy-done.4), kind=kOutput, calls=%fused_computation.186 | convolution fusion | flops 2416312320 | bytes 14155776 | tf_op jit(solution)/shard_map/dot_general | solution.py:25
  239.2 2.6 add_convert_fusion
  241.8 2.0 fusion.41
  245.1 3.5 copy.124
  248.5 3.7 all-to-all-start
  258.8 5.2 %multiply_reduce_fusion.3 = (f32[768]{0:T(1024)S(1)}, f32[512]{0:T(512)S(1)}, f32[512]{0:T(512)S(1)}, f32[768]{0:T(1024)S(1)}, f32[512,768]{1,0:T(8,128)S(1)}) fusion(f32[2,256,768]{2,1,0:T(8,128)S(1)} %copy-done.2, f32[512]{0:T(512)S(1)} %bitcast.207, f32[512]{0:T(512)S(1)} %bitcast.210, f32[768]{0:T(1024)S(1)} %reshape.376, ...), kind=kOutput, calls=%fused_computation.52 | convolution fusion | flops 1822553600 | bytes 9061376 | tf_op jit(solution)/shard_map/dot_general | solution.py:31
  267.6 3.6 fusion.18
  278.2 4.1 dynamic-slice_convert_fusion.1
  283.9 4.1 dynamic-slice_convert_fusion
  288.6 3.2 collective-permute-start.3
  292.7 8.8 %collective-permute-done.3 = bf16[1,2,1,1,1,1,8,512]{7,6,5,4,3,2,1,0:T(8,128)(2,1)S(1)} collective-permute-done((bf16[1,2,1,1,1,1,8,512]{7,6,5,4,3,2,1,0:T(8,128)(2,1)S(1)}, bf16[1,2,1,1,1,1,8,512]{7,6,5,4,3,2,1,0:T(8,128)(2,1)S(1)}, u32[]{:S(2)}, u32[]{:S(2)}) %collective-permute-start.3) | collective-permute-done | bytes 16416 | tf_op jit(solution)/shard_map/ppermute | solution.py:119
  312.0 5.2 %collective-permute-done.26 = bf16[1,2,1,2,2,24,512]{6,5,4,3,2,1,0:T(8,128)(2,1)S(1)} collective-permute-done((bf16[1,2,1,2,2,24,512]{6,5,4,3,2,1,0:T(8,128)(2,1)S(1)}, bf16[1,2,1,2,2,24,512]{6,5,4,3,2,1,0:T(8,128)(2,1)S(1)}, u32[]{:S(2)}, u32[]{:S(2)}) %collective-permute-start.26) | collective-permute-done | bytes 196640 | tf_op jit(solution)/shard_map/ppermute | solution.py:119
  319.6 3.4 collective-permute-done.27
  323.2 5.0 %collective-permute-done.11 = bf16[2,1,1,2,2,24,768]{6,5,4,3,2,1,0:T(8,128)(2,1)S(1)} collective-permute-done((bf16[2,1,1,2,2,24,768]{6,5,4,3,2,1,0:T(8,128)(2,1)S(1)}, bf16[2,1,1,2,2,24,768]{6,5,4,3,2,1,0:T(8,128)(2,1)S(1)}, u32[]{:S(2)}, u32[]{:S(2)}) %collective-permute-start.11) | collective-permute-done | bytes 294944 | tf_op jit(solution)/shard_map/ppermute | solution.py:119
  329.9 3.6 collective-permute-done.12
  333.7 3.1 convert_add_fusion.2
  345.9 10.4 %collective-permute-done.6 = bf16[1,2,1,2,2,24,2304]{6,5,4,3,2,1,0:T(8,128)(2,1)S(1)} collective-permute-done((bf16[1,2,1,2,2,24,2304]{6,5,4,3,2,1,0:T(8,128)(2,1)S(1)}, bf16[1,2,1,2,2,24,2304]{6,5,4,3,2,1,0:T(8,128)(2,1)S(1)}, u32[]{:S(2)}, u32[]{:S(2)}) %collective-permute-start.6) | collective-permute-done | bytes 884768 | tf_op jit(solution)/shard_map/ppermute | solution.py:119
  358.2 3.4 convert_add_fusion.1
  363.3 3.0 collective-permute-done.7
  368.2 2.4 convert_add_fusion
  371.0 4.7 %collective-permute-done.8 = bf16[1,2,1,1,1,24,2304]{6,5,4,3,2,1,0:T(8,128)(2,1)S(1)} collective-permute-done((bf16[1,2,1,1,1,24,2304]{6,5,4,3,2,1,0:T(8,128)(2,1)S(1)}, bf16[1,2,1,1,1,24,2304]{6,5,4,3,2,1,0:T(8,128)(2,1)S(1)}, u32[]{:S(2)}, u32[]{:S(2)}) %collective-permute-start.8) | collective-permute-done | bytes 221216 | tf_op jit(solution)/shard_map/ppermute | solution.py:119
  376.8 9.1 %collective-permute-done.16 = bf16[1,2,1,2,2,24,3072]{6,5,4,3,2,1,0:T(8,128)(2,1)S(1)} collective-permute-done((bf16[1,2,1,2,2,24,3072]{6,5,4,3,2,1,0:T(8,128)(2,1)S(1)}, bf16[1,2,1,2,2,24,3072]{6,5,4,3,2,1,0:T(8,128)(2,1)S(1)}, u32[]{:S(2)}, u32[]{:S(2)}) %collective-permute-start.16) | collective-permute-done | bytes 1179680 | tf_op jit(solution)/shard_map/ppermute | solution.py:119
  387.0 15.0 %collective-permute-done.9 = bf16[1,1,1,1,1,24,2304]{6,5,4,3,2,1,0:T(8,128)(2,1)S(1)} collective-permute-done((bf16[1,1,1,1,1,24,2304]{6,5,4,3,2,1,0:T(8,128)(2,1)S(1)}, bf16[1,1,1,1,1,24,2304]{6,5,4,3,2,1,0:T(8,128)(2,1)S(1)}, u32[]{:S(2)}, u32[]{:S(2)}) %collective-permute-start.9) | collective-permute-done | bytes 110624 | tf_op jit(solution)/shard_map/ppermute | solution.py:119
  406.0 3.4 copy.125
  411.3 3.2 collective-permute-done.22
  415.8 4.7 %collective-permute-done.18 = bf16[1,1,1,2,1,24,3072]{6,5,4,3,2,1,0:T(8,128)(2,1)S(1)} collective-permute-done((bf16[1,1,1,2,1,24,3072]{6,5,4,3,2,1,0:T(8,128)(2,1)S(1)}, bf16[1,1,1,2,1,24,3072]{6,5,4,3,2,1,0:T(8,128)(2,1)S(1)}, u32[]{:S(2)}, u32[]{:S(2)}) %collective-permute-start.18) | collective-permute-done | bytes 294944 | tf_op jit(solution)/shard_map/ppermute | solution.py:119
  421.7 1.9 collective-permute-done.23
  425.3 2.9 collective-permute-done.19
  429.0 2.4 collective-permute-done.24
  (316 shorter events, 88.1 us)
Async XLA Ops:
  7.2 150.7 %all-gather.3.cloned.1.call-start = ((), (), s32[]{:S(2)}) async-start(), calls=%async_computation.2 | async-start | bytes 10543104 | tf_op jit(solution)/shard_map/all_gather | solution.py:233
  9.1 139.3 %copy-start.34 = (s32[2,13]{1,0:T(2,128)S(1)}, s32[2,13]{1,0:T(2,128)}, u32[]{:S(2)}) copy-start(s32[2,13]{1,0:T(2,128)} %param.19) | copy-start | bytes 316
  9.1 139.8 %copy-start.23 = (bf16[2,256,768]{2,1,0:T(8,128)(2,1)S(1)}, bf16[2,256,768]{2,1,0:T(8,128)(2,1)}, u32[]{:S(2)}) copy-start(bf16[2,256,768]{2,1,0:T(8,128)(2,1)} %param.18) | copy-start | bytes 2359300
  9.1 143.0 %all-to-all-start.1 = ((bf16[64,32,512]{2,1,0:T(8,128)(2,1)}), bf16[64,32,512]{2,1,0:T(8,128)(2,1)}, u32[]{:S(2)}, u32[]{:S(2)}) async-start(bf16[64,32,512]{2,1,0:T(8,128)(2,1)} %param.35), calls=%async_computation.1 | async-start | bytes 4194304 | tf_op jit(solution)/shard_map/all_to_all | solution.py:290
  16.6 176.9 %all-gather.5.cloned.1.call-start = ((), (), s32[]{:S(2)}) async-start(), calls=%async_computation.3 | async-start | bytes 4866048 | tf_op jit(solution)/shard_map/all_gather | solution.py:240
  149.5 35.5 %copy-start.1 = (f32[2,256,768]{2,1,0:T(8,128)}, f32[2,256,768]{2,1,0:T(8,128)S(1)}, u32[]{:S(2)}) copy-start(f32[2,256,768]{2,1,0:T(8,128)S(1)} %get-tuple-element.30) | copy-start | bytes 4718596
  186.8 20.8 %copy-start.5 = (f32[512,768]{1,0:T(8,128)}, f32[512,768]{1,0:T(8,128)S(1)}, u32[]{:S(2)}) copy-start(f32[512,768]{1,0:T(8,128)S(1)} %get-tuple-element.50) | copy-start | bytes 4718596
  187.7 19.9 %copy-start.3 = (f32[512,768]{1,0:T(8,128)}, f32[512,768]{1,0:T(8,128)S(1)}, u32[]{:S(2)}) copy-start(f32[512,768]{1,0:T(8,128)S(1)} %fusion.49) | copy-start | bytes 4718596
  226.8 12.4 %slice-start.11 = ((s8[4718592]{0:T(1024)(128)(4,1)}), s8[4194304]{0:T(1024)(128)(4,1)S(1)}, s32[]{:S(2)}) async-start(s8[4718592]{0:T(1024)(128)(4,1)} %bitcast.221), calls=%async_computation.15 | async-start | bytes 8388608
  228.5 10.7 %slice-start.12 = ((s8[4718592]{0:T(1024)(128)(4,1)}), s8[524288]{0:T(1024)(128)(4,1)S(1)}, s32[]{:S(2)}) async-start(s8[4718592]{0:T(1024)(128)(4,1)} %bitcast.221), calls=%async_computation.16 | async-start | bytes 1048576
  248.5 157.5 %all-to-all-start = ((bf16[2,1024,512]{2,0,1:T(2,128)(2,1)}), bf16[2,1024,512]{2,0,1:T(2,128)(2,1)}, u32[]{:S(2)}, u32[]{:S(2)}) async-start(bf16[2,1024,512]{2,0,1:T(2,128)(2,1)} %copy.124), calls=%async_computation | async-start | bytes 4194304 | tf_op jit(solution)/shard_map/all_to_all | solution.py:289
  267.5 9.1 %collective-permute-start = (bf16[2,2,1,2,2,1,8,512]{7,6,5,4,3,2,1,0:T(8,128)(2,1)S(1)}, bf16[2,2,1,2,2,1,8,512]{7,6,5,4,3,2,1,0:T(8,128)(2,1)S(1)}, u32[]{:S(2)}, u32[]{:S(2)}) collective-permute-start(bf16[2,2,1,2,2,1,8,512]{7,6,5,4,3,2,1,0:T(8,128)(2,1)S(1)} %dynamic-slice_convert_fusion.19), channel_id=1, source_target_pairs={{0,4},{1,5},{2,6},{3,7},{4,0},{5,1},{6,2},{7,3},{8,12},{9,13},{10,... | collective-permute-start | bytes 393224 | tf_op jit(solution)/shard_map/ppermute | solution.py:119
  272.6 61.0 %collective-permute-start.5 = (bf16[2,2,1,2,2,24,2304]{6,5,4,3,2,1,0:T(8,128)(2,1)}, bf16[2,2,1,2,2,24,2304]{6,5,4,3,2,1,0:T(8,128)(2,1)}, u32[]{:S(2)}, u32[]{:S(2)}) collective-permute-start(bf16[2,2,1,2,2,24,2304]{6,5,4,3,2,1,0:T(8,128)(2,1)} %dynamic-slice_convert_fusion.2), channel_id=1, source_target_pairs={{0,4},{1,5},{2,6},{3,7},{4,0},{5,1},{6,2},{7,3},{8,12},{9,13},{10,... | collective-permute-start | bytes 5308424 | tf_op jit(solution)/shard_map/ppermute | solution.py:119
  276.0 42.6 %collective-permute-start.10 = (bf16[2,2,1,2,2,24,768]{6,5,4,3,2,1,0:T(8,128)(2,1)S(1)}, bf16[2,2,1,2,2,24,768]{6,5,4,3,2,1,0:T(8,128)(2,1)S(1)}, u32[]{:S(2)}, u32[]{:S(2)}) collective-permute-start(bf16[2,2,1,2,2,24,768]{6,5,4,3,2,1,0:T(8,128)(2,1)S(1)} %dynamic-slice_convert_fusion.8), channel_id=1, source_target_pairs={{0,4},{1,5},{2,6},{3,7},{4,0},{5,1},{6,2},{7,3},{8,12},{9,13},{10,... | collective-permute-start | bytes 1769480 | tf_op jit(solution)/shard_map/ppermute | solution.py:119
  276.6 5.7 %collective-permute-start.1 = (bf16[1,2,1,2,2,1,8,512]{7,6,5,4,3,2,1,0:T(8,128)(2,1)S(1)}, bf16[1,2,1,2,2,1,8,512]{7,6,5,4,3,2,1,0:T(8,128)(2,1)S(1)}, u32[]{:S(2)}, u32[]{:S(2)}) collective-permute-start(bf16[1,2,1,2,2,1,8,512]{7,6,5,4,3,2,1,0:T(8,128)(2,1)S(1)} %dynamic-slice_convert_fusion.23), channel_id=1, source_target_pairs={{0,16},{1,17},{2,18},{3,19},{4,20},{5,21},{6,22},{7,23},{8,24},{9,... | collective-permute-start | bytes 196616 | tf_op jit(solution)/shard_map/ppermute | solution.py:119
  282.3 75.9 %collective-permute-start.15 = (bf16[2,2,1,2,2,24,3072]{6,5,4,3,2,1,0:T(8,128)(2,1)}, bf16[2,2,1,2,2,24,3072]{6,5,4,3,2,1,0:T(8,128)(2,1)}, u32[]{:S(2)}, u32[]{:S(2)}) collective-permute-start(bf16[2,2,1,2,2,24,3072]{6,5,4,3,2,1,0:T(8,128)(2,1)} %dynamic-slice_convert_fusion.1), channel_id=1, source_target_pairs={{0,4},{1,5},{2,6},{3,7},{4,0},{5,1},{6,2},{7,3},{8,12},{9,13},{10,... | collective-permute-start | bytes 7077896 | tf_op jit(solution)/shard_map/ppermute | solution.py:119
  282.4 6.2 %collective-permute-start.2 = (bf16[1,2,1,2,1,1,8,512]{7,6,5,4,3,2,1,0:T(8,128)(2,1)S(1)}, bf16[1,2,1,2,1,1,8,512]{7,6,5,4,3,2,1,0:T(8,128)(2,1)S(1)}, u32[]{:S(2)}, u32[]{:S(2)}) collective-permute-start(bf16[1,2,1,2,1,1,8,512]{7,6,5,4,3,2,1,0:T(8,128)(2,1)S(1)} %dynamic-slice_convert_fusion.26), channel_id=1, source_target_pairs={{0,1},{1,0},{2,3},{3,2},{4,5},{5,4},{6,7},{7,6},{8,9},{9,8},{10,11... | collective-permute-start | bytes 98312 | tf_op jit(solution)/shard_map/ppermute | solution.py:119
  288.1 80.1 %collective-permute-start.20 = (bf16[2,2,1,2,2,96,768]{6,5,4,3,2,1,0:T(8,128)(2,1)}, bf16[2,2,1,2,2,96,768]{6,5,4,3,2,1,0:T(8,128)(2,1)}, u32[]{:S(2)}, u32[]{:S(2)}) collective-permute-start(bf16[2,2,1,2,2,96,768]{6,5,4,3,2,1,0:T(8,128)(2,1)} %dynamic-slice_convert_fusion), channel_id=1, source_target_pairs={{0,4},{1,5},{2,6},{3,7},{4,0},{5,1},{6,2},{7,3},{8,12},{9,13},{10,... | collective-permute-start | bytes 7077896 | tf_op jit(solution)/shard_map/ppermute | solution.py:119
  288.6 12.9 %collective-permute-start.3 = (bf16[1,2,1,1,1,1,8,512]{7,6,5,4,3,2,1,0:T(8,128)(2,1)S(1)}, bf16[1,2,1,1,1,1,8,512]{7,6,5,4,3,2,1,0:T(8,128)(2,1)S(1)}, u32[]{:S(2)}, u32[]{:S(2)}) collective-permute-start(bf16[1,2,1,1,1,1,8,512]{7,6,5,4,3,2,1,0:T(8,128)(2,1)S(1)} %dynamic-slice_convert_fusion.28), channel_id=1, source_target_pairs={{0,2},{1,3},{2,0},{3,1},{4,6},{5,7},{6,4},{7,5},{8,10},{9,11},{10,... | collective-permute-start | bytes 49160 | tf_op jit(solution)/shard_map/ppermute | solution.py:119
  292.7 25.9 %copy-start.12 = (f32[2,2,2,2,2,24,768]{6,5,4,3,2,1,0:T(8,128)S(1)}, f32[2,2,2,2,2,24,768]{6,5,4,3,2,1,0:T(8,128)}, u32[]{:S(2)}) copy-start(f32[2,2,2,2,2,24,768]{6,5,4,3,2,1,0:T(8,128)} %copy-done.11) | copy-start | bytes 7077892
  301.5 3.7 collective-permute-start.4
  305.2 3.2 collective-permute-start.25
  309.8 7.4 %collective-permute-start.26 = (bf16[1,2,1,2,2,24,512]{6,5,4,3,2,1,0:T(8,128)(2,1)S(1)}, bf16[1,2,1,2,2,24,512]{6,5,4,3,2,1,0:T(8,128)(2,1)S(1)}, u32[]{:S(2)}, u32[]{:S(2)}) collective-permute-start(bf16[1,2,1,2,2,24,512]{6,5,4,3,2,1,0:T(8,128)(2,1)S(1)} %dynamic-slice_convert_fusion.15), channel_id=1, source_target_pairs={{0,16},{1,17},{2,18},{3,19},{4,20},{5,21},{6,22},{7,23},{8,24},{9,... | collective-permute-start | bytes 589832 | tf_op jit(solution)/shard_map/ppermute | solution.py:119
  317.3 5.7 %collective-permute-start.27 = (bf16[1,1,1,2,2,24,512]{6,5,4,3,2,1,0:T(8,128)(2,1)S(1)}, bf16[1,1,1,2,2,24,512]{6,5,4,3,2,1,0:T(8,128)(2,1)S(1)}, u32[]{:S(2)}, u32[]{:S(2)}) collective-permute-start(bf16[1,1,1,2,2,24,512]{6,5,4,3,2,1,0:T(8,128)(2,1)S(1)} %dynamic-slice_convert_fusion.21), channel_id=1, source_target_pairs={{0,8},{1,9},{2,10},{3,11},{4,12},{5,13},{6,14},{7,15},{8,0},{9,1},... | collective-permute-start | bytes 294920 | tf_op jit(solution)/shard_map/ppermute | solution.py:119
  318.8 9.4 %collective-permute-start.11 = (bf16[2,1,1,2,2,24,768]{6,5,4,3,2,1,0:T(8,128)(2,1)S(1)}, bf16[2,1,1,2,2,24,768]{6,5,4,3,2,1,0:T(8,128)(2,1)S(1)}, u32[]{:S(2)}, u32[]{:S(2)}) collective-permute-start(bf16[2,1,1,2,2,24,768]{6,5,4,3,2,1,0:T(8,128)(2,1)S(1)} %dynamic-slice_convert_fusion.13), channel_id=1, source_target_pairs={{0,8},{1,9},{2,10},{3,11},{4,12},{5,13},{6,14},{7,15},{8,0},{9,1},... | collective-permute-start | bytes 884744 | tf_op jit(solution)/shard_map/ppermute | solution.py:119
  323.1 6.8 %collective-permute-start.28 = (bf16[1,1,1,2,1,24,512]{6,5,4,3,2,1,0:T(8,128)(2,1)S(1)}, bf16[1,1,1,2,1,24,512]{6,5,4,3,2,1,0:T(8,128)(2,1)S(1)}, u32[]{:S(2)}, u32[]{:S(2)}) collective-permute-start(bf16[1,1,1,2,1,24,512]{6,5,4,3,2,1,0:T(8,128)(2,1)S(1)} %dynamic-slice_convert_fusion.24), channel_id=1, source_target_pairs={{0,1},{1,0},{2,3},{3,2},{4,5},{5,4},{6,7},{7,6},{8,9},{9,8},{10,11... | collective-permute-start | bytes 147464 | tf_op jit(solution)/shard_map/ppermute | solution.py:119
  328.2 30.0 %slice-start.5 = ((s8[9437184]{0:T(1024)(128)(4,1)}), s8[4194304]{0:T(1024)(128)(4,1)S(1)}, s32[]{:S(2)}) async-start(s8[9437184]{0:T(1024)(128)(4,1)} %bitcast.173), calls=%async_computation.9 | async-start | bytes 8388608
  328.3 5.2 %collective-permute-start.12 = (bf16[1,1,1,2,2,24,768]{6,5,4,3,2,1,0:T(8,128)(2,1)S(1)}, bf16[1,1,1,2,2,24,768]{6,5,4,3,2,1,0:T(8,128)(2,1)S(1)}, u32[]{:S(2)}, u32[]{:S(2)}) collective-permute-start(bf16[1,1,1,2,2,24,768]{6,5,4,3,2,1,0:T(8,128)(2,1)S(1)} %dynamic-slice_convert_fusion.18), channel_id=1, source_target_pairs={{0,16},{1,17},{2,18},{3,19},{4,20},{5,21},{6,22},{7,23},{8,24},{9,... | collective-permute-start | bytes 442376 | tf_op jit(solution)/shard_map/ppermute | solution.py:119
  333.6 24.6 %slice-start.6 = ((s8[9437184]{0:T(1024)(128)(4,1)}), s8[4194304]{0:T(1024)(128)(4,1)S(1)}, s32[]{:S(2)}) async-start(s8[9437184]{0:T(1024)(128)(4,1)} %bitcast.173), calls=%async_computation.10 | async-start | bytes 8388608
  333.6 6.5 %collective-permute-start.13 = (bf16[1,1,1,2,1,24,768]{6,5,4,3,2,1,0:T(8,128)(2,1)S(1)}, bf16[1,1,1,2,1,24,768]{6,5,4,3,2,1,0:T(8,128)(2,1)S(1)}, u32[]{:S(2)}, u32[]{:S(2)}) collective-permute-start(bf16[1,1,1,2,1,24,768]{6,5,4,3,2,1,0:T(8,128)(2,1)S(1)} %dynamic-slice_convert_fusion.22), channel_id=1, source_target_pairs={{0,1},{1,0},{2,3},{3,2},{4,5},{5,4},{6,7},{7,6},{8,9},{9,8},{10,11... | collective-permute-start | bytes 221192 | tf_op jit(solution)/shard_map/ppermute | solution.py:119
  336.7 21.4 %slice-start.7 = ((s8[9437184]{0:T(1024)(128)(4,1)}), s8[1048576]{0:T(1024)(128)(4,1)S(1)}, s32[]{:S(2)}) async-start(s8[9437184]{0:T(1024)(128)(4,1)} %bitcast.173), calls=%async_computation.11 | async-start | bytes 2097152
  336.9 19.4 %collective-permute-start.6 = (bf16[1,2,1,2,2,24,2304]{6,5,4,3,2,1,0:T(8,128)(2,1)S(1)}, bf16[1,2,1,2,2,24,2304]{6,5,4,3,2,1,0:T(8,128)(2,1)S(1)}, u32[]{:S(2)}, u32[]{:S(2)}) collective-permute-start(bf16[1,2,1,2,2,24,2304]{6,5,4,3,2,1,0:T(8,128)(2,1)S(1)} %dynamic-slice_convert_fusion.5), channel_id=1, source_target_pairs={{0,16},{1,17},{2,18},{3,19},{4,20},{5,21},{6,22},{7,23},{8,24},{9,... | collective-permute-start | bytes 2654216 | tf_op jit(solution)/shard_map/ppermute | solution.py:119
  338.4 4.7 %collective-permute-start.29 = (bf16[1,1,1,1,1,24,512]{6,5,4,3,2,1,0:T(8,128)(2,1)S(1)}, bf16[1,1,1,1,1,24,512]{6,5,4,3,2,1,0:T(8,128)(2,1)S(1)}, u32[]{:S(2)}, u32[]{:S(2)}) collective-permute-start(bf16[1,1,1,1,1,24,512]{6,5,4,3,2,1,0:T(8,128)(2,1)S(1)} %dynamic-slice_convert_fusion.27), channel_id=1, source_target_pairs={{0,2},{1,3},{2,0},{3,1},{4,6},{5,7},{6,4},{7,5},{8,10},{9,11},{10,... | collective-permute-start | bytes 73736 | tf_op jit(solution)/shard_map/ppermute | solution.py:119
  340.1 5.1 %collective-permute-start.14 = (bf16[1,1,1,1,1,24,768]{6,5,4,3,2,1,0:T(8,128)(2,1)S(1)}, bf16[1,1,1,1,1,24,768]{6,5,4,3,2,1,0:T(8,128)(2,1)S(1)}, u32[]{:S(2)}, u32[]{:S(2)}) collective-permute-start(bf16[1,1,1,1,1,24,768]{6,5,4,3,2,1,0:T(8,128)(2,1)S(1)} %dynamic-slice_convert_fusion.25), channel_id=1, source_target_pairs={{0,2},{1,3},{2,0},{3,1},{4,6},{5,7},{6,4},{7,5},{8,10},{9,11},{10,... | collective-permute-start | bytes 110600 | tf_op jit(solution)/shard_map/ppermute | solution.py:119
  356.4 11.7 %slice-start = ((s8[9437184]{0:T(1024)(128)(4,1)}), s8[4194304]{0:T(1024)(128)(4,1)S(1)}, s32[]{:S(2)}) async-start(s8[9437184]{0:T(1024)(128)(4,1)} %bitcast.164), calls=%async_computation.4 | async-start | bytes 8388608
  356.5 11.7 %slice-start.1 = ((s8[9437184]{0:T(1024)(128)(4,1)}), s8[4194304]{0:T(1024)(128)(4,1)S(1)}, s32[]{:S(2)}) async-start(s8[9437184]{0:T(1024)(128)(4,1)} %bitcast.164), calls=%async_computation.5 | async-start | bytes 8388608
  356.5 11.7 %slice-start.2 = ((s8[9437184]{0:T(1024)(128)(4,1)}), s8[1048576]{0:T(1024)(128)(4,1)S(1)}, s32[]{:S(2)}) async-start(s8[9437184]{0:T(1024)(128)(4,1)} %bitcast.164), calls=%async_computation.6 | async-start | bytes 2097152
  356.5 9.8 %collective-permute-start.7 = (bf16[1,2,1,2,1,24,2304]{6,5,4,3,2,1,0:T(8,128)(2,1)S(1)}, bf16[1,2,1,2,1,24,2304]{6,5,4,3,2,1,0:T(8,128)(2,1)S(1)}, u32[]{:S(2)}, u32[]{:S(2)}) collective-permute-start(bf16[1,2,1,2,1,24,2304]{6,5,4,3,2,1,0:T(8,128)(2,1)S(1)} %dynamic-slice_convert_fusion.9), channel_id=1, source_target_pairs={{0,1},{1,0},{2,3},{3,2},{4,5},{5,4},{6,7},{7,6},{8,9},{9,8},{10,11... | collective-permute-start | bytes 1327112 | tf_op jit(solution)/shard_map/ppermute | solution.py:119
  361.8 24.1 %collective-permute-start.16 = (bf16[1,2,1,2,2,24,3072]{6,5,4,3,2,1,0:T(8,128)(2,1)S(1)}, bf16[1,2,1,2,2,24,3072]{6,5,4,3,2,1,0:T(8,128)(2,1)S(1)}, u32[]{:S(2)}, u32[]{:S(2)}) collective-permute-start(bf16[1,2,1,2,2,24,3072]{6,5,4,3,2,1,0:T(8,128)(2,1)S(1)} %dynamic-slice_convert_fusion.4), channel_id=1, source_target_pairs={{0,16},{1,17},{2,18},{3,19},{4,20},{5,21},{6,22},{7,23},{8,24},{9,... | collective-permute-start | bytes 3538952 | tf_op jit(solution)/shard_map/ppermute | solution.py:119
  366.4 9.3 %collective-permute-start.8 = (bf16[1,2,1,1,1,24,2304]{6,5,4,3,2,1,0:T(8,128)(2,1)S(1)}, bf16[1,2,1,1,1,24,2304]{6,5,4,3,2,1,0:T(8,128)(2,1)S(1)}, u32[]{:S(2)}, u32[]{:S(2)}) collective-permute-start(bf16[1,2,1,1,1,24,2304]{6,5,4,3,2,1,0:T(8,128)(2,1)S(1)} %dynamic-slice_convert_fusion.14), channel_id=1, source_target_pairs={{0,2},{1,3},{2,0},{3,1},{4,6},{5,7},{6,4},{7,5},{8,10},{9,11},{10,... | collective-permute-start | bytes 663560 | tf_op jit(solution)/shard_map/ppermute | solution.py:119
  370.8 32.0 %collective-permute-start.21 = (bf16[2,1,1,2,2,96,768]{6,5,4,3,2,1,0:T(8,128)(2,1)S(1)}, bf16[2,1,1,2,2,96,768]{6,5,4,3,2,1,0:T(8,128)(2,1)S(1)}, u32[]{:S(2)}, u32[]{:S(2)}) collective-permute-start(bf16[2,1,1,2,2,96,768]{6,5,4,3,2,1,0:T(8,128)(2,1)S(1)} %dynamic-slice_convert_fusion.3), channel_id=1, source_target_pairs={{0,8},{1,9},{2,10},{3,11},{4,12},{5,13},{6,14},{7,15},{8,0},{9,1},... | collective-permute-start | bytes 3538952 | tf_op jit(solution)/shard_map/ppermute | solution.py:119
  375.8 26.3 %collective-permute-start.9 = (bf16[1,1,1,1,1,24,2304]{6,5,4,3,2,1,0:T(8,128)(2,1)S(1)}, bf16[1,1,1,1,1,24,2304]{6,5,4,3,2,1,0:T(8,128)(2,1)S(1)}, u32[]{:S(2)}, u32[]{:S(2)}) collective-permute-start(bf16[1,1,1,1,1,24,2304]{6,5,4,3,2,1,0:T(8,128)(2,1)S(1)} %dynamic-slice_convert_fusion.20), channel_id=1, source_target_pairs={{0,8},{1,9},{2,10},{3,11},{4,12},{5,13},{6,14},{7,15},{8,0},{9,1},... | collective-permute-start | bytes 331784 | tf_op jit(solution)/shard_map/ppermute | solution.py:119
  386.2 23.2 %collective-permute-start.17 = (bf16[1,1,1,2,2,24,3072]{6,5,4,3,2,1,0:T(8,128)(2,1)S(1)}, bf16[1,1,1,2,2,24,3072]{6,5,4,3,2,1,0:T(8,128)(2,1)}, u32[]{:S(2)}, u32[]{:S(2)}) collective-permute-start(bf16[1,1,1,2,2,24,3072]{6,5,4,3,2,1,0:T(8,128)(2,1)S(1)} %dynamic-slice_convert_fusion.7), channel_id=1, source_target_pairs={{0,8},{1,9},{2,10},{3,11},{4,12},{5,13},{6,14},{7,15},{8,0},{9,1},... | collective-permute-start | bytes 1769480 | tf_op jit(solution)/shard_map/ppermute | solution.py:119
  404.5 10.1 %collective-permute-start.22 = (bf16[1,1,1,2,2,96,768]{6,5,4,3,2,1,0:T(8,128)(2,1)S(1)}, bf16[1,1,1,2,2,96,768]{6,5,4,3,2,1,0:T(8,128)(2,1)}, u32[]{:S(2)}, u32[]{:S(2)}) collective-permute-start(bf16[1,1,1,2,2,96,768]{6,5,4,3,2,1,0:T(8,128)(2,1)S(1)} %dynamic-slice_convert_fusion.6), channel_id=1, source_target_pairs={{0,16},{1,17},{2,18},{3,19},{4,20},{5,21},{6,22},{7,23},{8,24},{9,... | collective-permute-start | bytes 1769480 | tf_op jit(solution)/shard_map/ppermute | solution.py:119
  410.8 9.7 %collective-permute-start.18 = (bf16[1,1,1,2,1,24,3072]{6,5,4,3,2,1,0:T(8,128)(2,1)S(1)}, bf16[1,1,1,2,1,24,3072]{6,5,4,3,2,1,0:T(8,128)(2,1)S(1)}, u32[]{:S(2)}, u32[]{:S(2)}) collective-permute-start(bf16[1,1,1,2,1,24,3072]{6,5,4,3,2,1,0:T(8,128)(2,1)S(1)} %dynamic-slice_convert_fusion.12), channel_id=1, source_target_pairs={{0,1},{1,0},{2,3},{3,2},{4,5},{5,4},{6,7},{7,6},{8,9},{9,8},{10,11... | collective-permute-start | bytes 884744 | tf_op jit(solution)/shard_map/ppermute | solution.py:119
  415.8 7.9 %collective-permute-start.23 = (bf16[1,1,1,2,1,96,768]{6,5,4,3,2,1,0:T(8,128)(2,1)S(1)}, bf16[1,1,1,2,1,96,768]{6,5,4,3,2,1,0:T(8,128)(2,1)S(1)}, u32[]{:S(2)}, u32[]{:S(2)}) collective-permute-start(bf16[1,1,1,2,1,96,768]{6,5,4,3,2,1,0:T(8,128)(2,1)S(1)} %dynamic-slice_convert_fusion.11), channel_id=1, source_target_pairs={{0,1},{1,0},{2,3},{3,2},{4,5},{5,4},{6,7},{7,6},{8,9},{9,8},{10,11... | collective-permute-start | bytes 884744 | tf_op jit(solution)/shard_map/ppermute | solution.py:119
  420.6 7.7 %collective-permute-start.19 = (bf16[1,1,1,1,1,24,3072]{6,5,4,3,2,1,0:T(8,128)(2,1)S(1)}, bf16[1,1,1,1,1,24,3072]{6,5,4,3,2,1,0:T(8,128)(2,1)S(1)}, u32[]{:S(2)}, u32[]{:S(2)}) collective-permute-start(bf16[1,1,1,1,1,24,3072]{6,5,4,3,2,1,0:T(8,128)(2,1)S(1)} %dynamic-slice_convert_fusion.17), channel_id=1, source_target_pairs={{0,2},{1,3},{2,0},{3,1},{4,6},{5,7},{6,4},{7,5},{8,10},{9,11},{10,... | collective-permute-start | bytes 442376 | tf_op jit(solution)/shard_map/ppermute | solution.py:119
  423.8 7.7 %collective-permute-start.24 = (bf16[1,1,1,1,1,96,768]{6,5,4,3,2,1,0:T(8,128)(2,1)S(1)}, bf16[1,1,1,1,1,96,768]{6,5,4,3,2,1,0:T(8,128)(2,1)S(1)}, u32[]{:S(2)}, u32[]{:S(2)}) collective-permute-start(bf16[1,1,1,1,1,96,768]{6,5,4,3,2,1,0:T(8,128)(2,1)S(1)} %dynamic-slice_convert_fusion.16), channel_id=1, source_target_pairs={{0,2},{1,3},{2,0},{3,1},{4,6},{5,7},{6,4},{7,5},{8,10},{9,11},{10,... | collective-permute-start | bytes 442376 | tf_op jit(solution)/shard_map/ppermute | solution.py:119
  (44 other events, 208.1 us)
Sparse Core Ops, SparseCore 0:
  11.4 108.0 all-gather.2
  122.2 62.8 all-gather.4

commit v7 on v6

--- a/solution.py
+++ b/solution.py
@@ -121,6 +121,20 @@
         )
         current = keep + moved.astype(jnp.float32)
     return current.reshape((rows,) + grad.shape[1:])
+
+
+def ag_chain(block, n_bits, order):
+    me = lax.axis_index(AX)
+    n_dev = 2 ** n_bits
+    current = block.reshape((1,) * n_bits + block.shape)
+    for bit in reversed(order):
+        axis = n_bits - 1 - bit
+        mine = ((me >> bit) & 1) == 1
+        moved = lax.ppermute(current, AX, [(i, i ^ (1 << bit)) for i in range(n_dev)])
+        low = jnp.where(mine, moved, current)
+        high = jnp.where(mine, current, moved)
+        current = jnp.concatenate([low, high], axis=axis)
+    return current.reshape((n_dev * block.shape[0],) + block.shape[1:])
 
 
 def pack_rows(arrays, n_dev, dtype):
@@ -225,7 +239,7 @@
         packed_small, small_widths = pack_rows(
             [a.reshape(1, -1) for a in small], 1, jnp.bfloat16
         )
-        gathered_small = lax.all_gather(packed_small, AX, axis=0, tiled=True)
+        gathered_small = ag_chain(packed_small, n_bits, orders["x"])
         (wave_full, gain_one, shift_one, gain_two, shift_two, inner_bias, outer_bias,
          dec_shift, mask_full) = unpack_rows(gathered_small, small, small_widths, 1, n_dev)
         wide = (qkv_weight, out_weight, mlp_in, dec_weight)

time: 443 us -> 435 us (0.982)
  blocking collectives: 130 us -> 0 us
  waiting for transfers between devices: 88.8 us -> 204 us
  starting transfers between devices: 42.2 us -> 48 us
    all_gather x1 -> x0, blocking collectives: 130 us -> none  [local(): gathered_small = lax.all_gather(packed_small, AX, axis=0, tiled=True)]
    ppermute x0 -> x5, waiting for transfers between devices: none -> 54 us  [ag_chain(): moved = lax.ppermute(current, AX, [(i, i ^ 1 << bit) for i in range(n_dev)])]
    all_gather x1, waiting for transfers between devices: 0.01 us -> 29.5 us  [local(): outer_full = lax.all_gather(mlp_out, AX, axis=0, tiled=True)]
    all_gather x1, waiting for transfers between devices: 0.01 us -> 28.4 us  [local(): lax.all_gather(jnp.concatenate(wide, axis=1), AX, axis=0, tiled=True)]
    ppermute x0 -> x5, starting transfers between devices: none -> 9.27 us  [ag_chain(): moved = lax.ppermute(current, AX, [(i, i ^ 1 << bit) for i in range(n_dev)])]
    unnamed x127 -> x109, local copies, waits for them, and re-layouts: 12.1 us -> 12.8 us
  transfers between devices with their start and end apart: 34 -> 39, of which waited for: 18 -> 25; matrix products, arithmetic and copies ran while one was open for 22% -> 23% of each run, Pallas kernels for 0% -> 0%
where the time goes in v7:
time: 435 us; the launch traced here: 431 us
  waiting for transfers between devices  204 us (47%)
  matrix products  67.9 us (16%)
  local copies, waits for them, and re-layouts  62.2 us (14%)
  starting transfers between devices  48 us (11%)
  other arithmetic  33.7 us (8%)
  between operations  15.7 us (4%)
    ppermute x30, waiting for transfers between devices, rs_chain(): lax.ppermute(send.astype(jnp.bfloat16), AX, [(i, i ^ 1 << bit) for i in r...  88.1 us
    ppermute x5, waiting for transfers between devices, ag_chain(): moved = lax.ppermute(current, AX, [(i, i ^ 1 << bit) for i in range(n_dev)])  54 us
    ppermute x30, starting transfers between devices, rs_chain(): lax.ppermute(send.astype(jnp.bfloat16), AX, [(i, i ^ 1 << bit) for i in r...  31 us
    all_gather x1, waiting for transfers between devices, local(): outer_full = lax.all_gather(mlp_out, AX, axis=0, tiled=True)  29.5 us
    all_gather x1, waiting for transfers between devices, local(): lax.all_gather(jnp.concatenate(wide, axis=1), AX, axis=0, tiled=True)  28.4 us
    dot_general x5, matrix products, outer_cols(): lax.dot_general(left_op, right_op, (((1,), (1,)), ((), ())), preferred_el...  22 us
    dot_general x5, matrix products, inner_rows(): lax.dot_general(left_op, right_op, (((0,), (0,)), ((), ())), preferred_el...  16 us
    dot_general x5, matrix products, product(): return jnp.dot(left_op, right_op, preferred_element_type=jnp.float32)  15.1 us
  transfers between devices with their start and end apart: 39, of which 25 were waited for; matrix products, arithmetic and copies ran while one was open for 23% of the time, Pallas kernels for 0%

profile of v7, /device:TPU:0, one launch (start us, length us, event | category | flops | bytes accessed | tf_op | source)
XLA Modules:
  0.0 431.2 jit_solution(8293834177028307392)
XLA Ops:
  10.7 4.1 collective-permute-start
  14.8 4.0 all-to-all-start.1
  20.7 48.3 %collective-permute-done.1 = bf16[1,1,1,2,1,1,8,512]{7,6,4,3,2,1,0,5:T(8,128)(2,1)S(1)} collective-permute-done((bf16[1,1,1,2,1,1,8,512]{7,6,4,3,2,1,0,5:T(8,128)(2,1)S(1)}, bf16[1,1,1,2,1,1,8,512]{7,6,4,3,2,1,0,5:T(8,128)(2,1)S(1)}, u32[]{:S(2)}, u32[]{:S(2)}) %collective-permute-start.1) | collective-permute-done | bytes 16416 | tf_op jit(solution)/shard_map/ppermute | solution.py:133
  70.6 2.3 collective-permute-done.2
  74.9 2.4 collective-permute-done.3
  82.3 3.7 all-to-all-done.1
  92.0 28.4 %all-gather.3.cloned.1.call-done = bf16[768,6656]{1,0:T(8,128)(2,1)} async-done(((bf16[24,6656]{1,0:T(8,128)(2,1)}), bf16[768,6656]{1,0:T(8,128)(2,1)}) %all-gather.3.cloned.1.call-update) | async-done | bytes 10223632 | tf_op jit(solution)/shard_map/all_gather | solution.py:247
  120.4 4.0 convolution_convert_fusion
  125.4 2.3 copy.124
  127.7 2.9 reshape.332
  135.2 2.2 reshape.333
  138.5 4.8 %fusion.78 = (f32[2,12,256]{2,1,0:T(8,128)S(1)}, f32[2,12,256,256]{2,3,1,0:T(8,128)S(1)}) fusion(f32[2,12,256,256]{2,3,1,0:T(8,128)S(1)} %fusion.58), kind=kOutput, calls=%fused_computation.209 | output fusion | flops 6291711 | bytes 12607488 | tf_op jit(solution)/shard_map/sub | solution.py:167
  143.9 2.5 copy-done
  150.2 5.6 %multiply_convert_fusion.1 = (bf16[512,3072]{1,0:T(8,128)(2,1)}, f32[512,3072]{1,0:T(8,128)}) fusion(f32[3072]{0:T(1024)S(1)} %reshape.372, bf16[768,6656]{1,0:T(8,128)(2,1)S(1)} %bitcast.207, f32[512,768]{1,0:T(8,128)S(1)} %get-tuple-element.60, f32[768]{0:T(1024)S(1)} %reshape.371, f32[768]{0:T(1024)S(1)} %reshape.370, f32[512]{0:T(512)S(1)} %add_rsqrt_fusion, ...), kind=kOutput, calls=%fused_computation.11 | convolution fusion | flops 2427322368 | bytes 15753216 | tf_op jit(solution)/shard_map/dot_general | solution.py:21
  155.8 29.5 %all-gather.5.cloned.1.call-done = bf16[3072,768]{1,0:T(8,128)(2,1)} async-done(((bf16[96,768]{1,0:T(8,128)(2,1)}), bf16[3072,768]{1,0:T(8,128)(2,1)}) %all-gather.5.cloned.1.call-update) | async-done | bytes 4718608 | tf_op jit(solution)/shard_map/all_gather | solution.py:254
  185.3 7.6 %convert_reduce_fusion = (f32[3072]{0:T(1024)S(1)}, bf16[512,3072]{1,0:T(8,128)(2,1)S(1)}) fusion(f32[512,3072]{1,0:T(8,128)} %get-tuple-element.62, f32[3072]{0:T(1024)S(1)} %reshape.372, bf16[3072,768]{1,0:T(8,128)(2,1)} %all-gather.5.cloned.1.call-done, f32[512,768]{1,0:T(8,128)S(1)} %fusion.49), kind=kOutput, calls=%fused_computation.8 | convolution fusion | flops 2436756480 | bytes 15753216 | tf_op jit(solution)/shard_map/dot_general | solution.py:31
  193.0 6.5 %multiply_reduce_fusion.2 = (f32[768]{0:T(1024)S(1)}, f32[512]{0:T(512)S(1)}, f32[512]{0:T(512)S(1)}, f32[768]{0:T(1024)S(1)}, f32[512,768]{1,0:T(8,128)S(1)}) fusion(f32[512,768]{1,0:T(8,128)S(1)} %get-tuple-element.60, f32[512]{0:T(512)S(1)} %add_rsqrt_fusion, f32[512]{0:T(512)S(1)} %broadcast_multiply_fusion.4, f32[768]{0:T(1024)S(1)} %reshape.370, ...), kind=kOutput, calls=%fused_computation.51 | convolution fusion | flops 2419455488 | bytes 11027456 | tf_op jit(solution)/shard_map/dot_general | solution.py:31
  204.7 4.3 fusion.33
  209.4 3.8 multiply_reduce_fusion
  213.2 4.3 multiply_convert_fusion
  220.3 5.7 %fusion.75 = f32[768,3072]{1,0:T(8,128)} fusion(bf16[512,3072]{1,0:T(8,128)(2,1)S(1)} %copy-done.35, f32[512,768]{1,0:T(8,128)S(1)} %copy-done.6, f32[768]{0:T(1024)S(1)} %reshape.371, f32[768]{0:T(1024)S(1)} %reshape.370, f32[512]{0:T(512)S(1)} %add_rsqrt_fusion, f32[512]{0:T(512)S(1)} %broadcast_multiply_fusion.4), kind=kOutput, calls=%fused_computation.206 | convolution fusion | flops 2417885184 | bytes 14166016 | tf_op jit(solution)/shard_map/dot_general | solution.py:25
  226.0 5.0 %fusion.70 = f32[3072,768]{1,0:T(8,128)} fusion(bf16[512,3072]{1,0:T(8,128)(2,1)S(1)} %copy-done.22, f32[512,768]{1,0:T(8,128)S(1)} %copy-done.4), kind=kOutput, calls=%fused_computation.201 | convolution fusion | flops 2416312320 | bytes 14155776 | tf_op jit(solution)/shard_map/dot_general | solution.py:25
  231.1 2.6 add_convert_fusion
  237.0 3.5 copy.133
  240.4 3.7 all-to-all-start
  250.6 5.2 %multiply_reduce_fusion.3 = (f32[768]{0:T(1024)S(1)}, f32[512]{0:T(512)S(1)}, f32[512]{0:T(512)S(1)}, f32[768]{0:T(1024)S(1)}, f32[512,768]{1,0:T(8,128)S(1)}) fusion(f32[2,256,768]{2,1,0:T(8,128)S(1)} %copy-done.2, f32[512]{0:T(512)S(1)} %bitcast.215, f32[512]{0:T(512)S(1)} %bitcast.218, f32[768]{0:T(1024)S(1)} %reshape.368, ...), kind=kOutput, calls=%fused_computation.52 | convolution fusion | flops 1822553600 | bytes 9061376 | tf_op jit(solution)/shard_map/dot_general | solution.py:31
  259.5 3.6 fusion.18
  270.1 4.1 dynamic-slice_convert_fusion.1
  275.8 4.1 dynamic-slice_convert_fusion
  280.5 3.3 collective-permute-start.8
  284.7 8.8 %collective-permute-done.8 = bf16[1,2,1,1,1,1,8,512]{7,6,5,4,3,2,1,0:T(8,128)(2,1)S(1)} collective-permute-done((bf16[1,2,1,1,1,1,8,512]{7,6,5,4,3,2,1,0:T(8,128)(2,1)S(1)}, bf16[1,2,1,1,1,1,8,512]{7,6,5,4,3,2,1,0:T(8,128)(2,1)S(1)}, u32[]{:S(2)}, u32[]{:S(2)}) %collective-permute-start.8) | collective-permute-done | bytes 16416 | tf_op jit(solution)/shard_map/ppermute | solution.py:119
  303.9 5.2 %collective-permute-done.31 = bf16[1,2,1,2,2,24,512]{6,5,4,3,2,1,0:T(8,128)(2,1)S(1)} collective-permute-done((bf16[1,2,1,2,2,24,512]{6,5,4,3,2,1,0:T(8,128)(2,1)S(1)}, bf16[1,2,1,2,2,24,512]{6,5,4,3,2,1,0:T(8,128)(2,1)S(1)}, u32[]{:S(2)}, u32[]{:S(2)}) %collective-permute-start.31) | collective-permute-done | bytes 196640 | tf_op jit(solution)/shard_map/ppermute | solution.py:119
  311.6 3.4 collective-permute-done.32
  315.1 5.0 %collective-permute-done.16 = bf16[2,1,1,2,2,24,768]{6,5,4,3,2,1,0:T(8,128)(2,1)S(1)} collective-permute-done((bf16[2,1,1,2,2,24,768]{6,5,4,3,2,1,0:T(8,128)(2,1)S(1)}, bf16[2,1,1,2,2,24,768]{6,5,4,3,2,1,0:T(8,128)(2,1)S(1)}, u32[]{:S(2)}, u32[]{:S(2)}) %collective-permute-start.16) | collective-permute-done | bytes 294944 | tf_op jit(solution)/shard_map/ppermute | solution.py:119
  321.8 3.6 collective-permute-done.17
  325.6 3.1 convert_add_fusion.2
  337.8 10.4 %collective-permute-done.11 = bf16[1,2,1,2,2,24,2304]{6,5,4,3,2,1,0:T(8,128)(2,1)S(1)} collective-permute-done((bf16[1,2,1,2,2,24,2304]{6,5,4,3,2,1,0:T(8,128)(2,1)S(1)}, bf16[1,2,1,2,2,24,2304]{6,5,4,3,2,1,0:T(8,128)(2,1)S(1)}, u32[]{:S(2)}, u32[]{:S(2)}) %collective-permute-start.11) | collective-permute-done | bytes 884768 | tf_op jit(solution)/shard_map/ppermute | solution.py:119
  350.1 3.4 convert_add_fusion.1
  355.2 3.0 collective-permute-done.12
  360.1 2.4 convert_add_fusion
  362.9 4.7 %collective-permute-done.13 = bf16[1,2,1,1,1,24,2304]{6,5,4,3,2,1,0:T(8,128)(2,1)S(1)} collective-permute-done((bf16[1,2,1,1,1,24,2304]{6,5,4,3,2,1,0:T(8,128)(2,1)S(1)}, bf16[1,2,1,1,1,24,2304]{6,5,4,3,2,1,0:T(8,128)(2,1)S(1)}, u32[]{:S(2)}, u32[]{:S(2)}) %collective-permute-start.13) | collective-permute-done | bytes 221216 | tf_op jit(solution)/shard_map/ppermute | solution.py:119
  368.7 9.1 %collective-permute-done.21 = bf16[1,2,1,2,2,24,3072]{6,5,4,3,2,1,0:T(8,128)(2,1)S(1)} collective-permute-done((bf16[1,2,1,2,2,24,3072]{6,5,4,3,2,1,0:T(8,128)(2,1)S(1)}, bf16[1,2,1,2,2,24,3072]{6,5,4,3,2,1,0:T(8,128)(2,1)S(1)}, u32[]{:S(2)}, u32[]{:S(2)}) %collective-permute-start.21) | collective-permute-done | bytes 1179680 | tf_op jit(solution)/shard_map/ppermute | solution.py:119
  379.0 15.0 %collective-permute-done.14 = bf16[1,1,1,1,1,24,2304]{6,5,4,3,2,1,0:T(8,128)(2,1)S(1)} collective-permute-done((bf16[1,1,1,1,1,24,2304]{6,5,4,3,2,1,0:T(8,128)(2,1)S(1)}, bf16[1,1,1,1,1,24,2304]{6,5,4,3,2,1,0:T(8,128)(2,1)S(1)}, u32[]{:S(2)}, u32[]{:S(2)}) %collective-permute-start.14) | collective-permute-done | bytes 110624 | tf_op jit(solution)/shard_map/ppermute | solution.py:119
  397.9 3.4 copy.134
  403.2 3.2 collective-permute-done.27
  407.7 4.7 %collective-permute-done.23 = bf16[1,1,1,2,1,24,3072]{6,5,4,3,2,1,0:T(8,128)(2,1)S(1)} collective-permute-done((bf16[1,1,1,2,1,24,3072]{6,5,4,3,2,1,0:T(8,128)(2,1)S(1)}, bf16[1,1,1,2,1,24,3072]{6,5,4,3,2,1,0:T(8,128)(2,1)S(1)}, u32[]{:S(2)}, u32[]{:S(2)}) %collective-permute-start.23) | collective-permute-done | bytes 294944 | tf_op jit(solution)/shard_map/ppermute | solution.py:119
  417.2 2.9 collective-permute-done.24
  420.9 2.4 collective-permute-done.29
  (317 shorter events, 107.6 us)
Async XLA Ops:
  7.2 113.2 %all-gather.3.cloned.1.call-start = ((), (), s32[]{:S(2)}) async-start(), calls=%async_computation.2 | async-start | bytes 10543104 | tf_op jit(solution)/shard_map/all_gather | solution.py:247
  10.7 64.0 %copy-start.32 = (s32[2,256]{1,0:T(2,128)S(1)}, s32[2,256]{1,0:T(2,128)}, u32[]{:S(2)}) copy-start(s32[2,256]{1,0:T(2,128)} %param.20) | copy-start | bytes 6148
  10.7 66.8 %copy-start.33 = (s32[2,13]{1,0:T(2,128)S(1)}, s32[2,13]{1,0:T(2,128)}, u32[]{:S(2)}) copy-start(s32[2,13]{1,0:T(2,128)} %param.19) | copy-start | bytes 316
  10.7 8.2 %collective-permute-start = (bf16[1,1,1,1,1,1,8,512]{7,6,4,3,2,1,0,5:T(8,128)(2,1)S(1)}, bf16[1,1,1,1,1,1,8,512]{7,6,4,3,2,1,0,5:T(8,128)(2,1)S(1)}, u32[]{:S(2)}, u32[]{:S(2)}) collective-permute-start(bf16[1,1,1,1,1,1,8,512]{7,6,4,3,2,1,0,5:T(8,128)(2,1)S(1)} %bitcast.213), channel_id=1, source_target_pairs={{0,2},{1,3},{2,0},{3,1},{4,6},{5,7},{6,4},{7,5},{8,10},{9,11},{10,... | collective-permute-start | bytes 24584 | tf_op jit(solution)/shard_map/ppermute | solution.py:133
  14.8 71.2 %all-to-all-start.1 = ((bf16[64,32,512]{2,1,0:T(8,128)(2,1)}), bf16[64,32,512]{2,1,0:T(8,128)(2,1)}, u32[]{:S(2)}, u32[]{:S(2)}) async-start(bf16[64,32,512]{2,1,0:T(8,128)(2,1)} %param.35), calls=%async_computation.1 | async-start | bytes 4194304 | tf_op jit(solution)/shard_map/all_to_all | solution.py:304
  18.8 60.7 %copy-start.23 = (bf16[2,256,768]{2,1,0:T(8,128)(2,1)S(1)}, bf16[2,256,768]{2,1,0:T(8,128)(2,1)}, u32[]{:S(2)}) copy-start(bf16[2,256,768]{2,1,0:T(8,128)(2,1)} %param.18) | copy-start | bytes 2359300
  18.8 166.5 %all-gather.5.cloned.1.call-start = ((), (), s32[]{:S(2)}) async-start(), calls=%async_computation.3 | async-start | bytes 4866048 | tf_op jit(solution)/shard_map/all_gather | solution.py:254
  18.9 50.1 %collective-permute-start.1 = (bf16[1,1,1,2,1,1,8,512]{7,6,4,3,2,1,0,5:T(8,128)(2,1)S(1)}, bf16[1,1,1,2,1,1,8,512]{7,6,4,3,2,1,0,5:T(8,128)(2,1)S(1)}, u32[]{:S(2)}, u32[]{:S(2)}) collective-permute-start(bf16[1,1,1,2,1,1,8,512]{7,6,4,3,2,1,0,5:T(8,128)(2,1)S(1)} %pad_maximum_fusion.8), channel_id=1, source_target_pairs={{0,1},{1,0},{2,3},{3,2},{4,5},{5,4},{6,7},{7,6},{8,9},{9,8},{10,11... | collective-permute-start | bytes 49160 | tf_op jit(solution)/shard_map/ppermute | solution.py:133
  69.0 4.0 collective-permute-start.2
  73.0 4.3 %collective-permute-start.3 = (bf16[2,1,1,2,2,1,8,512]{7,6,4,3,2,1,0,5:T(8,128)(2,1)S(1)}, bf16[2,1,1,2,2,1,8,512]{7,6,4,3,2,1,0,5:T(8,128)(2,1)S(1)}, u32[]{:S(2)}, u32[]{:S(2)}) collective-permute-start(bf16[2,1,1,2,2,1,8,512]{7,6,4,3,2,1,0,5:T(8,128)(2,1)S(1)} %pad_maximum_fusion.6), channel_id=1, source_target_pairs={{0,8},{1,9},{2,10},{3,11},{4,12},{5,13},{6,14},{7,15},{8,0},{9,1},... | collective-permute-start | bytes 196616 | tf_op jit(solution)/shard_map/ppermute | solution.py:133
  77.4 1.4 collective-permute-start.4
  80.1 67.4 %copy-start.1 = (f32[2,256,768]{2,1,0:T(8,128)}, f32[2,256,768]{2,1,0:T(8,128)S(1)}, u32[]{:S(2)}) copy-start(f32[2,256,768]{2,1,0:T(8,128)S(1)} %get-tuple-element.30) | copy-start | bytes 4718596
  149.3 50.2 %copy-start.5 = (f32[512,768]{1,0:T(8,128)}, f32[512,768]{1,0:T(8,128)S(1)}, u32[]{:S(2)}) copy-start(f32[512,768]{1,0:T(8,128)S(1)} %get-tuple-element.60) | copy-start | bytes 4718596
  150.2 49.3 %copy-start.3 = (f32[512,768]{1,0:T(8,128)}, f32[512,768]{1,0:T(8,128)S(1)}, u32[]{:S(2)}) copy-start(f32[512,768]{1,0:T(8,128)S(1)} %fusion.49) | copy-start | bytes 4718596
  240.4 157.5 %all-to-all-start = ((bf16[2,1024,512]{2,0,1:T(2,128)(2,1)}), bf16[2,1024,512]{2,0,1:T(2,128)(2,1)}, u32[]{:S(2)}, u32[]{:S(2)}) async-start(bf16[2,1024,512]{2,0,1:T(2,128)(2,1)} %copy.133), calls=%async_computation | async-start | bytes 4194304 | tf_op jit(solution)/shard_map/all_to_all | solution.py:303
  259.3 9.0 %collective-permute-start.5 = (bf16[2,2,1,2,2,1,8,512]{7,6,5,4,3,2,1,0:T(8,128)(2,1)S(1)}, bf16[2,2,1,2,2,1,8,512]{7,6,5,4,3,2,1,0:T(8,128)(2,1)S(1)}, u32[]{:S(2)}, u32[]{:S(2)}) collective-permute-start(bf16[2,2,1,2,2,1,8,512]{7,6,5,4,3,2,1,0:T(8,128)(2,1)S(1)} %dynamic-slice_convert_fusion.19), channel_id=1, source_target_pairs={{0,4},{1,5},{2,6},{3,7},{4,0},{5,1},{6,2},{7,3},{8,12},{9,13},{10,... | collective-permute-start | bytes 393224 | tf_op jit(solution)/shard_map/ppermute | solution.py:119
  264.5 61.1 %collective-permute-start.10 = (bf16[2,2,1,2,2,24,2304]{6,5,4,3,2,1,0:T(8,128)(2,1)}, bf16[2,2,1,2,2,24,2304]{6,5,4,3,2,1,0:T(8,128)(2,1)}, u32[]{:S(2)}, u32[]{:S(2)}) collective-permute-start(bf16[2,2,1,2,2,24,2304]{6,5,4,3,2,1,0:T(8,128)(2,1)} %dynamic-slice_convert_fusion.2), channel_id=1, source_target_pairs={{0,4},{1,5},{2,6},{3,7},{4,0},{5,1},{6,2},{7,3},{8,12},{9,13},{10,... | collective-permute-start | bytes 5308424 | tf_op jit(solution)/shard_map/ppermute | solution.py:119
  267.8 42.7 %collective-permute-start.15 = (bf16[2,2,1,2,2,24,768]{6,5,4,3,2,1,0:T(8,128)(2,1)S(1)}, bf16[2,2,1,2,2,24,768]{6,5,4,3,2,1,0:T(8,128)(2,1)S(1)}, u32[]{:S(2)}, u32[]{:S(2)}) collective-permute-start(bf16[2,2,1,2,2,24,768]{6,5,4,3,2,1,0:T(8,128)(2,1)S(1)} %dynamic-slice_convert_fusion.8), channel_id=1, source_target_pairs={{0,4},{1,5},{2,6},{3,7},{4,0},{5,1},{6,2},{7,3},{8,12},{9,13},{10,... | collective-permute-start | bytes 1769480 | tf_op jit(solution)/shard_map/ppermute | solution.py:119
  268.5 5.7 %collective-permute-start.6 = (bf16[1,2,1,2,2,1,8,512]{7,6,5,4,3,2,1,0:T(8,128)(2,1)S(1)}, bf16[1,2,1,2,2,1,8,512]{7,6,5,4,3,2,1,0:T(8,128)(2,1)S(1)}, u32[]{:S(2)}, u32[]{:S(2)}) collective-permute-start(bf16[1,2,1,2,2,1,8,512]{7,6,5,4,3,2,1,0:T(8,128)(2,1)S(1)} %dynamic-slice_convert_fusion.23), channel_id=1, source_target_pairs={{0,16},{1,17},{2,18},{3,19},{4,20},{5,21},{6,22},{7,23},{8,24},{9,... | collective-permute-start | bytes 196616 | tf_op jit(solution)/shard_map/ppermute | solution.py:119
  274.2 75.9 %collective-permute-start.20 = (bf16[2,2,1,2,2,24,3072]{6,5,4,3,2,1,0:T(8,128)(2,1)}, bf16[2,2,1,2,2,24,3072]{6,5,4,3,2,1,0:T(8,128)(2,1)}, u32[]{:S(2)}, u32[]{:S(2)}) collective-permute-start(bf16[2,2,1,2,2,24,3072]{6,5,4,3,2,1,0:T(8,128)(2,1)} %dynamic-slice_convert_fusion.1), channel_id=1, source_target_pairs={{0,4},{1,5},{2,6},{3,7},{4,0},{5,1},{6,2},{7,3},{8,12},{9,13},{10,... | collective-permute-start | bytes 7077896 | tf_op jit(solution)/shard_map/ppermute | solution.py:119
  274.2 6.2 %collective-permute-start.7 = (bf16[1,2,1,2,1,1,8,512]{7,6,5,4,3,2,1,0:T(8,128)(2,1)S(1)}, bf16[1,2,1,2,1,1,8,512]{7,6,5,4,3,2,1,0:T(8,128)(2,1)S(1)}, u32[]{:S(2)}, u32[]{:S(2)}) collective-permute-start(bf16[1,2,1,2,1,1,8,512]{7,6,5,4,3,2,1,0:T(8,128)(2,1)S(1)} %dynamic-slice_convert_fusion.26), channel_id=1, source_target_pairs={{0,1},{1,0},{2,3},{3,2},{4,5},{5,4},{6,7},{7,6},{8,9},{9,8},{10,11... | collective-permute-start | bytes 98312 | tf_op jit(solution)/shard_map/ppermute | solution.py:119
  279.9 80.2 %collective-permute-start.25 = (bf16[2,2,1,2,2,96,768]{6,5,4,3,2,1,0:T(8,128)(2,1)}, bf16[2,2,1,2,2,96,768]{6,5,4,3,2,1,0:T(8,128)(2,1)}, u32[]{:S(2)}, u32[]{:S(2)}) collective-permute-start(bf16[2,2,1,2,2,96,768]{6,5,4,3,2,1,0:T(8,128)(2,1)} %dynamic-slice_convert_fusion), channel_id=1, source_target_pairs={{0,4},{1,5},{2,6},{3,7},{4,0},{5,1},{6,2},{7,3},{8,12},{9,13},{10,... | collective-permute-start | bytes 7077896 | tf_op jit(solution)/shard_map/ppermute | solution.py:119
  280.5 12.9 %collective-permute-start.8 = (bf16[1,2,1,1,1,1,8,512]{7,6,5,4,3,2,1,0:T(8,128)(2,1)S(1)}, bf16[1,2,1,1,1,1,8,512]{7,6,5,4,3,2,1,0:T(8,128)(2,1)S(1)}, u32[]{:S(2)}, u32[]{:S(2)}) collective-permute-start(bf16[1,2,1,1,1,1,8,512]{7,6,5,4,3,2,1,0:T(8,128)(2,1)S(1)} %dynamic-slice_convert_fusion.28), channel_id=1, source_target_pairs={{0,2},{1,3},{2,0},{3,1},{4,6},{5,7},{6,4},{7,5},{8,10},{9,11},{10,... | collective-permute-start | bytes 49160 | tf_op jit(solution)/shard_map/ppermute | solution.py:119
  284.6 25.9 %copy-start.12 = (f32[2,2,2,2,2,24,768]{6,5,4,3,2,1,0:T(8,128)S(1)}, f32[2,2,2,2,2,24,768]{6,5,4,3,2,1,0:T(8,128)}, u32[]{:S(2)}) copy-start(f32[2,2,2,2,2,24,768]{6,5,4,3,2,1,0:T(8,128)} %copy-done.11) | copy-start | bytes 7077892
  293.4 3.7 collective-permute-start.9
  297.1 3.2 collective-permute-start.30
  301.7 7.4 %collective-permute-start.31 = (bf16[1,2,1,2,2,24,512]{6,5,4,3,2,1,0:T(8,128)(2,1)S(1)}, bf16[1,2,1,2,2,24,512]{6,5,4,3,2,1,0:T(8,128)(2,1)S(1)}, u32[]{:S(2)}, u32[]{:S(2)}) collective-permute-start(bf16[1,2,1,2,2,24,512]{6,5,4,3,2,1,0:T(8,128)(2,1)S(1)} %dynamic-slice_convert_fusion.15), channel_id=1, source_target_pairs={{0,16},{1,17},{2,18},{3,19},{4,20},{5,21},{6,22},{7,23},{8,24},{9,... | collective-permute-start | bytes 589832 | tf_op jit(solution)/shard_map/ppermute | solution.py:119
  309.2 5.7 %collective-permute-start.32 = (bf16[1,1,1,2,2,24,512]{6,5,4,3,2,1,0:T(8,128)(2,1)S(1)}, bf16[1,1,1,2,2,24,512]{6,5,4,3,2,1,0:T(8,128)(2,1)S(1)}, u32[]{:S(2)}, u32[]{:S(2)}) collective-permute-start(bf16[1,1,1,2,2,24,512]{6,5,4,3,2,1,0:T(8,128)(2,1)S(1)} %dynamic-slice_convert_fusion.21), channel_id=1, source_target_pairs={{0,8},{1,9},{2,10},{3,11},{4,12},{5,13},{6,14},{7,15},{8,0},{9,1},... | collective-permute-start | bytes 294920 | tf_op jit(solution)/shard_map/ppermute | solution.py:119
  310.7 9.4 %collective-permute-start.16 = (bf16[2,1,1,2,2,24,768]{6,5,4,3,2,1,0:T(8,128)(2,1)S(1)}, bf16[2,1,1,2,2,24,768]{6,5,4,3,2,1,0:T(8,128)(2,1)S(1)}, u32[]{:S(2)}, u32[]{:S(2)}) collective-permute-start(bf16[2,1,1,2,2,24,768]{6,5,4,3,2,1,0:T(8,128)(2,1)S(1)} %dynamic-slice_convert_fusion.13), channel_id=1, source_target_pairs={{0,8},{1,9},{2,10},{3,11},{4,12},{5,13},{6,14},{7,15},{8,0},{9,1},... | collective-permute-start | bytes 884744 | tf_op jit(solution)/shard_map/ppermute | solution.py:119
  315.0 6.8 %collective-permute-start.33 = (bf16[1,1,1,2,1,24,512]{6,5,4,3,2,1,0:T(8,128)(2,1)S(1)}, bf16[1,1,1,2,1,24,512]{6,5,4,3,2,1,0:T(8,128)(2,1)S(1)}, u32[]{:S(2)}, u32[]{:S(2)}) collective-permute-start(bf16[1,1,1,2,1,24,512]{6,5,4,3,2,1,0:T(8,128)(2,1)S(1)} %dynamic-slice_convert_fusion.24), channel_id=1, source_target_pairs={{0,1},{1,0},{2,3},{3,2},{4,5},{5,4},{6,7},{7,6},{8,9},{9,8},{10,11... | collective-permute-start | bytes 147464 | tf_op jit(solution)/shard_map/ppermute | solution.py:119
  320.1 30.0 %slice-start.5 = ((s8[9437184]{0:T(1024)(128)(4,1)}), s8[4194304]{0:T(1024)(128)(4,1)S(1)}, s32[]{:S(2)}) async-start(s8[9437184]{0:T(1024)(128)(4,1)} %bitcast.180), calls=%async_computation.9 | async-start | bytes 8388608
  320.2 5.2 %collective-permute-start.17 = (bf16[1,1,1,2,2,24,768]{6,5,4,3,2,1,0:T(8,128)(2,1)S(1)}, bf16[1,1,1,2,2,24,768]{6,5,4,3,2,1,0:T(8,128)(2,1)S(1)}, u32[]{:S(2)}, u32[]{:S(2)}) collective-permute-start(bf16[1,1,1,2,2,24,768]{6,5,4,3,2,1,0:T(8,128)(2,1)S(1)} %dynamic-slice_convert_fusion.18), channel_id=1, source_target_pairs={{0,16},{1,17},{2,18},{3,19},{4,20},{5,21},{6,22},{7,23},{8,24},{9,... | collective-permute-start | bytes 442376 | tf_op jit(solution)/shard_map/ppermute | solution.py:119
  325.5 24.6 %slice-start.6 = ((s8[9437184]{0:T(1024)(128)(4,1)}), s8[4194304]{0:T(1024)(128)(4,1)S(1)}, s32[]{:S(2)}) async-start(s8[9437184]{0:T(1024)(128)(4,1)} %bitcast.180), calls=%async_computation.10 | async-start | bytes 8388608
  325.5 6.5 %collective-permute-start.18 = (bf16[1,1,1,2,1,24,768]{6,5,4,3,2,1,0:T(8,128)(2,1)S(1)}, bf16[1,1,1,2,1,24,768]{6,5,4,3,2,1,0:T(8,128)(2,1)S(1)}, u32[]{:S(2)}, u32[]{:S(2)}) collective-permute-start(bf16[1,1,1,2,1,24,768]{6,5,4,3,2,1,0:T(8,128)(2,1)S(1)} %dynamic-slice_convert_fusion.22), channel_id=1, source_target_pairs={{0,1},{1,0},{2,3},{3,2},{4,5},{5,4},{6,7},{7,6},{8,9},{9,8},{10,11... | collective-permute-start | bytes 221192 | tf_op jit(solution)/shard_map/ppermute | solution.py:119
  328.8 19.4 %collective-permute-start.11 = (bf16[1,2,1,2,2,24,2304]{6,5,4,3,2,1,0:T(8,128)(2,1)S(1)}, bf16[1,2,1,2,2,24,2304]{6,5,4,3,2,1,0:T(8,128)(2,1)S(1)}, u32[]{:S(2)}, u32[]{:S(2)}) collective-permute-start(bf16[1,2,1,2,2,24,2304]{6,5,4,3,2,1,0:T(8,128)(2,1)S(1)} %dynamic-slice_convert_fusion.5), channel_id=1, source_target_pairs={{0,16},{1,17},{2,18},{3,19},{4,20},{5,21},{6,22},{7,23},{8,24},{9,... | collective-permute-start | bytes 2654216 | tf_op jit(solution)/shard_map/ppermute | solution.py:119
  330.3 4.7 %collective-permute-start.34 = (bf16[1,1,1,1,1,24,512]{6,5,4,3,2,1,0:T(8,128)(2,1)S(1)}, bf16[1,1,1,1,1,24,512]{6,5,4,3,2,1,0:T(8,128)(2,1)S(1)}, u32[]{:S(2)}, u32[]{:S(2)}) collective-permute-start(bf16[1,1,1,1,1,24,512]{6,5,4,3,2,1,0:T(8,128)(2,1)S(1)} %dynamic-slice_convert_fusion.27), channel_id=1, source_target_pairs={{0,2},{1,3},{2,0},{3,1},{4,6},{5,7},{6,4},{7,5},{8,10},{9,11},{10,... | collective-permute-start | bytes 73736 | tf_op jit(solution)/shard_map/ppermute | solution.py:119
  332.0 5.1 %collective-permute-start.19 = (bf16[1,1,1,1,1,24,768]{6,5,4,3,2,1,0:T(8,128)(2,1)S(1)}, bf16[1,1,1,1,1,24,768]{6,5,4,3,2,1,0:T(8,128)(2,1)S(1)}, u32[]{:S(2)}, u32[]{:S(2)}) collective-permute-start(bf16[1,1,1,1,1,24,768]{6,5,4,3,2,1,0:T(8,128)(2,1)S(1)} %dynamic-slice_convert_fusion.25), channel_id=1, source_target_pairs={{0,2},{1,3},{2,0},{3,1},{4,6},{5,7},{6,4},{7,5},{8,10},{9,11},{10,... | collective-permute-start | bytes 110600 | tf_op jit(solution)/shard_map/ppermute | solution.py:119
  348.4 9.8 %collective-permute-start.12 = (bf16[1,2,1,2,1,24,2304]{6,5,4,3,2,1,0:T(8,128)(2,1)S(1)}, bf16[1,2,1,2,1,24,2304]{6,5,4,3,2,1,0:T(8,128)(2,1)S(1)}, u32[]{:S(2)}, u32[]{:S(2)}) collective-permute-start(bf16[1,2,1,2,1,24,2304]{6,5,4,3,2,1,0:T(8,128)(2,1)S(1)} %dynamic-slice_convert_fusion.9), channel_id=1, source_target_pairs={{0,1},{1,0},{2,3},{3,2},{4,5},{5,4},{6,7},{7,6},{8,9},{9,8},{10,11... | collective-permute-start | bytes 1327112 | tf_op jit(solution)/shard_map/ppermute | solution.py:119
  353.7 24.1 %collective-permute-start.21 = (bf16[1,2,1,2,2,24,3072]{6,5,4,3,2,1,0:T(8,128)(2,1)S(1)}, bf16[1,2,1,2,2,24,3072]{6,5,4,3,2,1,0:T(8,128)(2,1)S(1)}, u32[]{:S(2)}, u32[]{:S(2)}) collective-permute-start(bf16[1,2,1,2,2,24,3072]{6,5,4,3,2,1,0:T(8,128)(2,1)S(1)} %dynamic-slice_convert_fusion.4), channel_id=1, source_target_pairs={{0,16},{1,17},{2,18},{3,19},{4,20},{5,21},{6,22},{7,23},{8,24},{9,... | collective-permute-start | bytes 3538952 | tf_op jit(solution)/shard_map/ppermute | solution.py:119
  358.3 9.3 %collective-permute-start.13 = (bf16[1,2,1,1,1,24,2304]{6,5,4,3,2,1,0:T(8,128)(2,1)S(1)}, bf16[1,2,1,1,1,24,2304]{6,5,4,3,2,1,0:T(8,128)(2,1)S(1)}, u32[]{:S(2)}, u32[]{:S(2)}) collective-permute-start(bf16[1,2,1,1,1,24,2304]{6,5,4,3,2,1,0:T(8,128)(2,1)S(1)} %dynamic-slice_convert_fusion.14), channel_id=1, source_target_pairs={{0,2},{1,3},{2,0},{3,1},{4,6},{5,7},{6,4},{7,5},{8,10},{9,11},{10,... | collective-permute-start | bytes 663560 | tf_op jit(solution)/shard_map/ppermute | solution.py:119
  362.7 32.0 %collective-permute-start.26 = (bf16[2,1,1,2,2,96,768]{6,5,4,3,2,1,0:T(8,128)(2,1)S(1)}, bf16[2,1,1,2,2,96,768]{6,5,4,3,2,1,0:T(8,128)(2,1)S(1)}, u32[]{:S(2)}, u32[]{:S(2)}) collective-permute-start(bf16[2,1,1,2,2,96,768]{6,5,4,3,2,1,0:T(8,128)(2,1)S(1)} %dynamic-slice_convert_fusion.3), channel_id=1, source_target_pairs={{0,8},{1,9},{2,10},{3,11},{4,12},{5,13},{6,14},{7,15},{8,0},{9,1},... | collective-permute-start | bytes 3538952 | tf_op jit(solution)/shard_map/ppermute | solution.py:119
  367.7 26.3 %collective-permute-start.14 = (bf16[1,1,1,1,1,24,2304]{6,5,4,3,2,1,0:T(8,128)(2,1)S(1)}, bf16[1,1,1,1,1,24,2304]{6,5,4,3,2,1,0:T(8,128)(2,1)S(1)}, u32[]{:S(2)}, u32[]{:S(2)}) collective-permute-start(bf16[1,1,1,1,1,24,2304]{6,5,4,3,2,1,0:T(8,128)(2,1)S(1)} %dynamic-slice_convert_fusion.20), channel_id=1, source_target_pairs={{0,8},{1,9},{2,10},{3,11},{4,12},{5,13},{6,14},{7,15},{8,0},{9,1},... | collective-permute-start | bytes 331784 | tf_op jit(solution)/shard_map/ppermute | solution.py:119
  378.1 23.2 %collective-permute-start.22 = (bf16[1,1,1,2,2,24,3072]{6,5,4,3,2,1,0:T(8,128)(2,1)S(1)}, bf16[1,1,1,2,2,24,3072]{6,5,4,3,2,1,0:T(8,128)(2,1)}, u32[]{:S(2)}, u32[]{:S(2)}) collective-permute-start(bf16[1,1,1,2,2,24,3072]{6,5,4,3,2,1,0:T(8,128)(2,1)S(1)} %dynamic-slice_convert_fusion.7), channel_id=1, source_target_pairs={{0,8},{1,9},{2,10},{3,11},{4,12},{5,13},{6,14},{7,15},{8,0},{9,1},... | collective-permute-start | bytes 1769480 | tf_op jit(solution)/shard_map/ppermute | solution.py:119
  396.4 10.1 %collective-permute-start.27 = (bf16[1,1,1,2,2,96,768]{6,5,4,3,2,1,0:T(8,128)(2,1)S(1)}, bf16[1,1,1,2,2,96,768]{6,5,4,3,2,1,0:T(8,128)(2,1)}, u32[]{:S(2)}, u32[]{:S(2)}) collective-permute-start(bf16[1,1,1,2,2,96,768]{6,5,4,3,2,1,0:T(8,128)(2,1)S(1)} %dynamic-slice_convert_fusion.6), channel_id=1, source_target_pairs={{0,16},{1,17},{2,18},{3,19},{4,20},{5,21},{6,22},{7,23},{8,24},{9,... | collective-permute-start | bytes 1769480 | tf_op jit(solution)/shard_map/ppermute | solution.py:119
  402.7 9.7 %collective-permute-start.23 = (bf16[1,1,1,2,1,24,3072]{6,5,4,3,2,1,0:T(8,128)(2,1)S(1)}, bf16[1,1,1,2,1,24,3072]{6,5,4,3,2,1,0:T(8,128)(2,1)S(1)}, u32[]{:S(2)}, u32[]{:S(2)}) collective-permute-start(bf16[1,1,1,2,1,24,3072]{6,5,4,3,2,1,0:T(8,128)(2,1)S(1)} %dynamic-slice_convert_fusion.12), channel_id=1, source_target_pairs={{0,1},{1,0},{2,3},{3,2},{4,5},{5,4},{6,7},{7,6},{8,9},{9,8},{10,11... | collective-permute-start | bytes 884744 | tf_op jit(solution)/shard_map/ppermute | solution.py:119
  407.7 7.9 %collective-permute-start.28 = (bf16[1,1,1,2,1,96,768]{6,5,4,3,2,1,0:T(8,128)(2,1)S(1)}, bf16[1,1,1,2,1,96,768]{6,5,4,3,2,1,0:T(8,128)(2,1)S(1)}, u32[]{:S(2)}, u32[]{:S(2)}) collective-permute-start(bf16[1,1,1,2,1,96,768]{6,5,4,3,2,1,0:T(8,128)(2,1)S(1)} %dynamic-slice_convert_fusion.11), channel_id=1, source_target_pairs={{0,1},{1,0},{2,3},{3,2},{4,5},{5,4},{6,7},{7,6},{8,9},{9,8},{10,11... | collective-permute-start | bytes 884744 | tf_op jit(solution)/shard_map/ppermute | solution.py:119
  412.5 7.7 %collective-permute-start.24 = (bf16[1,1,1,1,1,24,3072]{6,5,4,3,2,1,0:T(8,128)(2,1)S(1)}, bf16[1,1,1,1,1,24,3072]{6,5,4,3,2,1,0:T(8,128)(2,1)S(1)}, u32[]{:S(2)}, u32[]{:S(2)}) collective-permute-start(bf16[1,1,1,1,1,24,3072]{6,5,4,3,2,1,0:T(8,128)(2,1)S(1)} %dynamic-slice_convert_fusion.17), channel_id=1, source_target_pairs={{0,2},{1,3},{2,0},{3,1},{4,6},{5,7},{6,4},{7,5},{8,10},{9,11},{10,... | collective-permute-start | bytes 442376 | tf_op jit(solution)/shard_map/ppermute | solution.py:119
  415.7 7.7 %collective-permute-start.29 = (bf16[1,1,1,1,1,96,768]{6,5,4,3,2,1,0:T(8,128)(2,1)S(1)}, bf16[1,1,1,1,1,96,768]{6,5,4,3,2,1,0:T(8,128)(2,1)S(1)}, u32[]{:S(2)}, u32[]{:S(2)}) collective-permute-start(bf16[1,1,1,1,1,96,768]{6,5,4,3,2,1,0:T(8,128)(2,1)S(1)} %dynamic-slice_convert_fusion.16), channel_id=1, source_target_pairs={{0,2},{1,3},{2,0},{3,1},{4,6},{5,7},{6,4},{7,5},{8,10},{9,11},{10,... | collective-permute-start | bytes 442376 | tf_op jit(solution)/shard_map/ppermute | solution.py:119
  (40 other events, 210.1 us)
Sparse Core Ops, SparseCore 0:
  11.4 108.9 all-gather.2
  123.2 62.0 all-gather.4

commit v8 on v7

--- a/solution.py
+++ b/solution.py
@@ -235,14 +235,14 @@
             mask_token,
         )
         small = (wave_table, norm1_gain, norm1_bias, norm2_gain, norm2_bias, mlp_in_bias,
-                 mlp_out_bias, dec_bias, mask_token)
+                 mlp_out_bias, dec_bias, mask_token, dec_weight)
         packed_small, small_widths = pack_rows(
             [a.reshape(1, -1) for a in small], 1, jnp.bfloat16
         )
         gathered_small = ag_chain(packed_small, n_bits, orders["x"])
         (wave_full, gain_one, shift_one, gain_two, shift_two, inner_bias, outer_bias,
-         dec_shift, mask_full) = unpack_rows(gathered_small, small, small_widths, 1, n_dev)
-        wide = (qkv_weight, out_weight, mlp_in, dec_weight)
+         dec_shift, mask_full, dec_full) = unpack_rows(gathered_small, small, small_widths, 1, n_dev)
+        wide = (qkv_weight, out_weight, mlp_in)
         wide_cols = [a.shape[1] for a in wide]
         gathered_wide = lax.all_gather(jnp.concatenate(wide, axis=1), AX, axis=0, tiled=True)
         wide_full = []
@@ -250,7 +250,7 @@
         for cols in wide_cols:
             wide_full.append(gathered_wide[:, offset : offset + cols])
             offset += cols
-        qkv_full, out_full, inner_full, dec_full = wide_full
+        qkv_full, out_full, inner_full = wide_full
         outer_full = lax.all_gather(mlp_out, AX, axis=0, tiled=True)
 
         chip_count, vis_len, feature_width = tokens.shape

time: 435 us -> 439 us (level)
  waiting for transfers between devices: 204 us -> 195 us
  local copies, waits for them, and re-layouts: 62.2 us -> 70.1 us
    all_to_all x1, waiting for transfers between devices: 3.71 us -> 70.7 us  [local(): lax.all_to_all(cot_decoded, AX, split_axis=0, concat_axis=1, tiled=True)]
    ppermute x5, waiting for transfers between devices: 54 us -> 11.1 us  [ag_chain(): moved = lax.ppermute(current, AX, [(i, i ^ 1 << bit) for i in range(n_dev)])]
    all_gather x1, waiting for transfers between devices: 28.4 us -> 0.29 us  [local(): lax.all_gather(jnp.concatenate(wide, axis=1), AX, axis=0, tiled=True)]
    all_gather x1, waiting for transfers between devices: 29.5 us -> 23.9 us  [local(): outer_full = lax.all_gather(mlp_out, AX, axis=0, tiled=True)]
    unnamed x109 -> x110, local copies, waits for them, and re-layouts: 12.8 us -> 15 us
  transfers between devices with their start and end apart: 39 -> 39, of which waited for: 25 -> 26; matrix products, arithmetic and copies ran while one was open for 23% -> 25% of each run, Pallas kernels for 0% -> 0%
where the time goes in v8:
time: 439 us; the launch traced here: 433 us
  waiting for transfers between devices  195 us (44%)
  local copies, waits for them, and re-layouts  70.1 us (16%)
  matrix products  69.9 us (16%)
  starting transfers between devices  47.7 us (11%)
  other arithmetic  35.2 us (8%)
  between operations  15.7 us (4%)
    ppermute x30, waiting for transfers between devices, rs_chain(): lax.ppermute(send.astype(jnp.bfloat16), AX, [(i, i ^ 1 << bit) for i in r...  88.1 us
    all_to_all x1, waiting for transfers between devices, local(): lax.all_to_all(cot_decoded, AX, split_axis=0, concat_axis=1, tiled=True)  70.7 us
    ppermute x30, starting transfers between devices, rs_chain(): lax.ppermute(send.astype(jnp.bfloat16), AX, [(i, i ^ 1 << bit) for i in r...  31 us
    all_gather x1, waiting for transfers between devices, local(): outer_full = lax.all_gather(mlp_out, AX, axis=0, tiled=True)  23.9 us
    dot_general x5, matrix products, outer_cols(): lax.dot_general(left_op, right_op, (((1,), (1,)), ((), ())), preferred_el...  23.4 us
    dot_general x5, matrix products, inner_rows(): lax.dot_general(left_op, right_op, (((0,), (0,)), ((), ())), preferred_el...  16 us
    unnamed x110, local copies, waits for them, and re-layouts  15 us
    dot_general x5, matrix products, product(): return jnp.dot(left_op, right_op, preferred_element_type=jnp.float32)  14.5 us
  transfers between devices with their start and end apart: 39, of which 26 were waited for; matrix products, arithmetic and copies ran while one was open for 25% of the time, Pallas kernels for 0%

profile of v8, /device:TPU:0, one launch (start us, length us, event | category | flops | bytes accessed | tf_op | source)
XLA Modules:
  0.0 433.4 jit_solution(4463436085294302582)
XLA Ops:
  11.7 4.1 collective-permute-start
  19.8 2.7 collective-permute-done.1
  24.3 4.7 %collective-permute-done.2 = bf16[1,1,1,2,2,1,8,2048]{7,6,4,3,2,1,0,5:T(8,128)(2,1)S(1)} collective-permute-done((bf16[1,1,1,2,2,1,8,2048]{7,6,4,3,2,1,0,5:T(8,128)(2,1)S(1)}, bf16[1,1,1,2,2,1,8,2048]{7,6,4,3,2,1,0,5:T(8,128)(2,1)S(1)}, u32[]{:S(2)}, u32[]{:S(2)}) %collective-permute-start.2) | collective-permute-done | bytes 131104 | tf_op jit(solution)/shard_map/ppermute | solution.py:133
  30.6 3.9 all-to-all-start.1
  44.4 70.7 %all-to-all-done.1 = bf16[64,32,512]{2,1,0:T(8,128)(2,1)} async-done(((bf16[64,32,512]{2,1,0:T(8,128)(2,1)}), bf16[64,32,512]{2,1,0:T(8,128)(2,1)}, u32[]{:S(2)}, u32[]{:S(2)}) %all-to-all-start.1) | async-done | bytes 2097184 | tf_op jit(solution)/shard_map/all_to_all | solution.py:304
  123.1 4.5 %convolution_convert_fusion = bf16[512,2304]{1,0:T(8,128)(2,1)S(1)} fusion(bf16[512,768]{1,0:T(8,128)(2,1)} %copy-done.24, bf16[768,6144]{1,0:T(8,128)(2,1)} %all-gather.3.cloned.1.call-done), kind=kOutput, calls=%fused_computation.20 | convolution fusion | flops 1813118976 | bytes 6684672 | tf_op jit(solution)/shard_map/dot_general | solution.py:21
  129.1 2.3 copy.124
  131.4 2.9 reshape.339
  136.6 2.9 reshape.341
  141.8 2.9 reshape.340
  144.8 2.4 fusion.55
  147.2 4.8 %fusion.75 = (f32[2,12,256]{2,1,0:T(8,128)S(1)}, f32[2,12,256,256]{2,3,1,0:T(8,128)S(1)}) fusion(f32[2,12,256,256]{2,3,1,0:T(8,128)S(1)} %fusion.55), kind=kOutput, calls=%fused_computation.206 | output fusion | flops 6291711 | bytes 12607488 | tf_op jit(solution)/shard_map/sub | solution.py:167
  152.6 2.5 copy-done
  158.8 5.9 %multiply_convert_fusion.1 = (bf16[512,3072]{1,0:T(8,128)(2,1)}, f32[512,3072]{1,0:T(8,128)}) fusion(f32[3072]{0:T(1024)S(1)} %reshape.380, bf16[768,6144]{1,0:T(8,128)(2,1)S(1)} %bitcast.214, f32[512,768]{1,0:T(8,128)S(1)} %get-tuple-element.60, f32[768]{0:T(1024)S(1)} %reshape.379, f32[768]{0:T(1024)S(1)} %reshape.378, f32[512]{0:T(512)S(1)} %add_rsqrt_fusion, ...), kind=kOutput, calls=%fused_computation.11 | convolution fusion | flops 2427322368 | bytes 15753216 | tf_op jit(solution)/shard_map/dot_general | solution.py:21
  164.7 23.9 %all-gather.5.cloned.1.call-done = bf16[3072,768]{1,0:T(8,128)(2,1)} async-done(((bf16[96,768]{1,0:T(8,128)(2,1)}), bf16[3072,768]{1,0:T(8,128)(2,1)}) %all-gather.5.cloned.1.call-update) | async-done | bytes 4718608 | tf_op jit(solution)/shard_map/all_gather | solution.py:254
  188.6 7.6 %convert_reduce_fusion = (f32[3072]{0:T(1024)S(1)}, bf16[512,3072]{1,0:T(8,128)(2,1)S(1)}) fusion(f32[512,3072]{1,0:T(8,128)} %get-tuple-element.62, f32[3072]{0:T(1024)S(1)} %reshape.380, bf16[3072,768]{1,0:T(8,128)(2,1)} %all-gather.5.cloned.1.call-done, f32[512,768]{1,0:T(8,128)S(1)} %fusion.77), kind=kOutput, calls=%fused_computation.8 | convolution fusion | flops 2436756480 | bytes 15753216 | tf_op jit(solution)/shard_map/dot_general | solution.py:31
  196.2 6.5 %multiply_reduce_fusion.2 = (f32[768]{0:T(1024)S(1)}, f32[512]{0:T(512)S(1)}, f32[512]{0:T(512)S(1)}, f32[768]{0:T(1024)S(1)}, f32[512,768]{1,0:T(8,128)S(1)}) fusion(f32[512,768]{1,0:T(8,128)S(1)} %copy-done.6, f32[512]{0:T(512)S(1)} %add_rsqrt_fusion, f32[512]{0:T(512)S(1)} %broadcast_multiply_fusion.4, f32[768]{0:T(1024)S(1)} %reshape.378, ...), kind=kOutput, calls=%fused_computation.51 | convolution fusion | flops 2419455488 | bytes 11027456 | tf_op jit(solution)/shard_map/dot_general | solution.py:31
  208.1 4.3 fusion.33
  212.8 3.7 multiply_reduce_fusion
  216.6 4.3 multiply_convert_fusion
  223.7 5.5 %fusion.72 = f32[768,3072]{1,0:T(8,128)} fusion(bf16[512,3072]{1,0:T(8,128)(2,1)S(1)} %copy-done.35, f32[512,768]{1,0:T(8,128)S(1)} %copy-done.7, f32[768]{0:T(1024)S(1)} %reshape.379, f32[768]{0:T(1024)S(1)} %reshape.378, f32[512]{0:T(512)S(1)} %add_rsqrt_fusion, f32[512]{0:T(512)S(1)} %broadcast_multiply_fusion.4), kind=kOutput, calls=%fused_computation.203 | convolution fusion | flops 2417885184 | bytes 14166016 | tf_op jit(solution)/shard_map/dot_general | solution.py:25
  229.2 5.2 %fusion.67 = f32[3072,768]{1,0:T(8,128)} fusion(bf16[512,3072]{1,0:T(8,128)(2,1)S(1)} %copy-done.21, f32[512,768]{1,0:T(8,128)S(1)} %copy-done.4), kind=kOutput, calls=%fused_computation.198 | convolution fusion | flops 2416312320 | bytes 14155776 | tf_op jit(solution)/shard_map/dot_general | solution.py:25
  234.5 2.6 add_convert_fusion
  239.2 3.5 copy.133
  242.7 3.5 all-to-all-start
  252.7 5.2 %multiply_reduce_fusion.3 = (f32[768]{0:T(1024)S(1)}, f32[512]{0:T(512)S(1)}, f32[512]{0:T(512)S(1)}, f32[768]{0:T(1024)S(1)}, f32[512,768]{1,0:T(8,128)S(1)}) fusion(f32[2,256,768]{2,1,0:T(8,128)S(1)} %copy-done.2, f32[512]{0:T(512)S(1)} %bitcast.223, f32[512]{0:T(512)S(1)} %bitcast.226, f32[768]{0:T(1024)S(1)} %reshape.376, ...), kind=kOutput, calls=%fused_computation.52 | convolution fusion | flops 1822553600 | bytes 9061376 | tf_op jit(solution)/shard_map/dot_general | solution.py:31
  261.5 3.6 fusion.18
  272.3 4.1 dynamic-slice_convert_fusion.1
  278.0 4.1 dynamic-slice_convert_fusion
  282.7 3.3 collective-permute-start.8
  286.9 8.8 %collective-permute-done.8 = bf16[1,2,1,1,1,1,8,512]{7,6,5,4,3,2,1,0:T(8,128)(2,1)S(1)} collective-permute-done((bf16[1,2,1,1,1,1,8,512]{7,6,5,4,3,2,1,0:T(8,128)(2,1)S(1)}, bf16[1,2,1,1,1,1,8,512]{7,6,5,4,3,2,1,0:T(8,128)(2,1)S(1)}, u32[]{:S(2)}, u32[]{:S(2)}) %collective-permute-start.8) | collective-permute-done | bytes 16416 | tf_op jit(solution)/shard_map/ppermute | solution.py:119
  306.1 5.2 %collective-permute-done.31 = bf16[1,2,1,2,2,24,512]{6,5,4,3,2,1,0:T(8,128)(2,1)S(1)} collective-permute-done((bf16[1,2,1,2,2,24,512]{6,5,4,3,2,1,0:T(8,128)(2,1)S(1)}, bf16[1,2,1,2,2,24,512]{6,5,4,3,2,1,0:T(8,128)(2,1)S(1)}, u32[]{:S(2)}, u32[]{:S(2)}) %collective-permute-start.31) | collective-permute-done | bytes 196640 | tf_op jit(solution)/shard_map/ppermute | solution.py:119
  313.8 3.4 collective-permute-done.32
  317.3 5.0 %collective-permute-done.16 = bf16[2,1,1,2,2,24,768]{6,5,4,3,2,1,0:T(8,128)(2,1)S(1)} collective-permute-done((bf16[2,1,1,2,2,24,768]{6,5,4,3,2,1,0:T(8,128)(2,1)S(1)}, bf16[2,1,1,2,2,24,768]{6,5,4,3,2,1,0:T(8,128)(2,1)S(1)}, u32[]{:S(2)}, u32[]{:S(2)}) %collective-permute-start.16) | collective-permute-done | bytes 294944 | tf_op jit(solution)/shard_map/ppermute | solution.py:119
  324.0 3.6 collective-permute-done.17
  327.8 3.1 convert_add_fusion.2
  340.0 10.4 %collective-permute-done.11 = bf16[1,2,1,2,2,24,2304]{6,5,4,3,2,1,0:T(8,128)(2,1)S(1)} collective-permute-done((bf16[1,2,1,2,2,24,2304]{6,5,4,3,2,1,0:T(8,128)(2,1)S(1)}, bf16[1,2,1,2,2,24,2304]{6,5,4,3,2,1,0:T(8,128)(2,1)S(1)}, u32[]{:S(2)}, u32[]{:S(2)}) %collective-permute-start.11) | collective-permute-done | bytes 884768 | tf_op jit(solution)/shard_map/ppermute | solution.py:119
  352.4 3.4 convert_add_fusion.1
  357.5 3.0 collective-permute-done.12
  362.4 2.4 convert_add_fusion
  365.2 4.6 %collective-permute-done.13 = bf16[1,2,1,1,1,24,2304]{6,5,4,3,2,1,0:T(8,128)(2,1)S(1)} collective-permute-done((bf16[1,2,1,1,1,24,2304]{6,5,4,3,2,1,0:T(8,128)(2,1)S(1)}, bf16[1,2,1,1,1,24,2304]{6,5,4,3,2,1,0:T(8,128)(2,1)S(1)}, u32[]{:S(2)}, u32[]{:S(2)}) %collective-permute-start.13) | collective-permute-done | bytes 221216 | tf_op jit(solution)/shard_map/ppermute | solution.py:119
  370.9 9.1 %collective-permute-done.21 = bf16[1,2,1,2,2,24,3072]{6,5,4,3,2,1,0:T(8,128)(2,1)S(1)} collective-permute-done((bf16[1,2,1,2,2,24,3072]{6,5,4,3,2,1,0:T(8,128)(2,1)S(1)}, bf16[1,2,1,2,2,24,3072]{6,5,4,3,2,1,0:T(8,128)(2,1)S(1)}, u32[]{:S(2)}, u32[]{:S(2)}) %collective-permute-start.21) | collective-permute-done | bytes 1179680 | tf_op jit(solution)/shard_map/ppermute | solution.py:119
  381.2 15.0 %collective-permute-done.14 = bf16[1,1,1,1,1,24,2304]{6,5,4,3,2,1,0:T(8,128)(2,1)S(1)} collective-permute-done((bf16[1,1,1,1,1,24,2304]{6,5,4,3,2,1,0:T(8,128)(2,1)S(1)}, bf16[1,1,1,1,1,24,2304]{6,5,4,3,2,1,0:T(8,128)(2,1)S(1)}, u32[]{:S(2)}, u32[]{:S(2)}) %collective-permute-start.14) | collective-permute-done | bytes 110624 | tf_op jit(solution)/shard_map/ppermute | solution.py:119
  400.2 3.4 copy.134
  405.5 3.2 collective-permute-done.27
  410.0 4.6 %collective-permute-done.23 = bf16[1,1,1,2,1,24,3072]{6,5,4,3,2,1,0:T(8,128)(2,1)S(1)} collective-permute-done((bf16[1,1,1,2,1,24,3072]{6,5,4,3,2,1,0:T(8,128)(2,1)S(1)}, bf16[1,1,1,2,1,24,3072]{6,5,4,3,2,1,0:T(8,128)(2,1)S(1)}, u32[]{:S(2)}, u32[]{:S(2)}) %collective-permute-start.23) | collective-permute-done | bytes 294944 | tf_op jit(solution)/shard_map/ppermute | solution.py:119
  419.5 2.9 collective-permute-done.24
  423.2 2.4 collective-permute-done.29
  (320 shorter events, 115.7 us)
Async XLA Ops:
  7.2 116.0 %all-gather.3.cloned.1.call-start = ((), (), s32[]{:S(2)}) async-start(), calls=%async_computation.2 | async-start | bytes 9732096 | tf_op jit(solution)/shard_map/all_gather | solution.py:247
  11.7 6.4 %collective-permute-start = (bf16[1,1,1,1,1,1,8,2048]{7,6,4,3,2,1,0,5:T(8,128)(2,1)S(1)}, bf16[1,1,1,1,1,1,8,2048]{7,6,4,3,2,1,0,5:T(8,128)(2,1)S(1)}, u32[]{:S(2)}, u32[]{:S(2)}) collective-permute-start(bf16[1,1,1,1,1,1,8,2048]{7,6,4,3,2,1,0,5:T(8,128)(2,1)S(1)} %bitcast.215), channel_id=1, source_target_pairs={{0,2},{1,3},{2,0},{3,1},{4,6},{5,7},{6,4},{7,5},{8,10},{9,11},{10,... | collective-permute-start | bytes 98312 | tf_op jit(solution)/shard_map/ppermute | solution.py:133
  18.1 4.3 collective-permute-start.1
  22.5 6.5 %collective-permute-start.2 = (bf16[1,1,1,2,2,1,8,2048]{7,6,4,3,2,1,0,5:T(8,128)(2,1)S(1)}, bf16[1,1,1,2,2,1,8,2048]{7,6,4,3,2,1,0,5:T(8,128)(2,1)S(1)}, u32[]{:S(2)}, u32[]{:S(2)}) collective-permute-start(bf16[1,1,1,2,2,1,8,2048]{7,6,4,3,2,1,0,5:T(8,128)(2,1)S(1)} %pad_maximum_fusion.7), channel_id=1, source_target_pairs={{0,16},{1,17},{2,18},{3,19},{4,20},{5,21},{6,22},{7,23},{8,24},{9,... | collective-permute-start | bytes 393224 | tf_op jit(solution)/shard_map/ppermute | solution.py:133
  29.1 6.4 %collective-permute-start.3 = (bf16[2,1,1,2,2,1,8,2048]{7,6,4,3,2,1,0,5:T(8,128)(2,1)S(1)}, bf16[2,1,1,2,2,1,8,2048]{7,6,4,3,2,1,0,5:T(8,128)(2,1)S(1)}, u32[]{:S(2)}, u32[]{:S(2)}) collective-permute-start(bf16[2,1,1,2,2,1,8,2048]{7,6,4,3,2,1,0,5:T(8,128)(2,1)S(1)} %pad_maximum_fusion.6), channel_id=1, source_target_pairs={{0,8},{1,9},{2,10},{3,11},{4,12},{5,13},{6,14},{7,15},{8,0},{9,1},... | collective-permute-start | bytes 786440 | tf_op jit(solution)/shard_map/ppermute | solution.py:133
  30.6 84.6 %all-to-all-start.1 = ((bf16[64,32,512]{2,1,0:T(8,128)(2,1)}), bf16[64,32,512]{2,1,0:T(8,128)(2,1)}, u32[]{:S(2)}, u32[]{:S(2)}) async-start(bf16[64,32,512]{2,1,0:T(8,128)(2,1)} %param.35), calls=%async_computation.1 | async-start | bytes 4194304 | tf_op jit(solution)/shard_map/all_to_all | solution.py:304
  34.5 154.0 %all-gather.5.cloned.1.call-start = ((), (), s32[]{:S(2)}) async-start(), calls=%async_computation.3 | async-start | bytes 4866048 | tf_op jit(solution)/shard_map/all_gather | solution.py:254
  35.6 2.0 collective-permute-start.4
  40.9 115.2 %copy-start.1 = (f32[2,256,768]{2,1,0:T(8,128)}, f32[2,256,768]{2,1,0:T(8,128)S(1)}, u32[]{:S(2)}) copy-start(f32[2,256,768]{2,1,0:T(8,128)S(1)} %get-tuple-element.39) | copy-start | bytes 4718596
  43.2 73.8 %copy-start.24 = (bf16[512,768]{1,0:T(8,128)(2,1)}, bf16[512,768]{1,0:T(8,128)(2,1)S(1)}, u32[]{:S(2)}) copy-start(bf16[512,768]{1,0:T(8,128)(2,1)S(1)} %add_convert_fusion.2) | copy-start | bytes 2359300
  122.8 79.9 %copy-start.3 = (f32[512,768]{1,0:T(8,128)}, f32[512,768]{1,0:T(8,128)S(1)}, u32[]{:S(2)}) copy-start(f32[512,768]{1,0:T(8,128)S(1)} %fusion.77) | copy-start | bytes 4718596
  222.0 12.4 %slice-start.11 = ((s8[4718592]{0:T(1024)(128)(4,1)}), s8[4194304]{0:T(1024)(128)(4,1)S(1)}, s32[]{:S(2)}) async-start(s8[4718592]{0:T(1024)(128)(4,1)} %bitcast.237), calls=%async_computation.15 | async-start | bytes 8388608
  242.7 157.5 %all-to-all-start = ((bf16[2,1024,512]{2,0,1:T(2,128)(2,1)}), bf16[2,1024,512]{2,0,1:T(2,128)(2,1)}, u32[]{:S(2)}, u32[]{:S(2)}) async-start(bf16[2,1024,512]{2,0,1:T(2,128)(2,1)} %copy.133), calls=%async_computation | async-start | bytes 4194304 | tf_op jit(solution)/shard_map/all_to_all | solution.py:303
  261.4 9.1 %collective-permute-start.5 = (bf16[2,2,1,2,2,1,8,512]{7,6,5,4,3,2,1,0:T(8,128)(2,1)S(1)}, bf16[2,2,1,2,2,1,8,512]{7,6,5,4,3,2,1,0:T(8,128)(2,1)S(1)}, u32[]{:S(2)}, u32[]{:S(2)}) collective-permute-start(bf16[2,2,1,2,2,1,8,512]{7,6,5,4,3,2,1,0:T(8,128)(2,1)S(1)} %dynamic-slice_convert_fusion.19), channel_id=1, source_target_pairs={{0,4},{1,5},{2,6},{3,7},{4,0},{5,1},{6,2},{7,3},{8,12},{9,13},{10,... | collective-permute-start | bytes 393224 | tf_op jit(solution)/shard_map/ppermute | solution.py:119
  266.7 61.2 %collective-permute-start.10 = (bf16[2,2,1,2,2,24,2304]{6,5,4,3,2,1,0:T(8,128)(2,1)}, bf16[2,2,1,2,2,24,2304]{6,5,4,3,2,1,0:T(8,128)(2,1)}, u32[]{:S(2)}, u32[]{:S(2)}) collective-permute-start(bf16[2,2,1,2,2,24,2304]{6,5,4,3,2,1,0:T(8,128)(2,1)} %dynamic-slice_convert_fusion.2), channel_id=1, source_target_pairs={{0,4},{1,5},{2,6},{3,7},{4,0},{5,1},{6,2},{7,3},{8,12},{9,13},{10,... | collective-permute-start | bytes 5308424 | tf_op jit(solution)/shard_map/ppermute | solution.py:119
  270.0 42.7 %collective-permute-start.15 = (bf16[2,2,1,2,2,24,768]{6,5,4,3,2,1,0:T(8,128)(2,1)S(1)}, bf16[2,2,1,2,2,24,768]{6,5,4,3,2,1,0:T(8,128)(2,1)S(1)}, u32[]{:S(2)}, u32[]{:S(2)}) collective-permute-start(bf16[2,2,1,2,2,24,768]{6,5,4,3,2,1,0:T(8,128)(2,1)S(1)} %dynamic-slice_convert_fusion.8), channel_id=1, source_target_pairs={{0,4},{1,5},{2,6},{3,7},{4,0},{5,1},{6,2},{7,3},{8,12},{9,13},{10,... | collective-permute-start | bytes 1769480 | tf_op jit(solution)/shard_map/ppermute | solution.py:119
  270.6 5.7 %collective-permute-start.6 = (bf16[1,2,1,2,2,1,8,512]{7,6,5,4,3,2,1,0:T(8,128)(2,1)S(1)}, bf16[1,2,1,2,2,1,8,512]{7,6,5,4,3,2,1,0:T(8,128)(2,1)S(1)}, u32[]{:S(2)}, u32[]{:S(2)}) collective-permute-start(bf16[1,2,1,2,2,1,8,512]{7,6,5,4,3,2,1,0:T(8,128)(2,1)S(1)} %dynamic-slice_convert_fusion.23), channel_id=1, source_target_pairs={{0,16},{1,17},{2,18},{3,19},{4,20},{5,21},{6,22},{7,23},{8,24},{9,... | collective-permute-start | bytes 196616 | tf_op jit(solution)/shard_map/ppermute | solution.py:119
  276.4 76.0 %collective-permute-start.20 = (bf16[2,2,1,2,2,24,3072]{6,5,4,3,2,1,0:T(8,128)(2,1)}, bf16[2,2,1,2,2,24,3072]{6,5,4,3,2,1,0:T(8,128)(2,1)}, u32[]{:S(2)}, u32[]{:S(2)}) collective-permute-start(bf16[2,2,1,2,2,24,3072]{6,5,4,3,2,1,0:T(8,128)(2,1)} %dynamic-slice_convert_fusion.1), channel_id=1, source_target_pairs={{0,4},{1,5},{2,6},{3,7},{4,0},{5,1},{6,2},{7,3},{8,12},{9,13},{10,... | collective-permute-start | bytes 7077896 | tf_op jit(solution)/shard_map/ppermute | solution.py:119
  276.4 6.2 %collective-permute-start.7 = (bf16[1,2,1,2,1,1,8,512]{7,6,5,4,3,2,1,0:T(8,128)(2,1)S(1)}, bf16[1,2,1,2,1,1,8,512]{7,6,5,4,3,2,1,0:T(8,128)(2,1)S(1)}, u32[]{:S(2)}, u32[]{:S(2)}) collective-permute-start(bf16[1,2,1,2,1,1,8,512]{7,6,5,4,3,2,1,0:T(8,128)(2,1)S(1)} %dynamic-slice_convert_fusion.26), channel_id=1, source_target_pairs={{0,1},{1,0},{2,3},{3,2},{4,5},{5,4},{6,7},{7,6},{8,9},{9,8},{10,11... | collective-permute-start | bytes 98312 | tf_op jit(solution)/shard_map/ppermute | solution.py:119
  282.1 80.2 %collective-permute-start.25 = (bf16[2,2,1,2,2,96,768]{6,5,4,3,2,1,0:T(8,128)(2,1)}, bf16[2,2,1,2,2,96,768]{6,5,4,3,2,1,0:T(8,128)(2,1)}, u32[]{:S(2)}, u32[]{:S(2)}) collective-permute-start(bf16[2,2,1,2,2,96,768]{6,5,4,3,2,1,0:T(8,128)(2,1)} %dynamic-slice_convert_fusion), channel_id=1, source_target_pairs={{0,4},{1,5},{2,6},{3,7},{4,0},{5,1},{6,2},{7,3},{8,12},{9,13},{10,... | collective-permute-start | bytes 7077896 | tf_op jit(solution)/shard_map/ppermute | solution.py:119
  282.7 13.0 %collective-permute-start.8 = (bf16[1,2,1,1,1,1,8,512]{7,6,5,4,3,2,1,0:T(8,128)(2,1)S(1)}, bf16[1,2,1,1,1,1,8,512]{7,6,5,4,3,2,1,0:T(8,128)(2,1)S(1)}, u32[]{:S(2)}, u32[]{:S(2)}) collective-permute-start(bf16[1,2,1,1,1,1,8,512]{7,6,5,4,3,2,1,0:T(8,128)(2,1)S(1)} %dynamic-slice_convert_fusion.28), channel_id=1, source_target_pairs={{0,2},{1,3},{2,0},{3,1},{4,6},{5,7},{6,4},{7,5},{8,10},{9,11},{10,... | collective-permute-start | bytes 49160 | tf_op jit(solution)/shard_map/ppermute | solution.py:119
  286.9 25.9 %copy-start.13 = (f32[2,2,2,2,2,24,768]{6,5,4,3,2,1,0:T(8,128)S(1)}, f32[2,2,2,2,2,24,768]{6,5,4,3,2,1,0:T(8,128)}, u32[]{:S(2)}) copy-start(f32[2,2,2,2,2,24,768]{6,5,4,3,2,1,0:T(8,128)} %copy-done.12) | copy-start | bytes 7077892
  295.7 3.7 collective-permute-start.9
  299.4 3.2 collective-permute-start.30
  304.0 7.4 %collective-permute-start.31 = (bf16[1,2,1,2,2,24,512]{6,5,4,3,2,1,0:T(8,128)(2,1)S(1)}, bf16[1,2,1,2,2,24,512]{6,5,4,3,2,1,0:T(8,128)(2,1)S(1)}, u32[]{:S(2)}, u32[]{:S(2)}) collective-permute-start(bf16[1,2,1,2,2,24,512]{6,5,4,3,2,1,0:T(8,128)(2,1)S(1)} %dynamic-slice_convert_fusion.15), channel_id=1, source_target_pairs={{0,16},{1,17},{2,18},{3,19},{4,20},{5,21},{6,22},{7,23},{8,24},{9,... | collective-permute-start | bytes 589832 | tf_op jit(solution)/shard_map/ppermute | solution.py:119
  311.5 5.7 %collective-permute-start.32 = (bf16[1,1,1,2,2,24,512]{6,5,4,3,2,1,0:T(8,128)(2,1)S(1)}, bf16[1,1,1,2,2,24,512]{6,5,4,3,2,1,0:T(8,128)(2,1)S(1)}, u32[]{:S(2)}, u32[]{:S(2)}) collective-permute-start(bf16[1,1,1,2,2,24,512]{6,5,4,3,2,1,0:T(8,128)(2,1)S(1)} %dynamic-slice_convert_fusion.21), channel_id=1, source_target_pairs={{0,8},{1,9},{2,10},{3,11},{4,12},{5,13},{6,14},{7,15},{8,0},{9,1},... | collective-permute-start | bytes 294920 | tf_op jit(solution)/shard_map/ppermute | solution.py:119
  313.0 9.4 %collective-permute-start.16 = (bf16[2,1,1,2,2,24,768]{6,5,4,3,2,1,0:T(8,128)(2,1)S(1)}, bf16[2,1,1,2,2,24,768]{6,5,4,3,2,1,0:T(8,128)(2,1)S(1)}, u32[]{:S(2)}, u32[]{:S(2)}) collective-permute-start(bf16[2,1,1,2,2,24,768]{6,5,4,3,2,1,0:T(8,128)(2,1)S(1)} %dynamic-slice_convert_fusion.13), channel_id=1, source_target_pairs={{0,8},{1,9},{2,10},{3,11},{4,12},{5,13},{6,14},{7,15},{8,0},{9,1},... | collective-permute-start | bytes 884744 | tf_op jit(solution)/shard_map/ppermute | solution.py:119
  317.2 6.8 %collective-permute-start.33 = (bf16[1,1,1,2,1,24,512]{6,5,4,3,2,1,0:T(8,128)(2,1)S(1)}, bf16[1,1,1,2,1,24,512]{6,5,4,3,2,1,0:T(8,128)(2,1)S(1)}, u32[]{:S(2)}, u32[]{:S(2)}) collective-permute-start(bf16[1,1,1,2,1,24,512]{6,5,4,3,2,1,0:T(8,128)(2,1)S(1)} %dynamic-slice_convert_fusion.24), channel_id=1, source_target_pairs={{0,1},{1,0},{2,3},{3,2},{4,5},{5,4},{6,7},{7,6},{8,9},{9,8},{10,11... | collective-permute-start | bytes 147464 | tf_op jit(solution)/shard_map/ppermute | solution.py:119
  322.3 30.0 %slice-start.5 = ((s8[9437184]{0:T(1024)(128)(4,1)}), s8[4194304]{0:T(1024)(128)(4,1)S(1)}, s32[]{:S(2)}) async-start(s8[9437184]{0:T(1024)(128)(4,1)} %bitcast.185), calls=%async_computation.9 | async-start | bytes 8388608
  322.5 5.2 %collective-permute-start.17 = (bf16[1,1,1,2,2,24,768]{6,5,4,3,2,1,0:T(8,128)(2,1)S(1)}, bf16[1,1,1,2,2,24,768]{6,5,4,3,2,1,0:T(8,128)(2,1)S(1)}, u32[]{:S(2)}, u32[]{:S(2)}) collective-permute-start(bf16[1,1,1,2,2,24,768]{6,5,4,3,2,1,0:T(8,128)(2,1)S(1)} %dynamic-slice_convert_fusion.18), channel_id=1, source_target_pairs={{0,16},{1,17},{2,18},{3,19},{4,20},{5,21},{6,22},{7,23},{8,24},{9,... | collective-permute-start | bytes 442376 | tf_op jit(solution)/shard_map/ppermute | solution.py:119
  327.7 24.6 %slice-start.6 = ((s8[9437184]{0:T(1024)(128)(4,1)}), s8[4194304]{0:T(1024)(128)(4,1)S(1)}, s32[]{:S(2)}) async-start(s8[9437184]{0:T(1024)(128)(4,1)} %bitcast.185), calls=%async_computation.10 | async-start | bytes 8388608
  327.7 6.5 %collective-permute-start.18 = (bf16[1,1,1,2,1,24,768]{6,5,4,3,2,1,0:T(8,128)(2,1)S(1)}, bf16[1,1,1,2,1,24,768]{6,5,4,3,2,1,0:T(8,128)(2,1)S(1)}, u32[]{:S(2)}, u32[]{:S(2)}) collective-permute-start(bf16[1,1,1,2,1,24,768]{6,5,4,3,2,1,0:T(8,128)(2,1)S(1)} %dynamic-slice_convert_fusion.22), channel_id=1, source_target_pairs={{0,1},{1,0},{2,3},{3,2},{4,5},{5,4},{6,7},{7,6},{8,9},{9,8},{10,11... | collective-permute-start | bytes 221192 | tf_op jit(solution)/shard_map/ppermute | solution.py:119
  330.9 21.4 %slice-start.7 = ((s8[9437184]{0:T(1024)(128)(4,1)}), s8[1048576]{0:T(1024)(128)(4,1)S(1)}, s32[]{:S(2)}) async-start(s8[9437184]{0:T(1024)(128)(4,1)} %bitcast.185), calls=%async_computation.11 | async-start | bytes 2097152
  331.0 19.4 %collective-permute-start.11 = (bf16[1,2,1,2,2,24,2304]{6,5,4,3,2,1,0:T(8,128)(2,1)S(1)}, bf16[1,2,1,2,2,24,2304]{6,5,4,3,2,1,0:T(8,128)(2,1)S(1)}, u32[]{:S(2)}, u32[]{:S(2)}) collective-permute-start(bf16[1,2,1,2,2,24,2304]{6,5,4,3,2,1,0:T(8,128)(2,1)S(1)} %dynamic-slice_convert_fusion.5), channel_id=1, source_target_pairs={{0,16},{1,17},{2,18},{3,19},{4,20},{5,21},{6,22},{7,23},{8,24},{9,... | collective-permute-start | bytes 2654216 | tf_op jit(solution)/shard_map/ppermute | solution.py:119
  332.6 4.7 %collective-permute-start.34 = (bf16[1,1,1,1,1,24,512]{6,5,4,3,2,1,0:T(8,128)(2,1)S(1)}, bf16[1,1,1,1,1,24,512]{6,5,4,3,2,1,0:T(8,128)(2,1)S(1)}, u32[]{:S(2)}, u32[]{:S(2)}) collective-permute-start(bf16[1,1,1,1,1,24,512]{6,5,4,3,2,1,0:T(8,128)(2,1)S(1)} %dynamic-slice_convert_fusion.27), channel_id=1, source_target_pairs={{0,2},{1,3},{2,0},{3,1},{4,6},{5,7},{6,4},{7,5},{8,10},{9,11},{10,... | collective-permute-start | bytes 73736 | tf_op jit(solution)/shard_map/ppermute | solution.py:119
  334.3 5.1 %collective-permute-start.19 = (bf16[1,1,1,1,1,24,768]{6,5,4,3,2,1,0:T(8,128)(2,1)S(1)}, bf16[1,1,1,1,1,24,768]{6,5,4,3,2,1,0:T(8,128)(2,1)S(1)}, u32[]{:S(2)}, u32[]{:S(2)}) collective-permute-start(bf16[1,1,1,1,1,24,768]{6,5,4,3,2,1,0:T(8,128)(2,1)S(1)} %dynamic-slice_convert_fusion.25), channel_id=1, source_target_pairs={{0,2},{1,3},{2,0},{3,1},{4,6},{5,7},{6,4},{7,5},{8,10},{9,11},{10,... | collective-permute-start | bytes 110600 | tf_op jit(solution)/shard_map/ppermute | solution.py:119
  350.6 11.8 %slice-start = ((s8[9437184]{0:T(1024)(128)(4,1)}), s8[4194304]{0:T(1024)(128)(4,1)S(1)}, s32[]{:S(2)}) async-start(s8[9437184]{0:T(1024)(128)(4,1)} %bitcast.176), calls=%async_computation.4 | async-start | bytes 8388608
  350.7 9.8 %collective-permute-start.12 = (bf16[1,2,1,2,1,24,2304]{6,5,4,3,2,1,0:T(8,128)(2,1)S(1)}, bf16[1,2,1,2,1,24,2304]{6,5,4,3,2,1,0:T(8,128)(2,1)S(1)}, u32[]{:S(2)}, u32[]{:S(2)}) collective-permute-start(bf16[1,2,1,2,1,24,2304]{6,5,4,3,2,1,0:T(8,128)(2,1)S(1)} %dynamic-slice_convert_fusion.9), channel_id=1, source_target_pairs={{0,1},{1,0},{2,3},{3,2},{4,5},{5,4},{6,7},{7,6},{8,9},{9,8},{10,11... | collective-permute-start | bytes 1327112 | tf_op jit(solution)/shard_map/ppermute | solution.py:119
  355.9 24.1 %collective-permute-start.21 = (bf16[1,2,1,2,2,24,3072]{6,5,4,3,2,1,0:T(8,128)(2,1)S(1)}, bf16[1,2,1,2,2,24,3072]{6,5,4,3,2,1,0:T(8,128)(2,1)S(1)}, u32[]{:S(2)}, u32[]{:S(2)}) collective-permute-start(bf16[1,2,1,2,2,24,3072]{6,5,4,3,2,1,0:T(8,128)(2,1)S(1)} %dynamic-slice_convert_fusion.4), channel_id=1, source_target_pairs={{0,16},{1,17},{2,18},{3,19},{4,20},{5,21},{6,22},{7,23},{8,24},{9,... | collective-permute-start | bytes 3538952 | tf_op jit(solution)/shard_map/ppermute | solution.py:119
  360.6 9.3 %collective-permute-start.13 = (bf16[1,2,1,1,1,24,2304]{6,5,4,3,2,1,0:T(8,128)(2,1)S(1)}, bf16[1,2,1,1,1,24,2304]{6,5,4,3,2,1,0:T(8,128)(2,1)S(1)}, u32[]{:S(2)}, u32[]{:S(2)}) collective-permute-start(bf16[1,2,1,1,1,24,2304]{6,5,4,3,2,1,0:T(8,128)(2,1)S(1)} %dynamic-slice_convert_fusion.14), channel_id=1, source_target_pairs={{0,2},{1,3},{2,0},{3,1},{4,6},{5,7},{6,4},{7,5},{8,10},{9,11},{10,... | collective-permute-start | bytes 663560 | tf_op jit(solution)/shard_map/ppermute | solution.py:119
  364.9 32.0 %collective-permute-start.26 = (bf16[2,1,1,2,2,96,768]{6,5,4,3,2,1,0:T(8,128)(2,1)S(1)}, bf16[2,1,1,2,2,96,768]{6,5,4,3,2,1,0:T(8,128)(2,1)S(1)}, u32[]{:S(2)}, u32[]{:S(2)}) collective-permute-start(bf16[2,1,1,2,2,96,768]{6,5,4,3,2,1,0:T(8,128)(2,1)S(1)} %dynamic-slice_convert_fusion.3), channel_id=1, source_target_pairs={{0,8},{1,9},{2,10},{3,11},{4,12},{5,13},{6,14},{7,15},{8,0},{9,1},... | collective-permute-start | bytes 3538952 | tf_op jit(solution)/shard_map/ppermute | solution.py:119
  369.9 26.3 %collective-permute-start.14 = (bf16[1,1,1,1,1,24,2304]{6,5,4,3,2,1,0:T(8,128)(2,1)S(1)}, bf16[1,1,1,1,1,24,2304]{6,5,4,3,2,1,0:T(8,128)(2,1)S(1)}, u32[]{:S(2)}, u32[]{:S(2)}) collective-permute-start(bf16[1,1,1,1,1,24,2304]{6,5,4,3,2,1,0:T(8,128)(2,1)S(1)} %dynamic-slice_convert_fusion.20), channel_id=1, source_target_pairs={{0,8},{1,9},{2,10},{3,11},{4,12},{5,13},{6,14},{7,15},{8,0},{9,1},... | collective-permute-start | bytes 331784 | tf_op jit(solution)/shard_map/ppermute | solution.py:119
  380.4 23.3 %collective-permute-start.22 = (bf16[1,1,1,2,2,24,3072]{6,5,4,3,2,1,0:T(8,128)(2,1)S(1)}, bf16[1,1,1,2,2,24,3072]{6,5,4,3,2,1,0:T(8,128)(2,1)}, u32[]{:S(2)}, u32[]{:S(2)}) collective-permute-start(bf16[1,1,1,2,2,24,3072]{6,5,4,3,2,1,0:T(8,128)(2,1)S(1)} %dynamic-slice_convert_fusion.7), channel_id=1, source_target_pairs={{0,8},{1,9},{2,10},{3,11},{4,12},{5,13},{6,14},{7,15},{8,0},{9,1},... | collective-permute-start | bytes 1769480 | tf_op jit(solution)/shard_map/ppermute | solution.py:119
  398.6 10.1 %collective-permute-start.27 = (bf16[1,1,1,2,2,96,768]{6,5,4,3,2,1,0:T(8,128)(2,1)S(1)}, bf16[1,1,1,2,2,96,768]{6,5,4,3,2,1,0:T(8,128)(2,1)}, u32[]{:S(2)}, u32[]{:S(2)}) collective-permute-start(bf16[1,1,1,2,2,96,768]{6,5,4,3,2,1,0:T(8,128)(2,1)S(1)} %dynamic-slice_convert_fusion.6), channel_id=1, source_target_pairs={{0,16},{1,17},{2,18},{3,19},{4,20},{5,21},{6,22},{7,23},{8,24},{9,... | collective-permute-start | bytes 1769480 | tf_op jit(solution)/shard_map/ppermute | solution.py:119
  405.0 9.6 %collective-permute-start.23 = (bf16[1,1,1,2,1,24,3072]{6,5,4,3,2,1,0:T(8,128)(2,1)S(1)}, bf16[1,1,1,2,1,24,3072]{6,5,4,3,2,1,0:T(8,128)(2,1)S(1)}, u32[]{:S(2)}, u32[]{:S(2)}) collective-permute-start(bf16[1,1,1,2,1,24,3072]{6,5,4,3,2,1,0:T(8,128)(2,1)S(1)} %dynamic-slice_convert_fusion.12), channel_id=1, source_target_pairs={{0,1},{1,0},{2,3},{3,2},{4,5},{5,4},{6,7},{7,6},{8,9},{9,8},{10,11... | collective-permute-start | bytes 884744 | tf_op jit(solution)/shard_map/ppermute | solution.py:119
  409.9 7.9 %collective-permute-start.28 = (bf16[1,1,1,2,1,96,768]{6,5,4,3,2,1,0:T(8,128)(2,1)S(1)}, bf16[1,1,1,2,1,96,768]{6,5,4,3,2,1,0:T(8,128)(2,1)S(1)}, u32[]{:S(2)}, u32[]{:S(2)}) collective-permute-start(bf16[1,1,1,2,1,96,768]{6,5,4,3,2,1,0:T(8,128)(2,1)S(1)} %dynamic-slice_convert_fusion.11), channel_id=1, source_target_pairs={{0,1},{1,0},{2,3},{3,2},{4,5},{5,4},{6,7},{7,6},{8,9},{9,8},{10,11... | collective-permute-start | bytes 884744 | tf_op jit(solution)/shard_map/ppermute | solution.py:119
  414.7 7.7 %collective-permute-start.24 = (bf16[1,1,1,1,1,24,3072]{6,5,4,3,2,1,0:T(8,128)(2,1)S(1)}, bf16[1,1,1,1,1,24,3072]{6,5,4,3,2,1,0:T(8,128)(2,1)S(1)}, u32[]{:S(2)}, u32[]{:S(2)}) collective-permute-start(bf16[1,1,1,1,1,24,3072]{6,5,4,3,2,1,0:T(8,128)(2,1)S(1)} %dynamic-slice_convert_fusion.17), channel_id=1, source_target_pairs={{0,2},{1,3},{2,0},{3,1},{4,6},{5,7},{6,4},{7,5},{8,10},{9,11},{10,... | collective-permute-start | bytes 442376 | tf_op jit(solution)/shard_map/ppermute | solution.py:119
  417.9 7.7 %collective-permute-start.29 = (bf16[1,1,1,1,1,96,768]{6,5,4,3,2,1,0:T(8,128)(2,1)S(1)}, bf16[1,1,1,1,1,96,768]{6,5,4,3,2,1,0:T(8,128)(2,1)S(1)}, u32[]{:S(2)}, u32[]{:S(2)}) collective-permute-start(bf16[1,1,1,1,1,96,768]{6,5,4,3,2,1,0:T(8,128)(2,1)S(1)} %dynamic-slice_convert_fusion.16), channel_id=1, source_target_pairs={{0,2},{1,3},{2,0},{3,1},{4,6},{5,7},{6,4},{7,5},{8,10},{9,11},{10,... | collective-permute-start | bytes 442376 | tf_op jit(solution)/shard_map/ppermute | solution.py:119
  (40 other events, 182.3 us)
Sparse Core Ops, SparseCore 0:
  11.4 111.7 all-gather.2
  125.9 62.5 all-gather.4

commit v9 on v7

--- a/solution.py
+++ b/solution.py
@@ -353,14 +353,29 @@
         small_grads = (grad_wave_table, grad_norm1_gain, grad_norm1_bias, grad_norm2_gain,
                        grad_norm2_bias, grad_mlp_in_bias, grad_mlp_out_bias, grad_dec_bias,
                        grad_mask_token)
-        packed_sg, sg_widths = pack_rows(small_grads, n_dev, jnp.float32)
-        reduced_sg = rs_chain(packed_sg, n_bits, orders["yz"])
-        (sum_wave, sum_g1, sum_b1, sum_g2, sum_b2, sum_ib, sum_ob, sum_db,
-         sum_mask) = unpack_rows(reduced_sg, small_grads, sg_widths, n_dev, 1)
-        sum_dec = rs_chain(grad_dec_weight, n_bits, orders["y"])
+        rows_block = grad_out_weight.shape[0] // n_dev
+        sg_flat = [g.reshape(n_dev, -1) for g in small_grads]
+        sg_widths = [f.shape[1] for f in sg_flat]
+        sg_cols = -(-sum(sg_widths) // (rows_block * 128)) * 128
+        sg_pad = rows_block * sg_cols - sum(sg_widths)
+        sg_block = jnp.concatenate(
+            sg_flat + [jnp.zeros((n_dev, sg_pad), jnp.float32)], axis=1
+        ).reshape(n_dev * rows_block, sg_cols)
+        joined = jnp.concatenate([grad_out_weight, grad_dec_weight, sg_block], axis=1)
+        reduced_joined = rs_chain(joined, n_bits, orders["yz"])
+        out_cols = grad_out_weight.shape[1]
+        dec_cols = grad_dec_weight.shape[1]
+        sum_out = reduced_joined[:, :out_cols]
+        sum_dec = reduced_joined[:, out_cols : out_cols + dec_cols]
+        sg_sum = reduced_joined[:, out_cols + dec_cols :].reshape(-1)
+        sg_parts = []
+        offset = 0
+        for g, width in zip(small_grads, sg_widths):
+            sg_parts.append(sg_sum[offset : offset + width].reshape((g.shape[0] // n_dev,) + g.shape[1:]))
+            offset += width
+        (sum_wave, sum_g1, sum_b1, sum_g2, sum_b2, sum_ib, sum_ob, sum_db, sum_mask) = sg_parts
         sum_mlp_out = rs_chain(grad_mlp_out, n_bits, orders["x"])
         sum_mlp_in = rs_chain(grad_mlp_in, n_bits, orders["y"])
-        sum_out = rs_chain(grad_out_weight, n_bits, orders["x"])
         sum_qkv = rs_chain(grad_qkv_weight, n_bits, orders["yz"])
         summed = (sum_wave, sum_g1, sum_b1, sum_qkv, sum_out, sum_g2, sum_b2, sum_mlp_in,
                   sum_ib, sum_mlp_out, sum_ob, sum_dec, sum_db, sum_mask)

time: 435 us -> 429 us (0.986)
  local copies, waits for them, and re-layouts: 62.2 us -> 72.3 us
  starting transfers between devices: 48 us -> 39.3 us
  waiting for transfers between devices: 204 us -> 197 us
    ppermute x30 -> x20, starting transfers between devices: 31 us -> 22.5 us  [rs_chain(): lax.ppermute(send.astype(jnp.bfloat16), AX, [(i, i ^ 1 << bit) for i in r...]
    convert_element_type x30 -> x20, local copies, waits for them, and re-layouts: 11.5 us -> 5.66 us  [rs_chain(): send.astype(jnp.bfloat16)]
    dot_general x5, matrix products: 16 us -> 10.4 us  [inner_rows(): lax.dot_general(left_op, right_op, (((0,), (0,)), ((), ())), preferred_el...]
    ppermute x30 -> x20, waiting for transfers between devices: 88.1 us -> 82.6 us  [rs_chain(): lax.ppermute(send.astype(jnp.bfloat16), AX, [(i, i ^ 1 << bit) for i in r...]
    reshape x9 -> x10, local copies, waits for them, and re-layouts: 0.74 us -> 5.6 us  [the longest x9 4.99 us: local(): sg_flat = [g.reshape(n_dev, -1) for g in small_grads]]
    unnamed x109 -> x136, local copies, waits for them, and re-layouts: 12.8 us -> 17.1 us
    add x24 -> x16, other arithmetic: 14 us -> 13.3 us  [rs_chain(): current = keep + moved.astype(jnp.float32)]
  transfers between devices with their start and end apart: 39 -> 29, of which waited for: 25 -> 21; matrix products, arithmetic and copies ran while one was open for 23% -> 26% of each run, Pallas kernels for 0% -> 0%
where the time goes in v9:
time: 429 us; the launch traced here: 424 us
  waiting for transfers between devices  197 us (46%)
  local copies, waits for them, and re-layouts  72.3 us (17%)
  matrix products  67.4 us (16%)
  starting transfers between devices  39.3 us (9%)
  other arithmetic  32.7 us (8%)
  between operations  15.6 us (4%)
    ppermute x20, waiting for transfers between devices, rs_chain(): lax.ppermute(send.astype(jnp.bfloat16), AX, [(i, i ^ 1 << bit) for i in r...  82.6 us
    ppermute x5, waiting for transfers between devices, ag_chain(): moved = lax.ppermute(current, AX, [(i, i ^ 1 << bit) for i in range(n_dev)])  54 us
    all_gather x1, waiting for transfers between devices, local(): outer_full = lax.all_gather(mlp_out, AX, axis=0, tiled=True)  29.5 us
    all_gather x1, waiting for transfers between devices, local(): lax.all_gather(jnp.concatenate(wide, axis=1), AX, axis=0, tiled=True)  27.3 us
    dot_general x5, matrix products, outer_cols(): lax.dot_general(left_op, right_op, (((1,), (1,)), ((), ())), preferred_el...  23.7 us
    ppermute x20, starting transfers between devices, rs_chain(): lax.ppermute(send.astype(jnp.bfloat16), AX, [(i, i ^ 1 << bit) for i in r...  22.5 us
    dot_general x5, matrix products, product(): return jnp.dot(left_op, right_op, preferred_element_type=jnp.float32)  17.4 us
    unnamed x136, local copies, waits for them, and re-layouts  17.1 us
  transfers between devices with their start and end apart: 29, of which 21 were waited for; matrix products, arithmetic and copies ran while one was open for 26% of the time, Pallas kernels for 0%

profile of v9, /device:TPU:0, one launch (start us, length us, event | category | flops | bytes accessed | tf_op | source)
XLA Modules:
  0.0 424.5 jit_solution(15637993287099463248)
XLA Ops:
  10.7 4.1 collective-permute-start
  14.8 4.0 all-to-all-start.1
  20.7 48.3 %collective-permute-done.1 = bf16[1,1,1,2,1,1,8,512]{7,6,4,3,2,1,0,5:T(8,128)(2,1)S(1)} collective-permute-done((bf16[1,1,1,2,1,1,8,512]{7,6,4,3,2,1,0,5:T(8,128)(2,1)S(1)}, bf16[1,1,1,2,1,1,8,512]{7,6,4,3,2,1,0,5:T(8,128)(2,1)S(1)}, u32[]{:S(2)}, u32[]{:S(2)}) %collective-permute-start.1) | collective-permute-done | bytes 16416 | tf_op jit(solution)/shard_map/ppermute | solution.py:133
  70.6 2.3 collective-permute-done.2
  74.9 2.4 collective-permute-done.3
  82.3 3.7 all-to-all-done.1
  93.1 27.3 %all-gather.3.cloned.1.call-done = bf16[768,6656]{1,0:T(8,128)(2,1)} async-done(((bf16[24,6656]{1,0:T(8,128)(2,1)}), bf16[768,6656]{1,0:T(8,128)(2,1)}) %all-gather.3.cloned.1.call-update) | async-done | bytes 10223632 | tf_op jit(solution)/shard_map/all_gather | solution.py:247
  120.4 4.0 convolution_convert_fusion
  125.4 2.3 copy.118
  127.7 2.9 reshape.314
  131.8 2.2 reshape.316
  135.2 2.2 reshape.315
  138.5 4.8 %fusion.80 = (f32[2,12,256]{2,1,0:T(8,128)S(1)}, f32[2,12,256,256]{2,3,1,0:T(8,128)S(1)}) fusion(f32[2,12,256,256]{2,3,1,0:T(8,128)S(1)} %fusion.58), kind=kOutput, calls=%fused_computation.184 | output fusion | flops 6291711 | bytes 12607488 | tf_op jit(solution)/shard_map/sub | solution.py:167
  143.9 2.5 copy-done.1
  150.3 5.6 %multiply_convert_fusion.1 = (bf16[512,3072]{1,0:T(8,128)(2,1)}, f32[512,3072]{1,0:T(8,128)}) fusion(f32[3072]{0:T(1024)S(1)} %reshape.346, bf16[768,6656]{1,0:T(8,128)(2,1)S(1)} %bitcast.181, f32[512,768]{1,0:T(8,128)S(1)} %get-tuple-element.60, f32[768]{0:T(1024)S(1)} %reshape.345, f32[768]{0:T(1024)S(1)} %reshape.344, f32[512]{0:T(512)S(1)} %add_rsqrt_fusion, ...), kind=kOutput, calls=%fused_computation.11 | convolution fusion | flops 2427322368 | bytes 15753216 | tf_op jit(solution)/shard_map/dot_general | solution.py:21
  155.8 29.5 %all-gather.5.cloned.1.call-done = bf16[3072,768]{1,0:T(8,128)(2,1)} async-done(((bf16[96,768]{1,0:T(8,128)(2,1)}), bf16[3072,768]{1,0:T(8,128)(2,1)}) %all-gather.5.cloned.1.call-update) | async-done | bytes 4718608 | tf_op jit(solution)/shard_map/all_gather | solution.py:254
  185.3 8.1 %convert_reduce_fusion = (f32[3072]{0:T(1024)}, bf16[512,3072]{1,0:T(8,128)(2,1)S(1)}) fusion(f32[512,3072]{1,0:T(8,128)} %get-tuple-element.62, f32[3072]{0:T(1024)S(1)} %reshape.346, bf16[3072,768]{1,0:T(8,128)(2,1)} %all-gather.5.cloned.1.call-done, f32[512,768]{1,0:T(8,128)S(1)} %fusion.49), kind=kOutput, calls=%fused_computation.8 | convolution fusion | flops 2436756480 | bytes 15753216 | tf_op jit(solution)/shard_map/dot_general | solution.py:31
  193.4 7.1 %multiply_reduce_fusion.2 = (f32[768]{0:T(1024)}, f32[512]{0:T(512)S(1)}, f32[512]{0:T(512)S(1)}, f32[768]{0:T(1024)}, f32[512,768]{1,0:T(8,128)S(1)}) fusion(f32[512,768]{1,0:T(8,128)S(1)} %get-tuple-element.60, f32[512]{0:T(512)S(1)} %add_rsqrt_fusion, f32[512]{0:T(512)S(1)} %broadcast_multiply_fusion.4, f32[768]{0:T(1024)S(1)} %reshape.344, ...), kind=kOutput, calls=%fused_computation.54 | convolution fusion | flops 2419455488 | bytes 11027456 | tf_op jit(solution)/shard_map/dot_general | solution.py:31
  206.3 4.2 %fusion.33 = bf16[2,256,12,64]{1,3,2,0:T(8,128)(2,1)S(1)} fusion(bf16[2,256,12,64]{1,0,3,2:T(2,128)(2,1)} %reshape.320, f32[2,12,256,256]{2,3,1,0:T(8,128)} %copy-done.1, f32[2,12,256]{2,1,0:T(8,128)S(1)} %get-tuple-element.57), kind=kOutput, calls=%fused_computation.79 | convolution fusion | flops 204865536 | bytes 7888896 | tf_op jit(solution)/shard_map/chqk,cqhd->ckhd/dot_general | solution.py:179
  211.1 3.8 multiply_reduce_fusion
  214.9 4.3 %multiply_convert_fusion = bf16[2,12,256,256]{2,3,1,0:T(8,128)(2,1)S(1)} fusion(f32[2,12,256,256]{2,3,1,0:T(8,128)} %get-tuple-element.65, f32[2,12,256]{2,1,0:T(8,128)S(1)} %get-tuple-element.64, f32[2,12,256,256]{2,3,1,0:T(8,128)S(1)} %bitcast.152, f32[2,12,256]{2,1,0:T(8,128)S(1)} %get-tuple-element.57), kind=kLoop, calls=%fused_computation.9 | loop fusion | flops 6291456 | bytes 15777792 | tf_op jit(solution)/shard_map/convert_element_type | solution.py:186
  222.9 5.0 %add_convert_fusion = bf16[512,768]{1,0:T(8,128)(2,1)S(1)} fusion(f32[512,768]{1,0:T(8,128)S(1)} %copy-done.7, bf16[512,3072]{1,0:T(8,128)(2,1)S(1)} %copy-done.20, bf16[3072,768]{1,0:T(8,128)(2,1)} %all-gather.5.cloned.1.call-done, f32[768]{0:T(1024)S(1)} %reshape.347), kind=kOutput, calls=%fused_computation.62 | convolution fusion | flops 2417098752 | bytes 10226688 | tf_op jit(solution)/shard_map/dot_general | solution.py:21
  231.3 3.5 copy.127
  234.8 3.5 all-to-all-start
  245.8 2.3 copy.142
  248.1 5.8 %multiply_reduce_fusion.3 = (f32[768]{0:T(1024)}, f32[512]{0:T(512)S(1)}, f32[512]{0:T(512)S(1)}, f32[768]{0:T(1024)}, f32[512,768]{1,0:T(8,128)S(1)}) fusion(f32[2,256,768]{2,1,0:T(8,128)S(1)} %copy-done.3, f32[512]{0:T(512)S(1)} %bitcast.188, f32[512]{0:T(512)S(1)} %bitcast.191, f32[768]{0:T(1024)S(1)} %reshape.342, ...), kind=kOutput, calls=%fused_computation.55 | convolution fusion | flops 1822553600 | bytes 9061376 | tf_op jit(solution)/shard_map/dot_general | solution.py:31
  260.8 2.4 concatenate.42
  263.1 2.2 copy.163
  265.4 2.3 copy.145
  272.8 3.1 fusion.75
  281.5 2.7 fusion.70
  284.2 10.9 %collective-permute-done.6 = bf16[1,2,1,2,2,24,1536]{6,5,4,3,2,1,0:T(8,128)(2,1)S(1)} collective-permute-done((bf16[1,2,1,2,2,24,1536]{6,5,4,3,2,1,0:T(8,128)(2,1)S(1)}, bf16[1,2,1,2,2,24,1536]{6,5,4,3,2,1,0:T(8,128)(2,1)S(1)}, u32[]{:S(2)}, u32[]{:S(2)}) %collective-permute-start.6) | collective-permute-done | bytes 589856 | tf_op jit(solution)/shard_map/ppermute | solution.py:119
  300.4 3.5 collective-permute-done.7
  304.0 3.4 collective-permute-start.8
  309.3 4.1 collective-permute-done.8
  322.3 15.1 %collective-permute-done.11 = bf16[1,2,1,2,2,24,2304]{6,5,4,3,2,1,0:T(8,128)(2,1)} collective-permute-done((bf16[1,2,1,2,2,24,2304]{6,5,4,3,2,1,0:T(8,128)(2,1)}, bf16[1,2,1,2,2,24,2304]{6,5,4,3,2,1,0:T(8,128)(2,1)}, u32[]{:S(2)}, u32[]{:S(2)}) %collective-permute-start.11) | collective-permute-done | bytes 884768 | tf_op jit(solution)/shard_map/ppermute | solution.py:119
  339.4 4.0 convert_add_fusion.1
  344.8 4.7 %collective-permute-done.12 = bf16[1,2,1,2,1,24,2304]{6,5,4,3,2,1,0:T(8,128)(2,1)S(1)} collective-permute-done((bf16[1,2,1,2,1,24,2304]{6,5,4,3,2,1,0:T(8,128)(2,1)S(1)}, bf16[1,2,1,2,1,24,2304]{6,5,4,3,2,1,0:T(8,128)(2,1)S(1)}, u32[]{:S(2)}, u32[]{:S(2)}) %collective-permute-start.12) | collective-permute-done | bytes 442400 | tf_op jit(solution)/shard_map/ppermute | solution.py:119
  349.6 2.1 collective-permute-start.13
  351.7 2.4 convert_add_fusion
  354.9 5.3 %collective-permute-done.13 = bf16[1,2,1,1,1,24,2304]{6,5,4,3,2,1,0:T(8,128)(2,1)S(1)} collective-permute-done((bf16[1,2,1,1,1,24,2304]{6,5,4,3,2,1,0:T(8,128)(2,1)S(1)}, bf16[1,2,1,1,1,24,2304]{6,5,4,3,2,1,0:T(8,128)(2,1)S(1)}, u32[]{:S(2)}, u32[]{:S(2)}) %collective-permute-start.13) | collective-permute-done | bytes 221216 | tf_op jit(solution)/shard_map/ppermute | solution.py:119
  361.9 7.6 %collective-permute-done.16 = bf16[1,2,1,2,2,24,3072]{6,5,4,3,2,1,0:T(8,128)(2,1)S(1)} collective-permute-done((bf16[1,2,1,2,2,24,3072]{6,5,4,3,2,1,0:T(8,128)(2,1)S(1)}, bf16[1,2,1,2,2,24,3072]{6,5,4,3,2,1,0:T(8,128)(2,1)S(1)}, u32[]{:S(2)}, u32[]{:S(2)}) %collective-permute-start.16) | collective-permute-done | bytes 1179680 | tf_op jit(solution)/shard_map/ppermute | solution.py:119
  370.9 14.6 %collective-permute-done.14 = bf16[1,1,1,1,1,24,2304]{6,5,4,3,2,1,0:T(8,128)(2,1)S(1)} collective-permute-done((bf16[1,1,1,1,1,24,2304]{6,5,4,3,2,1,0:T(8,128)(2,1)S(1)}, bf16[1,1,1,1,1,24,2304]{6,5,4,3,2,1,0:T(8,128)(2,1)S(1)}, u32[]{:S(2)}, u32[]{:S(2)}) %collective-permute-start.14) | collective-permute-done | bytes 110624 | tf_op jit(solution)/shard_map/ppermute | solution.py:119
  388.1 3.4 copy.128
  391.6 3.4 collective-permute-done.17
  401.1 5.5 %collective-permute-done.18 = bf16[1,1,1,2,1,24,3072]{6,5,4,3,2,1,0:T(8,128)(2,1)S(1)} collective-permute-done((bf16[1,1,1,2,1,24,3072]{6,5,4,3,2,1,0:T(8,128)(2,1)S(1)}, bf16[1,1,1,2,1,24,3072]{6,5,4,3,2,1,0:T(8,128)(2,1)S(1)}, u32[]{:S(2)}, u32[]{:S(2)}) %collective-permute-start.18) | collective-permute-done | bytes 294944 | tf_op jit(solution)/shard_map/ppermute | solution.py:119
  406.9 3.3 collective-permute-done.23
  411.7 3.4 collective-permute-done.19
  (305 shorter events, 103.8 us)
Async XLA Ops:
  7.2 113.2 %all-gather.3.cloned.1.call-start = ((), (), s32[]{:S(2)}) async-start(), calls=%async_computation.2 | async-start | bytes 10543104 | tf_op jit(solution)/shard_map/all_gather | solution.py:247
  10.7 64.0 %copy-start.50 = (s32[2,256]{1,0:T(2,128)S(1)}, s32[2,256]{1,0:T(2,128)}, u32[]{:S(2)}) copy-start(s32[2,256]{1,0:T(2,128)} %param.20) | copy-start | bytes 6148
  10.7 66.8 %copy-start.51 = (s32[2,13]{1,0:T(2,128)S(1)}, s32[2,13]{1,0:T(2,128)}, u32[]{:S(2)}) copy-start(s32[2,13]{1,0:T(2,128)} %param.19) | copy-start | bytes 316
  10.7 8.2 %collective-permute-start = (bf16[1,1,1,1,1,1,8,512]{7,6,4,3,2,1,0,5:T(8,128)(2,1)S(1)}, bf16[1,1,1,1,1,1,8,512]{7,6,4,3,2,1,0,5:T(8,128)(2,1)S(1)}, u32[]{:S(2)}, u32[]{:S(2)}) collective-permute-start(bf16[1,1,1,1,1,1,8,512]{7,6,4,3,2,1,0,5:T(8,128)(2,1)S(1)} %bitcast.183), channel_id=1, source_target_pairs={{0,2},{1,3},{2,0},{3,1},{4,6},{5,7},{6,4},{7,5},{8,10},{9,11},{10,... | collective-permute-start | bytes 24584 | tf_op jit(solution)/shard_map/ppermute | solution.py:133
  14.8 71.2 %all-to-all-start.1 = ((bf16[64,32,512]{2,1,0:T(8,128)(2,1)}), bf16[64,32,512]{2,1,0:T(8,128)(2,1)}, u32[]{:S(2)}, u32[]{:S(2)}) async-start(bf16[64,32,512]{2,1,0:T(8,128)(2,1)} %param.35), calls=%async_computation.1 | async-start | bytes 4194304 | tf_op jit(solution)/shard_map/all_to_all | solution.py:304
  18.8 60.7 %copy-start.23 = (bf16[2,256,768]{2,1,0:T(8,128)(2,1)S(1)}, bf16[2,256,768]{2,1,0:T(8,128)(2,1)}, u32[]{:S(2)}) copy-start(bf16[2,256,768]{2,1,0:T(8,128)(2,1)} %param.18) | copy-start | bytes 2359300
  18.8 166.5 %all-gather.5.cloned.1.call-start = ((), (), s32[]{:S(2)}) async-start(), calls=%async_computation.3 | async-start | bytes 4866048 | tf_op jit(solution)/shard_map/all_gather | solution.py:254
  18.9 50.1 %collective-permute-start.1 = (bf16[1,1,1,2,1,1,8,512]{7,6,4,3,2,1,0,5:T(8,128)(2,1)S(1)}, bf16[1,1,1,2,1,1,8,512]{7,6,4,3,2,1,0,5:T(8,128)(2,1)S(1)}, u32[]{:S(2)}, u32[]{:S(2)}) collective-permute-start(bf16[1,1,1,2,1,1,8,512]{7,6,4,3,2,1,0,5:T(8,128)(2,1)S(1)} %pad_maximum_fusion.9), channel_id=1, source_target_pairs={{0,1},{1,0},{2,3},{3,2},{4,5},{5,4},{6,7},{7,6},{8,9},{9,8},{10,11... | collective-permute-start | bytes 49160 | tf_op jit(solution)/shard_map/ppermute | solution.py:133
  69.0 4.0 collective-permute-start.2
  73.0 4.3 %collective-permute-start.3 = (bf16[2,1,1,2,2,1,8,512]{7,6,4,3,2,1,0,5:T(8,128)(2,1)S(1)}, bf16[2,1,1,2,2,1,8,512]{7,6,4,3,2,1,0,5:T(8,128)(2,1)S(1)}, u32[]{:S(2)}, u32[]{:S(2)}) collective-permute-start(bf16[2,1,1,2,2,1,8,512]{7,6,4,3,2,1,0,5:T(8,128)(2,1)S(1)} %pad_maximum_fusion.7), channel_id=1, source_target_pairs={{0,8},{1,9},{2,10},{3,11},{4,12},{5,13},{6,14},{7,15},{8,0},{9,1},... | collective-permute-start | bytes 196616 | tf_op jit(solution)/shard_map/ppermute | solution.py:133
  77.4 1.4 collective-permute-start.4
  80.1 67.4 %copy-start.2 = (f32[2,256,768]{2,1,0:T(8,128)}, f32[2,256,768]{2,1,0:T(8,128)S(1)}, u32[]{:S(2)}) copy-start(f32[2,256,768]{2,1,0:T(8,128)S(1)} %get-tuple-element.30) | copy-start | bytes 4718596
  80.4 69.9 %copy-start.44 = (f32[768]{0:T(1024)}, f32[768]{0:T(1024)S(1)}, u32[]{:S(2)}) copy-start(f32[768]{0:T(1024)S(1)} %reshape.345) | copy-start | bytes 9220
  80.5 120.0 %copy-start.38 = (f32[768]{0:T(1024)}, f32[768]{0:T(1024)S(1)}, u32[]{:S(2)}) copy-start(f32[768]{0:T(1024)S(1)} %reshape.344) | copy-start | bytes 9220
  138.5 9.0 %slice-start.5 = ((s8[10223616]{0:T(1024)(128)(4,1)}), s8[4194304]{0:T(1024)(128)(4,1)S(1)}, s32[]{:S(2)}) async-start(s8[10223616]{0:T(1024)(128)(4,1)} %bitcast.180), calls=%async_computation.9 | async-start | bytes 8388608
  149.3 51.2 %copy-start.6 = (f32[512,768]{1,0:T(8,128)}, f32[512,768]{1,0:T(8,128)S(1)}, u32[]{:S(2)}) copy-start(f32[512,768]{1,0:T(8,128)S(1)} %get-tuple-element.60) | copy-start | bytes 4718596
  149.3 51.2 %copy-start.36 = (f32[512]{0:T(512)}, f32[512]{0:T(512)S(1)}, u32[]{:S(2)}) copy-start(f32[512]{0:T(512)S(1)} %broadcast_multiply_fusion.4) | copy-start | bytes 6148
  149.6 50.9 %copy-start.42 = (f32[512]{0:T(512)}, f32[512]{0:T(512)S(1)}, u32[]{:S(2)}) copy-start(f32[512]{0:T(512)S(1)} %add_rsqrt_fusion) | copy-start | bytes 6148
  150.3 50.3 %copy-start.4 = (f32[512,768]{1,0:T(8,128)}, f32[512,768]{1,0:T(8,128)S(1)}, u32[]{:S(2)}) copy-start(f32[512,768]{1,0:T(8,128)S(1)} %fusion.49) | copy-start | bytes 4718596
  193.4 7.1 %copy-start.52 = (bf16[512,3072]{1,0:T(8,128)(2,1)}, bf16[512,3072]{1,0:T(8,128)(2,1)S(1)}, u32[]{:S(2)}) copy-start(bf16[512,3072]{1,0:T(8,128)(2,1)S(1)} %get-tuple-element.68) | copy-start | bytes 9437188
  234.8 153.3 %all-to-all-start = ((bf16[2,1024,512]{2,0,1:T(2,128)(2,1)}), bf16[2,1024,512]{2,0,1:T(2,128)(2,1)}, u32[]{:S(2)}, u32[]{:S(2)}) async-start(bf16[2,1024,512]{2,0,1:T(2,128)(2,1)} %copy.127), calls=%async_computation | async-start | bytes 4194304 | tf_op jit(solution)/shard_map/all_to_all | solution.py:303
  260.8 6.9 %copy-start.10 = (f32[512,768]{1,0:T(8,128)S(1)}, f32[512,768]{1,0:T(8,128)}, u32[]{:S(2)}) copy-start(f32[512,768]{1,0:T(8,128)} %copy-done.8) | copy-start | bytes 4718596
  271.7 6.3 %collective-permute-start.5 = (bf16[2,2,1,2,2,24,1536]{6,5,4,3,2,1,0:T(8,128)(2,1)S(1)}, bf16[2,2,1,2,2,24,1536]{6,5,4,3,2,1,0:T(8,128)(2,1)S(1)}, u32[]{:S(2)}, u32[]{:S(2)}) collective-permute-start(bf16[2,2,1,2,2,24,1536]{6,5,4,3,2,1,0:T(8,128)(2,1)S(1)} %dynamic-slice_convert_fusion.5), channel_id=1, source_target_pairs={{0,4},{1,5},{2,6},{3,7},{4,0},{5,1},{6,2},{7,3},{8,12},{9,13},{10,... | collective-permute-start | bytes 3538952 | tf_op jit(solution)/shard_map/ppermute | solution.py:119
  275.9 20.5 %copy-start.19 = (f32[768,3072]{1,0:T(8,128)}, f32[768,3072]{1,0:T(8,128)S(1)}, u32[]{:S(2)}) copy-start(f32[768,3072]{1,0:T(8,128)S(1)} %fusion.75) | copy-start | bytes 28311556
  278.5 16.6 %collective-permute-start.6 = (bf16[1,2,1,2,2,24,1536]{6,5,4,3,2,1,0:T(8,128)(2,1)S(1)}, bf16[1,2,1,2,2,24,1536]{6,5,4,3,2,1,0:T(8,128)(2,1)S(1)}, u32[]{:S(2)}, u32[]{:S(2)}) collective-permute-start(bf16[1,2,1,2,2,24,1536]{6,5,4,3,2,1,0:T(8,128)(2,1)S(1)} %dynamic-slice_convert_fusion.9), channel_id=1, source_target_pairs={{0,16},{1,17},{2,18},{3,19},{4,20},{5,21},{6,22},{7,23},{8,24},{9,... | collective-permute-start | bytes 1769480 | tf_op jit(solution)/shard_map/ppermute | solution.py:119
  280.2 27.1 %collective-permute-start.10 = (bf16[2,2,1,2,2,24,2304]{6,5,4,3,2,1,0:T(8,128)(2,1)S(1)}, bf16[2,2,1,2,2,24,2304]{6,5,4,3,2,1,0:T(8,128)(2,1)}, u32[]{:S(2)}, u32[]{:S(2)}) collective-permute-start(bf16[2,2,1,2,2,24,2304]{6,5,4,3,2,1,0:T(8,128)(2,1)S(1)} %dynamic-slice_convert_fusion.2), channel_id=1, source_target_pairs={{0,4},{1,5},{2,6},{3,7},{4,0},{5,1},{6,2},{7,3},{8,12},{9,13},{10,... | collective-permute-start | bytes 5308424 | tf_op jit(solution)/shard_map/ppermute | solution.py:119
  284.2 19.8 %copy-start = (f32[3072,768]{1,0:T(8,128)}, f32[3072,768]{1,0:T(8,128)S(1)}, u32[]{:S(2)}) copy-start(f32[3072,768]{1,0:T(8,128)S(1)} %fusion.70) | copy-start | bytes 28311556
  295.2 8.6 %collective-permute-start.7 = (bf16[1,2,1,2,1,24,1536]{6,5,4,3,2,1,0:T(8,128)(2,1)S(1)}, bf16[1,2,1,2,1,24,1536]{6,5,4,3,2,1,0:T(8,128)(2,1)S(1)}, u32[]{:S(2)}, u32[]{:S(2)}) collective-permute-start(bf16[1,2,1,2,1,24,1536]{6,5,4,3,2,1,0:T(8,128)(2,1)S(1)} %dynamic-slice_convert_fusion.13), channel_id=1, source_target_pairs={{0,1},{1,0},{2,3},{3,2},{4,5},{5,4},{6,7},{7,6},{8,9},{9,8},{10,11... | collective-permute-start | bytes 884744 | tf_op jit(solution)/shard_map/ppermute | solution.py:119
  298.1 41.3 %collective-permute-start.15 = (bf16[2,2,1,2,2,24,3072]{6,5,4,3,2,1,0:T(8,128)(2,1)}, bf16[2,2,1,2,2,24,3072]{6,5,4,3,2,1,0:T(8,128)(2,1)}, u32[]{:S(2)}, u32[]{:S(2)}) collective-permute-start(bf16[2,2,1,2,2,24,3072]{6,5,4,3,2,1,0:T(8,128)(2,1)} %dynamic-slice_convert_fusion.1), channel_id=1, source_target_pairs={{0,4},{1,5},{2,6},{3,7},{4,0},{5,1},{6,2},{7,3},{8,12},{9,13},{10,... | collective-permute-start | bytes 7077896 | tf_op jit(solution)/shard_map/ppermute | solution.py:119
  299.9 51.9 %collective-permute-start.20 = (bf16[2,2,1,2,2,96,768]{6,5,4,3,2,1,0:T(8,128)(2,1)}, bf16[2,2,1,2,2,96,768]{6,5,4,3,2,1,0:T(8,128)(2,1)}, u32[]{:S(2)}, u32[]{:S(2)}) collective-permute-start(bf16[2,2,1,2,2,96,768]{6,5,4,3,2,1,0:T(8,128)(2,1)} %dynamic-slice_convert_fusion), channel_id=1, source_target_pairs={{0,4},{1,5},{2,6},{3,7},{4,0},{5,1},{6,2},{7,3},{8,12},{9,13},{10,... | collective-permute-start | bytes 7077896 | tf_op jit(solution)/shard_map/ppermute | solution.py:119
  304.0 9.4 %collective-permute-start.8 = (bf16[1,2,1,1,1,24,1536]{6,5,4,3,2,1,0:T(8,128)(2,1)S(1)}, bf16[1,2,1,1,1,24,1536]{6,5,4,3,2,1,0:T(8,128)(2,1)S(1)}, u32[]{:S(2)}, u32[]{:S(2)}) collective-permute-start(bf16[1,2,1,1,1,24,1536]{6,5,4,3,2,1,0:T(8,128)(2,1)S(1)} %dynamic-slice_convert_fusion.17), channel_id=1, source_target_pairs={{0,2},{1,3},{2,0},{3,1},{4,6},{5,7},{6,4},{7,5},{8,10},{9,11},{10,... | collective-permute-start | bytes 442376 | tf_op jit(solution)/shard_map/ppermute | solution.py:119
  313.4 4.4 %collective-permute-start.9 = (bf16[1,1,1,1,1,24,1536]{6,5,4,3,2,1,0:T(8,128)(2,1)S(1)}, bf16[1,1,1,1,1,24,1536]{6,5,4,3,2,1,0:T(8,128)(2,1)S(1)}, u32[]{:S(2)}, u32[]{:S(2)}) collective-permute-start(bf16[1,1,1,1,1,24,1536]{6,5,4,3,2,1,0:T(8,128)(2,1)S(1)} %dynamic-slice_convert_fusion.19), channel_id=1, source_target_pairs={{0,8},{1,9},{2,10},{3,11},{4,12},{5,13},{6,14},{7,15},{8,0},{9,1},... | collective-permute-start | bytes 221192 | tf_op jit(solution)/shard_map/ppermute | solution.py:119
  316.2 21.2 %collective-permute-start.11 = (bf16[1,2,1,2,2,24,2304]{6,5,4,3,2,1,0:T(8,128)(2,1)}, bf16[1,2,1,2,2,24,2304]{6,5,4,3,2,1,0:T(8,128)(2,1)}, u32[]{:S(2)}, u32[]{:S(2)}) collective-permute-start(bf16[1,2,1,2,2,24,2304]{6,5,4,3,2,1,0:T(8,128)(2,1)} %dynamic-slice_convert_fusion.6), channel_id=1, source_target_pairs={{0,16},{1,17},{2,18},{3,19},{4,20},{5,21},{6,22},{7,23},{8,24},{9,... | collective-permute-start | bytes 2654216 | tf_op jit(solution)/shard_map/ppermute | solution.py:119
  338.7 13.0 %slice-start = ((s8[9437184]{0:T(1024)(128)(4,1)}), s8[4194304]{0:T(1024)(128)(4,1)S(1)}, s32[]{:S(2)}) async-start(s8[9437184]{0:T(1024)(128)(4,1)} %bitcast.148), calls=%async_computation.4 | async-start | bytes 8388608
  338.8 12.9 %slice-start.1 = ((s8[9437184]{0:T(1024)(128)(4,1)}), s8[4194304]{0:T(1024)(128)(4,1)S(1)}, s32[]{:S(2)}) async-start(s8[9437184]{0:T(1024)(128)(4,1)} %bitcast.148), calls=%async_computation.5 | async-start | bytes 8388608
  338.8 12.9 %slice-start.2 = ((s8[9437184]{0:T(1024)(128)(4,1)}), s8[1048576]{0:T(1024)(128)(4,1)S(1)}, s32[]{:S(2)}) async-start(s8[9437184]{0:T(1024)(128)(4,1)} %bitcast.148), calls=%async_computation.6 | async-start | bytes 2097152
  338.8 10.6 %collective-permute-start.12 = (bf16[1,2,1,2,1,24,2304]{6,5,4,3,2,1,0:T(8,128)(2,1)S(1)}, bf16[1,2,1,2,1,24,2304]{6,5,4,3,2,1,0:T(8,128)(2,1)S(1)}, u32[]{:S(2)}, u32[]{:S(2)}) collective-permute-start(bf16[1,2,1,2,1,24,2304]{6,5,4,3,2,1,0:T(8,128)(2,1)S(1)} %dynamic-slice_convert_fusion.10), channel_id=1, source_target_pairs={{0,1},{1,0},{2,3},{3,2},{4,5},{5,4},{6,7},{7,6},{8,9},{9,8},{10,11... | collective-permute-start | bytes 1327112 | tf_op jit(solution)/shard_map/ppermute | solution.py:119
  343.6 25.9 %collective-permute-start.16 = (bf16[1,2,1,2,2,24,3072]{6,5,4,3,2,1,0:T(8,128)(2,1)S(1)}, bf16[1,2,1,2,2,24,3072]{6,5,4,3,2,1,0:T(8,128)(2,1)S(1)}, u32[]{:S(2)}, u32[]{:S(2)}) collective-permute-start(bf16[1,2,1,2,2,24,3072]{6,5,4,3,2,1,0:T(8,128)(2,1)S(1)} %dynamic-slice_convert_fusion.4), channel_id=1, source_target_pairs={{0,16},{1,17},{2,18},{3,19},{4,20},{5,21},{6,22},{7,23},{8,24},{9,... | collective-permute-start | bytes 3538952 | tf_op jit(solution)/shard_map/ppermute | solution.py:119
  349.6 10.7 %collective-permute-start.13 = (bf16[1,2,1,1,1,24,2304]{6,5,4,3,2,1,0:T(8,128)(2,1)S(1)}, bf16[1,2,1,1,1,24,2304]{6,5,4,3,2,1,0:T(8,128)(2,1)S(1)}, u32[]{:S(2)}, u32[]{:S(2)}) collective-permute-start(bf16[1,2,1,1,1,24,2304]{6,5,4,3,2,1,0:T(8,128)(2,1)S(1)} %dynamic-slice_convert_fusion.14), channel_id=1, source_target_pairs={{0,2},{1,3},{2,0},{3,1},{4,6},{5,7},{6,4},{7,5},{8,10},{9,11},{10,... | collective-permute-start | bytes 663560 | tf_op jit(solution)/shard_map/ppermute | solution.py:119
  354.3 32.0 %collective-permute-start.21 = (bf16[2,1,1,2,2,96,768]{6,5,4,3,2,1,0:T(8,128)(2,1)S(1)}, bf16[2,1,1,2,2,96,768]{6,5,4,3,2,1,0:T(8,128)(2,1)S(1)}, u32[]{:S(2)}, u32[]{:S(2)}) collective-permute-start(bf16[2,1,1,2,2,96,768]{6,5,4,3,2,1,0:T(8,128)(2,1)S(1)} %dynamic-slice_convert_fusion.3), channel_id=1, source_target_pairs={{0,8},{1,9},{2,10},{3,11},{4,12},{5,13},{6,14},{7,15},{8,0},{9,1},... | collective-permute-start | bytes 3538952 | tf_op jit(solution)/shard_map/ppermute | solution.py:119
  360.3 25.2 %collective-permute-start.14 = (bf16[1,1,1,1,1,24,2304]{6,5,4,3,2,1,0:T(8,128)(2,1)S(1)}, bf16[1,1,1,1,1,24,2304]{6,5,4,3,2,1,0:T(8,128)(2,1)S(1)}, u32[]{:S(2)}, u32[]{:S(2)}) collective-permute-start(bf16[1,1,1,1,1,24,2304]{6,5,4,3,2,1,0:T(8,128)(2,1)S(1)} %dynamic-slice_convert_fusion.18), channel_id=1, source_target_pairs={{0,8},{1,9},{2,10},{3,11},{4,12},{5,13},{6,14},{7,15},{8,0},{9,1},... | collective-permute-start | bytes 331784 | tf_op jit(solution)/shard_map/ppermute | solution.py:119
  369.8 25.1 %collective-permute-start.17 = (bf16[1,1,1,2,2,24,3072]{6,5,4,3,2,1,0:T(8,128)(2,1)S(1)}, bf16[1,1,1,2,2,24,3072]{6,5,4,3,2,1,0:T(8,128)(2,1)}, u32[]{:S(2)}, u32[]{:S(2)}) collective-permute-start(bf16[1,1,1,2,2,24,3072]{6,5,4,3,2,1,0:T(8,128)(2,1)S(1)} %dynamic-slice_convert_fusion.8), channel_id=1, source_target_pairs={{0,8},{1,9},{2,10},{3,11},{4,12},{5,13},{6,14},{7,15},{8,0},{9,1},... | collective-permute-start | bytes 1769480 | tf_op jit(solution)/shard_map/ppermute | solution.py:119
  388.0 10.1 %collective-permute-start.22 = (bf16[1,1,1,2,2,96,768]{6,5,4,3,2,1,0:T(8,128)(2,1)S(1)}, bf16[1,1,1,2,2,96,768]{6,5,4,3,2,1,0:T(8,128)(2,1)}, u32[]{:S(2)}, u32[]{:S(2)}) collective-permute-start(bf16[1,1,1,2,2,96,768]{6,5,4,3,2,1,0:T(8,128)(2,1)S(1)} %dynamic-slice_convert_fusion.7), channel_id=1, source_target_pairs={{0,16},{1,17},{2,18},{3,19},{4,20},{5,21},{6,22},{7,23},{8,24},{9,... | collective-permute-start | bytes 1769480 | tf_op jit(solution)/shard_map/ppermute | solution.py:119
  391.6 6.5 %copy-start.12 = (f32[2,1,1,2,2,96,768]{6,5,4,3,2,1,0:T(8,128)S(1)}, f32[2,1,1,2,2,96,768]{6,5,4,3,2,1,0:T(8,128)}, u32[]{:S(2)}) copy-start(f32[2,1,1,2,2,96,768]{6,5,4,3,2,1,0:T(8,128)} %copy-done.11) | copy-start | bytes 7077892
  396.1 10.4 %collective-permute-start.18 = (bf16[1,1,1,2,1,24,3072]{6,5,4,3,2,1,0:T(8,128)(2,1)S(1)}, bf16[1,1,1,2,1,24,3072]{6,5,4,3,2,1,0:T(8,128)(2,1)S(1)}, u32[]{:S(2)}, u32[]{:S(2)}) collective-permute-start(bf16[1,1,1,2,1,24,3072]{6,5,4,3,2,1,0:T(8,128)(2,1)S(1)} %dynamic-slice_convert_fusion.12), channel_id=1, source_target_pairs={{0,1},{1,0},{2,3},{3,2},{4,5},{5,4},{6,7},{7,6},{8,9},{9,8},{10,11... | collective-permute-start | bytes 884744 | tf_op jit(solution)/shard_map/ppermute | solution.py:119
  399.3 10.9 %collective-permute-start.23 = (bf16[1,1,1,2,1,96,768]{6,5,4,3,2,1,0:T(8,128)(2,1)S(1)}, bf16[1,1,1,2,1,96,768]{6,5,4,3,2,1,0:T(8,128)(2,1)S(1)}, u32[]{:S(2)}, u32[]{:S(2)}) collective-permute-start(bf16[1,1,1,2,1,96,768]{6,5,4,3,2,1,0:T(8,128)(2,1)S(1)} %dynamic-slice_convert_fusion.11), channel_id=1, source_target_pairs={{0,1},{1,0},{2,3},{3,2},{4,5},{5,4},{6,7},{7,6},{8,9},{9,8},{10,11... | collective-permute-start | bytes 884744 | tf_op jit(solution)/shard_map/ppermute | solution.py:119
  406.7 8.4 %collective-permute-start.19 = (bf16[1,1,1,1,1,24,3072]{6,5,4,3,2,1,0:T(8,128)(2,1)S(1)}, bf16[1,1,1,1,1,24,3072]{6,5,4,3,2,1,0:T(8,128)(2,1)S(1)}, u32[]{:S(2)}, u32[]{:S(2)}) collective-permute-start(bf16[1,1,1,1,1,24,3072]{6,5,4,3,2,1,0:T(8,128)(2,1)S(1)} %dynamic-slice_convert_fusion.16), channel_id=1, source_target_pairs={{0,2},{1,3},{2,0},{3,1},{4,6},{5,7},{6,4},{7,5},{8,10},{9,11},{10,... | collective-permute-start | bytes 442376 | tf_op jit(solution)/shard_map/ppermute | solution.py:119
  410.3 6.3 %collective-permute-start.24 = (bf16[1,1,1,1,1,96,768]{6,5,4,3,2,1,0:T(8,128)(2,1)S(1)}, bf16[1,1,1,1,1,96,768]{6,5,4,3,2,1,0:T(8,128)(2,1)S(1)}, u32[]{:S(2)}, u32[]{:S(2)}) collective-permute-start(bf16[1,1,1,1,1,96,768]{6,5,4,3,2,1,0:T(8,128)(2,1)S(1)} %dynamic-slice_convert_fusion.15), channel_id=1, source_target_pairs={{0,2},{1,3},{2,0},{3,1},{4,6},{5,7},{6,4},{7,5},{8,10},{9,11},{10,... | collective-permute-start | bytes 442376 | tf_op jit(solution)/shard_map/ppermute | solution.py:119
  (43 other events, 121.0 us)
Sparse Core Ops, SparseCore 0:
  11.4 108.9 all-gather.2
  123.2 62.0 all-gather.4

commit v10 on v9

--- a/solution.py
+++ b/solution.py
@@ -361,13 +361,17 @@
         sg_block = jnp.concatenate(
             sg_flat + [jnp.zeros((n_dev, sg_pad), jnp.float32)], axis=1
         ).reshape(n_dev * rows_block, sg_cols)
-        joined = jnp.concatenate([grad_out_weight, grad_dec_weight, sg_block], axis=1)
+        joined = jnp.concatenate(
+            [grad_qkv_weight, grad_out_weight, grad_dec_weight, sg_block], axis=1
+        )
         reduced_joined = rs_chain(joined, n_bits, orders["yz"])
+        qkv_cols = grad_qkv_weight.shape[1]
         out_cols = grad_out_weight.shape[1]
         dec_cols = grad_dec_weight.shape[1]
-        sum_out = reduced_joined[:, :out_cols]
-        sum_dec = reduced_joined[:, out_cols : out_cols + dec_cols]
-        sg_sum = reduced_joined[:, out_cols + dec_cols :].reshape(-1)
+        sum_qkv = reduced_joined[:, :qkv_cols]
+        sum_out = reduced_joined[:, qkv_cols : qkv_cols + out_cols]
+        sum_dec = reduced_joined[:, qkv_cols + out_cols : qkv_cols + out_cols + dec_cols]
+        sg_sum = reduced_joined[:, qkv_cols + out_cols + dec_cols :].reshape(-1)
         sg_parts = []
         offset = 0
         for g, width in zip(small_grads, sg_widths):
@@ -376,7 +380,6 @@
         (sum_wave, sum_g1, sum_b1, sum_g2, sum_b2, sum_ib, sum_ob, sum_db, sum_mask) = sg_parts
         sum_mlp_out = rs_chain(grad_mlp_out, n_bits, orders["x"])
         sum_mlp_in = rs_chain(grad_mlp_in, n_bits, orders["y"])
-        sum_qkv = rs_chain(grad_qkv_weight, n_bits, orders["yz"])
         summed = (sum_wave, sum_g1, sum_b1, sum_qkv, sum_out, sum_g2, sum_b2, sum_mlp_in,
                   sum_ib, sum_mlp_out, sum_ob, sum_dec, sum_db, sum_mask)
         return (decoded, grad_tokens, *summed)

time: 429 us -> 467 us (1.089)
  waiting for transfers between devices: 197 us -> 230 us
  starting transfers between devices: 39.3 us -> 33 us
  other arithmetic: 32.7 us -> 38.9 us
    ppermute x20 -> x15, waiting for transfers between devices: 82.6 us -> 114 us  [rs_chain(): lax.ppermute(send.astype(jnp.bfloat16), AX, [(i, i ^ 1 << bit) for i in r...]
    convert_element_type x20 -> x15, local copies, waits for them, and re-layouts: 5.66 us -> 12.3 us  [rs_chain(): send.astype(jnp.bfloat16)]
    ppermute x20 -> x15, starting transfers between devices: 22.5 us -> 15.9 us  [rs_chain(): lax.ppermute(send.astype(jnp.bfloat16), AX, [(i, i ^ 1 << bit) for i in r...]
    add x16 -> x12, other arithmetic: 13.3 us -> 16.9 us  [rs_chain(): current = keep + moved.astype(jnp.float32)]
    unnamed x136 -> x124, local copies, waits for them, and re-layouts: 17.1 us -> 18.2 us
  transfers between devices with their start and end apart: 29 -> 24, of which waited for: 21 -> 14; matrix products, arithmetic and copies ran while one was open for 26% -> 19% of each run, Pallas kernels for 0% -> 0%
where the time goes in v10:
time: 467 us; the launch traced here: 462 us
  waiting for transfers between devices  230 us (49%)
  local copies, waits for them, and re-layouts  74.6 us (16%)
  matrix products  70.4 us (15%)
  other arithmetic  38.9 us (8%)
  starting transfers between devices  33 us (7%)
  between operations  15.5 us (3%)
    ppermute x15, waiting for transfers between devices, rs_chain(): lax.ppermute(send.astype(jnp.bfloat16), AX, [(i, i ^ 1 << bit) for i in r...  114 us
    ppermute x5, waiting for transfers between devices, ag_chain(): moved = lax.ppermute(current, AX, [(i, i ^ 1 << bit) for i in range(n_dev)])  53.3 us
    all_gather x1, waiting for transfers between devices, local(): outer_full = lax.all_gather(mlp_out, AX, axis=0, tiled=True)  29.5 us
    all_gather x1, waiting for transfers between devices, local(): lax.all_gather(jnp.concatenate(wide, axis=1), AX, axis=0, tiled=True)  28.5 us
    dot_general x5, matrix products, outer_cols(): lax.dot_general(left_op, right_op, (((1,), (1,)), ((), ())), preferred_el...  22.5 us
    dot_general x5, matrix products, product(): return jnp.dot(left_op, right_op, preferred_element_type=jnp.float32)  19 us
    unnamed x124, local copies, waits for them, and re-layouts  18.2 us
    add x12, other arithmetic, rs_chain(): current = keep + moved.astype(jnp.float32)  16.9 us
  transfers between devices with their start and end apart: 24, of which 14 were waited for; matrix products, arithmetic and copies ran while one was open for 19% of the time, Pallas kernels for 0%

profile of v10, /device:TPU:0, one launch (start us, length us, event | category | flops | bytes accessed | tf_op | source)
XLA Modules:
  0.0 462.2 jit_solution(12938327405233961434)
XLA Ops:
  10.7 4.1 collective-permute-start
  14.8 4.0 all-to-all-start.1
  21.4 47.6 %collective-permute-done.1 = bf16[1,1,1,2,1,1,8,512]{7,6,4,3,2,1,0,5:T(8,128)(2,1)S(1)} collective-permute-done((bf16[1,1,1,2,1,1,8,512]{7,6,4,3,2,1,0,5:T(8,128)(2,1)S(1)}, bf16[1,1,1,2,1,1,8,512]{7,6,4,3,2,1,0,5:T(8,128)(2,1)S(1)}, u32[]{:S(2)}, u32[]{:S(2)}) %collective-permute-start.1) | collective-permute-done | bytes 16416 | tf_op jit(solution)/shard_map/ppermute | solution.py:133
  70.6 2.3 collective-permute-done.2
  74.9 2.4 collective-permute-done.3
  82.7 3.3 all-to-all-done.1
  86.0 2.1 copy.129
  91.9 28.5 %all-gather.3.cloned.1.call-done = bf16[768,6656]{1,0:T(8,128)(2,1)} async-done(((bf16[24,6656]{1,0:T(8,128)(2,1)}), bf16[768,6656]{1,0:T(8,128)(2,1)}) %all-gather.3.cloned.1.call-update) | async-done | bytes 10223632 | tf_op jit(solution)/shard_map/all_gather | solution.py:247
  120.4 4.0 convolution_convert_fusion
  125.4 2.3 copy.118
  127.7 2.9 reshape.311
  131.8 2.2 reshape.313
  135.2 2.2 reshape.312
  138.5 4.8 %fusion.80 = (f32[2,12,256]{2,1,0:T(8,128)S(1)}, f32[2,12,256,256]{2,3,1,0:T(8,128)S(1)}) fusion(f32[2,12,256,256]{2,3,1,0:T(8,128)S(1)} %fusion.58), kind=kOutput, calls=%fused_computation.174 | output fusion | flops 6291711 | bytes 12607488 | tf_op jit(solution)/shard_map/sub | solution.py:167
  143.9 2.5 copy-done.2
  150.3 5.6 %multiply_convert_fusion.1 = (bf16[512,3072]{1,0:T(8,128)(2,1)}, f32[512,3072]{1,0:T(8,128)}) fusion(f32[3072]{0:T(1024)S(1)} %reshape.342, bf16[768,6656]{1,0:T(8,128)(2,1)S(1)} %bitcast.181, f32[512,768]{1,0:T(8,128)S(1)} %get-tuple-element.60, f32[768]{0:T(1024)S(1)} %reshape.341, f32[768]{0:T(1024)S(1)} %reshape.340, f32[512]{0:T(512)S(1)} %add_rsqrt_fusion, ...), kind=kOutput, calls=%fused_computation.12 | convolution fusion | flops 2427322368 | bytes 15753216 | tf_op jit(solution)/shard_map/dot_general | solution.py:21
  155.8 29.5 %all-gather.5.cloned.1.call-done = bf16[3072,768]{1,0:T(8,128)(2,1)} async-done(((bf16[96,768]{1,0:T(8,128)(2,1)}), bf16[3072,768]{1,0:T(8,128)(2,1)}) %all-gather.5.cloned.1.call-update) | async-done | bytes 4718608 | tf_op jit(solution)/shard_map/all_gather | solution.py:254
  185.3 7.5 %convert_reduce_fusion = (f32[3072]{0:T(1024)S(1)}, bf16[512,3072]{1,0:T(8,128)(2,1)S(1)}) fusion(f32[512,3072]{1,0:T(8,128)} %get-tuple-element.62, f32[3072]{0:T(1024)S(1)} %reshape.342, bf16[3072,768]{1,0:T(8,128)(2,1)} %all-gather.5.cloned.1.call-done, f32[512,768]{1,0:T(8,128)S(1)} %fusion.49), kind=kOutput, calls=%fused_computation.9 | convolution fusion | flops 2436756480 | bytes 15753216 | tf_op jit(solution)/shard_map/dot_general | solution.py:31
  192.8 7.1 %multiply_reduce_fusion.2 = (f32[768]{0:T(1024)}, f32[512]{0:T(512)S(1)}, f32[512]{0:T(512)S(1)}, f32[768]{0:T(1024)}, f32[512,768]{1,0:T(8,128)S(1)}) fusion(f32[512,768]{1,0:T(8,128)S(1)} %get-tuple-element.60, f32[512]{0:T(512)S(1)} %add_rsqrt_fusion, f32[512]{0:T(512)S(1)} %broadcast_multiply_fusion.4, f32[768]{0:T(1024)S(1)} %reshape.340, ...), kind=kOutput, calls=%fused_computation.52 | convolution fusion | flops 2419455488 | bytes 11027456 | tf_op jit(solution)/shard_map/dot_general | solution.py:31
  201.7 2.1 convolution_convert_fusion.1
  205.2 4.3 fusion.33
  209.9 3.9 multiply_reduce_fusion
  213.8 4.3 multiply_convert_fusion
  220.9 5.7 %fusion.75 = f32[768,3072]{1,0:T(8,128)} fusion(bf16[512,3072]{1,0:T(8,128)(2,1)S(1)} %copy-done.45, f32[512,768]{1,0:T(8,128)S(1)} %copy-done.9, f32[768]{0:T(1024)S(1)} %copy-done.38, f32[768]{0:T(1024)S(1)} %reshape.340, f32[512]{0:T(512)S(1)} %add_rsqrt_fusion, f32[512]{0:T(512)S(1)} %broadcast_multiply_fusion.4), kind=kOutput, calls=%fused_computation.169 | convolution fusion | flops 2417885184 | bytes 14166016 | tf_op jit(solution)/shard_map/dot_general | solution.py:25
  234.1 2.3 copy.142
  236.4 5.2 %multiply_reduce_fusion.3 = (f32[768]{0:T(1024)S(1)}, f32[512]{0:T(512)S(1)}, f32[512]{0:T(512)S(1)}, f32[768]{0:T(1024)S(1)}, f32[512,768]{1,0:T(8,128)S(1)}) fusion(f32[2,256,768]{2,1,0:T(8,128)S(1)} %copy-done.4, f32[512]{0:T(512)S(1)} %bitcast.188, f32[512]{0:T(512)S(1)} %bitcast.191, f32[768]{0:T(1024)S(1)} %reshape.338, ...), kind=kOutput, calls=%fused_computation.53 | convolution fusion | flops 1822553600 | bytes 9061376 | tf_op jit(solution)/shard_map/dot_general | solution.py:31
  245.2 6.8 %add_convert_fusion = bf16[512,768]{1,0:T(8,128)(2,1)} fusion(f32[512,768]{1,0:T(8,128)S(1)} %copy-done.9, bf16[512,3072]{1,0:T(8,128)(2,1)} %get-tuple-element.61, bf16[3072,768]{1,0:T(8,128)(2,1)} %all-gather.5.cloned.1.call-done, f32[768]{0:T(1024)S(1)} %copy-done.36), kind=kOutput, calls=%fused_computation.60 | convolution fusion | flops 2417098752 | bytes 10226688 | tf_op jit(solution)/shard_map/dot_general | solution.py:21
  252.0 2.5 copy.146
  256.3 2.3 fusion.18
  258.6 4.2 dynamic-slice_convert_fusion.2
  264.7 4.4 pad_maximum_fusion
  271.7 3.3 copy-done.23
  275.0 2.7 fusion.70
  277.7 3.5 copy-done.1
  285.3 3.5 copy.127
  288.8 3.7 all-to-all-start
  292.5 4.1 convert_add_fusion.2
  299.6 3.7 convert_add_fusion.1
  306.0 2.5 convert_add_fusion
  308.5 34.6 %collective-permute-done.11 = bf16[1,2,1,2,2,24,3072]{6,5,4,3,2,1,0:T(8,128)(2,1)} collective-permute-done((bf16[1,2,1,2,2,24,3072]{6,5,4,3,2,1,0:T(8,128)(2,1)}, bf16[1,2,1,2,2,24,3072]{6,5,4,3,2,1,0:T(8,128)(2,1)}, u32[]{:S(2)}, u32[]{:S(2)}) %collective-permute-start.11) | collective-permute-done | bytes 1179680 | tf_op jit(solution)/shard_map/ppermute | solution.py:119
  353.6 3.6 copy.128
  357.1 3.7 collective-permute-done.12
  364.0 31.2 %collective-permute-done.17 = bf16[1,1,1,2,2,96,768]{6,5,4,3,2,1,0:T(8,128)(2,1)} collective-permute-done((bf16[1,1,1,2,2,96,768]{6,5,4,3,2,1,0:T(8,128)(2,1)}, bf16[1,1,1,2,2,96,768]{6,5,4,3,2,1,0:T(8,128)(2,1)}, u32[]{:S(2)}, u32[]{:S(2)}) %collective-permute-start.17) | collective-permute-done | bytes 589856 | tf_op jit(solution)/shard_map/ppermute | solution.py:119
  399.5 2.6 collective-permute-start.14
  402.0 9.5 %collective-permute-done.18 = bf16[1,1,1,2,1,96,768]{6,5,4,3,2,1,0:T(8,128)(2,1)S(1)} collective-permute-done((bf16[1,1,1,2,1,96,768]{6,5,4,3,2,1,0:T(8,128)(2,1)S(1)}, bf16[1,1,1,2,1,96,768]{6,5,4,3,2,1,0:T(8,128)(2,1)S(1)}, u32[]{:S(2)}, u32[]{:S(2)}) %collective-permute-start.18) | collective-permute-done | bytes 294944 | tf_op jit(solution)/shard_map/ppermute | solution.py:119
  411.7 15.2 %collective-permute-done.7 = bf16[1,2,1,2,1,24,3840]{6,5,4,3,2,1,0:T(8,128)(2,1)S(1)} collective-permute-done((bf16[1,2,1,2,1,24,3840]{6,5,4,3,2,1,0:T(8,128)(2,1)S(1)}, bf16[1,2,1,2,1,24,3840]{6,5,4,3,2,1,0:T(8,128)(2,1)S(1)}, u32[]{:S(2)}, u32[]{:S(2)}) %collective-permute-start.7) | collective-permute-done | bytes 737312 | tf_op jit(solution)/shard_map/ppermute | solution.py:119
  429.4 15.2 %collective-permute-done.8 = bf16[1,2,1,1,1,24,3840]{6,5,4,3,2,1,0:T(8,128)(2,1)S(1)} collective-permute-done((bf16[1,2,1,1,1,24,3840]{6,5,4,3,2,1,0:T(8,128)(2,1)S(1)}, bf16[1,2,1,1,1,24,3840]{6,5,4,3,2,1,0:T(8,128)(2,1)S(1)}, u32[]{:S(2)}, u32[]{:S(2)}) %collective-permute-start.8) | collective-permute-done | bytes 368672 | tf_op jit(solution)/shard_map/ppermute | solution.py:119
  445.7 5.0 %collective-permute-done.9 = bf16[1,1,1,1,1,24,3840]{6,5,4,3,2,1,0:T(8,128)(2,1)S(1)} collective-permute-done((bf16[1,1,1,1,1,24,3840]{6,5,4,3,2,1,0:T(8,128)(2,1)S(1)}, bf16[1,1,1,1,1,24,3840]{6,5,4,3,2,1,0:T(8,128)(2,1)S(1)}, u32[]{:S(2)}, u32[]{:S(2)}) %collective-permute-start.9) | collective-permute-done | bytes 184352 | tf_op jit(solution)/shard_map/ppermute | solution.py:119
  (275 shorter events, 86.5 us)
Async XLA Ops:
  7.2 113.2 %all-gather.3.cloned.1.call-start = ((), (), s32[]{:S(2)}) async-start(), calls=%async_computation.2 | async-start | bytes 10543104 | tf_op jit(solution)/shard_map/all_gather | solution.py:247
  10.7 64.0 %copy-start.41 = (s32[2,256]{1,0:T(2,128)S(1)}, s32[2,256]{1,0:T(2,128)}, u32[]{:S(2)}) copy-start(s32[2,256]{1,0:T(2,128)} %param.20) | copy-start | bytes 6148
  10.7 66.8 %copy-start.43 = (s32[2,13]{1,0:T(2,128)S(1)}, s32[2,13]{1,0:T(2,128)}, u32[]{:S(2)}) copy-start(s32[2,13]{1,0:T(2,128)} %param.19) | copy-start | bytes 316
  10.7 8.9 %collective-permute-start = (bf16[1,1,1,1,1,1,8,512]{7,6,4,3,2,1,0,5:T(8,128)(2,1)S(1)}, bf16[1,1,1,1,1,1,8,512]{7,6,4,3,2,1,0,5:T(8,128)(2,1)S(1)}, u32[]{:S(2)}, u32[]{:S(2)}) collective-permute-start(bf16[1,1,1,1,1,1,8,512]{7,6,4,3,2,1,0,5:T(8,128)(2,1)S(1)} %bitcast.183), channel_id=1, source_target_pairs={{0,2},{1,3},{2,0},{3,1},{4,6},{5,7},{6,4},{7,5},{8,10},{9,11},{10,... | collective-permute-start | bytes 24584 | tf_op jit(solution)/shard_map/ppermute | solution.py:133
  14.8 71.2 %all-to-all-start.1 = ((bf16[64,32,512]{2,1,0:T(8,128)(2,1)}), bf16[64,32,512]{2,1,0:T(8,128)(2,1)}, u32[]{:S(2)}, u32[]{:S(2)}) async-start(bf16[64,32,512]{2,1,0:T(8,128)(2,1)} %param.35), calls=%async_computation.1 | async-start | bytes 4194304 | tf_op jit(solution)/shard_map/all_to_all | solution.py:304
  18.8 60.7 %copy-start.24 = (bf16[2,256,768]{2,1,0:T(8,128)(2,1)S(1)}, bf16[2,256,768]{2,1,0:T(8,128)(2,1)}, u32[]{:S(2)}) copy-start(bf16[2,256,768]{2,1,0:T(8,128)(2,1)} %param.18) | copy-start | bytes 2359300
  18.8 166.5 %all-gather.5.cloned.1.call-start = ((), (), s32[]{:S(2)}) async-start(), calls=%async_computation.3 | async-start | bytes 4866048 | tf_op jit(solution)/shard_map/all_gather | solution.py:254
  19.6 49.4 %collective-permute-start.1 = (bf16[1,1,1,2,1,1,8,512]{7,6,4,3,2,1,0,5:T(8,128)(2,1)S(1)}, bf16[1,1,1,2,1,1,8,512]{7,6,4,3,2,1,0,5:T(8,128)(2,1)S(1)}, u32[]{:S(2)}, u32[]{:S(2)}) collective-permute-start(bf16[1,1,1,2,1,1,8,512]{7,6,4,3,2,1,0,5:T(8,128)(2,1)S(1)} %pad_maximum_fusion.9), channel_id=1, source_target_pairs={{0,1},{1,0},{2,3},{3,2},{4,5},{5,4},{6,7},{7,6},{8,9},{9,8},{10,11... | collective-permute-start | bytes 49160 | tf_op jit(solution)/shard_map/ppermute | solution.py:133
  69.0 4.0 collective-permute-start.2
  73.0 4.3 collective-permute-start.3
  77.4 1.4 collective-permute-start.4
  80.1 67.4 %copy-start.3 = (f32[2,256,768]{2,1,0:T(8,128)}, f32[2,256,768]{2,1,0:T(8,128)S(1)}, u32[]{:S(2)}) copy-start(f32[2,256,768]{2,1,0:T(8,128)S(1)} %get-tuple-element.30) | copy-start | bytes 4718596
  80.4 69.9 %copy-start.37 = (f32[768]{0:T(1024)}, f32[768]{0:T(1024)S(1)}, u32[]{:S(2)}) copy-start(f32[768]{0:T(1024)S(1)} %reshape.341) | copy-start | bytes 9220
  138.5 9.0 %slice-start.7 = ((s8[10223616]{0:T(1024)(128)(4,1)}), s8[4194304]{0:T(1024)(128)(4,1)S(1)}, s32[]{:S(2)}) async-start(s8[10223616]{0:T(1024)(128)(4,1)} %bitcast.180), calls=%async_computation.11 | async-start | bytes 8388608
  143.3 5.1 %slice-start.9 = ((s8[10223616]{0:T(1024)(128)(4,1)}), s8[1835008]{0:T(1024)(128)(4,1)S(1)}, s32[]{:S(2)}) async-start(s8[10223616]{0:T(1024)(128)(4,1)} %bitcast.180), calls=%async_computation.13 | async-start | bytes 3670016
  149.3 50.6 %copy-start.8 = (f32[512,768]{1,0:T(8,128)}, f32[512,768]{1,0:T(8,128)S(1)}, u32[]{:S(2)}) copy-start(f32[512,768]{1,0:T(8,128)S(1)} %get-tuple-element.60) | copy-start | bytes 4718596
  150.2 49.7 %copy-start.6 = (f32[512,768]{1,0:T(8,128)}, f32[512,768]{1,0:T(8,128)S(1)}, u32[]{:S(2)}) copy-start(f32[512,768]{1,0:T(8,128)S(1)} %fusion.49) | copy-start | bytes 4718596
  192.8 7.1 %copy-start.44 = (bf16[512,3072]{1,0:T(8,128)(2,1)}, bf16[512,3072]{1,0:T(8,128)(2,1)S(1)}, u32[]{:S(2)}) copy-start(bf16[512,3072]{1,0:T(8,128)(2,1)S(1)} %get-tuple-element.68) | copy-start | bytes 9437188
  204.1 5.3 %slice-start.3 = ((s8[6291456]{0:T(1024)(128)(4,1)}), s8[2097152]{0:T(1024)(128)(4,1)S(1)}, s32[]{:S(2)}) async-start(s8[6291456]{0:T(1024)(128)(4,1)} %bitcast.149), calls=%async_computation.7 | async-start | bytes 4194304
  230.9 5.4 %copy-start.4 = (f32[2,256,768]{2,1,0:T(8,128)S(1)}, f32[2,256,768]{2,1,0:T(8,128)}, u32[]{:S(2)}) copy-start(f32[2,256,768]{2,1,0:T(8,128)} %copy-done.3) | copy-start | bytes 4718596
  236.4 5.2 %copy-start.11 = (f32[512,768]{1,0:T(8,128)S(1)}, f32[512,768]{1,0:T(8,128)}, u32[]{:S(2)}) copy-start(f32[512,768]{1,0:T(8,128)} %copy-done.10) | copy-start | bytes 4718596
  245.2 9.3 %copy-start.17 = (bf16[96,8,2,256]{3,1,2,0:T(8,128)(2,1)S(1)}, bf16[96,8,2,256]{3,1,2,0:T(8,128)(2,1)}, u32[]{:S(2)}) copy-start(bf16[96,8,2,256]{3,1,2,0:T(8,128)(2,1)} %copy-done.16) | copy-start | bytes 2359300
  262.8 29.7 %collective-permute-start.10 = (bf16[2,2,1,2,2,24,3072]{6,5,4,3,2,1,0:T(8,128)(2,1)}, bf16[2,2,1,2,2,24,3072]{6,5,4,3,2,1,0:T(8,128)(2,1)}, u32[]{:S(2)}, u32[]{:S(2)}) collective-permute-start(bf16[2,2,1,2,2,24,3072]{6,5,4,3,2,1,0:T(8,128)(2,1)} %dynamic-slice_convert_fusion.2), channel_id=1, source_target_pairs={{0,4},{1,5},{2,6},{3,7},{4,0},{5,1},{6,2},{7,3},{8,12},{9,13},{10,... | collective-permute-start | bytes 7077896 | tf_op jit(solution)/shard_map/ppermute | solution.py:119
  269.2 8.5 %copy-start = (f32[2,2,2,2,2,24,3840]{6,5,4,3,2,1,0:T(8,128)}, f32[2,2,2,2,2,24,3840]{6,5,4,3,2,1,0:T(8,128)S(1)}, u32[]{:S(2)}) copy-start(f32[2,2,2,2,2,24,3840]{6,5,4,3,2,1,0:T(8,128)S(1)} %pad_maximum_fusion) | copy-start | bytes 35389444
  269.2 5.8 %copy-start.23 = (bf16[512,3072]{1,0:T(8,128)(2,1)S(1)}, bf16[512,3072]{1,0:T(8,128)(2,1)}, u32[]{:S(2)}) copy-start(bf16[512,3072]{1,0:T(8,128)(2,1)} %get-tuple-element.61) | copy-start | bytes 9437188
  271.2 34.8 %collective-permute-start.5 = (bf16[2,2,1,2,2,24,3840]{6,5,4,3,2,1,0:T(8,128)(2,1)}, bf16[2,2,1,2,2,24,3840]{6,5,4,3,2,1,0:T(8,128)(2,1)}, u32[]{:S(2)}, u32[]{:S(2)}) collective-permute-start(bf16[2,2,1,2,2,24,3840]{6,5,4,3,2,1,0:T(8,128)(2,1)} %dynamic-slice_convert_fusion), channel_id=1, source_target_pairs={{0,4},{1,5},{2,6},{3,7},{4,0},{5,1},{6,2},{7,3},{8,12},{9,13},{10,... | collective-permute-start | bytes 8847368 | tf_op jit(solution)/shard_map/ppermute | solution.py:119
  281.5 18.2 %collective-permute-start.15 = (bf16[2,2,1,2,2,96,768]{6,5,4,3,2,1,0:T(8,128)(2,1)S(1)}, bf16[2,2,1,2,2,96,768]{6,5,4,3,2,1,0:T(8,128)(2,1)}, u32[]{:S(2)}, u32[]{:S(2)}) collective-permute-start(bf16[2,2,1,2,2,96,768]{6,5,4,3,2,1,0:T(8,128)(2,1)S(1)} %dynamic-slice_convert_fusion.1), channel_id=1, source_target_pairs={{0,4},{1,5},{2,6},{3,7},{4,0},{5,1},{6,2},{7,3},{8,12},{9,13},{10,... | collective-permute-start | bytes 7077896 | tf_op jit(solution)/shard_map/ppermute | solution.py:119
  288.8 64.8 %all-to-all-start = ((bf16[2,1024,512]{2,0,1:T(2,128)(2,1)}), bf16[2,1024,512]{2,0,1:T(2,128)(2,1)}, u32[]{:S(2)}, u32[]{:S(2)}) async-start(bf16[2,1024,512]{2,0,1:T(2,128)(2,1)} %copy.127), calls=%async_computation | async-start | bytes 4194304 | tf_op jit(solution)/shard_map/all_to_all | solution.py:303
  292.5 13.5 %slice-start = ((s8[11796480]{0:T(1024)(128)(4,1)}), s8[4194304]{0:T(1024)(128)(4,1)S(1)}, s32[]{:S(2)}) async-start(s8[11796480]{0:T(1024)(128)(4,1)} %bitcast.145), calls=%async_computation.4 | async-start | bytes 8388608
  292.5 13.5 %slice-start.1 = ((s8[11796480]{0:T(1024)(128)(4,1)}), s8[4194304]{0:T(1024)(128)(4,1)S(1)}, s32[]{:S(2)}) async-start(s8[11796480]{0:T(1024)(128)(4,1)} %bitcast.145), calls=%async_computation.5 | async-start | bytes 8388608
  297.9 8.1 %slice-start.2 = ((s8[11796480]{0:T(1024)(128)(4,1)}), s8[3407872]{0:T(1024)(128)(4,1)S(1)}, s32[]{:S(2)}) async-start(s8[11796480]{0:T(1024)(128)(4,1)} %bitcast.145), calls=%async_computation.6 | async-start | bytes 6815744
  297.9 45.2 %collective-permute-start.11 = (bf16[1,2,1,2,2,24,3072]{6,5,4,3,2,1,0:T(8,128)(2,1)}, bf16[1,2,1,2,2,24,3072]{6,5,4,3,2,1,0:T(8,128)(2,1)}, u32[]{:S(2)}, u32[]{:S(2)}) collective-permute-start(bf16[1,2,1,2,2,24,3072]{6,5,4,3,2,1,0:T(8,128)(2,1)} %dynamic-slice_convert_fusion.5), channel_id=1, source_target_pairs={{0,16},{1,17},{2,18},{3,19},{4,20},{5,21},{6,22},{7,23},{8,24},{9,... | collective-permute-start | bytes 3538952 | tf_op jit(solution)/shard_map/ppermute | solution.py:119
  304.5 44.2 %collective-permute-start.16 = (bf16[2,1,1,2,2,96,768]{6,5,4,3,2,1,0:T(8,128)(2,1)}, bf16[2,1,1,2,2,96,768]{6,5,4,3,2,1,0:T(8,128)(2,1)}, u32[]{:S(2)}, u32[]{:S(2)}) collective-permute-start(bf16[2,1,1,2,2,96,768]{6,5,4,3,2,1,0:T(8,128)(2,1)} %dynamic-slice_convert_fusion.4), channel_id=1, source_target_pairs={{0,8},{1,9},{2,10},{3,11},{4,12},{5,13},{6,14},{7,15},{8,0},{9,1},... | collective-permute-start | bytes 3538952 | tf_op jit(solution)/shard_map/ppermute | solution.py:119
  308.5 38.5 %copy-start.5 = (f32[2,2,1,2,2,24,3840]{6,5,4,3,2,1,0:T(8,128)}, f32[2,2,1,2,2,24,3840]{6,5,4,3,2,1,0:T(8,128)S(1)}, u32[]{:S(2)}) copy-start(f32[2,2,1,2,2,24,3840]{6,5,4,3,2,1,0:T(8,128)S(1)} %convert_add_fusion) | copy-start | bytes 17694724
  344.7 5.6 %copy-start.13 = (f32[1,2,1,2,2,24,3072]{6,5,4,3,2,1,0:T(8,128)}, f32[1,2,1,2,2,24,3072]{6,5,4,3,2,1,0:T(8,128)S(1)}, u32[]{:S(2)}) copy-start(f32[1,2,1,2,2,24,3072]{6,5,4,3,2,1,0:T(8,128)S(1)} %convert_add_fusion.5) | copy-start | bytes 7077892
  345.7 15.2 %collective-permute-start.12 = (bf16[1,1,1,2,2,24,3072]{6,5,4,3,2,1,0:T(8,128)(2,1)}, bf16[1,1,1,2,2,24,3072]{6,5,4,3,2,1,0:T(8,128)(2,1)}, u32[]{:S(2)}, u32[]{:S(2)}) collective-permute-start(bf16[1,1,1,2,2,24,3072]{6,5,4,3,2,1,0:T(8,128)(2,1)} %dynamic-slice_convert_fusion.8), channel_id=1, source_target_pairs={{0,8},{1,9},{2,10},{3,11},{4,12},{5,13},{6,14},{7,15},{8,0},{9,1},... | collective-permute-start | bytes 1769480 | tf_op jit(solution)/shard_map/ppermute | solution.py:119
  348.3 50.1 %collective-permute-start.6 = (bf16[1,2,1,2,2,24,3840]{6,5,4,3,2,1,0:T(8,128)(2,1)}, bf16[1,2,1,2,2,24,3840]{6,5,4,3,2,1,0:T(8,128)(2,1)S(1)}, u32[]{:S(2)}, u32[]{:S(2)}) collective-permute-start(bf16[1,2,1,2,2,24,3840]{6,5,4,3,2,1,0:T(8,128)(2,1)} %dynamic-slice_convert_fusion.3), channel_id=1, source_target_pairs={{0,16},{1,17},{2,18},{3,19},{4,20},{5,21},{6,22},{7,23},{8,24},{9,... | collective-permute-start | bytes 4423688 | tf_op jit(solution)/shard_map/ppermute | solution.py:119
  348.7 49.8 %slice-start.5 = ((s8[5898240]{0:T(1024)(128)(4,1)}), s8[1703936]{0:T(1024)(128)(4,1)S(1)}, s32[]{:S(2)}) async-start(s8[5898240]{0:T(1024)(128)(4,1)} %bitcast.151), calls=%async_computation.9 | async-start | bytes 3407872
  351.9 43.3 %collective-permute-start.17 = (bf16[1,1,1,2,2,96,768]{6,5,4,3,2,1,0:T(8,128)(2,1)}, bf16[1,1,1,2,2,96,768]{6,5,4,3,2,1,0:T(8,128)(2,1)}, u32[]{:S(2)}, u32[]{:S(2)}) collective-permute-start(bf16[1,1,1,2,2,96,768]{6,5,4,3,2,1,0:T(8,128)(2,1)} %dynamic-slice_convert_fusion.7), channel_id=1, source_target_pairs={{0,16},{1,17},{2,18},{3,19},{4,20},{5,21},{6,22},{7,23},{8,24},{9,... | collective-permute-start | bytes 1769480 | tf_op jit(solution)/shard_map/ppermute | solution.py:119
  353.6 7.3 %copy-start.14 = (f32[1,2,1,2,2,24,3072]{6,5,4,3,2,1,0:T(8,128)S(1)}, f32[1,2,1,2,2,24,3072]{6,5,4,3,2,1,0:T(8,128)}, u32[]{:S(2)}) copy-start(f32[1,2,1,2,2,24,3072]{6,5,4,3,2,1,0:T(8,128)} %copy-done.13) | copy-start | bytes 7077892
  353.6 44.9 %slice-start.6 = ((s8[5898240]{0:T(1024)(128)(4,1)}), s8[4194304]{0:T(1024)(128)(4,1)S(1)}, s32[]{:S(2)}) async-start(s8[5898240]{0:T(1024)(128)(4,1)} %bitcast.151), calls=%async_computation.10 | async-start | bytes 8388608
  362.1 37.3 %collective-permute-start.13 = (bf16[1,1,1,2,1,24,3072]{6,5,4,3,2,1,0:T(8,128)(2,1)S(1)}, bf16[1,1,1,2,1,24,3072]{6,5,4,3,2,1,0:T(8,128)(2,1)S(1)}, u32[]{:S(2)}, u32[]{:S(2)}) collective-permute-start(bf16[1,1,1,2,1,24,3072]{6,5,4,3,2,1,0:T(8,128)(2,1)S(1)} %dynamic-slice_convert_fusion.11), channel_id=1, source_target_pairs={{0,1},{1,0},{2,3},{3,2},{4,5},{5,4},{6,7},{7,6},{8,9},{9,8},{10,11... | collective-permute-start | bytes 884744 | tf_op jit(solution)/shard_map/ppermute | solution.py:119
  396.8 14.7 %collective-permute-start.18 = (bf16[1,1,1,2,1,96,768]{6,5,4,3,2,1,0:T(8,128)(2,1)S(1)}, bf16[1,1,1,2,1,96,768]{6,5,4,3,2,1,0:T(8,128)(2,1)S(1)}, u32[]{:S(2)}, u32[]{:S(2)}) collective-permute-start(bf16[1,1,1,2,1,96,768]{6,5,4,3,2,1,0:T(8,128)(2,1)S(1)} %dynamic-slice_convert_fusion.10), channel_id=1, source_target_pairs={{0,1},{1,0},{2,3},{3,2},{4,5},{5,4},{6,7},{7,6},{8,9},{9,8},{10,11... | collective-permute-start | bytes 884744 | tf_op jit(solution)/shard_map/ppermute | solution.py:119
  398.8 28.0 %collective-permute-start.7 = (bf16[1,2,1,2,1,24,3840]{6,5,4,3,2,1,0:T(8,128)(2,1)S(1)}, bf16[1,2,1,2,1,24,3840]{6,5,4,3,2,1,0:T(8,128)(2,1)S(1)}, u32[]{:S(2)}, u32[]{:S(2)}) collective-permute-start(bf16[1,2,1,2,1,24,3840]{6,5,4,3,2,1,0:T(8,128)(2,1)S(1)} %dynamic-slice_convert_fusion.6), channel_id=1, source_target_pairs={{0,1},{1,0},{2,3},{3,2},{4,5},{5,4},{6,7},{7,6},{8,9},{9,8},{10,11... | collective-permute-start | bytes 2211848 | tf_op jit(solution)/shard_map/ppermute | solution.py:119
  399.5 29.2 %collective-permute-start.14 = (bf16[1,1,1,1,1,24,3072]{6,5,4,3,2,1,0:T(8,128)(2,1)S(1)}, bf16[1,1,1,1,1,24,3072]{6,5,4,3,2,1,0:T(8,128)(2,1)S(1)}, u32[]{:S(2)}, u32[]{:S(2)}) collective-permute-start(bf16[1,1,1,1,1,24,3072]{6,5,4,3,2,1,0:T(8,128)(2,1)S(1)} %dynamic-slice_convert_fusion.14), channel_id=1, source_target_pairs={{0,2},{1,3},{2,0},{3,1},{4,6},{5,7},{6,4},{7,5},{8,10},{9,11},{10,... | collective-permute-start | bytes 442376 | tf_op jit(solution)/shard_map/ppermute | solution.py:119
  411.6 33.3 %collective-permute-start.19 = (bf16[1,1,1,1,1,96,768]{6,5,4,3,2,1,0:T(8,128)(2,1)S(1)}, bf16[1,1,1,1,1,96,768]{6,5,4,3,2,1,0:T(8,128)(2,1)S(1)}, u32[]{:S(2)}, u32[]{:S(2)}) collective-permute-start(bf16[1,1,1,1,1,96,768]{6,5,4,3,2,1,0:T(8,128)(2,1)S(1)} %dynamic-slice_convert_fusion.13), channel_id=1, source_target_pairs={{0,2},{1,3},{2,0},{3,1},{4,6},{5,7},{6,4},{7,5},{8,10},{9,11},{10,... | collective-permute-start | bytes 442376 | tf_op jit(solution)/shard_map/ppermute | solution.py:119
  427.1 17.5 %collective-permute-start.8 = (bf16[1,2,1,1,1,24,3840]{6,5,4,3,2,1,0:T(8,128)(2,1)S(1)}, bf16[1,2,1,1,1,24,3840]{6,5,4,3,2,1,0:T(8,128)(2,1)S(1)}, u32[]{:S(2)}, u32[]{:S(2)}) collective-permute-start(bf16[1,2,1,1,1,24,3840]{6,5,4,3,2,1,0:T(8,128)(2,1)S(1)} %dynamic-slice_convert_fusion.9), channel_id=1, source_target_pairs={{0,2},{1,3},{2,0},{3,1},{4,6},{5,7},{6,4},{7,5},{8,10},{9,11},{10,... | collective-permute-start | bytes 1105928 | tf_op jit(solution)/shard_map/ppermute | solution.py:119
  444.7 5.9 %collective-permute-start.9 = (bf16[1,1,1,1,1,24,3840]{6,5,4,3,2,1,0:T(8,128)(2,1)S(1)}, bf16[1,1,1,1,1,24,3840]{6,5,4,3,2,1,0:T(8,128)(2,1)S(1)}, u32[]{:S(2)}, u32[]{:S(2)}) collective-permute-start(bf16[1,1,1,1,1,24,3840]{6,5,4,3,2,1,0:T(8,128)(2,1)S(1)} %dynamic-slice_convert_fusion.12), channel_id=1, source_target_pairs={{0,8},{1,9},{2,10},{3,11},{4,12},{5,13},{6,14},{7,15},{8,0},{9,1},... | collective-permute-start | bytes 552968 | tf_op jit(solution)/shard_map/ppermute | solution.py:119
  (32 other events, 80.1 us)
Sparse Core Ops, SparseCore 0:
  11.4 108.9 all-gather.2
  123.2 62.0 all-gather.4

commit v11 on v9

--- a/solution.py
+++ b/solution.py
@@ -234,14 +234,16 @@
             dec_bias,
             mask_token,
         )
+        out_split = mlp_out.shape[1] // 2
         small = (wave_table, norm1_gain, norm1_bias, norm2_gain, norm2_bias, mlp_in_bias,
-                 mlp_out_bias, dec_bias, mask_token)
+                 mlp_out_bias, dec_bias, mask_token, mlp_out[:, out_split:])
         packed_small, small_widths = pack_rows(
             [a.reshape(1, -1) for a in small], 1, jnp.bfloat16
         )
         gathered_small = ag_chain(packed_small, n_bits, orders["x"])
         (wave_full, gain_one, shift_one, gain_two, shift_two, inner_bias, outer_bias,
-         dec_shift, mask_full) = unpack_rows(gathered_small, small, small_widths, 1, n_dev)
+         dec_shift, mask_full, outer_right) = unpack_rows(
+            gathered_small, small, small_widths, 1, n_dev)
         wide = (qkv_weight, out_weight, mlp_in, dec_weight)
         wide_cols = [a.shape[1] for a in wide]
         gathered_wide = lax.all_gather(jnp.concatenate(wide, axis=1), AX, axis=0, tiled=True)
@@ -251,7 +253,8 @@
             wide_full.append(gathered_wide[:, offset : offset + cols])
             offset += cols
         qkv_full, out_full, inner_full, dec_full = wide_full
-        outer_full = lax.all_gather(mlp_out, AX, axis=0, tiled=True)
+        outer_left = lax.all_gather(mlp_out[:, :out_split], AX, axis=0, tiled=True)
+        outer_full = jnp.concatenate([outer_left, outer_right], axis=1)
 
         chip_count, vis_len, feature_width = tokens.shape
         row_count = chip_count * vis_len

time: 429 us -> 458 us (1.068)
  local copies, waits for them, and re-layouts: 72.3 us -> 101 us
  waiting for transfers between devices: 197 us -> 190 us
    all_to_all x1, waiting for transfers between devices: 3.69 us -> 48.9 us  [local(): lax.all_to_all(cot_decoded, AX, split_axis=0, concat_axis=1, tiled=True)]
    all_gather x1, waiting for transfers between devices: 29.5 us -> 0.01 us  [local(): outer_left = lax.all_gather(mlp_out[:, :out_split], AX, axis=0, tiled=True)]
    ppermute x5, waiting for transfers between devices: 54 us -> 34.5 us  [ag_chain(): moved = lax.ppermute(current, AX, [(i, i ^ 1 << bit) for i in range(n_dev)])]
    unnamed x136 -> x150, local copies, waits for them, and re-layouts: 17.1 us -> 30.8 us
    reshape x1 -> x2, local copies, waits for them, and re-layouts: 0.13 us -> 6.12 us  [unpack_rows(): out.append(piece.reshape((leading * a.shape[0] // n_dev,) + a.shape[1:]))]
    dot_general x5, matrix products: 23.7 us -> 18.1 us  [outer_cols(): lax.dot_general(left_op, right_op, (((1,), (1,)), ((), ())), preferred_el...]
  transfers between devices with their start and end apart: 29 -> 29, of which waited for: 21 -> 21; matrix products, arithmetic and copies ran while one was open for 26% -> 24% of each run, Pallas kernels for 0% -> 0%
where the time goes in v11:
time: 458 us; the launch traced here: 452 us
  waiting for transfers between devices  190 us (41%)
  local copies, waits for them, and re-layouts  101 us (22%)
  matrix products  64.9 us (14%)
  starting transfers between devices  43.8 us (10%)
  other arithmetic  36.4 us (8%)
  between operations  15.6 us (3%)
    ppermute x20, waiting for transfers between devices, rs_chain(): lax.ppermute(send.astype(jnp.bfloat16), AX, [(i, i ^ 1 << bit) for i in r...  82 us
    all_to_all x1, waiting for transfers between devices, local(): lax.all_to_all(cot_decoded, AX, split_axis=0, concat_axis=1, tiled=True)  48.9 us
    ppermute x5, waiting for transfers between devices, ag_chain(): moved = lax.ppermute(current, AX, [(i, i ^ 1 << bit) for i in range(n_dev)])  34.5 us
    unnamed x150, local copies, waits for them, and re-layouts  30.8 us
    all_gather x1, waiting for transfers between devices, local(): lax.all_gather(jnp.concatenate(wide, axis=1), AX, axis=0, tiled=True)  24.9 us
    ppermute x20, starting transfers between devices, rs_chain(): lax.ppermute(send.astype(jnp.bfloat16), AX, [(i, i ^ 1 << bit) for i in r...  24.6 us
    dot_general x5, matrix products, outer_cols(): lax.dot_general(left_op, right_op, (((1,), (1,)), ((), ())), preferred_el...  18.1 us
    dot_general x5, matrix products, product(): return jnp.dot(left_op, right_op, preferred_element_type=jnp.float32)  16.6 us
  transfers between devices with their start and end apart: 29, of which 21 were waited for; matrix products, arithmetic and copies ran while one was open for 24% of the time, Pallas kernels for 0%

profile of v11, /device:TPU:0, one launch (start us, length us, event | category | flops | bytes accessed | tf_op | source)
XLA Modules:
  0.0 452.1 jit_solution(10064067449519192140)
XLA Ops:
  18.4 2.3 dynamic-update-slice.11
  21.6 4.1 collective-permute-start
  25.7 5.0 %collective-permute-done = bf16[1,1,1,1,1,1,8,5120]{7,6,4,3,2,1,0,5:T(8,128)(2,1)S(1)} collective-permute-done((bf16[1,1,1,1,1,1,8,5120]{7,6,4,3,2,1,0,5:T(8,128)(2,1)S(1)}, bf16[1,1,1,1,1,1,8,5120]{7,6,4,3,2,1,0,5:T(8,128)(2,1)S(1)}, u32[]{:S(2)}, u32[]{:S(2)}) %collective-permute-start) | collective-permute-done | bytes 81952 | tf_op jit(solution)/shard_map/ppermute | solution.py:133
  31.4 5.0 %collective-permute-done.1 = bf16[1,1,1,2,1,1,8,5120]{7,6,4,3,2,1,0,5:T(8,128)(2,1)S(1)} collective-permute-done((bf16[1,1,1,2,1,1,8,5120]{7,6,4,3,2,1,0,5:T(8,128)(2,1)S(1)}, bf16[1,1,1,2,1,1,8,5120]{7,6,4,3,2,1,0,5:T(8,128)(2,1)S(1)}, u32[]{:S(2)}, u32[]{:S(2)}) %collective-permute-start.1) | collective-permute-done | bytes 163872 | tf_op jit(solution)/shard_map/ppermute | solution.py:133
  38.0 7.8 %collective-permute-done.2 = bf16[1,1,1,2,2,1,8,5120]{7,6,4,3,2,1,0,5:T(8,128)(2,1)S(1)} collective-permute-done((bf16[1,1,1,2,2,1,8,5120]{7,6,4,3,2,1,0,5:T(8,128)(2,1)S(1)}, bf16[1,1,1,2,2,1,8,5120]{7,6,4,3,2,1,0,5:T(8,128)(2,1)S(1)}, u32[]{:S(2)}, u32[]{:S(2)}) %collective-permute-start.2) | collective-permute-done | bytes 327712 | tf_op jit(solution)/shard_map/ppermute | solution.py:133
  46.7 16.7 %collective-permute-done.3 = bf16[2,1,1,2,2,1,8,5120]{7,6,4,3,2,1,0,5:T(8,128)(2,1)S(1)} collective-permute-done((bf16[2,1,1,2,2,1,8,5120]{7,6,4,3,2,1,0,5:T(8,128)(2,1)S(1)}, bf16[2,1,1,2,2,1,8,5120]{7,6,4,3,2,1,0,5:T(8,128)(2,1)S(1)}, u32[]{:S(2)}, u32[]{:S(2)}) %collective-permute-start.3) | collective-permute-done | bytes 655392 | tf_op jit(solution)/shard_map/ppermute | solution.py:133
  63.8 8.1 %all-to-all-start.1 = ((bf16[64,32,512]{2,1,0:T(8,128)(2,1)}), bf16[64,32,512]{2,1,0:T(8,128)(2,1)}, u32[]{:S(2)}, u32[]{:S(2)}) async-start(bf16[64,32,512]{2,1,0:T(8,128)(2,1)} %param.35), calls=%async_computation.1 | async-start | bytes 4194304 | tf_op jit(solution)/shard_map/all_to_all | solution.py:307
  83.5 4.4 reshape.325
  90.5 48.9 %all-to-all-done.1 = bf16[64,32,512]{2,1,0:T(8,128)(2,1)} async-done(((bf16[64,32,512]{2,1,0:T(8,128)(2,1)}), bf16[64,32,512]{2,1,0:T(8,128)(2,1)}, u32[]{:S(2)}, u32[]{:S(2)}) %all-to-all-start.1) | async-done | bytes 2097184 | tf_op jit(solution)/shard_map/all_to_all | solution.py:307
  146.0 3.6 constant_dynamic-update-slice_fusion.2
  151.4 24.9 %all-gather.3.cloned.1.call-done = bf16[768,6656]{1,0:T(8,128)(2,1)} async-done(((bf16[24,6656]{1,0:T(8,128)(2,1)}), bf16[768,6656]{1,0:T(8,128)(2,1)}) %all-gather.3.cloned.1.call-update) | async-done | bytes 10223632 | tf_op jit(solution)/shard_map/all_gather | solution.py:249
  176.3 4.0 convolution_convert_fusion
  182.5 2.9 reshape.321
  188.8 2.3 copy.122
  191.1 3.1 reshape.322
  196.3 4.8 %fusion.81 = (f32[2,12,256]{2,1,0:T(8,128)S(1)}, f32[2,12,256,256]{2,3,1,0:T(8,128)S(1)}) fusion(f32[2,12,256,256]{2,3,1,0:T(8,128)S(1)} %fusion.58), kind=kOutput, calls=%fused_computation.189 | output fusion | flops 6291711 | bytes 12607488 | tf_op jit(solution)/shard_map/sub | solution.py:167
  201.8 2.5 copy-done.1
  208.1 4.7 %multiply_convert_fusion.1 = (bf16[512,3072]{1,0:T(8,128)(2,1)}, f32[512,3072]{1,0:T(8,128)S(1)}) fusion(f32[3072]{0:T(1024)S(1)} %reshape.354, bf16[768,6656]{1,0:T(8,128)(2,1)S(1)} %bitcast.187, f32[512,768]{1,0:T(8,128)S(1)} %get-tuple-element.62, f32[768]{0:T(1024)S(1)} %reshape.353, f32[768]{0:T(1024)S(1)} %reshape.352, f32[512]{0:T(512)S(1)} %add_rsqrt_fusion, ...), kind=kOutput, calls=%fused_computation.11 | convolution fusion | flops 2427322368 | bytes 15753216 | tf_op jit(solution)/shard_map/dot_general | solution.py:21
  212.8 7.3 %convert_reduce_fusion = (f32[3072]{0:T(1024)}, bf16[512,3072]{1,0:T(8,128)(2,1)S(1)}) fusion(f32[512,3072]{1,0:T(8,128)S(1)} %get-tuple-element.64, f32[3072]{0:T(1024)S(1)} %reshape.354, bf16[3072,768]{1,0:T(8,128)(2,1)} %constant_dynamic-update-slice_fusion.1, f32[512,768]{1,0:T(8,128)S(1)} %fusion.49), kind=kOutput, calls=%fused_computation.8 | convolution fusion | flops 2436756480 | bytes 15753216 | tf_op jit(solution)/shard_map/dot_general | solution.py:31
  220.1 3.5 multiply_reduce_fusion.2
  228.1 3.1 reshape.328
  231.2 5.2 %fusion.33 = bf16[2,256,12,64]{1,3,2,0:T(8,128)(2,1)} fusion(bf16[2,256,12,64]{1,0,3,2:T(2,128)(2,1)} %reshape.328, f32[2,12,256,256]{2,3,1,0:T(8,128)} %copy-done.1, f32[2,12,256]{2,1,0:T(8,128)S(1)} %get-tuple-element.59), kind=kOutput, calls=%fused_computation.83 | convolution fusion | flops 204865536 | bytes 7888896 | tf_op jit(solution)/shard_map/chqk,cqhd->ckhd/dot_general | solution.py:179
  236.3 3.9 multiply_reduce_fusion
  240.2 4.3 multiply_convert_fusion
  249.1 5.0 %add_convert_fusion = bf16[512,768]{1,0:T(8,128)(2,1)S(1)} fusion(f32[512,768]{1,0:T(8,128)S(1)} %copy-done.7, bf16[512,3072]{1,0:T(8,128)(2,1)S(1)} %copy-done.19, bf16[3072,768]{1,0:T(8,128)(2,1)} %constant_dynamic-update-slice_fusion.1, f32[768]{0:T(1024)S(1)} %reshape.355), kind=kOutput, calls=%fused_computation.63 | convolution fusion | flops 2417098752 | bytes 10226688 | tf_op jit(solution)/shard_map/dot_general | solution.py:21
  257.4 3.5 copy.130
  260.9 3.8 all-to-all-start
  274.4 5.8 %multiply_reduce_fusion.3 = (f32[768]{0:T(1024)}, f32[512]{0:T(512)S(1)}, f32[512]{0:T(512)S(1)}, f32[768]{0:T(1024)}, f32[512,768]{1,0:T(8,128)S(1)}) fusion(f32[2,256,768]{2,1,0:T(8,128)S(1)} %copy-done.3, f32[512]{0:T(512)S(1)} %bitcast.194, f32[512]{0:T(512)S(1)} %bitcast.197, f32[768]{0:T(1024)S(1)} %reshape.350, ...), kind=kOutput, calls=%fused_computation.56 | convolution fusion | flops 1822553600 | bytes 9061376 | tf_op jit(solution)/shard_map/dot_general | solution.py:31
  287.1 2.3 concatenate.46
  291.7 2.3 copy.148
  299.1 3.1 fusion.75
  307.8 2.7 fusion.70
  310.5 10.9 %collective-permute-done.6 = bf16[1,2,1,2,2,24,1536]{6,5,4,3,2,1,0:T(8,128)(2,1)S(1)} collective-permute-done((bf16[1,2,1,2,2,24,1536]{6,5,4,3,2,1,0:T(8,128)(2,1)S(1)}, bf16[1,2,1,2,2,24,1536]{6,5,4,3,2,1,0:T(8,128)(2,1)S(1)}, u32[]{:S(2)}, u32[]{:S(2)}) %collective-permute-start.6) | collective-permute-done | bytes 589856 | tf_op jit(solution)/shard_map/ppermute | solution.py:119
  326.8 3.3 collective-permute-done.7
  330.3 3.5 collective-permute-start.8
  335.7 4.2 collective-permute-done.8
  348.8 15.0 %collective-permute-done.11 = bf16[1,2,1,2,2,24,2304]{6,5,4,3,2,1,0:T(8,128)(2,1)} collective-permute-done((bf16[1,2,1,2,2,24,2304]{6,5,4,3,2,1,0:T(8,128)(2,1)}, bf16[1,2,1,2,2,24,2304]{6,5,4,3,2,1,0:T(8,128)(2,1)}, u32[]{:S(2)}, u32[]{:S(2)}) %collective-permute-start.11) | collective-permute-done | bytes 884768 | tf_op jit(solution)/shard_map/ppermute | solution.py:119
  365.4 3.8 convert_add_fusion.1
  371.1 5.0 %collective-permute-done.12 = bf16[1,2,1,2,1,24,2304]{6,5,4,3,2,1,0:T(8,128)(2,1)S(1)} collective-permute-done((bf16[1,2,1,2,1,24,2304]{6,5,4,3,2,1,0:T(8,128)(2,1)S(1)}, bf16[1,2,1,2,1,24,2304]{6,5,4,3,2,1,0:T(8,128)(2,1)S(1)}, u32[]{:S(2)}, u32[]{:S(2)}) %collective-permute-start.12) | collective-permute-done | bytes 442400 | tf_op jit(solution)/shard_map/ppermute | solution.py:119
  377.6 2.4 convert_add_fusion
  380.9 6.4 %collective-permute-done.13 = bf16[1,2,1,1,1,24,2304]{6,5,4,3,2,1,0:T(8,128)(2,1)S(1)} collective-permute-done((bf16[1,2,1,1,1,24,2304]{6,5,4,3,2,1,0:T(8,128)(2,1)S(1)}, bf16[1,2,1,1,1,24,2304]{6,5,4,3,2,1,0:T(8,128)(2,1)S(1)}, u32[]{:S(2)}, u32[]{:S(2)}) %collective-permute-start.13) | collective-permute-done | bytes 221216 | tf_op jit(solution)/shard_map/ppermute | solution.py:119
  388.4 7.7 %collective-permute-done.16 = bf16[1,2,1,2,2,24,3072]{6,5,4,3,2,1,0:T(8,128)(2,1)S(1)} collective-permute-done((bf16[1,2,1,2,2,24,3072]{6,5,4,3,2,1,0:T(8,128)(2,1)S(1)}, bf16[1,2,1,2,2,24,3072]{6,5,4,3,2,1,0:T(8,128)(2,1)S(1)}, u32[]{:S(2)}, u32[]{:S(2)}) %collective-permute-start.16) | collective-permute-done | bytes 1179680 | tf_op jit(solution)/shard_map/ppermute | solution.py:119
  397.4 14.1 %collective-permute-done.14 = bf16[1,1,1,1,1,24,2304]{6,5,4,3,2,1,0:T(8,128)(2,1)S(1)} collective-permute-done((bf16[1,1,1,1,1,24,2304]{6,5,4,3,2,1,0:T(8,128)(2,1)S(1)}, bf16[1,1,1,1,1,24,2304]{6,5,4,3,2,1,0:T(8,128)(2,1)S(1)}, u32[]{:S(2)}, u32[]{:S(2)}) %collective-permute-start.14) | collective-permute-done | bytes 110624 | tf_op jit(solution)/shard_map/ppermute | solution.py:119
  414.3 3.4 copy.131
  417.7 3.0 collective-permute-done.17
  427.0 5.3 %collective-permute-done.18 = bf16[1,1,1,2,1,24,3072]{6,5,4,3,2,1,0:T(8,128)(2,1)S(1)} collective-permute-done((bf16[1,1,1,2,1,24,3072]{6,5,4,3,2,1,0:T(8,128)(2,1)S(1)}, bf16[1,1,1,2,1,24,3072]{6,5,4,3,2,1,0:T(8,128)(2,1)S(1)}, u32[]{:S(2)}, u32[]{:S(2)}) %collective-permute-start.18) | collective-permute-done | bytes 294944 | tf_op jit(solution)/shard_map/ppermute | solution.py:119
  436.1 3.1 collective-permute-start.24
  441.9 2.4 collective-permute-done.24
  (323 shorter events, 132.0 us)
Async XLA Ops:
  7.2 138.8 %all-gather.5.cloned.1.call-start = ((), (), s32[]{:S(2)}) async-start(), calls=%async_computation.3 | async-start | bytes 2433024 | tf_op jit(solution)/shard_map/all_gather | solution.py:256
  8.8 167.4 %all-gather.3.cloned.1.call-start = ((), (), s32[]{:S(2)}) async-start(), calls=%async_computation.2 | async-start | bytes 10543104 | tf_op jit(solution)/shard_map/all_gather | solution.py:249
  21.6 9.2 %collective-permute-start = (bf16[1,1,1,1,1,1,8,5120]{7,6,4,3,2,1,0,5:T(8,128)(2,1)S(1)}, bf16[1,1,1,1,1,1,8,5120]{7,6,4,3,2,1,0,5:T(8,128)(2,1)S(1)}, u32[]{:S(2)}, u32[]{:S(2)}) collective-permute-start(bf16[1,1,1,1,1,1,8,5120]{7,6,4,3,2,1,0,5:T(8,128)(2,1)S(1)} %bitcast.188), channel_id=1, source_target_pairs={{0,2},{1,3},{2,0},{3,1},{4,6},{5,7},{6,4},{7,5},{8,10},{9,11},{10,... | collective-permute-start | bytes 245768 | tf_op jit(solution)/shard_map/ppermute | solution.py:133
  30.8 5.6 %collective-permute-start.1 = (bf16[1,1,1,2,1,1,8,5120]{7,6,4,3,2,1,0,5:T(8,128)(2,1)S(1)}, bf16[1,1,1,2,1,1,8,5120]{7,6,4,3,2,1,0,5:T(8,128)(2,1)S(1)}, u32[]{:S(2)}, u32[]{:S(2)}) collective-permute-start(bf16[1,1,1,2,1,1,8,5120]{7,6,4,3,2,1,0,5:T(8,128)(2,1)S(1)} %pad_maximum_fusion.9), channel_id=1, source_target_pairs={{0,1},{1,0},{2,3},{3,2},{4,5},{5,4},{6,7},{7,6},{8,9},{9,8},{10,11... | collective-permute-start | bytes 491528 | tf_op jit(solution)/shard_map/ppermute | solution.py:133
  36.5 9.3 %collective-permute-start.2 = (bf16[1,1,1,2,2,1,8,5120]{7,6,4,3,2,1,0,5:T(8,128)(2,1)S(1)}, bf16[1,1,1,2,2,1,8,5120]{7,6,4,3,2,1,0,5:T(8,128)(2,1)S(1)}, u32[]{:S(2)}, u32[]{:S(2)}) collective-permute-start(bf16[1,1,1,2,2,1,8,5120]{7,6,4,3,2,1,0,5:T(8,128)(2,1)S(1)} %pad_maximum_fusion.7), channel_id=1, source_target_pairs={{0,16},{1,17},{2,18},{3,19},{4,20},{5,21},{6,22},{7,23},{8,24},{9,... | collective-permute-start | bytes 983048 | tf_op jit(solution)/shard_map/ppermute | solution.py:133
  45.9 17.5 %collective-permute-start.3 = (bf16[2,1,1,2,2,1,8,5120]{7,6,4,3,2,1,0,5:T(8,128)(2,1)S(1)}, bf16[2,1,1,2,2,1,8,5120]{7,6,4,3,2,1,0,5:T(8,128)(2,1)S(1)}, u32[]{:S(2)}, u32[]{:S(2)}) collective-permute-start(bf16[2,1,1,2,2,1,8,5120]{7,6,4,3,2,1,0,5:T(8,128)(2,1)S(1)} %pad_maximum_fusion.6), channel_id=1, source_target_pairs={{0,8},{1,9},{2,10},{3,11},{4,12},{5,13},{6,14},{7,15},{8,0},{9,1},... | collective-permute-start | bytes 1966088 | tf_op jit(solution)/shard_map/ppermute | solution.py:133
  63.7 8.3 %copy-start.51 = (s32[2,256]{1,0:T(2,128)S(1)}, s32[2,256]{1,0:T(2,128)}, u32[]{:S(2)}) copy-start(s32[2,256]{1,0:T(2,128)} %param.20) | copy-start | bytes 6148
  63.7 8.6 %copy-start.52 = (s32[2,13]{1,0:T(2,128)S(1)}, s32[2,13]{1,0:T(2,128)}, u32[]{:S(2)}) copy-start(s32[2,13]{1,0:T(2,128)} %param.19) | copy-start | bytes 316
  63.7 8.9 %collective-permute-start.4 = (bf16[2,2,1,2,2,1,8,5120]{7,6,4,3,2,1,0,5:T(8,128)(2,1)S(1)}, bf16[2,2,1,2,2,1,8,5120]{7,6,4,3,2,1,0,5:T(8,128)(2,1)}, u32[]{:S(2)}, u32[]{:S(2)}) collective-permute-start(bf16[2,2,1,2,2,1,8,5120]{7,6,4,3,2,1,0,5:T(8,128)(2,1)S(1)} %pad_maximum_fusion.3), channel_id=1, source_target_pairs={{0,4},{1,5},{2,6},{3,7},{4,0},{5,1},{6,2},{7,3},{8,12},{9,13},{10,... | collective-permute-start | bytes 3932168 | tf_op jit(solution)/shard_map/ppermute | solution.py:133
  63.8 75.6 %all-to-all-start.1 = ((bf16[64,32,512]{2,1,0:T(8,128)(2,1)}), bf16[64,32,512]{2,1,0:T(8,128)(2,1)}, u32[]{:S(2)}, u32[]{:S(2)}) async-start(bf16[64,32,512]{2,1,0:T(8,128)(2,1)} %param.35), calls=%async_computation.1 | async-start | bytes 4194304 | tf_op jit(solution)/shard_map/all_to_all | solution.py:307
  82.4 123.0 %copy-start.2 = (f32[2,256,768]{2,1,0:T(8,128)}, f32[2,256,768]{2,1,0:T(8,128)S(1)}, u32[]{:S(2)}) copy-start(f32[2,256,768]{2,1,0:T(8,128)S(1)} %get-tuple-element.41) | copy-start | bytes 4718596
  83.4 124.7 %copy-start.45 = (f32[768]{0:T(1024)}, f32[768]{0:T(1024)S(1)}, u32[]{:S(2)}) copy-start(f32[768]{0:T(1024)S(1)} %reshape.353) | copy-start | bytes 9220
  83.5 140.2 %copy-start.39 = (f32[768]{0:T(1024)}, f32[768]{0:T(1024)S(1)}, u32[]{:S(2)}) copy-start(f32[768]{0:T(1024)S(1)} %reshape.352) | copy-start | bytes 9220
  196.3 9.0 %slice-start.5 = ((s8[10223616]{0:T(1024)(128)(4,1)}), s8[4194304]{0:T(1024)(128)(4,1)S(1)}, s32[]{:S(2)}) async-start(s8[10223616]{0:T(1024)(128)(4,1)} %bitcast.186), calls=%async_computation.9 | async-start | bytes 8388608
  207.1 16.5 %copy-start.6 = (f32[512,768]{1,0:T(8,128)}, f32[512,768]{1,0:T(8,128)S(1)}, u32[]{:S(2)}) copy-start(f32[512,768]{1,0:T(8,128)S(1)} %get-tuple-element.62) | copy-start | bytes 4718596
  207.1 16.5 %copy-start.37 = (f32[512]{0:T(512)}, f32[512]{0:T(512)S(1)}, u32[]{:S(2)}) copy-start(f32[512]{0:T(512)S(1)} %broadcast_multiply_fusion.4) | copy-start | bytes 6148
  207.5 16.2 %copy-start.43 = (f32[512]{0:T(512)}, f32[512]{0:T(512)S(1)}, u32[]{:S(2)}) copy-start(f32[512]{0:T(512)S(1)} %add_rsqrt_fusion) | copy-start | bytes 6148
  208.1 15.6 %copy-start.4 = (f32[512,768]{1,0:T(8,128)}, f32[512,768]{1,0:T(8,128)S(1)}, u32[]{:S(2)}) copy-start(f32[512,768]{1,0:T(8,128)S(1)} %fusion.49) | copy-start | bytes 4718596
  228.1 8.2 %slice-start.3 = ((s8[6291456]{0:T(1024)(128)(4,1)}), s8[2097152]{0:T(1024)(128)(4,1)S(1)}, s32[]{:S(2)}) async-start(s8[6291456]{0:T(1024)(128)(4,1)} %bitcast.155), calls=%async_computation.7 | async-start | bytes 4194304
  260.9 153.4 %all-to-all-start = ((bf16[2,1024,512]{2,0,1:T(2,128)(2,1)}), bf16[2,1024,512]{2,0,1:T(2,128)(2,1)}, u32[]{:S(2)}, u32[]{:S(2)}) async-start(bf16[2,1024,512]{2,0,1:T(2,128)(2,1)} %copy.130), calls=%async_computation | async-start | bytes 4194304 | tf_op jit(solution)/shard_map/all_to_all | solution.py:306
  274.4 5.8 %copy-start.9 = (f32[512,768]{1,0:T(8,128)S(1)}, f32[512,768]{1,0:T(8,128)}, u32[]{:S(2)}) copy-start(f32[512,768]{1,0:T(8,128)} %copy-done.8) | copy-start | bytes 4718596
  287.1 6.9 %copy-start.10 = (f32[512,768]{1,0:T(8,128)S(1)}, f32[512,768]{1,0:T(8,128)}, u32[]{:S(2)}) copy-start(f32[512,768]{1,0:T(8,128)} %copy-done.8) | copy-start | bytes 4718596
  298.0 6.3 %collective-permute-start.5 = (bf16[2,2,1,2,2,24,1536]{6,5,4,3,2,1,0:T(8,128)(2,1)S(1)}, bf16[2,2,1,2,2,24,1536]{6,5,4,3,2,1,0:T(8,128)(2,1)S(1)}, u32[]{:S(2)}, u32[]{:S(2)}) collective-permute-start(bf16[2,2,1,2,2,24,1536]{6,5,4,3,2,1,0:T(8,128)(2,1)S(1)} %dynamic-slice_convert_fusion.5), channel_id=1, source_target_pairs={{0,4},{1,5},{2,6},{3,7},{4,0},{5,1},{6,2},{7,3},{8,12},{9,13},{10,... | collective-permute-start | bytes 3538952 | tf_op jit(solution)/shard_map/ppermute | solution.py:119
  302.2 20.6 %copy-start.18 = (f32[768,3072]{1,0:T(8,128)}, f32[768,3072]{1,0:T(8,128)S(1)}, u32[]{:S(2)}) copy-start(f32[768,3072]{1,0:T(8,128)S(1)} %fusion.75) | copy-start | bytes 28311556
  304.8 16.5 %collective-permute-start.6 = (bf16[1,2,1,2,2,24,1536]{6,5,4,3,2,1,0:T(8,128)(2,1)S(1)}, bf16[1,2,1,2,2,24,1536]{6,5,4,3,2,1,0:T(8,128)(2,1)S(1)}, u32[]{:S(2)}, u32[]{:S(2)}) collective-permute-start(bf16[1,2,1,2,2,24,1536]{6,5,4,3,2,1,0:T(8,128)(2,1)S(1)} %dynamic-slice_convert_fusion.9), channel_id=1, source_target_pairs={{0,16},{1,17},{2,18},{3,19},{4,20},{5,21},{6,22},{7,23},{8,24},{9,... | collective-permute-start | bytes 1769480 | tf_op jit(solution)/shard_map/ppermute | solution.py:119
  306.6 27.2 %collective-permute-start.10 = (bf16[2,2,1,2,2,24,2304]{6,5,4,3,2,1,0:T(8,128)(2,1)S(1)}, bf16[2,2,1,2,2,24,2304]{6,5,4,3,2,1,0:T(8,128)(2,1)}, u32[]{:S(2)}, u32[]{:S(2)}) collective-permute-start(bf16[2,2,1,2,2,24,2304]{6,5,4,3,2,1,0:T(8,128)(2,1)S(1)} %dynamic-slice_convert_fusion.2), channel_id=1, source_target_pairs={{0,4},{1,5},{2,6},{3,7},{4,0},{5,1},{6,2},{7,3},{8,12},{9,13},{10,... | collective-permute-start | bytes 5308424 | tf_op jit(solution)/shard_map/ppermute | solution.py:119
  310.5 19.8 %copy-start = (f32[3072,768]{1,0:T(8,128)}, f32[3072,768]{1,0:T(8,128)S(1)}, u32[]{:S(2)}) copy-start(f32[3072,768]{1,0:T(8,128)S(1)} %fusion.70) | copy-start | bytes 28311556
  321.5 8.6 %collective-permute-start.7 = (bf16[1,2,1,2,1,24,1536]{6,5,4,3,2,1,0:T(8,128)(2,1)S(1)}, bf16[1,2,1,2,1,24,1536]{6,5,4,3,2,1,0:T(8,128)(2,1)S(1)}, u32[]{:S(2)}, u32[]{:S(2)}) collective-permute-start(bf16[1,2,1,2,1,24,1536]{6,5,4,3,2,1,0:T(8,128)(2,1)S(1)} %dynamic-slice_convert_fusion.13), channel_id=1, source_target_pairs={{0,1},{1,0},{2,3},{3,2},{4,5},{5,4},{6,7},{7,6},{8,9},{9,8},{10,11... | collective-permute-start | bytes 884744 | tf_op jit(solution)/shard_map/ppermute | solution.py:119
  324.6 40.8 %collective-permute-start.15 = (bf16[2,2,1,2,2,24,3072]{6,5,4,3,2,1,0:T(8,128)(2,1)}, bf16[2,2,1,2,2,24,3072]{6,5,4,3,2,1,0:T(8,128)(2,1)}, u32[]{:S(2)}, u32[]{:S(2)}) collective-permute-start(bf16[2,2,1,2,2,24,3072]{6,5,4,3,2,1,0:T(8,128)(2,1)} %dynamic-slice_convert_fusion.1), channel_id=1, source_target_pairs={{0,4},{1,5},{2,6},{3,7},{4,0},{5,1},{6,2},{7,3},{8,12},{9,13},{10,... | collective-permute-start | bytes 7077896 | tf_op jit(solution)/shard_map/ppermute | solution.py:119
  326.3 51.3 %collective-permute-start.20 = (bf16[2,2,1,2,2,96,768]{6,5,4,3,2,1,0:T(8,128)(2,1)}, bf16[2,2,1,2,2,96,768]{6,5,4,3,2,1,0:T(8,128)(2,1)}, u32[]{:S(2)}, u32[]{:S(2)}) collective-permute-start(bf16[2,2,1,2,2,96,768]{6,5,4,3,2,1,0:T(8,128)(2,1)} %dynamic-slice_convert_fusion), channel_id=1, source_target_pairs={{0,4},{1,5},{2,6},{3,7},{4,0},{5,1},{6,2},{7,3},{8,12},{9,13},{10,... | collective-permute-start | bytes 7077896 | tf_op jit(solution)/shard_map/ppermute | solution.py:119
  330.3 9.6 %collective-permute-start.8 = (bf16[1,2,1,1,1,24,1536]{6,5,4,3,2,1,0:T(8,128)(2,1)S(1)}, bf16[1,2,1,1,1,24,1536]{6,5,4,3,2,1,0:T(8,128)(2,1)S(1)}, u32[]{:S(2)}, u32[]{:S(2)}) collective-permute-start(bf16[1,2,1,1,1,24,1536]{6,5,4,3,2,1,0:T(8,128)(2,1)S(1)} %dynamic-slice_convert_fusion.17), channel_id=1, source_target_pairs={{0,2},{1,3},{2,0},{3,1},{4,6},{5,7},{6,4},{7,5},{8,10},{9,11},{10,... | collective-permute-start | bytes 442376 | tf_op jit(solution)/shard_map/ppermute | solution.py:119
  339.9 4.4 collective-permute-start.9
  342.3 21.5 %collective-permute-start.11 = (bf16[1,2,1,2,2,24,2304]{6,5,4,3,2,1,0:T(8,128)(2,1)}, bf16[1,2,1,2,2,24,2304]{6,5,4,3,2,1,0:T(8,128)(2,1)}, u32[]{:S(2)}, u32[]{:S(2)}) collective-permute-start(bf16[1,2,1,2,2,24,2304]{6,5,4,3,2,1,0:T(8,128)(2,1)} %dynamic-slice_convert_fusion.6), channel_id=1, source_target_pairs={{0,16},{1,17},{2,18},{3,19},{4,20},{5,21},{6,22},{7,23},{8,24},{9,... | collective-permute-start | bytes 2654216 | tf_op jit(solution)/shard_map/ppermute | solution.py:119
  365.1 12.5 %slice-start = ((s8[9437184]{0:T(1024)(128)(4,1)}), s8[4194304]{0:T(1024)(128)(4,1)S(1)}, s32[]{:S(2)}) async-start(s8[9437184]{0:T(1024)(128)(4,1)} %bitcast.152), calls=%async_computation.4 | async-start | bytes 8388608
  365.2 12.4 %slice-start.1 = ((s8[9437184]{0:T(1024)(128)(4,1)}), s8[4194304]{0:T(1024)(128)(4,1)S(1)}, s32[]{:S(2)}) async-start(s8[9437184]{0:T(1024)(128)(4,1)} %bitcast.152), calls=%async_computation.5 | async-start | bytes 8388608
  365.2 12.4 %slice-start.2 = ((s8[9437184]{0:T(1024)(128)(4,1)}), s8[1048576]{0:T(1024)(128)(4,1)S(1)}, s32[]{:S(2)}) async-start(s8[9437184]{0:T(1024)(128)(4,1)} %bitcast.152), calls=%async_computation.6 | async-start | bytes 2097152
  365.2 10.9 %collective-permute-start.12 = (bf16[1,2,1,2,1,24,2304]{6,5,4,3,2,1,0:T(8,128)(2,1)S(1)}, bf16[1,2,1,2,1,24,2304]{6,5,4,3,2,1,0:T(8,128)(2,1)S(1)}, u32[]{:S(2)}, u32[]{:S(2)}) collective-permute-start(bf16[1,2,1,2,1,24,2304]{6,5,4,3,2,1,0:T(8,128)(2,1)S(1)} %dynamic-slice_convert_fusion.10), channel_id=1, source_target_pairs={{0,1},{1,0},{2,3},{3,2},{4,5},{5,4},{6,7},{7,6},{8,9},{9,8},{10,11... | collective-permute-start | bytes 1327112 | tf_op jit(solution)/shard_map/ppermute | solution.py:119
  369.4 26.7 %collective-permute-start.16 = (bf16[1,2,1,2,2,24,3072]{6,5,4,3,2,1,0:T(8,128)(2,1)S(1)}, bf16[1,2,1,2,2,24,3072]{6,5,4,3,2,1,0:T(8,128)(2,1)S(1)}, u32[]{:S(2)}, u32[]{:S(2)}) collective-permute-start(bf16[1,2,1,2,2,24,3072]{6,5,4,3,2,1,0:T(8,128)(2,1)S(1)} %dynamic-slice_convert_fusion.4), channel_id=1, source_target_pairs={{0,16},{1,17},{2,18},{3,19},{4,20},{5,21},{6,22},{7,23},{8,24},{9,... | collective-permute-start | bytes 3538952 | tf_op jit(solution)/shard_map/ppermute | solution.py:119
  376.3 10.9 %collective-permute-start.13 = (bf16[1,2,1,1,1,24,2304]{6,5,4,3,2,1,0:T(8,128)(2,1)S(1)}, bf16[1,2,1,1,1,24,2304]{6,5,4,3,2,1,0:T(8,128)(2,1)S(1)}, u32[]{:S(2)}, u32[]{:S(2)}) collective-permute-start(bf16[1,2,1,1,1,24,2304]{6,5,4,3,2,1,0:T(8,128)(2,1)S(1)} %dynamic-slice_convert_fusion.14), channel_id=1, source_target_pairs={{0,2},{1,3},{2,0},{3,1},{4,6},{5,7},{6,4},{7,5},{8,10},{9,11},{10,... | collective-permute-start | bytes 663560 | tf_op jit(solution)/shard_map/ppermute | solution.py:119
  380.2 32.0 %collective-permute-start.21 = (bf16[2,1,1,2,2,96,768]{6,5,4,3,2,1,0:T(8,128)(2,1)S(1)}, bf16[2,1,1,2,2,96,768]{6,5,4,3,2,1,0:T(8,128)(2,1)S(1)}, u32[]{:S(2)}, u32[]{:S(2)}) collective-permute-start(bf16[2,1,1,2,2,96,768]{6,5,4,3,2,1,0:T(8,128)(2,1)S(1)} %dynamic-slice_convert_fusion.3), channel_id=1, source_target_pairs={{0,8},{1,9},{2,10},{3,11},{4,12},{5,13},{6,14},{7,15},{8,0},{9,1},... | collective-permute-start | bytes 3538952 | tf_op jit(solution)/shard_map/ppermute | solution.py:119
  387.3 24.2 %collective-permute-start.14 = (bf16[1,1,1,1,1,24,2304]{6,5,4,3,2,1,0:T(8,128)(2,1)S(1)}, bf16[1,1,1,1,1,24,2304]{6,5,4,3,2,1,0:T(8,128)(2,1)S(1)}, u32[]{:S(2)}, u32[]{:S(2)}) collective-permute-start(bf16[1,1,1,1,1,24,2304]{6,5,4,3,2,1,0:T(8,128)(2,1)S(1)} %dynamic-slice_convert_fusion.18), channel_id=1, source_target_pairs={{0,8},{1,9},{2,10},{3,11},{4,12},{5,13},{6,14},{7,15},{8,0},{9,1},... | collective-permute-start | bytes 331784 | tf_op jit(solution)/shard_map/ppermute | solution.py:119
  396.4 24.3 %collective-permute-start.17 = (bf16[1,1,1,2,2,24,3072]{6,5,4,3,2,1,0:T(8,128)(2,1)S(1)}, bf16[1,1,1,2,2,24,3072]{6,5,4,3,2,1,0:T(8,128)(2,1)}, u32[]{:S(2)}, u32[]{:S(2)}) collective-permute-start(bf16[1,1,1,2,2,24,3072]{6,5,4,3,2,1,0:T(8,128)(2,1)S(1)} %dynamic-slice_convert_fusion.8), channel_id=1, source_target_pairs={{0,8},{1,9},{2,10},{3,11},{4,12},{5,13},{6,14},{7,15},{8,0},{9,1},... | collective-permute-start | bytes 1769480 | tf_op jit(solution)/shard_map/ppermute | solution.py:119
  413.9 10.1 %collective-permute-start.22 = (bf16[1,1,1,2,2,96,768]{6,5,4,3,2,1,0:T(8,128)(2,1)S(1)}, bf16[1,1,1,2,2,96,768]{6,5,4,3,2,1,0:T(8,128)(2,1)}, u32[]{:S(2)}, u32[]{:S(2)}) collective-permute-start(bf16[1,1,1,2,2,96,768]{6,5,4,3,2,1,0:T(8,128)(2,1)S(1)} %dynamic-slice_convert_fusion.7), channel_id=1, source_target_pairs={{0,16},{1,17},{2,18},{3,19},{4,20},{5,21},{6,22},{7,23},{8,24},{9,... | collective-permute-start | bytes 1769480 | tf_op jit(solution)/shard_map/ppermute | solution.py:119
  417.7 6.3 %copy-start.14 = (f32[2,1,1,2,2,96,768]{6,5,4,3,2,1,0:T(8,128)S(1)}, f32[2,1,1,2,2,96,768]{6,5,4,3,2,1,0:T(8,128)}, u32[]{:S(2)}) copy-start(f32[2,1,1,2,2,96,768]{6,5,4,3,2,1,0:T(8,128)} %copy-done.13) | copy-start | bytes 7077892
  422.0 10.3 %collective-permute-start.18 = (bf16[1,1,1,2,1,24,3072]{6,5,4,3,2,1,0:T(8,128)(2,1)S(1)}, bf16[1,1,1,2,1,24,3072]{6,5,4,3,2,1,0:T(8,128)(2,1)S(1)}, u32[]{:S(2)}, u32[]{:S(2)}) collective-permute-start(bf16[1,1,1,2,1,24,3072]{6,5,4,3,2,1,0:T(8,128)(2,1)S(1)} %dynamic-slice_convert_fusion.12), channel_id=1, source_target_pairs={{0,1},{1,0},{2,3},{3,2},{4,5},{5,4},{6,7},{7,6},{8,9},{9,8},{10,11... | collective-permute-start | bytes 884744 | tf_op jit(solution)/shard_map/ppermute | solution.py:119
  425.2 10.8 %collective-permute-start.23 = (bf16[1,1,1,2,1,96,768]{6,5,4,3,2,1,0:T(8,128)(2,1)S(1)}, bf16[1,1,1,2,1,96,768]{6,5,4,3,2,1,0:T(8,128)(2,1)S(1)}, u32[]{:S(2)}, u32[]{:S(2)}) collective-permute-start(bf16[1,1,1,2,1,96,768]{6,5,4,3,2,1,0:T(8,128)(2,1)S(1)} %dynamic-slice_convert_fusion.11), channel_id=1, source_target_pairs={{0,1},{1,0},{2,3},{3,2},{4,5},{5,4},{6,7},{7,6},{8,9},{9,8},{10,11... | collective-permute-start | bytes 884744 | tf_op jit(solution)/shard_map/ppermute | solution.py:119
  432.4 8.8 %collective-permute-start.19 = (bf16[1,1,1,1,1,24,3072]{6,5,4,3,2,1,0:T(8,128)(2,1)S(1)}, bf16[1,1,1,1,1,24,3072]{6,5,4,3,2,1,0:T(8,128)(2,1)S(1)}, u32[]{:S(2)}, u32[]{:S(2)}) collective-permute-start(bf16[1,1,1,1,1,24,3072]{6,5,4,3,2,1,0:T(8,128)(2,1)S(1)} %dynamic-slice_convert_fusion.16), channel_id=1, source_target_pairs={{0,2},{1,3},{2,0},{3,1},{4,6},{5,7},{6,4},{7,5},{8,10},{9,11},{10,... | collective-permute-start | bytes 442376 | tf_op jit(solution)/shard_map/ppermute | solution.py:119
  436.1 8.2 %collective-permute-start.24 = (bf16[1,1,1,1,1,96,768]{6,5,4,3,2,1,0:T(8,128)(2,1)S(1)}, bf16[1,1,1,1,1,96,768]{6,5,4,3,2,1,0:T(8,128)(2,1)S(1)}, u32[]{:S(2)}, u32[]{:S(2)}) collective-permute-start(bf16[1,1,1,1,1,96,768]{6,5,4,3,2,1,0:T(8,128)(2,1)S(1)} %dynamic-slice_convert_fusion.15), channel_id=1, source_target_pairs={{0,2},{1,3},{2,0},{3,1},{4,6},{5,7},{6,4},{7,5},{8,10},{9,11},{10,... | collective-permute-start | bytes 442376 | tf_op jit(solution)/shard_map/ppermute | solution.py:119
  (44 other events, 127.7 us)
Sparse Core Ops, SparseCore 0:
  11.4 61.8 all-gather.4
  76.6 99.5 all-gather.2

commit v12 on v9

--- a/solution.py
+++ b/solution.py
@@ -270,11 +270,10 @@
             residual, gain_one.astype(jnp.float32), shift_one.astype(jnp.float32)
         )
         act_one = norm_out_one.astype(jnp.bfloat16)
-        qkv_vals = product(act_one, qkv_full).astype(jnp.bfloat16)
         head_shape = (chip_count, vis_len, heads, HD)
-        queries = qkv_vals[:, :D].reshape(head_shape)
-        key_rows = qkv_vals[:, D : 2 * D].reshape(head_shape)
-        value_rows = qkv_vals[:, 2 * D :].reshape(head_shape)
+        queries = product(act_one, qkv_full[:, :D]).astype(jnp.bfloat16).reshape(head_shape)
+        key_rows = product(act_one, qkv_full[:, D : 2 * D]).astype(jnp.bfloat16).reshape(head_shape)
+        value_rows = product(act_one, qkv_full[:, 2 * D :]).astype(jnp.bfloat16).reshape(head_shape)
         mixture4, soft_full, soft_low = attend(queries, key_rows, value_rows)
         mixture = mixture4.reshape(row_count, D)
         res_one = residual + product(mixture, out_full)

time: 429 us -> 429 us (level)
  local copies, waits for them, and re-layouts: 72.3 us -> 66.6 us
    slice x4 -> x0, local copies, waits for them, and re-layouts: 5.64 us -> none  [the longest x1 2.29 us: local(): value_rows = qkv_vals[:, 2 * D:].reshape(head_shape)]
    dot_general x5 -> x7, matrix products: 17.4 us -> 21 us  [product(): return jnp.dot(left_op, right_op, preferred_element_type=jnp.float32)]
    unnamed x136 -> x138, local copies, waits for them, and re-layouts: 17.1 us -> 17.9 us
  transfers between devices with their start and end apart: 29 -> 29, of which waited for: 21 -> 22; matrix products, arithmetic and copies ran while one was open for 26% -> 26% of each run, Pallas kernels for 0% -> 0%
where the time goes in v12:
time: 429 us; the launch traced here: 424 us
  waiting for transfers between devices  198 us (46%)
  matrix products  71.1 us (17%)
  local copies, waits for them, and re-layouts  66.6 us (16%)
  starting transfers between devices  40.2 us (9%)
  other arithmetic  32.7 us (8%)
  between operations  15.6 us (4%)
    ppermute x20, waiting for transfers between devices, rs_chain(): lax.ppermute(send.astype(jnp.bfloat16), AX, [(i, i ^ 1 << bit) for i in r...  81.6 us
    ppermute x5, waiting for transfers between devices, ag_chain(): moved = lax.ppermute(current, AX, [(i, i ^ 1 << bit) for i in range(n_dev)])  54 us
    all_gather x1, waiting for transfers between devices, local(): outer_full = lax.all_gather(mlp_out, AX, axis=0, tiled=True)  31.6 us
    all_gather x1, waiting for transfers between devices, local(): lax.all_gather(jnp.concatenate(wide, axis=1), AX, axis=0, tiled=True)  27.3 us
    dot_general x5, matrix products, outer_cols(): lax.dot_general(left_op, right_op, (((1,), (1,)), ((), ())), preferred_el...  23.7 us
    ppermute x20, starting transfers between devices, rs_chain(): lax.ppermute(send.astype(jnp.bfloat16), AX, [(i, i ^ 1 << bit) for i in r...  23.4 us
    dot_general x7, matrix products, product(): return jnp.dot(left_op, right_op, preferred_element_type=jnp.float32)  21 us
    unnamed x138, local copies, waits for them, and re-layouts  17.9 us
  transfers between devices with their start and end apart: 29, of which 22 were waited for; matrix products, arithmetic and copies ran while one was open for 26% of the time, Pallas kernels for 0%

profile of v12, /device:TPU:0, one launch (start us, length us, event | category | flops | bytes accessed | tf_op | source)
XLA Modules:
  0.0 424.3 jit_solution(8729144956818633254)
XLA Ops:
  10.7 4.1 collective-permute-start
  14.8 4.0 all-to-all-start.1
  20.7 48.3 %collective-permute-done.1 = bf16[1,1,1,2,1,1,8,512]{7,6,4,3,2,1,0,5:T(8,128)(2,1)S(1)} collective-permute-done((bf16[1,1,1,2,1,1,8,512]{7,6,4,3,2,1,0,5:T(8,128)(2,1)S(1)}, bf16[1,1,1,2,1,1,8,512]{7,6,4,3,2,1,0,5:T(8,128)(2,1)S(1)}, u32[]{:S(2)}, u32[]{:S(2)}) %collective-permute-start.1) | collective-permute-done | bytes 16416 | tf_op jit(solution)/shard_map/ppermute | solution.py:133
  70.6 2.3 collective-permute-done.2
  74.9 2.4 collective-permute-done.3
  82.4 3.7 all-to-all-done.1
  86.0 2.1 copy.129
  93.1 27.3 %all-gather.3.cloned.1.call-done = bf16[768,6656]{1,0:T(8,128)(2,1)} async-done(((bf16[24,6656]{1,0:T(8,128)(2,1)}), bf16[768,6656]{1,0:T(8,128)(2,1)}) %all-gather.3.cloned.1.call-update) | async-done | bytes 10223632 | tf_op jit(solution)/shard_map/all_gather | solution.py:247
  120.4 2.9 convolution_convert_fusion.3
  128.3 2.6 convolution_convert_fusion.2
  132.1 2.2 reshape.315
  135.4 4.8 %fusion.81 = (f32[2,12,256]{2,1,0:T(8,128)S(1)}, f32[2,12,256,256]{2,3,1,0:T(8,128)S(1)}) fusion(f32[2,12,256,256]{2,3,1,0:T(8,128)S(1)} %fusion.60), kind=kOutput, calls=%fused_computation.187 | output fusion | flops 6291711 | bytes 12607488 | tf_op jit(solution)/shard_map/sub | solution.py:167
  140.9 2.5 copy-done.1
  148.1 5.6 %multiply_convert_fusion.1 = (bf16[512,3072]{1,0:T(8,128)(2,1)}, f32[512,3072]{1,0:T(8,128)}) fusion(f32[3072]{0:T(1024)S(1)} %reshape.346, bf16[768,6656]{1,0:T(8,128)(2,1)S(1)} %bitcast.183, f32[512,768]{1,0:T(8,128)S(1)} %get-tuple-element.57, f32[768]{0:T(1024)S(1)} %reshape.345, f32[768]{0:T(1024)S(1)} %reshape.344, f32[512]{0:T(512)S(1)} %add_rsqrt_fusion, ...), kind=kOutput, calls=%fused_computation.11 | convolution fusion | flops 2427322368 | bytes 15753216 | tf_op jit(solution)/shard_map/dot_general | solution.py:21
  153.7 31.6 %all-gather.5.cloned.1.call-done = bf16[3072,768]{1,0:T(8,128)(2,1)} async-done(((bf16[96,768]{1,0:T(8,128)(2,1)}), bf16[3072,768]{1,0:T(8,128)(2,1)}) %all-gather.5.cloned.1.call-update) | async-done | bytes 4718608 | tf_op jit(solution)/shard_map/all_gather | solution.py:254
  185.3 8.1 %convert_reduce_fusion = (f32[3072]{0:T(1024)}, bf16[512,3072]{1,0:T(8,128)(2,1)S(1)}) fusion(f32[512,3072]{1,0:T(8,128)} %get-tuple-element.59, f32[3072]{0:T(1024)S(1)} %reshape.346, bf16[3072,768]{1,0:T(8,128)(2,1)} %all-gather.5.cloned.1.call-done, f32[512,768]{1,0:T(8,128)S(1)} %fusion.51), kind=kOutput, calls=%fused_computation.8 | convolution fusion | flops 2436756480 | bytes 15753216 | tf_op jit(solution)/shard_map/dot_general | solution.py:31
  193.4 7.1 %multiply_reduce_fusion.2 = (f32[768]{0:T(1024)}, f32[512]{0:T(512)S(1)}, f32[512]{0:T(512)S(1)}, f32[768]{0:T(1024)}, f32[512,768]{1,0:T(8,128)S(1)}) fusion(f32[512,768]{1,0:T(8,128)S(1)} %get-tuple-element.57, f32[512]{0:T(512)S(1)} %add_rsqrt_fusion, f32[512]{0:T(512)S(1)} %broadcast_multiply_fusion.4, f32[768]{0:T(1024)S(1)} %reshape.344, ...), kind=kOutput, calls=%fused_computation.52 | convolution fusion | flops 2419455488 | bytes 11027456 | tf_op jit(solution)/shard_map/dot_general | solution.py:31
  202.9 2.1 convolution_convert_fusion
  206.4 4.3 %fusion.32 = bf16[2,256,12,64]{1,3,2,0:T(8,128)(2,1)S(1)} fusion(bf16[2,256,12,64]{1,0,3,2:T(2,128)(2,1)} %reshape.320, f32[2,12,256,256]{2,3,1,0:T(8,128)} %copy-done.1, f32[2,12,256]{2,1,0:T(8,128)S(1)} %get-tuple-element.54), kind=kOutput, calls=%fused_computation.80 | convolution fusion | flops 204865536 | bytes 7888896 | tf_op jit(solution)/shard_map/chqk,cqhd->ckhd/dot_general | solution.py:179
  211.1 3.8 multiply_reduce_fusion
  214.9 4.3 %multiply_convert_fusion = bf16[2,12,256,256]{2,3,1,0:T(8,128)(2,1)S(1)} fusion(f32[2,12,256,256]{2,3,1,0:T(8,128)} %get-tuple-element.62, f32[2,12,256]{2,1,0:T(8,128)S(1)} %get-tuple-element.61, f32[2,12,256,256]{2,3,1,0:T(8,128)S(1)} %bitcast.154, f32[2,12,256]{2,1,0:T(8,128)S(1)} %get-tuple-element.54), kind=kLoop, calls=%fused_computation.9 | loop fusion | flops 6291456 | bytes 15777792 | tf_op jit(solution)/shard_map/convert_element_type | solution.py:186
  223.0 5.0 %add_convert_fusion = bf16[512,768]{1,0:T(8,128)(2,1)S(1)} fusion(f32[512,768]{1,0:T(8,128)S(1)} %copy-done.7, bf16[512,3072]{1,0:T(8,128)(2,1)S(1)} %copy-done.20, bf16[3072,768]{1,0:T(8,128)(2,1)} %all-gather.5.cloned.1.call-done, f32[768]{0:T(1024)S(1)} %reshape.347), kind=kOutput, calls=%fused_computation.60 | convolution fusion | flops 2417098752 | bytes 10226688 | tf_op jit(solution)/shard_map/dot_general | solution.py:21
  231.4 3.5 copy.127
  234.9 3.5 all-to-all-start
  242.7 2.1 copy.135
  245.8 2.3 copy.142
  248.2 5.8 %multiply_reduce_fusion.3 = (f32[768]{0:T(1024)}, f32[512]{0:T(512)S(1)}, f32[512]{0:T(512)S(1)}, f32[768]{0:T(1024)}, f32[512,768]{1,0:T(8,128)S(1)}) fusion(f32[2,256,768]{2,1,0:T(8,128)S(1)} %copy-done.3, f32[512]{0:T(512)S(1)} %bitcast.190, f32[512]{0:T(512)S(1)} %bitcast.193, f32[768]{0:T(1024)S(1)} %reshape.342, ...), kind=kOutput, calls=%fused_computation.53 | convolution fusion | flops 1822553600 | bytes 9061376 | tf_op jit(solution)/shard_map/dot_general | solution.py:31
  260.8 2.4 concatenate.42
  263.2 2.2 copy.163
  265.4 2.3 copy.145
  272.8 3.1 fusion.77
  281.5 2.7 fusion.72
  284.2 10.9 %collective-permute-done.6 = bf16[1,2,1,2,2,24,1536]{6,5,4,3,2,1,0:T(8,128)(2,1)S(1)} collective-permute-done((bf16[1,2,1,2,2,24,1536]{6,5,4,3,2,1,0:T(8,128)(2,1)S(1)}, bf16[1,2,1,2,2,24,1536]{6,5,4,3,2,1,0:T(8,128)(2,1)S(1)}, u32[]{:S(2)}, u32[]{:S(2)}) %collective-permute-start.6) | collective-permute-done | bytes 589856 | tf_op jit(solution)/shard_map/ppermute | solution.py:119
  300.4 3.5 collective-permute-done.7
  304.0 3.5 collective-permute-start.8
  309.3 4.1 collective-permute-done.8
  322.4 15.0 %collective-permute-done.11 = bf16[1,2,1,2,2,24,2304]{6,5,4,3,2,1,0:T(8,128)(2,1)} collective-permute-done((bf16[1,2,1,2,2,24,2304]{6,5,4,3,2,1,0:T(8,128)(2,1)}, bf16[1,2,1,2,2,24,2304]{6,5,4,3,2,1,0:T(8,128)(2,1)}, u32[]{:S(2)}, u32[]{:S(2)}) %collective-permute-start.11) | collective-permute-done | bytes 884768 | tf_op jit(solution)/shard_map/ppermute | solution.py:119
  339.3 4.0 convert_add_fusion.1
  344.8 4.8 %collective-permute-done.12 = bf16[1,2,1,2,1,24,2304]{6,5,4,3,2,1,0:T(8,128)(2,1)S(1)} collective-permute-done((bf16[1,2,1,2,1,24,2304]{6,5,4,3,2,1,0:T(8,128)(2,1)S(1)}, bf16[1,2,1,2,1,24,2304]{6,5,4,3,2,1,0:T(8,128)(2,1)S(1)}, u32[]{:S(2)}, u32[]{:S(2)}) %collective-permute-start.12) | collective-permute-done | bytes 442400 | tf_op jit(solution)/shard_map/ppermute | solution.py:119
  351.7 2.4 convert_add_fusion
  354.9 5.6 %collective-permute-done.13 = bf16[1,2,1,1,1,24,2304]{6,5,4,3,2,1,0:T(8,128)(2,1)S(1)} collective-permute-done((bf16[1,2,1,1,1,24,2304]{6,5,4,3,2,1,0:T(8,128)(2,1)S(1)}, bf16[1,2,1,1,1,24,2304]{6,5,4,3,2,1,0:T(8,128)(2,1)S(1)}, u32[]{:S(2)}, u32[]{:S(2)}) %collective-permute-start.13) | collective-permute-done | bytes 221216 | tf_op jit(solution)/shard_map/ppermute | solution.py:119
  362.0 7.5 %collective-permute-done.16 = bf16[1,2,1,2,2,24,3072]{6,5,4,3,2,1,0:T(8,128)(2,1)S(1)} collective-permute-done((bf16[1,2,1,2,2,24,3072]{6,5,4,3,2,1,0:T(8,128)(2,1)S(1)}, bf16[1,2,1,2,2,24,3072]{6,5,4,3,2,1,0:T(8,128)(2,1)S(1)}, u32[]{:S(2)}, u32[]{:S(2)}) %collective-permute-start.16) | collective-permute-done | bytes 1179680 | tf_op jit(solution)/shard_map/ppermute | solution.py:119
  371.0 14.5 %collective-permute-done.14 = bf16[1,1,1,1,1,24,2304]{6,5,4,3,2,1,0:T(8,128)(2,1)S(1)} collective-permute-done((bf16[1,1,1,1,1,24,2304]{6,5,4,3,2,1,0:T(8,128)(2,1)S(1)}, bf16[1,1,1,1,1,24,2304]{6,5,4,3,2,1,0:T(8,128)(2,1)S(1)}, u32[]{:S(2)}, u32[]{:S(2)}) %collective-permute-start.14) | collective-permute-done | bytes 110624 | tf_op jit(solution)/shard_map/ppermute | solution.py:119
  388.1 3.4 copy.128
  391.5 3.4 collective-permute-done.17
  401.0 5.4 %collective-permute-done.18 = bf16[1,1,1,2,1,24,3072]{6,5,4,3,2,1,0:T(8,128)(2,1)S(1)} collective-permute-done((bf16[1,1,1,2,1,24,3072]{6,5,4,3,2,1,0:T(8,128)(2,1)S(1)}, bf16[1,1,1,2,1,24,3072]{6,5,4,3,2,1,0:T(8,128)(2,1)S(1)}, u32[]{:S(2)}, u32[]{:S(2)}) %collective-permute-start.18) | collective-permute-done | bytes 294944 | tf_op jit(solution)/shard_map/ppermute | solution.py:119
  407.2 3.0 collective-permute-done.23
  412.3 2.6 collective-permute-done.19
  (308 shorter events, 104.4 us)
Async XLA Ops:
  7.2 113.2 %all-gather.3.cloned.1.call-start = ((), (), s32[]{:S(2)}) async-start(), calls=%async_computation.2 | async-start | bytes 10543104 | tf_op jit(solution)/shard_map/all_gather | solution.py:247
  10.7 64.0 %copy-start.51 = (s32[2,256]{1,0:T(2,128)S(1)}, s32[2,256]{1,0:T(2,128)}, u32[]{:S(2)}) copy-start(s32[2,256]{1,0:T(2,128)} %param.20) | copy-start | bytes 6148
  10.7 66.8 %copy-start.52 = (s32[2,13]{1,0:T(2,128)S(1)}, s32[2,13]{1,0:T(2,128)}, u32[]{:S(2)}) copy-start(s32[2,13]{1,0:T(2,128)} %param.19) | copy-start | bytes 316
  10.7 8.2 %collective-permute-start = (bf16[1,1,1,1,1,1,8,512]{7,6,4,3,2,1,0,5:T(8,128)(2,1)S(1)}, bf16[1,1,1,1,1,1,8,512]{7,6,4,3,2,1,0,5:T(8,128)(2,1)S(1)}, u32[]{:S(2)}, u32[]{:S(2)}) collective-permute-start(bf16[1,1,1,1,1,1,8,512]{7,6,4,3,2,1,0,5:T(8,128)(2,1)S(1)} %bitcast.185), channel_id=1, source_target_pairs={{0,2},{1,3},{2,0},{3,1},{4,6},{5,7},{6,4},{7,5},{8,10},{9,11},{10,... | collective-permute-start | bytes 24584 | tf_op jit(solution)/shard_map/ppermute | solution.py:133
  14.8 71.2 %all-to-all-start.1 = ((bf16[64,32,512]{2,1,0:T(8,128)(2,1)}), bf16[64,32,512]{2,1,0:T(8,128)(2,1)}, u32[]{:S(2)}, u32[]{:S(2)}) async-start(bf16[64,32,512]{2,1,0:T(8,128)(2,1)} %param.35), calls=%async_computation.1 | async-start | bytes 4194304 | tf_op jit(solution)/shard_map/all_to_all | solution.py:303
  18.8 60.7 %copy-start.23 = (bf16[2,256,768]{2,1,0:T(8,128)(2,1)S(1)}, bf16[2,256,768]{2,1,0:T(8,128)(2,1)}, u32[]{:S(2)}) copy-start(bf16[2,256,768]{2,1,0:T(8,128)(2,1)} %param.18) | copy-start | bytes 2359300
  18.8 166.5 %all-gather.5.cloned.1.call-start = ((), (), s32[]{:S(2)}) async-start(), calls=%async_computation.3 | async-start | bytes 4866048 | tf_op jit(solution)/shard_map/all_gather | solution.py:254
  18.9 50.1 %collective-permute-start.1 = (bf16[1,1,1,2,1,1,8,512]{7,6,4,3,2,1,0,5:T(8,128)(2,1)S(1)}, bf16[1,1,1,2,1,1,8,512]{7,6,4,3,2,1,0,5:T(8,128)(2,1)S(1)}, u32[]{:S(2)}, u32[]{:S(2)}) collective-permute-start(bf16[1,1,1,2,1,1,8,512]{7,6,4,3,2,1,0,5:T(8,128)(2,1)S(1)} %pad_maximum_fusion.9), channel_id=1, source_target_pairs={{0,1},{1,0},{2,3},{3,2},{4,5},{5,4},{6,7},{7,6},{8,9},{9,8},{10,11... | collective-permute-start | bytes 49160 | tf_op jit(solution)/shard_map/ppermute | solution.py:133
  69.0 4.0 collective-permute-start.2
  73.0 4.3 %collective-permute-start.3 = (bf16[2,1,1,2,2,1,8,512]{7,6,4,3,2,1,0,5:T(8,128)(2,1)S(1)}, bf16[2,1,1,2,2,1,8,512]{7,6,4,3,2,1,0,5:T(8,128)(2,1)S(1)}, u32[]{:S(2)}, u32[]{:S(2)}) collective-permute-start(bf16[2,1,1,2,2,1,8,512]{7,6,4,3,2,1,0,5:T(8,128)(2,1)S(1)} %pad_maximum_fusion.7), channel_id=1, source_target_pairs={{0,8},{1,9},{2,10},{3,11},{4,12},{5,13},{6,14},{7,15},{8,0},{9,1},... | collective-permute-start | bytes 196616 | tf_op jit(solution)/shard_map/ppermute | solution.py:133
  77.4 1.4 collective-permute-start.4
  80.1 64.3 %copy-start.2 = (f32[2,256,768]{2,1,0:T(8,128)}, f32[2,256,768]{2,1,0:T(8,128)S(1)}, u32[]{:S(2)}) copy-start(f32[2,256,768]{2,1,0:T(8,128)S(1)} %get-tuple-element.27) | copy-start | bytes 4718596
  80.4 67.7 %copy-start.45 = (f32[768]{0:T(1024)}, f32[768]{0:T(1024)S(1)}, u32[]{:S(2)}) copy-start(f32[768]{0:T(1024)S(1)} %reshape.345) | copy-start | bytes 9220
  80.5 120.1 %copy-start.39 = (f32[768]{0:T(1024)}, f32[768]{0:T(1024)S(1)}, u32[]{:S(2)}) copy-start(f32[768]{0:T(1024)S(1)} %reshape.344) | copy-start | bytes 9220
  81.1 44.7 %copy-start.24 = (bf16[512,768]{1,0:T(8,128)(2,1)}, bf16[512,768]{1,0:T(8,128)(2,1)S(1)}, u32[]{:S(2)}) copy-start(bf16[512,768]{1,0:T(8,128)(2,1)S(1)} %add_convert_fusion.2) | copy-start | bytes 2359300
  135.4 9.0 %slice-start.5 = ((s8[10223616]{0:T(1024)(128)(4,1)}), s8[1835008]{0:T(1024)(128)(4,1)S(1)}, s32[]{:S(2)}) async-start(s8[10223616]{0:T(1024)(128)(4,1)} %bitcast.182), calls=%async_computation.9 | async-start | bytes 3670016
  147.1 53.4 %copy-start.6 = (f32[512,768]{1,0:T(8,128)}, f32[512,768]{1,0:T(8,128)S(1)}, u32[]{:S(2)}) copy-start(f32[512,768]{1,0:T(8,128)S(1)} %get-tuple-element.57) | copy-start | bytes 4718596
  147.2 53.4 %copy-start.37 = (f32[512]{0:T(512)}, f32[512]{0:T(512)S(1)}, u32[]{:S(2)}) copy-start(f32[512]{0:T(512)S(1)} %broadcast_multiply_fusion.4) | copy-start | bytes 6148
  147.5 53.1 %copy-start.43 = (f32[512]{0:T(512)}, f32[512]{0:T(512)S(1)}, u32[]{:S(2)}) copy-start(f32[512]{0:T(512)S(1)} %add_rsqrt_fusion) | copy-start | bytes 6148
  148.1 52.5 %copy-start.4 = (f32[512,768]{1,0:T(8,128)}, f32[512,768]{1,0:T(8,128)S(1)}, u32[]{:S(2)}) copy-start(f32[512,768]{1,0:T(8,128)S(1)} %fusion.51) | copy-start | bytes 4718596
  193.4 7.1 %copy-start.53 = (bf16[512,3072]{1,0:T(8,128)(2,1)}, bf16[512,3072]{1,0:T(8,128)(2,1)S(1)}, u32[]{:S(2)}) copy-start(bf16[512,3072]{1,0:T(8,128)(2,1)S(1)} %get-tuple-element.65) | copy-start | bytes 9437188
  234.9 153.2 %all-to-all-start = ((bf16[2,1024,512]{2,0,1:T(2,128)(2,1)}), bf16[2,1024,512]{2,0,1:T(2,128)(2,1)}, u32[]{:S(2)}, u32[]{:S(2)}) async-start(bf16[2,1024,512]{2,0,1:T(2,128)(2,1)} %copy.127), calls=%async_computation | async-start | bytes 4194304 | tf_op jit(solution)/shard_map/all_to_all | solution.py:302
  260.8 6.9 %copy-start.10 = (f32[512,768]{1,0:T(8,128)S(1)}, f32[512,768]{1,0:T(8,128)}, u32[]{:S(2)}) copy-start(f32[512,768]{1,0:T(8,128)} %copy-done.8) | copy-start | bytes 4718596
  271.7 6.3 %collective-permute-start.5 = (bf16[2,2,1,2,2,24,1536]{6,5,4,3,2,1,0:T(8,128)(2,1)S(1)}, bf16[2,2,1,2,2,24,1536]{6,5,4,3,2,1,0:T(8,128)(2,1)S(1)}, u32[]{:S(2)}, u32[]{:S(2)}) collective-permute-start(bf16[2,2,1,2,2,24,1536]{6,5,4,3,2,1,0:T(8,128)(2,1)S(1)} %dynamic-slice_convert_fusion.5), channel_id=1, source_target_pairs={{0,4},{1,5},{2,6},{3,7},{4,0},{5,1},{6,2},{7,3},{8,12},{9,13},{10,... | collective-permute-start | bytes 3538952 | tf_op jit(solution)/shard_map/ppermute | solution.py:119
  275.9 20.6 %copy-start.19 = (f32[768,3072]{1,0:T(8,128)}, f32[768,3072]{1,0:T(8,128)S(1)}, u32[]{:S(2)}) copy-start(f32[768,3072]{1,0:T(8,128)S(1)} %fusion.77) | copy-start | bytes 28311556
  278.4 16.6 %collective-permute-start.6 = (bf16[1,2,1,2,2,24,1536]{6,5,4,3,2,1,0:T(8,128)(2,1)S(1)}, bf16[1,2,1,2,2,24,1536]{6,5,4,3,2,1,0:T(8,128)(2,1)S(1)}, u32[]{:S(2)}, u32[]{:S(2)}) collective-permute-start(bf16[1,2,1,2,2,24,1536]{6,5,4,3,2,1,0:T(8,128)(2,1)S(1)} %dynamic-slice_convert_fusion.9), channel_id=1, source_target_pairs={{0,16},{1,17},{2,18},{3,19},{4,20},{5,21},{6,22},{7,23},{8,24},{9,... | collective-permute-start | bytes 1769480 | tf_op jit(solution)/shard_map/ppermute | solution.py:119
  280.3 27.2 %collective-permute-start.10 = (bf16[2,2,1,2,2,24,2304]{6,5,4,3,2,1,0:T(8,128)(2,1)S(1)}, bf16[2,2,1,2,2,24,2304]{6,5,4,3,2,1,0:T(8,128)(2,1)}, u32[]{:S(2)}, u32[]{:S(2)}) collective-permute-start(bf16[2,2,1,2,2,24,2304]{6,5,4,3,2,1,0:T(8,128)(2,1)S(1)} %dynamic-slice_convert_fusion.2), channel_id=1, source_target_pairs={{0,4},{1,5},{2,6},{3,7},{4,0},{5,1},{6,2},{7,3},{8,12},{9,13},{10,... | collective-permute-start | bytes 5308424 | tf_op jit(solution)/shard_map/ppermute | solution.py:119
  284.1 19.8 %copy-start = (f32[3072,768]{1,0:T(8,128)}, f32[3072,768]{1,0:T(8,128)S(1)}, u32[]{:S(2)}) copy-start(f32[3072,768]{1,0:T(8,128)S(1)} %fusion.72) | copy-start | bytes 28311556
  295.3 8.6 %collective-permute-start.7 = (bf16[1,2,1,2,1,24,1536]{6,5,4,3,2,1,0:T(8,128)(2,1)S(1)}, bf16[1,2,1,2,1,24,1536]{6,5,4,3,2,1,0:T(8,128)(2,1)S(1)}, u32[]{:S(2)}, u32[]{:S(2)}) collective-permute-start(bf16[1,2,1,2,1,24,1536]{6,5,4,3,2,1,0:T(8,128)(2,1)S(1)} %dynamic-slice_convert_fusion.13), channel_id=1, source_target_pairs={{0,1},{1,0},{2,3},{3,2},{4,5},{5,4},{6,7},{7,6},{8,9},{9,8},{10,11... | collective-permute-start | bytes 884744 | tf_op jit(solution)/shard_map/ppermute | solution.py:119
  298.2 41.2 %collective-permute-start.15 = (bf16[2,2,1,2,2,24,3072]{6,5,4,3,2,1,0:T(8,128)(2,1)}, bf16[2,2,1,2,2,24,3072]{6,5,4,3,2,1,0:T(8,128)(2,1)}, u32[]{:S(2)}, u32[]{:S(2)}) collective-permute-start(bf16[2,2,1,2,2,24,3072]{6,5,4,3,2,1,0:T(8,128)(2,1)} %dynamic-slice_convert_fusion.1), channel_id=1, source_target_pairs={{0,4},{1,5},{2,6},{3,7},{4,0},{5,1},{6,2},{7,3},{8,12},{9,13},{10,... | collective-permute-start | bytes 7077896 | tf_op jit(solution)/shard_map/ppermute | solution.py:119
  299.9 51.7 %collective-permute-start.20 = (bf16[2,2,1,2,2,96,768]{6,5,4,3,2,1,0:T(8,128)(2,1)}, bf16[2,2,1,2,2,96,768]{6,5,4,3,2,1,0:T(8,128)(2,1)}, u32[]{:S(2)}, u32[]{:S(2)}) collective-permute-start(bf16[2,2,1,2,2,96,768]{6,5,4,3,2,1,0:T(8,128)(2,1)} %dynamic-slice_convert_fusion), channel_id=1, source_target_pairs={{0,4},{1,5},{2,6},{3,7},{4,0},{5,1},{6,2},{7,3},{8,12},{9,13},{10,... | collective-permute-start | bytes 7077896 | tf_op jit(solution)/shard_map/ppermute | solution.py:119
  304.0 9.5 %collective-permute-start.8 = (bf16[1,2,1,1,1,24,1536]{6,5,4,3,2,1,0:T(8,128)(2,1)S(1)}, bf16[1,2,1,1,1,24,1536]{6,5,4,3,2,1,0:T(8,128)(2,1)S(1)}, u32[]{:S(2)}, u32[]{:S(2)}) collective-permute-start(bf16[1,2,1,1,1,24,1536]{6,5,4,3,2,1,0:T(8,128)(2,1)S(1)} %dynamic-slice_convert_fusion.17), channel_id=1, source_target_pairs={{0,2},{1,3},{2,0},{3,1},{4,6},{5,7},{6,4},{7,5},{8,10},{9,11},{10,... | collective-permute-start | bytes 442376 | tf_op jit(solution)/shard_map/ppermute | solution.py:119
  313.5 4.4 %collective-permute-start.9 = (bf16[1,1,1,1,1,24,1536]{6,5,4,3,2,1,0:T(8,128)(2,1)S(1)}, bf16[1,1,1,1,1,24,1536]{6,5,4,3,2,1,0:T(8,128)(2,1)S(1)}, u32[]{:S(2)}, u32[]{:S(2)}) collective-permute-start(bf16[1,1,1,1,1,24,1536]{6,5,4,3,2,1,0:T(8,128)(2,1)S(1)} %dynamic-slice_convert_fusion.19), channel_id=1, source_target_pairs={{0,8},{1,9},{2,10},{3,11},{4,12},{5,13},{6,14},{7,15},{8,0},{9,1},... | collective-permute-start | bytes 221192 | tf_op jit(solution)/shard_map/ppermute | solution.py:119
  316.1 21.3 %collective-permute-start.11 = (bf16[1,2,1,2,2,24,2304]{6,5,4,3,2,1,0:T(8,128)(2,1)}, bf16[1,2,1,2,2,24,2304]{6,5,4,3,2,1,0:T(8,128)(2,1)}, u32[]{:S(2)}, u32[]{:S(2)}) collective-permute-start(bf16[1,2,1,2,2,24,2304]{6,5,4,3,2,1,0:T(8,128)(2,1)} %dynamic-slice_convert_fusion.6), channel_id=1, source_target_pairs={{0,16},{1,17},{2,18},{3,19},{4,20},{5,21},{6,22},{7,23},{8,24},{9,... | collective-permute-start | bytes 2654216 | tf_op jit(solution)/shard_map/ppermute | solution.py:119
  338.8 12.9 %slice-start = ((s8[9437184]{0:T(1024)(128)(4,1)}), s8[4194304]{0:T(1024)(128)(4,1)S(1)}, s32[]{:S(2)}) async-start(s8[9437184]{0:T(1024)(128)(4,1)} %bitcast.150), calls=%async_computation.4 | async-start | bytes 8388608
  338.8 12.8 %slice-start.1 = ((s8[9437184]{0:T(1024)(128)(4,1)}), s8[4194304]{0:T(1024)(128)(4,1)S(1)}, s32[]{:S(2)}) async-start(s8[9437184]{0:T(1024)(128)(4,1)} %bitcast.150), calls=%async_computation.5 | async-start | bytes 8388608
  338.8 12.8 %slice-start.2 = ((s8[9437184]{0:T(1024)(128)(4,1)}), s8[1048576]{0:T(1024)(128)(4,1)S(1)}, s32[]{:S(2)}) async-start(s8[9437184]{0:T(1024)(128)(4,1)} %bitcast.150), calls=%async_computation.6 | async-start | bytes 2097152
  338.9 10.8 %collective-permute-start.12 = (bf16[1,2,1,2,1,24,2304]{6,5,4,3,2,1,0:T(8,128)(2,1)S(1)}, bf16[1,2,1,2,1,24,2304]{6,5,4,3,2,1,0:T(8,128)(2,1)S(1)}, u32[]{:S(2)}, u32[]{:S(2)}) collective-permute-start(bf16[1,2,1,2,1,24,2304]{6,5,4,3,2,1,0:T(8,128)(2,1)S(1)} %dynamic-slice_convert_fusion.10), channel_id=1, source_target_pairs={{0,1},{1,0},{2,3},{3,2},{4,5},{5,4},{6,7},{7,6},{8,9},{9,8},{10,11... | collective-permute-start | bytes 1327112 | tf_op jit(solution)/shard_map/ppermute | solution.py:119
  343.5 26.0 %collective-permute-start.16 = (bf16[1,2,1,2,2,24,3072]{6,5,4,3,2,1,0:T(8,128)(2,1)S(1)}, bf16[1,2,1,2,2,24,3072]{6,5,4,3,2,1,0:T(8,128)(2,1)S(1)}, u32[]{:S(2)}, u32[]{:S(2)}) collective-permute-start(bf16[1,2,1,2,2,24,3072]{6,5,4,3,2,1,0:T(8,128)(2,1)S(1)} %dynamic-slice_convert_fusion.4), channel_id=1, source_target_pairs={{0,16},{1,17},{2,18},{3,19},{4,20},{5,21},{6,22},{7,23},{8,24},{9,... | collective-permute-start | bytes 3538952 | tf_op jit(solution)/shard_map/ppermute | solution.py:119
  349.7 10.8 %collective-permute-start.13 = (bf16[1,2,1,1,1,24,2304]{6,5,4,3,2,1,0:T(8,128)(2,1)S(1)}, bf16[1,2,1,1,1,24,2304]{6,5,4,3,2,1,0:T(8,128)(2,1)S(1)}, u32[]{:S(2)}, u32[]{:S(2)}) collective-permute-start(bf16[1,2,1,1,1,24,2304]{6,5,4,3,2,1,0:T(8,128)(2,1)S(1)} %dynamic-slice_convert_fusion.14), channel_id=1, source_target_pairs={{0,2},{1,3},{2,0},{3,1},{4,6},{5,7},{6,4},{7,5},{8,10},{9,11},{10,... | collective-permute-start | bytes 663560 | tf_op jit(solution)/shard_map/ppermute | solution.py:119
  354.2 32.0 %collective-permute-start.21 = (bf16[2,1,1,2,2,96,768]{6,5,4,3,2,1,0:T(8,128)(2,1)S(1)}, bf16[2,1,1,2,2,96,768]{6,5,4,3,2,1,0:T(8,128)(2,1)S(1)}, u32[]{:S(2)}, u32[]{:S(2)}) collective-permute-start(bf16[2,1,1,2,2,96,768]{6,5,4,3,2,1,0:T(8,128)(2,1)S(1)} %dynamic-slice_convert_fusion.3), channel_id=1, source_target_pairs={{0,8},{1,9},{2,10},{3,11},{4,12},{5,13},{6,14},{7,15},{8,0},{9,1},... | collective-permute-start | bytes 3538952 | tf_op jit(solution)/shard_map/ppermute | solution.py:119
  360.6 24.9 %collective-permute-start.14 = (bf16[1,1,1,1,1,24,2304]{6,5,4,3,2,1,0:T(8,128)(2,1)S(1)}, bf16[1,1,1,1,1,24,2304]{6,5,4,3,2,1,0:T(8,128)(2,1)S(1)}, u32[]{:S(2)}, u32[]{:S(2)}) collective-permute-start(bf16[1,1,1,1,1,24,2304]{6,5,4,3,2,1,0:T(8,128)(2,1)S(1)} %dynamic-slice_convert_fusion.18), channel_id=1, source_target_pairs={{0,8},{1,9},{2,10},{3,11},{4,12},{5,13},{6,14},{7,15},{8,0},{9,1},... | collective-permute-start | bytes 331784 | tf_op jit(solution)/shard_map/ppermute | solution.py:119
  369.9 25.0 %collective-permute-start.17 = (bf16[1,1,1,2,2,24,3072]{6,5,4,3,2,1,0:T(8,128)(2,1)S(1)}, bf16[1,1,1,2,2,24,3072]{6,5,4,3,2,1,0:T(8,128)(2,1)}, u32[]{:S(2)}, u32[]{:S(2)}) collective-permute-start(bf16[1,1,1,2,2,24,3072]{6,5,4,3,2,1,0:T(8,128)(2,1)S(1)} %dynamic-slice_convert_fusion.8), channel_id=1, source_target_pairs={{0,8},{1,9},{2,10},{3,11},{4,12},{5,13},{6,14},{7,15},{8,0},{9,1},... | collective-permute-start | bytes 1769480 | tf_op jit(solution)/shard_map/ppermute | solution.py:119
  387.9 10.1 %collective-permute-start.22 = (bf16[1,1,1,2,2,96,768]{6,5,4,3,2,1,0:T(8,128)(2,1)S(1)}, bf16[1,1,1,2,2,96,768]{6,5,4,3,2,1,0:T(8,128)(2,1)}, u32[]{:S(2)}, u32[]{:S(2)}) collective-permute-start(bf16[1,1,1,2,2,96,768]{6,5,4,3,2,1,0:T(8,128)(2,1)S(1)} %dynamic-slice_convert_fusion.7), channel_id=1, source_target_pairs={{0,16},{1,17},{2,18},{3,19},{4,20},{5,21},{6,22},{7,23},{8,24},{9,... | collective-permute-start | bytes 1769480 | tf_op jit(solution)/shard_map/ppermute | solution.py:119
  396.1 10.4 %collective-permute-start.18 = (bf16[1,1,1,2,1,24,3072]{6,5,4,3,2,1,0:T(8,128)(2,1)S(1)}, bf16[1,1,1,2,1,24,3072]{6,5,4,3,2,1,0:T(8,128)(2,1)S(1)}, u32[]{:S(2)}, u32[]{:S(2)}) collective-permute-start(bf16[1,1,1,2,1,24,3072]{6,5,4,3,2,1,0:T(8,128)(2,1)S(1)} %dynamic-slice_convert_fusion.12), channel_id=1, source_target_pairs={{0,1},{1,0},{2,3},{3,2},{4,5},{5,4},{6,7},{7,6},{8,9},{9,8},{10,11... | collective-permute-start | bytes 884744 | tf_op jit(solution)/shard_map/ppermute | solution.py:119
  399.2 10.9 %collective-permute-start.23 = (bf16[1,1,1,2,1,96,768]{6,5,4,3,2,1,0:T(8,128)(2,1)S(1)}, bf16[1,1,1,2,1,96,768]{6,5,4,3,2,1,0:T(8,128)(2,1)S(1)}, u32[]{:S(2)}, u32[]{:S(2)}) collective-permute-start(bf16[1,1,1,2,1,96,768]{6,5,4,3,2,1,0:T(8,128)(2,1)S(1)} %dynamic-slice_convert_fusion.11), channel_id=1, source_target_pairs={{0,1},{1,0},{2,3},{3,2},{4,5},{5,4},{6,7},{7,6},{8,9},{9,8},{10,11... | collective-permute-start | bytes 884744 | tf_op jit(solution)/shard_map/ppermute | solution.py:119
  406.6 8.4 %collective-permute-start.19 = (bf16[1,1,1,1,1,24,3072]{6,5,4,3,2,1,0:T(8,128)(2,1)S(1)}, bf16[1,1,1,1,1,24,3072]{6,5,4,3,2,1,0:T(8,128)(2,1)S(1)}, u32[]{:S(2)}, u32[]{:S(2)}) collective-permute-start(bf16[1,1,1,1,1,24,3072]{6,5,4,3,2,1,0:T(8,128)(2,1)S(1)} %dynamic-slice_convert_fusion.16), channel_id=1, source_target_pairs={{0,2},{1,3},{2,0},{3,1},{4,6},{5,7},{6,4},{7,5},{8,10},{9,11},{10,... | collective-permute-start | bytes 442376 | tf_op jit(solution)/shard_map/ppermute | solution.py:119
  410.2 6.3 %collective-permute-start.24 = (bf16[1,1,1,1,1,96,768]{6,5,4,3,2,1,0:T(8,128)(2,1)S(1)}, bf16[1,1,1,1,1,96,768]{6,5,4,3,2,1,0:T(8,128)(2,1)S(1)}, u32[]{:S(2)}, u32[]{:S(2)}) collective-permute-start(bf16[1,1,1,1,1,96,768]{6,5,4,3,2,1,0:T(8,128)(2,1)S(1)} %dynamic-slice_convert_fusion.15), channel_id=1, source_target_pairs={{0,2},{1,3},{2,0},{3,1},{4,6},{5,7},{6,4},{7,5},{8,10},{9,11},{10,... | collective-permute-start | bytes 442376 | tf_op jit(solution)/shard_map/ppermute | solution.py:119
  (44 other events, 130.8 us)
Sparse Core Ops, SparseCore 0:
  11.4 108.9 all-gather.2
  123.2 62.0 all-gather.4

commit v13 on v12

--- a/solution.py
+++ b/solution.py
@@ -331,16 +331,16 @@
         grad_queries, grad_keys, grad_values = attend_back(
             queries, key_rows, value_rows, soft_full, soft_low, grad_mixed
         )
-        grad_qkv = jnp.concatenate(
-            [
-                grad_queries.reshape(row_count, D),
-                grad_keys.reshape(row_count, D),
-                grad_values.reshape(row_count, D),
-            ],
-            axis=1,
-        ).astype(jnp.bfloat16)
-        grad_qkv_weight = inner_rows(act_one, grad_qkv)
-        grad_act_one = outer_cols(grad_qkv, qkv_full)
+        grad_parts = [
+            g.reshape(row_count, D).astype(jnp.bfloat16)
+            for g in (grad_queries, grad_keys, grad_values)
+        ]
+        grad_qkv_weight = jnp.concatenate([inner_rows(act_one, g) for g in grad_parts], axis=1)
+        grad_act_one = (
+            outer_cols(grad_parts[0], qkv_full[:, :D])
+            + outer_cols(grad_parts[1], qkv_full[:, D : 2 * D])
+            + outer_cols(grad_parts[2], qkv_full[:, 2 * D :])
+        )
         grad_norm_one, grad_norm1_gain, grad_norm1_bias = norm_backward(
             grad_act_one, normed_one, inverse_one, gain_one.astype(jnp.float32)
         )

time: 429 us -> 460 us (1.072)
  matrix products: 71.1 us -> 84.5 us
  local copies, waits for them, and re-layouts: 66.6 us -> 75 us
  other arithmetic: 32.7 us -> 38.1 us
    all_to_all x1, waiting for transfers between devices: 3.66 us -> 43.8 us  [local(): lax.all_to_all(cot_decoded, AX, split_axis=0, concat_axis=1, tiled=True)]
    ppermute x5, waiting for transfers between devices: 54 us -> 18.5 us  [ag_chain(): moved = lax.ppermute(current, AX, [(i, i ^ 1 << bit) for i in range(n_dev)])]
    concatenate x0 -> x1, local copies, waits for them, and re-layouts: none -> 8.27 us  [local(): jnp.concatenate([inner_rows(act_one, g) for g in grad_parts], axis=1)]
    dot_general x5 -> x7, matrix products: 10.4 us -> 17.3 us  [inner_rows(): lax.dot_general(left_op, right_op, (((0,), (0,)), ((), ())), preferred_el...]
    reshape x3 -> x0, local copies, waits for them, and re-layouts: 4.69 us -> none  [the longest x1 2.35 us: local(): grad_queries.reshape(row_count, D)]
    dot_general x5 -> x7, matrix products: 23.7 us -> 26.4 us  [outer_cols(): lax.dot_general(left_op, right_op, (((1,), (1,)), ((), ())), preferred_el...]
    unnamed x138 -> x142, local copies, waits for them, and re-layouts: 17.9 us -> 20.2 us
  transfers between devices with their start and end apart: 29 -> 29, of which waited for: 22 -> 22; matrix products, arithmetic and copies ran while one was open for 26% -> 27% of each run, Pallas kernels for 0% -> 0%
where the time goes in v13:
time: 460 us; the launch traced here: 455 us
  waiting for transfers between devices  202 us (44%)
  matrix products  84.5 us (18%)
  local copies, waits for them, and re-layouts  75 us (16%)
  starting transfers between devices  40 us (9%)
  other arithmetic  38.1 us (8%)
  between operations  15.6 us (3%)
    ppermute x20, waiting for transfers between devices, rs_chain(): lax.ppermute(send.astype(jnp.bfloat16), AX, [(i, i ^ 1 << bit) for i in r...  80 us
    all_to_all x1, waiting for transfers between devices, local(): lax.all_to_all(cot_decoded, AX, split_axis=0, concat_axis=1, tiled=True)  43.8 us
    all_gather x1, waiting for transfers between devices, local(): outer_full = lax.all_gather(mlp_out, AX, axis=0, tiled=True)  33.6 us
    dot_general x7, matrix products, outer_cols(): lax.dot_general(left_op, right_op, (((1,), (1,)), ((), ())), preferred_el...  26.4 us
    all_gather x1, waiting for transfers between devices, local(): lax.all_gather(jnp.concatenate(wide, axis=1), AX, axis=0, tiled=True)  25.6 us
    ppermute x20, starting transfers between devices, rs_chain(): lax.ppermute(send.astype(jnp.bfloat16), AX, [(i, i ^ 1 << bit) for i in r...  22.7 us
    dot_general x7, matrix products, product(): return jnp.dot(left_op, right_op, preferred_element_type=jnp.float32)  20.2 us
    unnamed x142, local copies, waits for them, and re-layouts  20.2 us
  transfers between devices with their start and end apart: 29, of which 22 were waited for; matrix products, arithmetic and copies ran while one was open for 27% of the time, Pallas kernels for 0%

profile of v13, /device:TPU:0, one launch (start us, length us, event | category | flops | bytes accessed | tf_op | source)
XLA Modules:
  0.0 454.8 jit_solution(8665365627380295420)
XLA Ops:
  10.7 4.1 collective-permute-start
  18.4 5.0 %all-to-all-start.1 = ((bf16[64,32,512]{2,1,0:T(8,128)(2,1)}), bf16[64,32,512]{2,1,0:T(8,128)(2,1)}, u32[]{:S(2)}, u32[]{:S(2)}) async-start(bf16[64,32,512]{2,1,0:T(8,128)(2,1)} %param.35), calls=%async_computation.1 | async-start | bytes 4194304 | tf_op jit(solution)/shard_map/all_to_all | solution.py:303
  25.3 11.6 %collective-permute-done.2 = bf16[1,1,1,2,2,1,8,512]{7,6,4,3,2,1,0,5:T(8,128)(2,1)S(1)} collective-permute-done((bf16[1,1,1,2,2,1,8,512]{7,6,4,3,2,1,0,5:T(8,128)(2,1)S(1)}, bf16[1,1,1,2,2,1,8,512]{7,6,4,3,2,1,0,5:T(8,128)(2,1)S(1)}, u32[]{:S(2)}, u32[]{:S(2)}) %collective-permute-start.2) | collective-permute-done | bytes 32800 | tf_op jit(solution)/shard_map/ppermute | solution.py:133
  38.0 4.2 collective-permute-done.3
  47.3 43.8 %all-to-all-done.1 = bf16[64,32,512]{2,1,0:T(8,128)(2,1)} async-done(((bf16[64,32,512]{2,1,0:T(8,128)(2,1)}), bf16[64,32,512]{2,1,0:T(8,128)(2,1)}, u32[]{:S(2)}, u32[]{:S(2)}) %all-to-all-start.1) | async-done | bytes 2097184 | tf_op jit(solution)/shard_map/all_to_all | solution.py:303
  97.9 25.6 %all-gather.3.cloned.1.call-done = bf16[768,6656]{1,0:T(8,128)(2,1)} async-done(((bf16[24,6656]{1,0:T(8,128)(2,1)}), bf16[768,6656]{1,0:T(8,128)(2,1)}) %all-gather.3.cloned.1.call-update) | async-done | bytes 10223632 | tf_op jit(solution)/shard_map/all_gather | solution.py:247
  129.7 2.6 convolution_convert_fusion.2
  136.7 4.8 %fusion.81 = (f32[2,12,256]{2,1,0:T(8,128)S(1)}, f32[2,12,256,256]{2,3,1,0:T(8,128)S(1)}) fusion(f32[2,12,256,256]{2,3,1,0:T(8,128)S(1)} %fusion.62), kind=kOutput, calls=%fused_computation.189 | output fusion | flops 6291711 | bytes 12607488 | tf_op jit(solution)/shard_map/sub | solution.py:167
  142.2 2.5 copy-done.1
  149.6 5.5 %multiply_convert_fusion.1 = (bf16[512,3072]{1,0:T(8,128)(2,1)}, f32[512,3072]{1,0:T(8,128)}) fusion(f32[3072]{0:T(1024)S(1)} %reshape.405, bf16[768,6656]{1,0:T(8,128)(2,1)S(1)} %bitcast.193, f32[512,768]{1,0:T(8,128)S(1)} %get-tuple-element.59, f32[768]{0:T(1024)S(1)} %reshape.404, f32[768]{0:T(1024)S(1)} %reshape.403, f32[512]{0:T(512)S(1)} %add_rsqrt_fusion, ...), kind=kOutput, calls=%fused_computation.12 | convolution fusion | flops 2427322368 | bytes 15753216 | tf_op jit(solution)/shard_map/dot_general | solution.py:21
  155.1 33.6 %all-gather.5.cloned.1.call-done = bf16[3072,768]{1,0:T(8,128)(2,1)} async-done(((bf16[96,768]{1,0:T(8,128)(2,1)}), bf16[3072,768]{1,0:T(8,128)(2,1)}) %all-gather.5.cloned.1.call-update) | async-done | bytes 4718608 | tf_op jit(solution)/shard_map/all_gather | solution.py:254
  188.8 8.0 %convert_reduce_fusion = (f32[3072]{0:T(1024)}, bf16[512,3072]{1,0:T(8,128)(2,1)S(1)}) fusion(f32[512,3072]{1,0:T(8,128)} %get-tuple-element.61, f32[3072]{0:T(1024)S(1)} %reshape.405, bf16[3072,768]{1,0:T(8,128)(2,1)} %all-gather.5.cloned.1.call-done, f32[512,768]{1,0:T(8,128)S(1)} %fusion.53), kind=kOutput, calls=%fused_computation.9 | convolution fusion | flops 2436756480 | bytes 15753216 | tf_op jit(solution)/shard_map/dot_general | solution.py:31
  196.8 7.1 %multiply_reduce_fusion.2 = (f32[768]{0:T(1024)}, f32[512]{0:T(512)S(1)}, f32[512]{0:T(512)S(1)}, f32[768]{0:T(1024)}, f32[512,768]{1,0:T(8,128)S(1)}) fusion(f32[512,768]{1,0:T(8,128)S(1)} %copy-done.5, f32[512]{0:T(512)S(1)} %add_rsqrt_fusion, f32[512]{0:T(512)S(1)} %broadcast_multiply_fusion.4, f32[768]{0:T(1024)S(1)} %reshape.403, ...), kind=kOutput, calls=%fused_computation.49 | convolution fusion | flops 2419455488 | bytes 11027456 | tf_op jit(solution)/shard_map/dot_general | solution.py:31
  206.3 3.0 convolution_convert_fusion
  209.3 2.3 copy.125
  211.6 3.3 reshape.381
  214.9 5.1 %fusion.28 = bf16[2,256,12,64]{1,3,2,0:T(8,128)(2,1)} fusion(bf16[2,256,12,64]{1,0,3,2:T(2,128)(2,1)} %reshape.381, f32[2,12,256,256]{2,3,1,0:T(8,128)} %copy-done.1, f32[2,12,256]{2,1,0:T(8,128)S(1)} %get-tuple-element.56), kind=kOutput, calls=%fused_computation.78 | convolution fusion | flops 204865536 | bytes 7888896 | tf_op jit(solution)/shard_map/chqk,cqhd->ckhd/dot_general | solution.py:179
  220.1 6.8 %multiply_reduce_fusion = (f32[2,12,256]{2,1,0:T(8,128)S(1)}, f32[2,12,256,256]{2,3,1,0:T(8,128)}) fusion(f32[2,12,256,256]{2,3,1,0:T(8,128)} %copy-done.1, f32[2,12,256]{2,1,0:T(8,128)S(1)} %get-tuple-element.56, bf16[2,256,12,64]{1,0,3,2:T(2,128)(2,1)S(1)} %copy-done.34, bf16[2,256,12,64]{1,0,3,2:T(2,128)(2,1)S(1)} %copy-done.35), kind=kOutput, calls=%fused_computation.11 | convolution fusion | flops 206039040 | bytes 14204928 | tf_op jit(solution)/shard_map/cqhd,ckhd->chqk/dot_general | solution.py:182
  226.9 4.3 multiply_convert_fusion
  235.4 5.0 %add_convert_fusion.1 = bf16[512,768]{1,0:T(8,128)(2,1)S(1)} fusion(f32[512,768]{1,0:T(8,128)S(1)} %copy-done.6, bf16[512,3072]{1,0:T(8,128)(2,1)S(1)} %copy-done.24, bf16[3072,768]{1,0:T(8,128)(2,1)} %all-gather.5.cloned.1.call-done, f32[768]{0:T(1024)S(1)} %reshape.406), kind=kOutput, calls=%fused_computation.58 | convolution fusion | flops 2417098752 | bytes 10226688 | tf_op jit(solution)/shard_map/dot_general | solution.py:21
  243.7 3.5 copy.122
  247.1 3.7 all-to-all-start
  265.9 3.5 multiply_reduce_fusion.3
  276.2 2.3 concatenate.40
  278.6 2.3 copy.154
  286.9 2.4 copy-done.3
  291.7 3.1 pad_maximum_fusion
  294.8 8.3 %copy.138 = f32[768,2304]{1,0:T(8,128)} copy(f32[768,2304]{0,1:T(8,128)} %pad_maximum_fusion) | data formatting | bytes 14155776 | tf_op jit(solution)/shard_map/concatenate | solution.py:338
  303.2 5.4 %fusion.77 = f32[768,3072]{1,0:T(8,128)S(1)} fusion(bf16[512,3072]{1,0:T(8,128)(2,1)} %copy-done.54, f32[512,768]{1,0:T(8,128)} %copy-done.4, f32[768]{0:T(1024)S(1)} %copy-done.49, f32[768]{0:T(1024)S(1)} %copy-done.43, f32[512]{0:T(512)S(1)} %copy-done.47, f32[512]{0:T(512)S(1)} %copy-done.39), kind=kOutput, calls=%fused_computation.185 | convolution fusion | flops 2417885184 | bytes 14166016 | tf_op jit(solution)/shard_map/dot_general | solution.py:25
  308.6 2.7 convert_add_fusion.5
  316.2 2.7 fusion.71
  318.9 8.0 %collective-permute-done.6 = bf16[1,2,1,2,2,24,1536]{6,5,4,3,2,1,0:T(8,128)(2,1)S(1)} collective-permute-done((bf16[1,2,1,2,2,24,1536]{6,5,4,3,2,1,0:T(8,128)(2,1)S(1)}, bf16[1,2,1,2,2,24,1536]{6,5,4,3,2,1,0:T(8,128)(2,1)S(1)}, u32[]{:S(2)}, u32[]{:S(2)}) %collective-permute-start.6) | collective-permute-done | bytes 589856 | tf_op jit(solution)/shard_map/ppermute | solution.py:119
  332.9 2.6 collective-permute-done.7
  335.6 2.6 collective-permute-start.8
  338.6 5.4 %collective-permute-done.8 = bf16[1,2,1,1,1,24,1536]{6,5,4,3,2,1,0:T(8,128)(2,1)S(1)} collective-permute-done((bf16[1,2,1,1,1,24,1536]{6,5,4,3,2,1,0:T(8,128)(2,1)S(1)}, bf16[1,2,1,1,1,24,1536]{6,5,4,3,2,1,0:T(8,128)(2,1)S(1)}, u32[]{:S(2)}, u32[]{:S(2)}) %collective-permute-start.8) | collective-permute-done | bytes 147488 | tf_op jit(solution)/shard_map/ppermute | solution.py:119
  352.9 14.3 %collective-permute-done.11 = bf16[1,2,1,2,2,24,2304]{6,5,4,3,2,1,0:T(8,128)(2,1)} collective-permute-done((bf16[1,2,1,2,2,24,2304]{6,5,4,3,2,1,0:T(8,128)(2,1)}, bf16[1,2,1,2,2,24,2304]{6,5,4,3,2,1,0:T(8,128)(2,1)}, u32[]{:S(2)}, u32[]{:S(2)}) %collective-permute-start.11) | collective-permute-done | bytes 884768 | tf_op jit(solution)/shard_map/ppermute | solution.py:119
  369.3 4.1 convert_add_fusion.1
  375.2 3.5 collective-permute-done.12
  378.8 2.5 collective-permute-start.13
  381.3 2.4 convert_add_fusion
  384.5 4.4 collective-permute-done.13
  389.8 9.2 %collective-permute-done.16 = bf16[1,2,1,2,2,24,3072]{6,5,4,3,2,1,0:T(8,128)(2,1)S(1)} collective-permute-done((bf16[1,2,1,2,2,24,3072]{6,5,4,3,2,1,0:T(8,128)(2,1)S(1)}, bf16[1,2,1,2,2,24,3072]{6,5,4,3,2,1,0:T(8,128)(2,1)S(1)}, u32[]{:S(2)}, u32[]{:S(2)}) %collective-permute-start.16) | collective-permute-done | bytes 1179680 | tf_op jit(solution)/shard_map/ppermute | solution.py:119
  399.9 15.2 %collective-permute-done.14 = bf16[1,1,1,1,1,24,2304]{6,5,4,3,2,1,0:T(8,128)(2,1)S(1)} collective-permute-done((bf16[1,1,1,1,1,24,2304]{6,5,4,3,2,1,0:T(8,128)(2,1)S(1)}, bf16[1,1,1,1,1,24,2304]{6,5,4,3,2,1,0:T(8,128)(2,1)S(1)}, u32[]{:S(2)}, u32[]{:S(2)}) %collective-permute-start.14) | collective-permute-done | bytes 110624 | tf_op jit(solution)/shard_map/ppermute | solution.py:119
  419.2 3.4 copy.123
  430.6 4.3 collective-permute-done.18
  435.1 4.1 collective-permute-done.23
  440.0 2.7 collective-permute-done.19
  443.5 3.5 collective-permute-done.24
  (316 shorter events, 118.7 us)
Async XLA Ops:
  7.2 116.3 %all-gather.3.cloned.1.call-start = ((), (), s32[]{:S(2)}) async-start(), calls=%async_computation.2 | async-start | bytes 10543104 | tf_op jit(solution)/shard_map/all_gather | solution.py:247
  10.7 5.8 %collective-permute-start = (bf16[1,1,1,1,1,1,8,512]{7,6,4,3,2,1,0,5:T(8,128)(2,1)S(1)}, bf16[1,1,1,1,1,1,8,512]{7,6,4,3,2,1,0,5:T(8,128)(2,1)S(1)}, u32[]{:S(2)}, u32[]{:S(2)}) collective-permute-start(bf16[1,1,1,1,1,1,8,512]{7,6,4,3,2,1,0,5:T(8,128)(2,1)S(1)} %bitcast.202), channel_id=1, source_target_pairs={{0,2},{1,3},{2,0},{3,1},{4,6},{5,7},{6,4},{7,5},{8,10},{9,11},{10,... | collective-permute-start | bytes 24584 | tf_op jit(solution)/shard_map/ppermute | solution.py:133
  16.5 21.3 %copy-start.52 = (s32[2,256]{1,0:T(2,128)S(1)}, s32[2,256]{1,0:T(2,128)}, u32[]{:S(2)}) copy-start(s32[2,256]{1,0:T(2,128)} %param.20) | copy-start | bytes 6148
  16.5 25.9 %copy-start.53 = (s32[2,13]{1,0:T(2,128)S(1)}, s32[2,13]{1,0:T(2,128)}, u32[]{:S(2)}) copy-start(s32[2,13]{1,0:T(2,128)} %param.19) | copy-start | bytes 316
  16.5 7.0 %collective-permute-start.1 = (bf16[1,1,1,2,1,1,8,512]{7,6,4,3,2,1,0,5:T(8,128)(2,1)S(1)}, bf16[1,1,1,2,1,1,8,512]{7,6,4,3,2,1,0,5:T(8,128)(2,1)S(1)}, u32[]{:S(2)}, u32[]{:S(2)}) collective-permute-start(bf16[1,1,1,2,1,1,8,512]{7,6,4,3,2,1,0,5:T(8,128)(2,1)S(1)} %pad_maximum_fusion.7), channel_id=1, source_target_pairs={{0,1},{1,0},{2,3},{3,2},{4,5},{5,4},{6,7},{7,6},{8,9},{9,8},{10,11... | collective-permute-start | bytes 49160 | tf_op jit(solution)/shard_map/ppermute | solution.py:133
  18.4 72.6 %all-to-all-start.1 = ((bf16[64,32,512]{2,1,0:T(8,128)(2,1)}), bf16[64,32,512]{2,1,0:T(8,128)(2,1)}, u32[]{:S(2)}, u32[]{:S(2)}) async-start(bf16[64,32,512]{2,1,0:T(8,128)(2,1)} %param.35), calls=%async_computation.1 | async-start | bytes 4194304 | tf_op jit(solution)/shard_map/all_to_all | solution.py:303
  23.4 21.0 %copy-start.17 = (bf16[2,256,768]{2,1,0:T(8,128)(2,1)S(1)}, bf16[2,256,768]{2,1,0:T(8,128)(2,1)}, u32[]{:S(2)}) copy-start(bf16[2,256,768]{2,1,0:T(8,128)(2,1)} %param.18) | copy-start | bytes 2359300
  23.4 165.3 %all-gather.5.cloned.1.call-start = ((), (), s32[]{:S(2)}) async-start(), calls=%async_computation.3 | async-start | bytes 4866048 | tf_op jit(solution)/shard_map/all_gather | solution.py:254
  23.5 13.4 %collective-permute-start.2 = (bf16[1,1,1,2,2,1,8,512]{7,6,4,3,2,1,0,5:T(8,128)(2,1)S(1)}, bf16[1,1,1,2,2,1,8,512]{7,6,4,3,2,1,0,5:T(8,128)(2,1)S(1)}, u32[]{:S(2)}, u32[]{:S(2)}) collective-permute-start(bf16[1,1,1,2,2,1,8,512]{7,6,4,3,2,1,0,5:T(8,128)(2,1)S(1)} %pad_maximum_fusion.6), channel_id=1, source_target_pairs={{0,16},{1,17},{2,18},{3,19},{4,20},{5,21},{6,22},{7,23},{8,24},{9,... | collective-permute-start | bytes 98312 | tf_op jit(solution)/shard_map/ppermute | solution.py:133
  37.0 5.2 %collective-permute-start.3 = (bf16[2,1,1,2,2,1,8,512]{7,6,4,3,2,1,0,5:T(8,128)(2,1)S(1)}, bf16[2,1,1,2,2,1,8,512]{7,6,4,3,2,1,0,5:T(8,128)(2,1)S(1)}, u32[]{:S(2)}, u32[]{:S(2)}) collective-permute-start(bf16[2,1,1,2,2,1,8,512]{7,6,4,3,2,1,0,5:T(8,128)(2,1)S(1)} %pad_maximum_fusion.5), channel_id=1, source_target_pairs={{0,8},{1,9},{2,10},{3,11},{4,12},{5,13},{6,14},{7,15},{8,0},{9,1},... | collective-permute-start | bytes 196616 | tf_op jit(solution)/shard_map/ppermute | solution.py:133
  42.3 1.4 collective-permute-start.4
  45.3 104.2 %copy-start.48 = (f32[768]{0:T(1024)}, f32[768]{0:T(1024)S(1)}, u32[]{:S(2)}) copy-start(f32[768]{0:T(1024)S(1)} %reshape.404) | copy-start | bytes 9220
  45.4 158.5 %copy-start.42 = (f32[768]{0:T(1024)}, f32[768]{0:T(1024)S(1)}, u32[]{:S(2)}) copy-start(f32[768]{0:T(1024)S(1)} %reshape.403) | copy-start | bytes 9220
  47.3 76.2 %copy-start.36 = (bf16[512,768]{1,0:T(8,128)(2,1)}, bf16[512,768]{1,0:T(8,128)(2,1)S(1)}, u32[]{:S(2)}) copy-start(bf16[512,768]{1,0:T(8,128)(2,1)S(1)} %add_convert_fusion.3) | copy-start | bytes 2359300
  136.7 9.0 %slice-start.7 = ((s8[10223616]{0:T(1024)(128)(4,1)}), s8[1835008]{0:T(1024)(128)(4,1)S(1)}, s32[]{:S(2)}) async-start(s8[10223616]{0:T(1024)(128)(4,1)} %bitcast.192), calls=%async_computation.11 | async-start | bytes 3670016
  148.5 55.4 %copy-start.38 = (f32[512]{0:T(512)}, f32[512]{0:T(512)S(1)}, u32[]{:S(2)}) copy-start(f32[512]{0:T(512)S(1)} %broadcast_multiply_fusion.4) | copy-start | bytes 6148
  148.8 55.1 %copy-start.46 = (f32[512]{0:T(512)}, f32[512]{0:T(512)S(1)}, u32[]{:S(2)}) copy-start(f32[512]{0:T(512)S(1)} %add_rsqrt_fusion) | copy-start | bytes 6148
  214.9 12.0 %slice-start.3 = ((s8[6291456]{0:T(1024)(128)(4,1)}), s8[4194304]{0:T(1024)(128)(4,1)S(1)}, s32[]{:S(2)}) async-start(s8[6291456]{0:T(1024)(128)(4,1)} %bitcast.156), calls=%async_computation.7 | async-start | bytes 8388608
  247.1 172.1 %all-to-all-start = ((bf16[2,1024,512]{2,0,1:T(2,128)(2,1)}), bf16[2,1024,512]{2,0,1:T(2,128)(2,1)}, u32[]{:S(2)}, u32[]{:S(2)}) async-start(bf16[2,1024,512]{2,0,1:T(2,128)(2,1)} %copy.122), calls=%async_computation | async-start | bytes 4194304 | tf_op jit(solution)/shard_map/all_to_all | solution.py:302
  290.5 18.1 %collective-permute-start.5 = (bf16[2,2,1,2,2,24,1536]{6,5,4,3,2,1,0:T(8,128)(2,1)}, bf16[2,2,1,2,2,24,1536]{6,5,4,3,2,1,0:T(8,128)(2,1)}, u32[]{:S(2)}, u32[]{:S(2)}) collective-permute-start(bf16[2,2,1,2,2,24,1536]{6,5,4,3,2,1,0:T(8,128)(2,1)} %dynamic-slice_convert_fusion.5), channel_id=1, source_target_pairs={{0,4},{1,5},{2,6},{3,7},{4,0},{5,1},{6,2},{7,3},{8,12},{9,13},{10,... | collective-permute-start | bytes 3538952 | tf_op jit(solution)/shard_map/ppermute | solution.py:119
  294.8 8.3 %copy-start.43 = (f32[768]{0:T(1024)S(1)}, f32[768]{0:T(1024)}, u32[]{:S(2)}) copy-start(f32[768]{0:T(1024)} %copy-done.42) | copy-start | bytes 9220
  294.8 8.3 %copy-start.47 = (f32[512]{0:T(512)S(1)}, f32[512]{0:T(512)}, u32[]{:S(2)}) copy-start(f32[512]{0:T(512)} %copy-done.46) | copy-start | bytes 6148
  294.8 8.3 %copy-start.49 = (f32[768]{0:T(1024)S(1)}, f32[768]{0:T(1024)}, u32[]{:S(2)}) copy-start(f32[768]{0:T(1024)} %copy-done.48) | copy-start | bytes 9220
  294.8 13.8 %slice-start.5 = ((s8[4718592]{0:T(1024)(128)(4,1)}), s8[524288]{0:T(1024)(128)(4,1)S(1)}, s32[]{:S(2)}) async-start(s8[4718592]{0:T(1024)(128)(4,1)} %bitcast.160), calls=%async_computation.9 | async-start | bytes 1048576
  308.6 20.4 %copy-start.23 = (f32[768,3072]{1,0:T(8,128)}, f32[768,3072]{1,0:T(8,128)S(1)}, u32[]{:S(2)}) copy-start(f32[768,3072]{1,0:T(8,128)S(1)} %fusion.77) | copy-start | bytes 28311556
  311.4 15.5 %collective-permute-start.6 = (bf16[1,2,1,2,2,24,1536]{6,5,4,3,2,1,0:T(8,128)(2,1)S(1)}, bf16[1,2,1,2,2,24,1536]{6,5,4,3,2,1,0:T(8,128)(2,1)S(1)}, u32[]{:S(2)}, u32[]{:S(2)}) collective-permute-start(bf16[1,2,1,2,2,24,1536]{6,5,4,3,2,1,0:T(8,128)(2,1)S(1)} %dynamic-slice_convert_fusion.9), channel_id=1, source_target_pairs={{0,16},{1,17},{2,18},{3,19},{4,20},{5,21},{6,22},{7,23},{8,24},{9,... | collective-permute-start | bytes 1769480 | tf_op jit(solution)/shard_map/ppermute | solution.py:119
  315.5 22.7 %collective-permute-start.10 = (bf16[2,2,1,2,2,24,2304]{6,5,4,3,2,1,0:T(8,128)(2,1)S(1)}, bf16[2,2,1,2,2,24,2304]{6,5,4,3,2,1,0:T(8,128)(2,1)S(1)}, u32[]{:S(2)}, u32[]{:S(2)}) collective-permute-start(bf16[2,2,1,2,2,24,2304]{6,5,4,3,2,1,0:T(8,128)(2,1)S(1)} %dynamic-slice_convert_fusion.2), channel_id=1, source_target_pairs={{0,4},{1,5},{2,6},{3,7},{4,0},{5,1},{6,2},{7,3},{8,12},{9,13},{10,... | collective-permute-start | bytes 5308424 | tf_op jit(solution)/shard_map/ppermute | solution.py:119
  318.9 13.5 %copy-start = (f32[3072,768]{1,0:T(8,128)}, f32[3072,768]{1,0:T(8,128)S(1)}, u32[]{:S(2)}) copy-start(f32[3072,768]{1,0:T(8,128)S(1)} %fusion.71) | copy-start | bytes 28311556
  327.2 8.4 %collective-permute-start.7 = (bf16[1,2,1,2,1,24,1536]{6,5,4,3,2,1,0:T(8,128)(2,1)S(1)}, bf16[1,2,1,2,1,24,1536]{6,5,4,3,2,1,0:T(8,128)(2,1)S(1)}, u32[]{:S(2)}, u32[]{:S(2)}) collective-permute-start(bf16[1,2,1,2,1,24,1536]{6,5,4,3,2,1,0:T(8,128)(2,1)S(1)} %dynamic-slice_convert_fusion.13), channel_id=1, source_target_pairs={{0,1},{1,0},{2,3},{3,2},{4,5},{5,4},{6,7},{7,6},{8,9},{9,8},{10,11... | collective-permute-start | bytes 884744 | tf_op jit(solution)/shard_map/ppermute | solution.py:119
  330.6 38.7 %collective-permute-start.15 = (bf16[2,2,1,2,2,24,3072]{6,5,4,3,2,1,0:T(8,128)(2,1)}, bf16[2,2,1,2,2,24,3072]{6,5,4,3,2,1,0:T(8,128)(2,1)}, u32[]{:S(2)}, u32[]{:S(2)}) collective-permute-start(bf16[2,2,1,2,2,24,3072]{6,5,4,3,2,1,0:T(8,128)(2,1)} %dynamic-slice_convert_fusion.1), channel_id=1, source_target_pairs={{0,4},{1,5},{2,6},{3,7},{4,0},{5,1},{6,2},{7,3},{8,12},{9,13},{10,... | collective-permute-start | bytes 7077896 | tf_op jit(solution)/shard_map/ppermute | solution.py:119
  332.4 48.9 %collective-permute-start.20 = (bf16[2,2,1,2,2,96,768]{6,5,4,3,2,1,0:T(8,128)(2,1)}, bf16[2,2,1,2,2,96,768]{6,5,4,3,2,1,0:T(8,128)(2,1)}, u32[]{:S(2)}, u32[]{:S(2)}) collective-permute-start(bf16[2,2,1,2,2,96,768]{6,5,4,3,2,1,0:T(8,128)(2,1)} %dynamic-slice_convert_fusion), channel_id=1, source_target_pairs={{0,4},{1,5},{2,6},{3,7},{4,0},{5,1},{6,2},{7,3},{8,12},{9,13},{10,... | collective-permute-start | bytes 7077896 | tf_op jit(solution)/shard_map/ppermute | solution.py:119
  335.6 8.4 %collective-permute-start.8 = (bf16[1,2,1,1,1,24,1536]{6,5,4,3,2,1,0:T(8,128)(2,1)S(1)}, bf16[1,2,1,1,1,24,1536]{6,5,4,3,2,1,0:T(8,128)(2,1)S(1)}, u32[]{:S(2)}, u32[]{:S(2)}) collective-permute-start(bf16[1,2,1,1,1,24,1536]{6,5,4,3,2,1,0:T(8,128)(2,1)S(1)} %dynamic-slice_convert_fusion.17), channel_id=1, source_target_pairs={{0,2},{1,3},{2,0},{3,1},{4,6},{5,7},{6,4},{7,5},{8,10},{9,11},{10,... | collective-permute-start | bytes 442376 | tf_op jit(solution)/shard_map/ppermute | solution.py:119
  344.1 4.4 collective-permute-start.9
  346.6 20.6 %collective-permute-start.11 = (bf16[1,2,1,2,2,24,2304]{6,5,4,3,2,1,0:T(8,128)(2,1)}, bf16[1,2,1,2,2,24,2304]{6,5,4,3,2,1,0:T(8,128)(2,1)}, u32[]{:S(2)}, u32[]{:S(2)}) collective-permute-start(bf16[1,2,1,2,2,24,2304]{6,5,4,3,2,1,0:T(8,128)(2,1)} %dynamic-slice_convert_fusion.6), channel_id=1, source_target_pairs={{0,16},{1,17},{2,18},{3,19},{4,20},{5,21},{6,22},{7,23},{8,24},{9,... | collective-permute-start | bytes 2654216 | tf_op jit(solution)/shard_map/ppermute | solution.py:119
  368.6 12.7 %slice-start = ((s8[9437184]{0:T(1024)(128)(4,1)}), s8[4194304]{0:T(1024)(128)(4,1)S(1)}, s32[]{:S(2)}) async-start(s8[9437184]{0:T(1024)(128)(4,1)} %bitcast.153), calls=%async_computation.4 | async-start | bytes 8388608
  368.6 12.7 %slice-start.1 = ((s8[9437184]{0:T(1024)(128)(4,1)}), s8[4194304]{0:T(1024)(128)(4,1)S(1)}, s32[]{:S(2)}) async-start(s8[9437184]{0:T(1024)(128)(4,1)} %bitcast.153), calls=%async_computation.5 | async-start | bytes 8388608
  368.7 12.7 %slice-start.2 = ((s8[9437184]{0:T(1024)(128)(4,1)}), s8[1048576]{0:T(1024)(128)(4,1)S(1)}, s32[]{:S(2)}) async-start(s8[9437184]{0:T(1024)(128)(4,1)} %bitcast.153), calls=%async_computation.6 | async-start | bytes 2097152
  368.7 10.0 %collective-permute-start.12 = (bf16[1,2,1,2,1,24,2304]{6,5,4,3,2,1,0:T(8,128)(2,1)S(1)}, bf16[1,2,1,2,1,24,2304]{6,5,4,3,2,1,0:T(8,128)(2,1)S(1)}, u32[]{:S(2)}, u32[]{:S(2)}) collective-permute-start(bf16[1,2,1,2,1,24,2304]{6,5,4,3,2,1,0:T(8,128)(2,1)S(1)} %dynamic-slice_convert_fusion.10), channel_id=1, source_target_pairs={{0,1},{1,0},{2,3},{3,2},{4,5},{5,4},{6,7},{7,6},{8,9},{9,8},{10,11... | collective-permute-start | bytes 1327112 | tf_op jit(solution)/shard_map/ppermute | solution.py:119
  373.6 25.5 %collective-permute-start.16 = (bf16[1,2,1,2,2,24,3072]{6,5,4,3,2,1,0:T(8,128)(2,1)S(1)}, bf16[1,2,1,2,2,24,3072]{6,5,4,3,2,1,0:T(8,128)(2,1)S(1)}, u32[]{:S(2)}, u32[]{:S(2)}) collective-permute-start(bf16[1,2,1,2,2,24,3072]{6,5,4,3,2,1,0:T(8,128)(2,1)S(1)} %dynamic-slice_convert_fusion.4), channel_id=1, source_target_pairs={{0,16},{1,17},{2,18},{3,19},{4,20},{5,21},{6,22},{7,23},{8,24},{9,... | collective-permute-start | bytes 3538952 | tf_op jit(solution)/shard_map/ppermute | solution.py:119
  378.8 10.1 %collective-permute-start.13 = (bf16[1,2,1,1,1,24,2304]{6,5,4,3,2,1,0:T(8,128)(2,1)S(1)}, bf16[1,2,1,1,1,24,2304]{6,5,4,3,2,1,0:T(8,128)(2,1)S(1)}, u32[]{:S(2)}, u32[]{:S(2)}) collective-permute-start(bf16[1,2,1,1,1,24,2304]{6,5,4,3,2,1,0:T(8,128)(2,1)S(1)} %dynamic-slice_convert_fusion.14), channel_id=1, source_target_pairs={{0,2},{1,3},{2,0},{3,1},{4,6},{5,7},{6,4},{7,5},{8,10},{9,11},{10,... | collective-permute-start | bytes 663560 | tf_op jit(solution)/shard_map/ppermute | solution.py:119
  383.9 32.0 %collective-permute-start.21 = (bf16[2,1,1,2,2,96,768]{6,5,4,3,2,1,0:T(8,128)(2,1)S(1)}, bf16[2,1,1,2,2,96,768]{6,5,4,3,2,1,0:T(8,128)(2,1)S(1)}, u32[]{:S(2)}, u32[]{:S(2)}) collective-permute-start(bf16[2,1,1,2,2,96,768]{6,5,4,3,2,1,0:T(8,128)(2,1)S(1)} %dynamic-slice_convert_fusion.3), channel_id=1, source_target_pairs={{0,8},{1,9},{2,10},{3,11},{4,12},{5,13},{6,14},{7,15},{8,0},{9,1},... | collective-permute-start | bytes 3538952 | tf_op jit(solution)/shard_map/ppermute | solution.py:119
  389.0 26.1 %collective-permute-start.14 = (bf16[1,1,1,1,1,24,2304]{6,5,4,3,2,1,0:T(8,128)(2,1)S(1)}, bf16[1,1,1,1,1,24,2304]{6,5,4,3,2,1,0:T(8,128)(2,1)S(1)}, u32[]{:S(2)}, u32[]{:S(2)}) collective-permute-start(bf16[1,1,1,1,1,24,2304]{6,5,4,3,2,1,0:T(8,128)(2,1)S(1)} %dynamic-slice_convert_fusion.18), channel_id=1, source_target_pairs={{0,8},{1,9},{2,10},{3,11},{4,12},{5,13},{6,14},{7,15},{8,0},{9,1},... | collective-permute-start | bytes 331784 | tf_op jit(solution)/shard_map/ppermute | solution.py:119
  399.4 24.5 %collective-permute-start.17 = (bf16[1,1,1,2,2,24,3072]{6,5,4,3,2,1,0:T(8,128)(2,1)S(1)}, bf16[1,1,1,2,2,24,3072]{6,5,4,3,2,1,0:T(8,128)(2,1)}, u32[]{:S(2)}, u32[]{:S(2)}) collective-permute-start(bf16[1,1,1,2,2,24,3072]{6,5,4,3,2,1,0:T(8,128)(2,1)S(1)} %dynamic-slice_convert_fusion.8), channel_id=1, source_target_pairs={{0,8},{1,9},{2,10},{3,11},{4,12},{5,13},{6,14},{7,15},{8,0},{9,1},... | collective-permute-start | bytes 1769480 | tf_op jit(solution)/shard_map/ppermute | solution.py:119
  417.6 10.1 %collective-permute-start.22 = (bf16[1,1,1,2,2,96,768]{6,5,4,3,2,1,0:T(8,128)(2,1)S(1)}, bf16[1,1,1,2,2,96,768]{6,5,4,3,2,1,0:T(8,128)(2,1)}, u32[]{:S(2)}, u32[]{:S(2)}) collective-permute-start(bf16[1,1,1,2,2,96,768]{6,5,4,3,2,1,0:T(8,128)(2,1)S(1)} %dynamic-slice_convert_fusion.7), channel_id=1, source_target_pairs={{0,16},{1,17},{2,18},{3,19},{4,20},{5,21},{6,22},{7,23},{8,24},{9,... | collective-permute-start | bytes 1769480 | tf_op jit(solution)/shard_map/ppermute | solution.py:119
  425.1 9.8 %collective-permute-start.18 = (bf16[1,1,1,2,1,24,3072]{6,5,4,3,2,1,0:T(8,128)(2,1)S(1)}, bf16[1,1,1,2,1,24,3072]{6,5,4,3,2,1,0:T(8,128)(2,1)S(1)}, u32[]{:S(2)}, u32[]{:S(2)}) collective-permute-start(bf16[1,1,1,2,1,24,3072]{6,5,4,3,2,1,0:T(8,128)(2,1)S(1)} %dynamic-slice_convert_fusion.12), channel_id=1, source_target_pairs={{0,1},{1,0},{2,3},{3,2},{4,5},{5,4},{6,7},{7,6},{8,9},{9,8},{10,11... | collective-permute-start | bytes 884744 | tf_op jit(solution)/shard_map/ppermute | solution.py:119
  428.9 10.3 %collective-permute-start.23 = (bf16[1,1,1,2,1,96,768]{6,5,4,3,2,1,0:T(8,128)(2,1)S(1)}, bf16[1,1,1,2,1,96,768]{6,5,4,3,2,1,0:T(8,128)(2,1)S(1)}, u32[]{:S(2)}, u32[]{:S(2)}) collective-permute-start(bf16[1,1,1,2,1,96,768]{6,5,4,3,2,1,0:T(8,128)(2,1)S(1)} %dynamic-slice_convert_fusion.11), channel_id=1, source_target_pairs={{0,1},{1,0},{2,3},{3,2},{4,5},{5,4},{6,7},{7,6},{8,9},{9,8},{10,11... | collective-permute-start | bytes 884744 | tf_op jit(solution)/shard_map/ppermute | solution.py:119
  435.0 7.8 %collective-permute-start.19 = (bf16[1,1,1,1,1,24,3072]{6,5,4,3,2,1,0:T(8,128)(2,1)S(1)}, bf16[1,1,1,1,1,24,3072]{6,5,4,3,2,1,0:T(8,128)(2,1)S(1)}, u32[]{:S(2)}, u32[]{:S(2)}) collective-permute-start(bf16[1,1,1,1,1,24,3072]{6,5,4,3,2,1,0:T(8,128)(2,1)S(1)} %dynamic-slice_convert_fusion.16), channel_id=1, source_target_pairs={{0,2},{1,3},{2,0},{3,1},{4,6},{5,7},{6,4},{7,5},{8,10},{9,11},{10,... | collective-permute-start | bytes 442376 | tf_op jit(solution)/shard_map/ppermute | solution.py:119
  439.3 7.7 %collective-permute-start.24 = (bf16[1,1,1,1,1,96,768]{6,5,4,3,2,1,0:T(8,128)(2,1)S(1)}, bf16[1,1,1,1,1,96,768]{6,5,4,3,2,1,0:T(8,128)(2,1)S(1)}, u32[]{:S(2)}, u32[]{:S(2)}) collective-permute-start(bf16[1,1,1,1,1,96,768]{6,5,4,3,2,1,0:T(8,128)(2,1)S(1)} %dynamic-slice_convert_fusion.15), channel_id=1, source_target_pairs={{0,2},{1,3},{2,0},{3,1},{4,6},{5,7},{6,4},{7,5},{8,10},{9,11},{10,... | collective-permute-start | bytes 442376 | tf_op jit(solution)/shard_map/ppermute | solution.py:119
  (46 other events, 157.7 us)
Sparse Core Ops, SparseCore 0:
  11.4 112.0 all-gather.2
  126.3 62.4 all-gather.4
